TPU v7x, 32 devices: a whole 2x2x4 slice. The times are simulated.
32 devices in a mesh: dp: 8 (over y, x, core), ctx: 4 (over z).
Axes of the slice: x: 2, y: 2, z: 4, core: 2. Of those that a mesh axis runs over, the one named last changes fastest.
Arguments:
- inputs: bfloat16 [16, 1024, 768], P('dp', 'ctx'), may hold values from -6 to 6
- lengths: int32 [16], P('dp'), may hold values from 921 to 1024, as said below
- ln1_gain: bfloat16 [768], P(('dp', 'ctx')), may hold values from 0.5 to 1.5
- ln1_bias: bfloat16 [768], P(('dp', 'ctx')), may hold values from -4 to 4
- query_weight: bfloat16 [768, 768], P(('dp', 'ctx')), may hold values from -0.3125 to 0.3125
- query_bias: bfloat16 [768], P(('dp', 'ctx')), may hold values from -4 to 4
- key_weight: bfloat16 [768, 768], P(('dp', 'ctx')), may hold values from -0.3125 to 0.3125
- value_weight: bfloat16 [768, 768], P(('dp', 'ctx')), may hold values from -0.21875 to 0.21875
- value_bias: bfloat16 [768], P(('dp', 'ctx')), may hold values from -0.75 to 0.75
- out_weight: bfloat16 [768, 768], P(('dp', 'ctx')), may hold values from -1.75 to 1.75
- out_bias: bfloat16 [768], P(('dp', 'ctx')), may hold values from -4 to 4
- ln2_gain: bfloat16 [768], P(('dp', 'ctx')), may hold values from 0.5 to 1.5
- ln2_bias: bfloat16 [768], P(('dp', 'ctx')), may hold values from -4 to 4
- ffn_in_weight: bfloat16 [768, 3072], P(('dp', 'ctx')), may hold values from -0.21875 to 0.21875
- ffn_in_bias: bfloat16 [3072], P(('dp', 'ctx')), may hold values from -4 to 4
- ffn_out_weight: bfloat16 [3072, 768], P(('dp', 'ctx')), may hold values from -0.15625 to 0.15625
- ffn_out_bias: bfloat16 [768], P(('dp', 'ctx')), may hold values from -4 to 4
- out_grad: bfloat16 [16, 1024, 768], P('dp', 'ctx'), may hold values from -6 to 6
Outputs:
- output: bfloat16 [16, 1024, 768], P('dp', 'ctx')
- input_grad: bfloat16 [16, 1024, 768], P('dp', 'ctx')
- grad_ln1_gain: float32 [768], P(('dp', 'ctx'))
- grad_ln1_bias: float32 [768], P(('dp', 'ctx'))
- grad_query: float32 [768, 768], P(('dp', 'ctx'))
- grad_query_bias: float32 [768], P(('dp', 'ctx'))
- grad_key: float32 [768, 768], P(('dp', 'ctx'))
- grad_value: float32 [768, 768], P(('dp', 'ctx'))
- grad_value_bias: float32 [768], P(('dp', 'ctx'))
- grad_out: float32 [768, 768], P(('dp', 'ctx'))
- grad_out_bias: float32 [768], P(('dp', 'ctx'))
- grad_ln2_gain: float32 [768], P(('dp', 'ctx'))
- grad_ln2_bias: float32 [768], P(('dp', 'ctx'))
- grad_ffn_in: float32 [768, 3072], P(('dp', 'ctx'))
- grad_ffn_in_bias: float32 [3072], P(('dp', 'ctx'))
- grad_ffn_out: float32 [3072, 768], P(('dp', 'ctx'))
- grad_ffn_out_bias: float32 [768], P(('dp', 'ctx'))
Inputs may be any that keep to these rules, and one draw needn't show every extreme that they name: `lengths`: A sequence's molecules occupy positions 0 to its length - 1; some sequence has exactly 1024, some exactly 921.
All inputs are finite; a program needn't handle non-finite values.
Results may differ from a plain program's by a relative error of at most 0.015.
Values may be sent and summed in bfloat16 or wider, within the bound.
No kernel may reach another device: no remote copies, remote signals or barrier semaphores. Data moves between devices by JAX's collectives and lax.ppermute only.
A program may use at most 192 MiB of HBM per device.

v0:
```python
import jax
import jax.numpy as jnp
from jax import lax
from jax.sharding import PartitionSpec as P

H = 12
HD = 64


def layer_norm(tok_rows, gain, shift):
    center = tok_rows - jnp.mean(tok_rows, axis=-1, keepdims=True)
    spread = jnp.mean(center * center, axis=-1, keepdims=True)
    return center * lax.rsqrt(spread + 1e-06) * gain + shift


def gelu_exact(values):
    return jax.nn.gelu(values, approximate=False)


def outer_product(left_rows, right_rows):
    return lax.dot_general(
        left_rows, right_rows, (((0,), (0,)), ((), ())), preferred_element_type=jnp.float32
    )


def back_product(grad_rows, weight):
    return lax.dot_general(
        grad_rows, weight, (((1,), (1,)), ((), ())), preferred_element_type=jnp.float32
    )


def column_sum(grad_rows):
    return jnp.sum(grad_rows.astype(jnp.float32), axis=0)


def fetch(shards):
    return (
        lax.all_gather(shards[0], ("dp", "ctx"), axis=0, tiled=True),
        lax.all_gather(shards[1], ("dp", "ctx"), axis=0, tiled=True),
        lax.all_gather(shards[2], ("dp", "ctx"), axis=0, tiled=True),
        lax.all_gather(shards[3], ("dp", "ctx"), axis=0, tiled=True),
        lax.all_gather(shards[4], ("dp", "ctx"), axis=0, tiled=True),
        lax.all_gather(shards[5], ("dp", "ctx"), axis=0, tiled=True),
        lax.all_gather(shards[6], ("dp", "ctx"), axis=0, tiled=True),
        lax.all_gather(shards[7], ("dp", "ctx"), axis=0, tiled=True),
        lax.all_gather(shards[8], ("dp", "ctx"), axis=0, tiled=True),
        lax.all_gather(shards[9], ("dp", "ctx"), axis=0, tiled=True),
        lax.all_gather(shards[10], ("dp", "ctx"), axis=0, tiled=True),
        lax.all_gather(shards[11], ("dp", "ctx"), axis=0, tiled=True),
        lax.all_gather(shards[12], ("dp", "ctx"), axis=0, tiled=True),
        lax.all_gather(shards[13], ("dp", "ctx"), axis=0, tiled=True),
        lax.all_gather(shards[14], ("dp", "ctx"), axis=0, tiled=True),
    )


def forward(tok_block, length, full_set):
    (
        ln1_gain,
        ln1_bias,
        query_weight,
        query_bias,
        key_weight,
        value_weight,
        value_bias,
        out_weight,
        out_bias,
        ln2_gain,
        ln2_bias,
        ffn_in_weight,
        ffn_in_bias,
        ffn_out_weight,
        ffn_out_bias,
    ) = full_set
    seq_rows = tok_block.shape[0]
    tok_rows = tok_block.astype(jnp.float32)
    normed = layer_norm(
        tok_rows, ln1_gain.astype(jnp.float32), ln1_bias.astype(jnp.float32)
    ).astype(jnp.bfloat16)
    queries = (
        jnp.dot(normed, query_weight, preferred_element_type=jnp.float32)
        + query_bias.astype(jnp.float32)
    ).astype(jnp.bfloat16)
    key_rows = jnp.dot(normed, key_weight, preferred_element_type=jnp.float32).astype(jnp.bfloat16)
    value_rows = (
        jnp.dot(normed, value_weight, preferred_element_type=jnp.float32)
        + value_bias.astype(jnp.float32)
    ).astype(jnp.bfloat16)
    all_keys, all_values = (
        lax.all_gather(key_rows, "ctx", axis=0, tiled=True),
        lax.all_gather(value_rows, "ctx", axis=0, tiled=True),
    )
    total_rows = all_keys.shape[0]
    query_heads = queries.reshape(seq_rows, H, HD)
    key_heads = all_keys.reshape(total_rows, H, HD)
    value_heads = all_values.reshape(total_rows, H, HD)
    scores = jnp.einsum(
        "qhd,khd->hqk", query_heads, key_heads, preferred_element_type=jnp.float32
    ) * HD ** (-0.5)
    valid = jnp.arange(total_rows) < length
    scores = jnp.where(valid[None, None, :], scores, -1e30)
    log_total = jax.nn.logsumexp(scores, axis=-1)
    attn_probs = jax.nn.softmax(scores, axis=-1)
    low_probs = attn_probs.astype(jnp.bfloat16)
    mixed_rows = jnp.einsum(
        "hqk,khd->qhd", low_probs, value_heads, preferred_element_type=jnp.float32
    )
    mixed_rows = mixed_rows.reshape(seq_rows, H * HD).astype(jnp.bfloat16)
    middle = (
        tok_rows
        + jnp.dot(mixed_rows, out_weight, preferred_element_type=jnp.float32)
        + out_bias.astype(jnp.float32)
    )
    normed_two = layer_norm(
        middle, ln2_gain.astype(jnp.float32), ln2_bias.astype(jnp.float32)
    ).astype(jnp.bfloat16)
    ffn_pre = jnp.dot(
        normed_two, ffn_in_weight, preferred_element_type=jnp.float32
    ) + ffn_in_bias.astype(jnp.float32)
    ffn_act = gelu_exact(ffn_pre).astype(jnp.bfloat16)
    result = (
        middle
        + jnp.dot(ffn_act, ffn_out_weight, preferred_element_type=jnp.float32)
        + ffn_out_bias.astype(jnp.float32)
    )
    kept = (
        tok_rows,
        normed,
        query_heads,
        key_heads,
        value_heads,
        attn_probs,
        low_probs,
        mixed_rows,
        middle,
        normed_two,
        ffn_pre,
        ffn_act,
        log_total,
        length,
    )
    return (result.astype(jnp.bfloat16), kept)


def backward(kept, cot_block, full_set):
    (
        ln1_gain,
        ln1_bias,
        query_weight,
        query_bias,
        key_weight,
        value_weight,
        value_bias,
        out_weight,
        out_bias,
        ln2_gain,
        ln2_bias,
        ffn_in_weight,
        ffn_in_bias,
        ffn_out_weight,
        ffn_out_bias,
    ) = full_set
    (
        tok_rows,
        normed,
        query_heads,
        key_heads,
        value_heads,
        attn_probs,
        low_probs,
        mixed_rows,
        middle,
        normed_two,
        ffn_pre,
        ffn_act,
        log_total,
        length,
    ) = kept
    seq_rows = tok_rows.shape[0]
    total_rows = key_heads.shape[0]
    score_scale = HD ** (-0.5)
    d_out = cot_block.astype(jnp.float32)
    d_ffn_out = d_out.astype(jnp.bfloat16)
    grad_ffn_out_bias = column_sum(d_ffn_out)
    grad_ffn_out = outer_product(ffn_act, d_ffn_out)
    d_act = back_product(d_ffn_out, ffn_out_weight)
    unused, gelu_back = jax.vjp(gelu_exact, ffn_pre)
    d_pre = gelu_back(d_act)[0].astype(jnp.bfloat16)
    grad_ffn_in_bias = column_sum(d_pre)
    grad_ffn_in = outer_product(normed_two, d_pre)
    d_normed_two = back_product(d_pre, ffn_in_weight)
    unused, second_back = jax.vjp(
        layer_norm, middle, ln2_gain.astype(jnp.float32), ln2_bias.astype(jnp.float32)
    )
    d_middle, grad_ln2_gain, grad_ln2_bias = second_back(d_normed_two)
    d_middle = d_middle + d_out
    d_branch = d_middle.astype(jnp.bfloat16)
    grad_out_bias = column_sum(d_branch)
    grad_out = outer_product(mixed_rows, d_branch)
    d_mixed = back_product(d_branch, out_weight).astype(jnp.bfloat16).reshape(seq_rows, H, HD)
    d_probs = jnp.einsum("qhd,khd->hqk", d_mixed, value_heads, preferred_element_type=jnp.float32)
    row_inner = jnp.sum(attn_probs * d_probs, axis=-1, keepdims=True)
    d_scores = (attn_probs * (d_probs - row_inner)).astype(jnp.bfloat16)
    d_query = (
        jnp.einsum("hqk,khd->qhd", d_scores, key_heads, preferred_element_type=jnp.float32)
        * score_scale
    )
    d_query = d_query.reshape(seq_rows, H * HD).astype(jnp.bfloat16)
    key_terms = (
        jnp.einsum("hqk,qhd->khd", d_scores, query_heads, preferred_element_type=jnp.float32)
        * score_scale
    )
    value_terms = jnp.einsum("hqk,qhd->khd", low_probs, d_mixed, preferred_element_type=jnp.float32)
    key_sums, value_sums = (
        lax.psum_scatter(
            key_terms.reshape(total_rows, H * HD).astype(jnp.bfloat16),
            "ctx",
            scatter_dimension=0,
            tiled=True,
        ).astype(jnp.float32),
        lax.psum_scatter(
            value_terms.reshape(total_rows, H * HD).astype(jnp.bfloat16),
            "ctx",
            scatter_dimension=0,
            tiled=True,
        ).astype(jnp.float32),
    )
    d_key = key_sums.astype(jnp.bfloat16)
    d_value = value_sums.astype(jnp.bfloat16)
    grad_query_bias = column_sum(d_query)
    grad_value_bias = column_sum(d_value)
    grad_query = outer_product(normed, d_query)
    grad_key = outer_product(normed, d_key)
    grad_value = outer_product(normed, d_value)
    d_normed = (
        back_product(d_query, query_weight)
        + back_product(d_key, key_weight)
        + back_product(d_value, value_weight)
    )
    unused, first_back = jax.vjp(
        layer_norm, tok_rows, ln1_gain.astype(jnp.float32), ln1_bias.astype(jnp.float32)
    )
    d_rows, grad_ln1_gain, grad_ln1_bias = first_back(d_normed)
    d_input = (d_middle + d_rows).astype(jnp.bfloat16)
    grads = (
        grad_ln1_gain,
        grad_ln1_bias,
        grad_query,
        grad_query_bias,
        grad_key,
        grad_value,
        grad_value_bias,
        grad_out,
        grad_out_bias,
        grad_ln2_gain,
        grad_ln2_bias,
        grad_ffn_in,
        grad_ffn_in_bias,
        grad_ffn_out,
        grad_ffn_out_bias,
    )
    return (d_input, grads)


def per_device(
    inputs,
    lengths,
    ln1_gain,
    ln1_bias,
    query_weight,
    query_bias,
    key_weight,
    value_weight,
    value_bias,
    out_weight,
    out_bias,
    ln2_gain,
    ln2_bias,
    ffn_in_weight,
    ffn_in_bias,
    ffn_out_weight,
    ffn_out_bias,
    out_grad,
):
    shards = (
        ln1_gain,
        ln1_bias,
        query_weight,
        query_bias,
        key_weight,
        value_weight,
        value_bias,
        out_weight,
        out_bias,
        ln2_gain,
        ln2_bias,
        ffn_in_weight,
        ffn_in_bias,
        ffn_out_weight,
        ffn_out_bias,
    )

    def forward_step(counter, seq_entry):
        tok_block, length = seq_entry
        result, kept = forward(tok_block, length, fetch(shards))
        return (counter, result)

    counter, output = lax.scan(forward_step, jnp.zeros((), jnp.int32), (inputs, lengths))

    def backward_step(totals, seq_entry):
        tok_block, length, cot_block = seq_entry
        full_set = fetch(shards)
        unused, kept = forward(tok_block, length, full_set)
        d_input, grads = backward(kept, cot_block, full_set)
        return (jax.tree.map(jnp.add, totals, grads), d_input)

    groups = lax.axis_size(("dp", "ctx"))
    start_totals = tuple(
        (
            jnp.zeros((shard_item.shape[0] * groups,) + shard_item.shape[1:], jnp.float32)
            for shard_item in shards
        )
    )
    totals, input_grad = lax.scan(backward_step, start_totals, (inputs, lengths, out_grad))
    grad_shards = lax.psum_scatter(totals, ("dp", "ctx"), scatter_dimension=0, tiled=True)
    return (output, input_grad) + tuple(grad_shards)


def solution(mesh):
    return jax.shard_map(
        per_device,
        mesh=mesh,
        in_specs=(
            P("dp", "ctx", None),
            P("dp"),
            P(("dp", "ctx")),
            P(("dp", "ctx")),
            P(("dp", "ctx"), None),
            P(("dp", "ctx")),
            P(("dp", "ctx"), None),
            P(("dp", "ctx"), None),
            P(("dp", "ctx")),
            P(("dp", "ctx"), None),
            P(("dp", "ctx")),
            P(("dp", "ctx")),
            P(("dp", "ctx")),
            P(("dp", "ctx"), None),
            P(("dp", "ctx")),
            P(("dp", "ctx"), None),
            P(("dp", "ctx")),
            P("dp", "ctx", None),
        ),
        out_specs=(
            P("dp", "ctx", None),
            P("dp", "ctx", None),
            P(("dp", "ctx")),
            P(("dp", "ctx")),
            P(("dp", "ctx"), None),
            P(("dp", "ctx")),
            P(("dp", "ctx"), None),
            P(("dp", "ctx"), None),
            P(("dp", "ctx")),
            P(("dp", "ctx"), None),
            P(("dp", "ctx")),
            P(("dp", "ctx")),
            P(("dp", "ctx")),
            P(("dp", "ctx"), None),
            P(("dp", "ctx")),
            P(("dp", "ctx"), None),
            P(("dp", "ctx")),
        ),
        check_vma=False,
    )
```

profile of v0, /device:TPU:0, one launch (start us, length us, event | category | flops | bytes accessed | tf_op | source)
XLA Modules:
  0.0 2723.2 jit_solution(3749500177245971645)
XLA Ops:
  8.2 888.4 %while.51 = (s32[]{:T(128)}, bf16[2,256,768]{2,1,0:T(8,128)(2,1)S(1)}, bf16[2,256,768]{2,1,0:T(8,128)(2,1)}, bf16[24]{0:T(256)(128)(2,1)}, bf16[24]{0:T(256)(128...) while((s32[]{:T(128)}, ...), condition=%wide.region_7.8_spmd, body=%wide.region_0.7_spmd.sunk | while | flops 4508832256 | bytes 116793320 | solution.py:307
  18.1 42.5 %all-reduce.39 = (bf16[768]{0:T(1024)(128)(2,1)S(1)}, bf16[768]{0:T(1024)(128)(2,1)S(1)}, bf16[768]{0:T(1024)(128)(2,1)S(1)}, bf16[768]{0:T(1024)(128)(2,1)S(1)}...) all-reduce(bf16[768]{0:T(1024)(128)(2,1)S(1)} %dynamic-update-slice, ...), channel_id=1, replica_groups=mesh['dp'=8,'ctx'=4] {'dp','ctx'}, use_global_device_ids=true, to_apply=%add.2 | all-reduce | flops 9216 | bytes 36864 | tf_op jit(solution)/shard_map/while
  71.7 52.9 %all-gather.17.cloned.1.call-done = bf16[768,768]{1,0:T(8,128)(2,1)} async-done(((bf16[24,768]{1,0:T(8,128)(2,1)}), bf16[768,768]{1,0:T(8,128)(2,1)}) %all-gather.17.cloned.1.call-update) | async-done | bytes 1179664 | tf_op jit(solution)/shard_map/while/body/eval_jaxpr/all_gather | solution.py:43
  132.9 47.5 %all-gather.21.cloned.1.call-done = bf16[768,768]{1,0:T(8,128)(2,1)} async-done(((bf16[24,768]{1,0:T(8,128)(2,1)}), bf16[768,768]{1,0:T(8,128)(2,1)}) %all-gather.21.cloned.1.call-update) | async-done | bytes 1179664 | tf_op jit(solution)/shard_map/while/body/eval_jaxpr/all_gather | solution.py:40
  274.2 37.6 %all-gather.27.cloned.1.call-done = bf16[768,768]{1,0:T(8,128)(2,1)} async-done(((bf16[24,768]{1,0:T(8,128)(2,1)}), bf16[768,768]{1,0:T(8,128)(2,1)}) %all-gather.27.cloned.1.call-update) | async-done | bytes 1179664 | tf_op jit(solution)/shard_map/while/body/eval_jaxpr/all_gather | solution.py:45
  313.9 63.2 %all-gather.29.cloned.1.call-done = bf16[3072,768]{1,0:T(8,128)(2,1)} async-done(((bf16[96,768]{1,0:T(8,128)(2,1)}), bf16[3072,768]{1,0:T(8,128)(2,1)}) %all-gather.29.cloned.1.call-update) | async-done | bytes 4718608 | tf_op jit(solution)/shard_map/while/body/eval_jaxpr/all_gather | solution.py:51
  377.1 64.7 %all-gather.31.cloned.1.call-done = bf16[768,3072]{1,0:T(8,128)(2,1)} async-done(((bf16[24,3072]{1,0:T(8,128)(2,1)}), bf16[768,3072]{1,0:T(8,128)(2,1)}) %all-gather.31.cloned.1.call-update) | async-done | bytes 4718608 | tf_op jit(solution)/shard_map/while/body/eval_jaxpr/all_gather | solution.py:49
  464.4 39.8 %all-reduce.39 = (bf16[768]{0:T(1024)(128)(2,1)S(1)}, bf16[768]{0:T(1024)(128)(2,1)S(1)}, bf16[768]{0:T(1024)(128)(2,1)S(1)}, bf16[768]{0:T(1024)(128)(2,1)S(1)}...) all-reduce(bf16[768]{0:T(1024)(128)(2,1)S(1)} %dynamic-update-slice, ...), channel_id=1, replica_groups=mesh['dp'=8,'ctx'=4] {'dp','ctx'}, use_global_device_ids=true, to_apply=%add.2 | all-reduce | flops 9216 | bytes 36864 | tf_op jit(solution)/shard_map/while
  513.7 52.9 %all-gather.17.cloned.1.call-done = bf16[768,768]{1,0:T(8,128)(2,1)} async-done(((bf16[24,768]{1,0:T(8,128)(2,1)}), bf16[768,768]{1,0:T(8,128)(2,1)}) %all-gather.17.cloned.1.call-update) | async-done | bytes 1179664 | tf_op jit(solution)/shard_map/while/body/eval_jaxpr/all_gather | solution.py:43
  574.6 47.8 %all-gather.21.cloned.1.call-done = bf16[768,768]{1,0:T(8,128)(2,1)} async-done(((bf16[24,768]{1,0:T(8,128)(2,1)}), bf16[768,768]{1,0:T(8,128)(2,1)}) %all-gather.21.cloned.1.call-update) | async-done | bytes 1179664 | tf_op jit(solution)/shard_map/while/body/eval_jaxpr/all_gather | solution.py:40
  756.1 63.1 %all-gather.29.cloned.1.call-done = bf16[3072,768]{1,0:T(8,128)(2,1)} async-done(((bf16[96,768]{1,0:T(8,128)(2,1)}), bf16[3072,768]{1,0:T(8,128)(2,1)}) %all-gather.29.cloned.1.call-update) | async-done | bytes 4718608 | tf_op jit(solution)/shard_map/while/body/eval_jaxpr/all_gather | solution.py:51
  819.2 64.6 %all-gather.31.cloned.1.call-done = bf16[768,3072]{1,0:T(8,128)(2,1)} async-done(((bf16[24,3072]{1,0:T(8,128)(2,1)}), bf16[768,3072]{1,0:T(8,128)(2,1)}) %all-gather.31.cloned.1.call-update) | async-done | bytes 4718608 | tf_op jit(solution)/shard_map/while/body/eval_jaxpr/all_gather | solution.py:49
  897.8 1116.4 %while.52 = (s32[]{:T(128)}, f32[768]{0:T(1024)}, f32[768]{0:T(1024)}, f32[768,768]{1,0:T(8,128)}, f32[768]{0:T(1024)}, /*index=5*/f32[768,768]{1,0:T(8,128)}, f...) while((s32[]{:T(128)}, f32[768]{0:T(1024)}, ...), condition=%wide.region_31.32_spmd.clone, body=%wide.region_8.31_spmd.clone.sunk | while | flops 12278196224 | bytes 516163296 | solution.py:323
  930.1 39.5 %all-reduce.40 = (bf16[768]{0:T(1024)(128)(2,1)S(1)}, bf16[768]{0:T(1024)(128)(2,1)S(1)}, bf16[3072]{0:T(1024)(128)(2,1)S(1)}, bf16[768]{0:T(1024)(128)(2,1)S(1)...) all-reduce(bf16[768]{0:T(1024)(128)(2,1)S(1)} %dynamic-update-slice, ...), channel_id=1, replica_groups=mesh['dp'=8,'ctx'=4] {'dp','ctx'}, use_global_device_ids=true, to_apply=%add.10 | all-reduce | flops 8448 | bytes 33792 | tf_op jit(solution)/shard_map/while
  980.1 52.9 %all-gather.33.cloned.1.call-done = bf16[768,768]{1,0:T(8,128)(2,1)} async-done(((bf16[24,768]{1,0:T(8,128)(2,1)}), bf16[768,768]{1,0:T(8,128)(2,1)}) %all-gather.33.cloned.1.call-update) | async-done | bytes 1179664 | tf_op jit(solution)/shard_map/while/body/eval_jaxpr/all_gather | solution.py:42
  1039.0 49.7 %all-gather.37.cloned.1.call-done = bf16[768,768]{1,0:T(8,128)(2,1)} async-done(((bf16[24,768]{1,0:T(8,128)(2,1)}), bf16[768,768]{1,0:T(8,128)(2,1)}) %all-gather.37.cloned.1.call-update) | async-done | bytes 1179664 | tf_op jit(solution)/shard_map/while/body/eval_jaxpr/all_gather | solution.py:40
  1179.5 39.8 %all-gather.43.cloned.1.call-done = bf16[768,768]{1,0:T(8,128)(2,1)} async-done(((bf16[24,768]{1,0:T(8,128)(2,1)}), bf16[768,768]{1,0:T(8,128)(2,1)}) %all-gather.43.cloned.1.call-update) | async-done | bytes 1179664 | tf_op jit(solution)/shard_map/while/body/eval_jaxpr/all_gather | solution.py:45
  1221.4 63.2 %all-gather.45.cloned.1.call-done = bf16[768,3072]{1,0:T(8,128)(2,1)} async-done(((bf16[24,3072]{1,0:T(8,128)(2,1)}), bf16[768,3072]{1,0:T(8,128)(2,1)}) %all-gather.45.cloned.1.call-update) | async-done | bytes 4718608 | tf_op jit(solution)/shard_map/while/body/eval_jaxpr/all_gather | solution.py:49
  1290.1 59.1 %all-gather.47.cloned.1.call-done = bf16[3072,768]{1,0:T(8,128)(2,1)} async-done(((bf16[96,768]{1,0:T(8,128)(2,1)}), bf16[3072,768]{1,0:T(8,128)(2,1)}) %all-gather.47.cloned.1.call-update) | async-done | bytes 4718608 | tf_op jit(solution)/shard_map/while/body/eval_jaxpr/all_gather | solution.py:51
  1476.3 39.7 %all-reduce.40 = (bf16[768]{0:T(1024)(128)(2,1)S(1)}, bf16[768]{0:T(1024)(128)(2,1)S(1)}, bf16[3072]{0:T(1024)(128)(2,1)S(1)}, bf16[768]{0:T(1024)(128)(2,1)S(1)...) all-reduce(bf16[768]{0:T(1024)(128)(2,1)S(1)} %dynamic-update-slice, ...), channel_id=1, replica_groups=mesh['dp'=8,'ctx'=4] {'dp','ctx'}, use_global_device_ids=true, to_apply=%add.10 | all-reduce | flops 8448 | bytes 33792 | tf_op jit(solution)/shard_map/while
  1526.7 53.0 %all-gather.33.cloned.1.call-done = bf16[768,768]{1,0:T(8,128)(2,1)} async-done(((bf16[24,768]{1,0:T(8,128)(2,1)}), bf16[768,768]{1,0:T(8,128)(2,1)}) %all-gather.33.cloned.1.call-update) | async-done | bytes 1179664 | tf_op jit(solution)/shard_map/while/body/eval_jaxpr/all_gather | solution.py:42
  1585.7 49.7 %all-gather.37.cloned.1.call-done = bf16[768,768]{1,0:T(8,128)(2,1)} async-done(((bf16[24,768]{1,0:T(8,128)(2,1)}), bf16[768,768]{1,0:T(8,128)(2,1)}) %all-gather.37.cloned.1.call-update) | async-done | bytes 1179664 | tf_op jit(solution)/shard_map/while/body/eval_jaxpr/all_gather | solution.py:40
  1726.2 39.8 %all-gather.43.cloned.1.call-done = bf16[768,768]{1,0:T(8,128)(2,1)} async-done(((bf16[24,768]{1,0:T(8,128)(2,1)}), bf16[768,768]{1,0:T(8,128)(2,1)}) %all-gather.43.cloned.1.call-update) | async-done | bytes 1179664 | tf_op jit(solution)/shard_map/while/body/eval_jaxpr/all_gather | solution.py:45
  1768.1 63.1 %all-gather.45.cloned.1.call-done = bf16[768,3072]{1,0:T(8,128)(2,1)} async-done(((bf16[24,3072]{1,0:T(8,128)(2,1)}), bf16[768,3072]{1,0:T(8,128)(2,1)}) %all-gather.45.cloned.1.call-update) | async-done | bytes 4718608 | tf_op jit(solution)/shard_map/while/body/eval_jaxpr/all_gather | solution.py:49
  1836.7 59.3 %all-gather.47.cloned.1.call-done = bf16[3072,768]{1,0:T(8,128)(2,1)} async-done(((bf16[96,768]{1,0:T(8,128)(2,1)}), bf16[3072,768]{1,0:T(8,128)(2,1)}) %all-gather.47.cloned.1.call-update) | async-done | bytes 4718608 | tf_op jit(solution)/shard_map/while/body/eval_jaxpr/all_gather | solution.py:51
  2018.2 40.0 %all-reduce.36 = (f32[768]{0:T(1024)S(1)}, f32[768]{0:T(1024)S(1)}, f32[768]{0:T(1024)S(1)}, f32[768]{0:T(1024)S(1)}, f32[768]{0:T(1024)S(1)}, /*index=5*/f32[76...) all-reduce(f32[768]{0:T(1024)S(1)} %copy-done.57, ...), channel_id=4, replica_groups=mesh['dp'=8,'ctx'=4] {'dp','ctx'}, use_global_device_ids=true, to_apply=%region_32.33.clone | all-reduce | flops 9216 | bytes 73728
  2063.5 55.5 %reduce-scatter.9.cloned.1.call-done = f32[24,768]{1,0:T(8,128)} async-done(((f32[768,768]{1,0:T(8,128)}), f32[24,768]{1,0:T(8,128)}) %reduce-scatter.9.cloned.1.call-update) | async-done | bytes 73744 | tf_op jit(solution)/shard_map/reduce_scatter | solution.py:324
  2119.1 104.4 %reduce-scatter.11.cloned.1.call-done = f32[24,768]{1,0:T(8,128)} async-done(((f32[768,768]{1,0:T(8,128)}), f32[24,768]{1,0:T(8,128)}) %reduce-scatter.11.cloned.1.call-update) | async-done | bytes 73744 | tf_op jit(solution)/shard_map/reduce_scatter | solution.py:324
  2223.5 104.3 %reduce-scatter.13.cloned.1.call-done = f32[24,768]{1,0:T(8,128)} async-done(((f32[768,768]{1,0:T(8,128)}), f32[24,768]{1,0:T(8,128)}) %reduce-scatter.13.cloned.1.call-update) | async-done | bytes 73744 | tf_op jit(solution)/shard_map/reduce_scatter | solution.py:324
  2327.8 104.5 %reduce-scatter.15.cloned.1.call-done = f32[24,768]{1,0:T(8,128)} async-done(((f32[768,768]{1,0:T(8,128)}), f32[24,768]{1,0:T(8,128)}) %reduce-scatter.15.cloned.1.call-update) | async-done | bytes 73744 | tf_op jit(solution)/shard_map/reduce_scatter | solution.py:324
  2432.3 141.7 %reduce-scatter.17.cloned.1.call-done = f32[24,3072]{1,0:T(8,128)} async-done(((f32[768,3072]{1,0:T(8,128)}), f32[24,3072]{1,0:T(8,128)}) %reduce-scatter.17.cloned.1.call-update) | async-done | bytes 294928 | tf_op jit(solution)/shard_map/reduce_scatter | solution.py:324
  2574.0 141.7 %reduce-scatter.19.cloned.1.call-done = f32[96,768]{1,0:T(8,128)} async-done(((f32[3072,768]{1,0:T(8,128)}), f32[96,768]{1,0:T(8,128)}) %reduce-scatter.19.cloned.1.call-update) | async-done | bytes 294928 | tf_op jit(solution)/shard_map/reduce_scatter | solution.py:324
  (639 shorter events, 803.8 us)
Async XLA Ops:
  9.0 115.6 %all-gather.17.cloned.1.call-start = ((), (), s32[]{:S(2)}) async-start(), calls=%async_computation.14 | async-start | bytes 1216512 | tf_op jit(solution)/shard_map/while/body/eval_jaxpr/all_gather | solution.py:43
  9.7 170.6 %all-gather.21.cloned.1.call-start = ((), (), s32[]{:S(2)}) async-start(), calls=%async_computation.16 | async-start | bytes 1216512 | tf_op jit(solution)/shard_map/while/body/eval_jaxpr/all_gather | solution.py:40
  10.5 207.8 %all-gather.25.cloned.1.call-start = ((), (), s32[]{:S(2)}) async-start(), calls=%async_computation.18 | async-start | bytes 1966080 | tf_op jit(solution)/shard_map/while/body/eval_jaxpr/all_gather | solution.py:89
  71.6 184.6 %all-gather.19.cloned.1.call-start = ((), (), s32[]{:S(2)}) async-start(), calls=%async_computation.15 | async-start | bytes 1966080 | tf_op jit(solution)/shard_map/while/body/eval_jaxpr/all_gather | solution.py:90
  127.2 184.6 %all-gather.27.cloned.1.call-start = ((), (), s32[]{:S(2)}) async-start(), calls=%async_computation.19 | async-start | bytes 1216512 | tf_op jit(solution)/shard_map/while/body/eval_jaxpr/all_gather | solution.py:45
  127.8 249.4 %all-gather.29.cloned.1.call-start = ((), (), s32[]{:S(2)}) async-start(), calls=%async_computation.20 | async-start | bytes 4866048 | tf_op jit(solution)/shard_map/while/body/eval_jaxpr/all_gather | solution.py:51
  128.5 313.3 %all-gather.31.cloned.1.call-start = ((), (), s32[]{:S(2)}) async-start(), calls=%async_computation.21 | async-start | bytes 4866048 | tf_op jit(solution)/shard_map/while/body/eval_jaxpr/all_gather | solution.py:49
  456.1 166.3 %all-gather.21.cloned.1.call-start = ((), (), s32[]{:S(2)}) async-start(), calls=%async_computation.16 | async-start | bytes 1216512 | tf_op jit(solution)/shard_map/while/body/eval_jaxpr/all_gather | solution.py:40
  456.8 203.5 %all-gather.25.cloned.1.call-start = ((), (), s32[]{:S(2)}) async-start(), calls=%async_computation.18 | async-start | bytes 1966080 | tf_op jit(solution)/shard_map/while/body/eval_jaxpr/all_gather | solution.py:89
  513.7 184.7 %all-gather.19.cloned.1.call-start = ((), (), s32[]{:S(2)}) async-start(), calls=%async_computation.15 | async-start | bytes 1966080 | tf_op jit(solution)/shard_map/while/body/eval_jaxpr/all_gather | solution.py:90
  569.2 184.7 %all-gather.27.cloned.1.call-start = ((), (), s32[]{:S(2)}) async-start(), calls=%async_computation.19 | async-start | bytes 1216512 | tf_op jit(solution)/shard_map/while/body/eval_jaxpr/all_gather | solution.py:45
  569.8 249.4 %all-gather.29.cloned.1.call-start = ((), (), s32[]{:S(2)}) async-start(), calls=%async_computation.20 | async-start | bytes 4866048 | tf_op jit(solution)/shard_map/while/body/eval_jaxpr/all_gather | solution.py:51
  570.4 313.4 %all-gather.31.cloned.1.call-start = ((), (), s32[]{:S(2)}) async-start(), calls=%async_computation.21 | async-start | bytes 4866048 | tf_op jit(solution)/shard_map/while/body/eval_jaxpr/all_gather | solution.py:49
  922.5 166.2 %all-gather.37.cloned.1.call-start = ((), (), s32[]{:S(2)}) async-start(), calls=%async_computation.24 | async-start | bytes 1216512 | tf_op jit(solution)/shard_map/while/body/eval_jaxpr/all_gather | solution.py:40
  923.3 202.8 %all-gather.41.cloned.1.call-start = ((), (), s32[]{:S(2)}) async-start(), calls=%async_computation.26 | async-start | bytes 1966080 | tf_op jit(solution)/shard_map/while/body/eval_jaxpr/all_gather | solution.py:90
  980.0 183.5 %all-gather.35.cloned.1.call-start = ((), (), s32[]{:S(2)}) async-start(), calls=%async_computation.23 | async-start | bytes 1966080 | tf_op jit(solution)/shard_map/while/body/eval_jaxpr/all_gather | solution.py:89
  1035.6 183.7 %all-gather.43.cloned.1.call-start = ((), (), s32[]{:S(2)}) async-start(), calls=%async_computation.27 | async-start | bytes 1216512 | tf_op jit(solution)/shard_map/while/body/eval_jaxpr/all_gather | solution.py:45
  1036.3 248.3 %all-gather.45.cloned.1.call-start = ((), (), s32[]{:S(2)}) async-start(), calls=%async_computation.28 | async-start | bytes 4866048 | tf_op jit(solution)/shard_map/while/body/eval_jaxpr/all_gather | solution.py:49
  1037.0 312.2 %all-gather.47.cloned.1.call-start = ((), (), s32[]{:S(2)}) async-start(), calls=%async_computation.29 | async-start | bytes 4866048 | tf_op jit(solution)/shard_map/while/body/eval_jaxpr/all_gather | solution.py:51
  1037.6 391.2 %reduce-scatter.21.cloned.1.call-start = ((), (), s32[]{:S(2)}) async-start(), calls=%async_computation.30 | async-start | bytes 1966080 | tf_op jit(solution)/shard_map/while/body/eval_jaxpr/reduce_scatter | solution.py:214
  1468.8 166.6 %all-gather.37.cloned.1.call-start = ((), (), s32[]{:S(2)}) async-start(), calls=%async_computation.24 | async-start | bytes 1216512 | tf_op jit(solution)/shard_map/while/body/eval_jaxpr/all_gather | solution.py:40
  1469.6 203.2 %all-gather.41.cloned.1.call-start = ((), (), s32[]{:S(2)}) async-start(), calls=%async_computation.26 | async-start | bytes 1966080 | tf_op jit(solution)/shard_map/while/body/eval_jaxpr/all_gather | solution.py:90
  1526.6 183.7 %all-gather.35.cloned.1.call-start = ((), (), s32[]{:S(2)}) async-start(), calls=%async_computation.23 | async-start | bytes 1966080 | tf_op jit(solution)/shard_map/while/body/eval_jaxpr/all_gather | solution.py:89
  1582.3 183.7 %all-gather.43.cloned.1.call-start = ((), (), s32[]{:S(2)}) async-start(), calls=%async_computation.27 | async-start | bytes 1216512 | tf_op jit(solution)/shard_map/while/body/eval_jaxpr/all_gather | solution.py:45
  1583.0 248.2 %all-gather.45.cloned.1.call-start = ((), (), s32[]{:S(2)}) async-start(), calls=%async_computation.28 | async-start | bytes 4866048 | tf_op jit(solution)/shard_map/while/body/eval_jaxpr/all_gather | solution.py:49
  1583.6 312.3 %all-gather.47.cloned.1.call-start = ((), (), s32[]{:S(2)}) async-start(), calls=%async_computation.29 | async-start | bytes 4866048 | tf_op jit(solution)/shard_map/while/body/eval_jaxpr/all_gather | solution.py:51
  1584.3 398.7 %reduce-scatter.21.cloned.1.call-start = ((), (), s32[]{:S(2)}) async-start(), calls=%async_computation.30 | async-start | bytes 1966080 | tf_op jit(solution)/shard_map/while/body/eval_jaxpr/reduce_scatter | solution.py:214
  2014.8 208.7 %reduce-scatter.11.cloned.1.call-start = ((), (), s32[]{:S(2)}) async-start(), calls=%async_computation.9 | async-start | bytes 2433024 | tf_op jit(solution)/shard_map/reduce_scatter | solution.py:324
  2015.4 312.4 %reduce-scatter.13.cloned.1.call-start = ((), (), s32[]{:S(2)}) async-start(), calls=%async_computation.10 | async-start | bytes 2433024 | tf_op jit(solution)/shard_map/reduce_scatter | solution.py:324
  2015.9 416.3 %reduce-scatter.15.cloned.1.call-start = ((), (), s32[]{:S(2)}) async-start(), calls=%async_computation.11 | async-start | bytes 2433024 | tf_op jit(solution)/shard_map/reduce_scatter | solution.py:324
  2016.7 557.3 %reduce-scatter.17.cloned.1.call-start = ((), (), s32[]{:S(2)}) async-start(), calls=%async_computation.12 | async-start | bytes 9732096 | tf_op jit(solution)/shard_map/reduce_scatter | solution.py:324
  2017.4 698.3 %reduce-scatter.19.cloned.1.call-start = ((), (), s32[]{:S(2)}) async-start(), calls=%async_computation.13 | async-start | bytes 9732096 | tf_op jit(solution)/shard_map/reduce_scatter | solution.py:324
  (142 other events, 4637.5 us)
Sparse Core Ops, SparseCore 0:
  11.9 56.9 all-gather.22
  71.7 52.8 all-gather.16
  127.4 52.9 all-gather.20
  182.3 35.9 all-gather.24
  220.3 35.8 all-gather.18
  258.9 52.8 all-gather.26
  314.6 62.5 all-gather.28
  379.9 61.8 all-gather.30
  458.4 52.5 all-gather.22
  513.6 52.9 all-gather.16
  569.4 52.9 all-gather.20
  624.4 35.9 all-gather.24
  662.5 35.8 all-gather.18
  701.1 52.8 all-gather.26
  756.6 62.5 all-gather.28
  821.8 61.8 all-gather.30
  924.7 52.6 all-gather.38
  980.0 52.9 all-gather.32
  1035.7 52.8 all-gather.36
  1090.1 35.9 all-gather.40
  1127.7 35.8 all-gather.34
  1166.4 52.8 all-gather.42
  1222.1 62.5 all-gather.44
  1287.3 61.8 all-gather.46
  1470.8 53.0 all-gather.38
  1526.7 52.8 all-gather.32
  1582.5 52.9 all-gather.36
  1636.8 35.9 all-gather.40
  1674.4 35.8 all-gather.34
  1713.1 52.8 all-gather.42
  1768.7 62.5 all-gather.44
  1834.0 61.8 all-gather.46
  (4 shorter events, 135.9 us)
Sparse Core Ops, SparseCore 1:
  2020.5 98.5 reduce-scatter.8
  2124.8 98.6 reduce-scatter.10
  2229.2 98.5 reduce-scatter.12
  2333.7 98.5 reduce-scatter.14
  2438.8 135.2 reduce-scatter.16
  2580.5 135.2 reduce-scatter.18
where the time goes:
time: 2740 us; the launch traced here: 2720 us
  waiting for transfers between devices  2090 us (76%)
  matrix products  274 us (10%)
  blocking collectives  201 us (7%)
  local copies, waits for them, and re-layouts  77.8 us (3%)
  other arithmetic  38.4 us (1%)
    reduce_scatter x6, waiting for transfers between devices, per_device(): lax.psum_scatter(totals, ('dp', 'ctx'), scatter_dimension=0, tiled=True)  652 us
    all_gather x4, waiting for transfers between devices, fetch(): lax.all_gather(shards[11], ('dp', 'ctx'), axis=0, tiled=True)  256 us
    all_gather x4, waiting for transfers between devices, fetch(): lax.all_gather(shards[13], ('dp', 'ctx'), axis=0, tiled=True)  245 us
    all_gather x4, waiting for transfers between devices, fetch(): lax.all_gather(shards[2], ('dp', 'ctx'), axis=0, tiled=True)  195 us
    while x4, blocking collectives  161 us
    all_gather x4, waiting for transfers between devices, fetch(): lax.all_gather(shards[7], ('dp', 'ctx'), axis=0, tiled=True)  155 us
    all_gather x4, waiting for transfers between devices, forward(): lax.all_gather(value_rows, 'ctx', axis=0, tiled=True)  143 us
    all_gather x4, waiting for transfers between devices, forward(): lax.all_gather(key_rows, 'ctx', axis=0, tiled=True)  142 us
  transfers between devices with their start and end apart: 42, of which 40 were waited for; matrix products, arithmetic and copies ran while one was open for 10% of the time, Pallas kernels for 0%

commit v1 on v0

v1 whole, which is shorter than its diff:
```python
import math

import jax
import jax.numpy as jnp
from jax import lax
from jax.sharding import PartitionSpec as P

H = 12
HD = 64
EPS = 1e-06
ALL = ("dp", "ctx")


def row_stats(rows):
    mean = jnp.mean(rows, axis=-1, keepdims=True)
    center = rows - mean
    rstd = lax.rsqrt(jnp.mean(center * center, axis=-1, keepdims=True) + EPS)
    return center * rstd, rstd


def norm_back(d_normed, xhat, rstd, gain):
    e = d_normed * gain
    mean_e = jnp.mean(e, axis=-1, keepdims=True)
    mean_ex = jnp.mean(e * xhat, axis=-1, keepdims=True)
    d_rows = (e - mean_e - xhat * mean_ex) * rstd
    return d_rows, jnp.sum(d_normed * xhat, axis=0), jnp.sum(d_normed, axis=0)


def mm(left, right):
    return jnp.dot(left, right, preferred_element_type=jnp.float32)


def outer(left_rows, right_rows):
    return lax.dot_general(
        left_rows, right_rows, (((0,), (0,)), ((), ())), preferred_element_type=jnp.float32
    )


def back(grad_rows, weight):
    return lax.dot_general(
        grad_rows, weight, (((1,), (1,)), ((), ())), preferred_element_type=jnp.float32
    )


def col_sum(rows):
    return jnp.sum(rows.astype(jnp.float32), axis=0)


def pack(pieces, sub):
    flat = jnp.concatenate([p.reshape(-1) for p in pieces])
    size = flat.shape[0]
    padded = -(-size // (sub * 128)) * sub * 128
    flat = jnp.pad(flat, (0, padded - size))
    return flat.reshape(sub, padded // sub)


def gather_all(shards, groups):
    sub = 16
    full = lax.all_gather(pack(shards, sub), ALL, axis=0, tiled=True).reshape(groups, -1)
    out, off = [], 0
    for s in shards:
        size = s.size
        piece = full[:, off:off + size].reshape((groups * s.shape[0],) + s.shape[1:])
        out.append(piece)
        off += size
    return out


def scatter_all(grads, groups):
    sub = 8
    parts = [g.reshape(groups, -1) for g in grads]
    flat = jnp.concatenate(parts, axis=1)
    size = flat.shape[1]
    padded = -(-size // (sub * 128)) * sub * 128
    flat = jnp.pad(flat, ((0, 0), (0, padded - size))).reshape(groups, sub, padded // sub)
    mine = lax.psum_scatter(flat, ALL, scatter_dimension=0, tiled=True).reshape(-1)
    out, off = [], 0
    for g in grads:
        size = g.size // groups
        out.append(mine[off:off + size].reshape((g.shape[0] // groups,) + g.shape[1:]))
        off += size
    return out


def per_device(inputs, lengths, *rest):
    shards = rest[:15]
    out_grad = rest[15]
    groups = lax.axis_size(ALL)
    (ln1_gain, ln1_bias, wq, bq, wk, wv, bv, wo, bo, ln2_gain, ln2_bias, wi, bi, wf, bf) = gather_all(
        shards, groups
    )
    f32 = lambda a: a.astype(jnp.float32)
    seqs, rows, width = inputs.shape
    n = seqs * rows
    x = f32(inputs).reshape(n, width)

    xhat1, rstd1 = row_stats(x)
    normed = (xhat1 * f32(ln1_gain) + f32(ln1_bias)).astype(jnp.bfloat16)
    q = (mm(normed, wq) + f32(bq)).astype(jnp.bfloat16)
    k = mm(normed, wk).astype(jnp.bfloat16)
    v = (mm(normed, wv) + f32(bv)).astype(jnp.bfloat16)
    k_all = lax.all_gather(k.reshape(seqs, rows, width), "ctx", axis=1, tiled=True)
    v_all = lax.all_gather(v.reshape(seqs, rows, width), "ctx", axis=1, tiled=True)
    total = k_all.shape[1]
    qh = q.reshape(seqs, rows, H, HD)
    kh = k_all.reshape(seqs, total, H, HD)
    vh = v_all.reshape(seqs, total, H, HD)
    scale = HD ** (-0.5)
    scores = jnp.einsum("sqhd,skhd->shqk", qh, kh, preferred_element_type=jnp.float32) * scale
    valid = jnp.arange(total)[None, :] < lengths[:, None]
    scores = jnp.where(valid[:, None, None, :], scores, -1e30)
    top = jnp.max(scores, axis=-1, keepdims=True)
    expd = jnp.exp(scores - top)
    probs = expd / jnp.sum(expd, axis=-1, keepdims=True)
    low_probs = probs.astype(jnp.bfloat16)
    mixed = jnp.einsum("shqk,skhd->sqhd", low_probs, vh, preferred_element_type=jnp.float32)
    mixed = mixed.reshape(n, width).astype(jnp.bfloat16)
    middle = x + mm(mixed, wo) + f32(bo)
    xhat2, rstd2 = row_stats(middle)
    normed_two = (xhat2 * f32(ln2_gain) + f32(ln2_bias)).astype(jnp.bfloat16)
    ffn_pre = mm(normed_two, wi) + f32(bi)
    cdf = 0.5 * (1.0 + lax.erf(ffn_pre * (1.0 / math.sqrt(2.0))))
    ffn_act = (ffn_pre * cdf).astype(jnp.bfloat16)
    result = middle + mm(ffn_act, wf) + f32(bf)
    output = result.astype(jnp.bfloat16).reshape(seqs, rows, width)

    g = f32(out_grad).reshape(n, width)
    g_low = g.astype(jnp.bfloat16)
    grad_bf = col_sum(g_low)
    grad_wf = outer(ffn_act, g_low)
    d_act = back(g_low, wf)
    pdf = jnp.exp(-0.5 * ffn_pre * ffn_pre) * (1.0 / math.sqrt(2.0 * math.pi))
    d_pre = (d_act * (cdf + ffn_pre * pdf)).astype(jnp.bfloat16)
    grad_bi = col_sum(d_pre)
    grad_wi = outer(normed_two, d_pre)
    d_normed_two = back(d_pre, wi)
    d_mid, grad_ln2_gain, grad_ln2_bias = norm_back(d_normed_two, xhat2, rstd2, f32(ln2_gain))
    d_middle = g + d_mid
    d_branch = d_middle.astype(jnp.bfloat16)
    grad_bo = col_sum(d_branch)
    grad_wo = outer(mixed, d_branch)
    d_mixed = back(d_branch, wo).astype(jnp.bfloat16).reshape(seqs, rows, H, HD)
    d_probs = jnp.einsum("sqhd,skhd->shqk", d_mixed, vh, preferred_element_type=jnp.float32)
    inner = jnp.sum(probs * d_probs, axis=-1, keepdims=True)
    d_scores = (probs * (d_probs - inner)).astype(jnp.bfloat16)
    d_q = jnp.einsum("shqk,skhd->sqhd", d_scores, kh, preferred_element_type=jnp.float32) * scale
    d_q = d_q.reshape(n, width).astype(jnp.bfloat16)
    k_terms = jnp.einsum("shqk,sqhd->skhd", d_scores, qh, preferred_element_type=jnp.float32) * scale
    v_terms = jnp.einsum("shqk,sqhd->skhd", low_probs, d_mixed, preferred_element_type=jnp.float32)
    d_k = lax.psum_scatter(
        k_terms.reshape(seqs, total, width).astype(jnp.bfloat16), "ctx", scatter_dimension=1, tiled=True
    ).reshape(n, width)
    d_v = lax.psum_scatter(
        v_terms.reshape(seqs, total, width).astype(jnp.bfloat16), "ctx", scatter_dimension=1, tiled=True
    ).reshape(n, width)
    grad_bq = col_sum(d_q)
    grad_bv = col_sum(d_v)
    grad_wq = outer(normed, d_q)
    grad_wk = outer(normed, d_k)
    grad_wv = outer(normed, d_v)
    d_normed = back(d_q, wq) + back(d_k, wk) + back(d_v, wv)
    d_x, grad_ln1_gain, grad_ln1_bias = norm_back(d_normed, xhat1, rstd1, f32(ln1_gain))
    input_grad = (d_middle + d_x).astype(jnp.bfloat16).reshape(seqs, rows, width)

    ffn_part = scatter_all((grad_ln2_gain, grad_ln2_bias, grad_wi, grad_bi), groups)
    ffn_out_part = scatter_all((grad_wf, grad_bf), groups)
    attn_part = scatter_all(
        (grad_ln1_gain, grad_ln1_bias, grad_wq, grad_bq, grad_wk, grad_wv, grad_bv, grad_wo, grad_bo), groups
    )
    return (output, input_grad) + tuple(attn_part) + tuple(ffn_part) + tuple(ffn_out_part)


def solution(mesh):
    row = P(("dp", "ctx"))
    mat = P(("dp", "ctx"), None)
    act = P("dp", "ctx", None)
    weight_specs = (row, row, mat, row, mat, mat, row, mat, row, row, row, mat, row, mat, row)
    return jax.shard_map(
        per_device,
        mesh=mesh,
        in_specs=(act, P("dp")) + weight_specs + (act,),
        out_specs=(act, act) + weight_specs,
        check_vma=False,
    )
```

time: 2740 us -> 1150 us (0.42)
  waiting for transfers between devices: 2090 us -> 715 us
  blocking collectives: 201 us -> 0 us
  local copies, waits for them, and re-layouts: 77.8 us -> 244 us
  matrix products: 274 us -> 136 us
    all_gather x32 -> x3, waiting for transfers between devices: 1370 us -> 173 us  [the longest x1 104 us: gather_all(): lax.all_gather(pack(shards, sub), ALL, axis=0, tiled=True)]
    reduce_scatter x10 -> x2, waiting for transfers between devices: 702 us -> 0.01 us  [the longest x1 0.01 us: per_device(): lax.psum_scatter(k_terms.reshape(seqs, total, width).astype(jnp.bfloat16)...]
    unnamed x6 -> x11, waiting for transfers between devices: 3.59 us -> 542 us
    while x4 -> x0, blocking collectives: 161 us -> none
    dot_general x56 -> x23, matrix products: 243 us -> 122 us  [the longest x6 26.9 us: outer(): lax.dot_general(left_rows, right_rows, (((0,), (0,)), ((), ())), preferre...]
    unnamed x25 -> x99, local copies, waits for them, and re-layouts: 5.42 us -> 100 us
    reshape x0 -> x39, local copies, waits for them, and re-layouts: none -> 81.4 us  [the longest x15 31.1 us: scatter_all(): parts = [g.reshape(groups, -1) for g in grads]]
    while x316 -> x0, local copies, waits for them, and re-layouts: 44.4 us -> none
  transfers between devices with their start and end apart: 42 -> 8, of which waited for: 40 -> 6; matrix products, arithmetic and copies ran while one was open for 10% -> 24% of each run, Pallas kernels for 0% -> 0%
where the time goes in v1:
time: 1150 us; the launch traced here: 1140 us
  waiting for transfers between devices  715 us (62%)
  local copies, waits for them, and re-layouts  244 us (21%)
  matrix products  136 us (12%)
  other arithmetic  28.6 us (2%)
  between operations  15.3 us (1%)
    unnamed x11, waiting for transfers between devices  542 us
    all_gather x1, waiting for transfers between devices, gather_all(): lax.all_gather(pack(shards, sub), ALL, axis=0, tiled=True)  104 us
    unnamed x99, local copies, waits for them, and re-layouts  100 us
    all_gather x1, waiting for transfers between devices, per_device(): lax.all_gather(v.reshape(seqs, rows, width), 'ctx', axis=1, tiled=True)  45.4 us
    reshape x15, local copies, waits for them, and re-layouts, scatter_all(): parts = [g.reshape(groups, -1) for g in grads]  31.1 us
    dot_general x6, matrix products, outer(): lax.dot_general(left_rows, right_rows, (((0,), (0,)), ((), ())), preferre...  26.9 us
    dot_general x6, matrix products, mm(): return jnp.dot(left, right, preferred_element_type=jnp.float32)  24.7 us
    all_gather x1, waiting for transfers between devices, per_device(): lax.all_gather(k.reshape(seqs, rows, width), 'ctx', axis=1, tiled=True)  23 us
  transfers between devices with their start and end apart: 8, of which 6 were waited for; matrix products, arithmetic and copies ran while one was open for 24% of the time, Pallas kernels for 0%

profile of v1, /device:TPU:0, one launch (start us, length us, event | category | flops | bytes accessed | tf_op | source)
XLA Modules:
  0.0 1139.6 jit_solution(15082515194192390119)
XLA Ops:
  12.6 10.5 concatenate.12
  26.2 104.1 %all-gather.4.cloned.1.call-done = bf16[512,13952]{1,0:T(8,128)(2,1)} async-done(((bf16[16,13952]{1,0:T(8,128)(2,1)}), bf16[512,13952]{1,0:T(8,128)(2,1)}) %all-gather.4.cloned.1.call-update) | async-done | bytes 14286864 | tf_op jit(solution)/shard_map/all_gather | solution.py:59
  130.3 13.3 %reshape.492 = bf16[32,223232]{1,0:T(8,128)(2,1)} reshape(bf16[512,13952]{1,0:T(8,128)(2,1)} %all-gather.4.cloned.1.call-done) | data formatting | bytes 28573696 | tf_op jit(solution)/shard_map/reshape | solution.py:59
  145.1 5.6 fusion.65
  163.3 10.1 fusion.64
  183.7 6.1 reshape.502
  189.9 6.1 reshape.503
  196.0 23.0 %all-gather.8.cloned.1.call-done = bf16[2,1024,768]{2,1,0:T(8,128)(2,1)} async-done(((bf16[2,256,768]{2,1,0:T(8,128)(2,1)}), bf16[2,1024,768]{2,1,0:T(8,128)(2,1)}) %all-gather.8.cloned.1.call-update) | async-done | bytes 3145744 | tf_op jit(solution)/shard_map/all_gather | solution.py:102
  223.7 14.2 %fusion.69 = (f32[2,12,256]{2,1,0:T(8,128)S(1)}, f32[2,12,256,1024]{3,2,1,0:T(8,128)}) fusion(pred[2,1024]{1,0:T(4,128)(4,1)S(1)} %copy-done.33, bf16[2,1024,12,64]{1,3,2,0:T(8,128)(2,1)} %bitcast.129, bf16[2,256,12,64]{1,0,3,2:T(2,128)(2,1)S(1)} %reshape.497), kind=kOutput, calls=%fused_computation.114 | convolution fusion | flops 830473216 | bytes 29124608 | tf_op jit(solution)/shard_map/sub | solution.py:113
  237.9 45.4 %all-gather.6.cloned.1.call-done = bf16[2,1024,768]{2,1,0:T(8,128)(2,1)} async-done(((bf16[2,256,768]{2,1,0:T(8,128)(2,1)}), bf16[2,1024,768]{2,1,0:T(8,128)(2,1)}) %all-gather.6.cloned.1.call-update) | async-done | bytes 3145744 | tf_op jit(solution)/shard_map/all_gather | solution.py:103
  288.0 11.5 %fusion.40 = bf16[2,256,12,64]{1,3,2,0:T(8,128)(2,1)S(1)} fusion(bf16[2,1024,12,64]{1,3,2,0:T(8,128)(2,1)} %bitcast.139, f32[2,12,256,1024]{3,2,1,0:T(8,128)} %get-tuple-element.57, f32[2,12,256]{2,1,0:T(8,128)S(1)} %get-tuple-element.56), kind=kOutput, calls=%fused_computation.73 | convolution fusion | flops 818282496 | bytes 29122560 | tf_op jit(solution)/shard_map/shqk,skhd->sqhd/dot_general | solution.py:116
  302.1 7.3 multiply_convert_fusion.2
  326.0 16.3 %multiply_reduce_fusion = (f32[2,12,256]{2,1,0:T(8,128)S(1)}, f32[2,12,256,1024]{3,2,1,0:T(8,128)}) fusion(f32[2,12,256,1024]{3,2,1,0:T(8,128)} %get-tuple-element.57, f32[2,12,256]{2,1,0:T(8,128)S(1)} %get-tuple-element.56, bf16[2,1024,12,64]{1,3,2,0:T(8,128)(2,1)S(1)} %bitcast.140, bf16[2,256,12,64]{1,0,3,2:T(2,128)(2,1)} %reshape.506), kind=kOutput, calls=%fused_computation.2 | convolution fusion | flops 824174592 | bytes 54312960 | tf_op jit(solution)/shard_map/sqhd,skhd->shqk/dot_general | solution.py:143
  342.3 16.5 %multiply_convert_fusion = bf16[2,12,256,1024]{3,2,1,0:T(8,128)(2,1)S(1)} fusion(f32[2,12,256,1024]{3,2,1,0:T(8,128)} %get-tuple-element.64, f32[2,12,256]{2,1,0:T(8,128)S(1)} %get-tuple-element.63, f32[2,12,256,1024]{3,2,1,0:T(8,128)} %get-tuple-element.57, f32[2,12,256]{2,1,0:T(8,128)S(1)} %get-tuple-element.56), kind=kLoop, calls=%fused_computation.1 | loop fusion | flops 25165824 | bytes 62963712 | tf_op jit(solution)/shard_map/convert_element_type | solution.py:145
  366.3 10.4 fusion.17
  380.9 7.2 fusion.62
  388.2 8.1 reshape.527
  399.2 28.4 %dynamic-update-slice.2 = f32[32,73872]{1,0:T(8,128)} dynamic-update-slice(f32[32,73872]{1,0:T(8,128)} %dynamic-update-slice.1, f32[32,73728]{1,0:T(8,128)} %reshape.527, s32[]{} %constant.70, s32[]{} %constant.72) | dynamic-update-slice | bytes 18874372
  433.4 5.4 copy.81
  440.2 8.3 fusion.78
  448.5 8.4 reshape.532
  461.3 5.4 copy.82
  468.6 8.6 convert_reduce_fusion.5
  519.1 9.3 dynamic-update-slice.6
  529.9 9.3 dynamic-update-slice.8
  539.3 9.3 dynamic-update-slice.9
  550.1 9.0 dynamic-update-slice.11
  565.2 5.4 copy.80
  571.4 7.4 add_convert_fusion
  580.3 122.5 %reduce-scatter.21.cloned.1.call-done = f32[1,8,9344]{2,1,0:T(8,128)} async-done(((f32[32,8,9344]{2,1,0:T(8,128)}), f32[1,8,9344]{2,1,0:T(8,128)}) %reduce-scatter.21.cloned.1.call-update) | async-done | bytes 299024
  704.5 210.9 %reduce-scatter.23.cloned.1.call-done = f32[1,8,9344]{2,1,0:T(8,128)} async-done(((f32[32,8,9344]{2,1,0:T(8,128)}), f32[1,8,9344]{2,1,0:T(8,128)}) %reduce-scatter.23.cloned.1.call-update) | async-done | bytes 299024
  919.0 209.0 %reduce-scatter.19.cloned.1.call-done = f32[1,8,9344]{2,1,0:T(8,128)} async-done(((f32[32,8,9344]{2,1,0:T(8,128)}), f32[1,8,9344]{2,1,0:T(8,128)}) %reduce-scatter.19.cloned.1.call-update) | async-done | bytes 299024
  (211 shorter events, 151.9 us)
Async XLA Ops:
  7.2 17.3 %copy-start.1 = (bf16[2,256,768]{2,1,0:T(8,128)(2,1)S(1)}, bf16[2,256,768]{2,1,0:T(8,128)(2,1)}, u32[]{:S(2)}) copy-start(bf16[2,256,768]{2,1,0:T(8,128)(2,1)} %param.18) | copy-start | bytes 2359300
  7.2 123.1 %all-gather.4.cloned.1.call-start = ((), (), s32[]{:S(2)}) async-start(), calls=%async_computation.5 | async-start | bytes 14733312 | tf_op jit(solution)/shard_map/all_gather | solution.py:59
  24.5 194.6 %all-gather.8.cloned.1.call-start = ((), (), s32[]{:S(2)}) async-start(), calls=%async_computation.7 | async-start | bytes 3932160 | tf_op jit(solution)/shard_map/all_gather | solution.py:102
  150.9 6.1 copy-start.24
  153.7 23.1 %copy-start.18 = (bf16[2,256,768]{2,1,0:T(8,128)(2,1)}, bf16[2,256,768]{2,1,0:T(8,128)(2,1)S(1)}, u32[]{:S(2)}) copy-start(bf16[2,256,768]{2,1,0:T(8,128)(2,1)S(1)} %fusion.25) | copy-start | bytes 2359300
  157.0 126.3 %all-gather.6.cloned.1.call-start = ((), (), s32[]{:S(2)}) async-start(), calls=%async_computation.6 | async-start | bytes 3932160 | tf_op jit(solution)/shard_map/all_gather | solution.py:103
  163.2 329.6 %reduce-scatter.15.cloned.1.call-start = ((), (), s32[]{:S(2)}) async-start(), calls=%async_computation.8 | async-start | bytes 3932160 | tf_op jit(solution)/shard_map/reduce_scatter | solution.py:150
  181.4 42.3 %copy-start.11 = (bf16[2,256,12,64]{1,0,3,2:T(2,128)(2,1)}, bf16[2,256,12,64]{1,0,3,2:T(2,128)(2,1)S(1)}, u32[]{:S(2)}) copy-start(bf16[2,256,12,64]{1,0,3,2:T(2,128)(2,1)S(1)} %reshape.497) | copy-start | bytes 2359300
  183.7 6.1 copy-start.22
  196.0 27.7 %copy-start.33 = (pred[2,1024]{1,0:T(4,128)(4,1)S(1)}, pred[2,1024]{1,0:T(4,128)(4,1)}, u32[]{:S(2)}) copy-start(pred[2,1024]{1,0:T(4,128)(4,1)} %iota_compare_fusion.1) | copy-start | bytes 6148
  300.8 8.7 slice-start
  301.7 15.5 %copy-start.8 = (f32[512,768]{1,0:T(8,128)}, f32[512,768]{1,0:T(8,128)S(1)}, u32[]{:S(2)}) copy-start(f32[512,768]{1,0:T(8,128)S(1)} %get-tuple-element.59) | copy-start | bytes 4718596
  302.1 7.4 copy-start.6
  302.1 7.4 slice-start.1
  302.1 12.1 %slice-start.2 = ((s8[4718592]{0:T(1024)(128)(4,1)}), s8[4194304]{0:T(1024)(128)(4,1)S(1)}, s32[]{:S(2)}) async-start(s8[4718592]{0:T(1024)(128)(4,1)} %bitcast.134), calls=%async_computation.15 | async-start | bytes 8388608
  309.4 4.7 slice-start.3
  319.1 6.9 copy-start.17
  342.3 16.5 %copy-start.12 = (bf16[2,256,12,64]{1,0,3,2:T(2,128)(2,1)S(1)}, bf16[2,256,12,64]{1,0,3,2:T(2,128)(2,1)}, u32[]{:S(2)}) copy-start(bf16[2,256,12,64]{1,0,3,2:T(2,128)(2,1)} %copy-done.11) | copy-start | bytes 2359300
  358.8 4.6 copy-start
  366.2 130.3 %reduce-scatter.17.cloned.1.call-start = ((), (), s32[]{:S(2)}) async-start(), calls=%async_computation.9 | async-start | bytes 3932160 | tf_op jit(solution)/shard_map/reduce_scatter | solution.py:153
  379.6 323.2 %reduce-scatter.21.cloned.1.call-start = ((), (), s32[]{:S(2)}) async-start(), calls=%async_computation.11 | async-start | bytes 9867264
  438.8 476.5 %reduce-scatter.23.cloned.1.call-start = ((), (), s32[]{:S(2)}) async-start(), calls=%async_computation.12 | async-start | bytes 9867264
  466.7 661.2 %reduce-scatter.19.cloned.1.call-start = ((), (), s32[]{:S(2)}) async-start(), calls=%async_computation.10 | async-start | bytes 9867264
  480.6 3.9 copy-start.4
  480.6 3.9 copy-start.15
  517.6 10.9 copy-start.23
  571.4 7.4 copy-start.29
  571.4 7.4 copy-start.28
  571.4 7.4 copy-start.10
  571.4 7.4 copy-start.25
  571.4 7.4 copy-start.26
  571.4 7.4 copy-start.27
  (16 other events, 29.7 us)
Sparse Core Ops, SparseCore 0:
  24.6 105.6 all-gather.3
  157.1 61.8 all-gather.7
  221.2 62.0 all-gather.5
  366.3 59.0 reduce-scatter.14
  427.6 60.3 reduce-scatter.16
  490.1 212.6 reduce-scatter.20
  705.1 210.2 reduce-scatter.22
  917.7 210.2 reduce-scatter.18

commit v2 on v1

--- a/solution.py
+++ b/solution.py
@@ -68,12 +68,12 @@
 
 def scatter_all(grads, groups):
     sub = 8
-    parts = [g.reshape(groups, -1) for g in grads]
+    parts = [g.reshape(groups, -1).astype(jnp.bfloat16) for g in grads]
     flat = jnp.concatenate(parts, axis=1)
     size = flat.shape[1]
     padded = -(-size // (sub * 128)) * sub * 128
     flat = jnp.pad(flat, ((0, 0), (0, padded - size))).reshape(groups, sub, padded // sub)
-    mine = lax.psum_scatter(flat, ALL, scatter_dimension=0, tiled=True).reshape(-1)
+    mine = lax.psum_scatter(flat, ALL, scatter_dimension=0, tiled=True).reshape(-1).astype(jnp.float32)
     out, off = [], 0
     for g in grads:
         size = g.size // groups

time: 1150 us -> 985 us (0.86)
  waiting for transfers between devices: 715 us -> 581 us
  local copies, waits for them, and re-layouts: 244 us -> 220 us
    unnamed x11, waiting for transfers between devices: 542 us -> 405 us
    reshape x18 -> x0, local copies, waits for them, and re-layouts: 34.1 us -> none  [the longest x15 31.1 us: scatter_all(): parts = [g.reshape(groups, -1) for g in grads]]
    convert_element_type x0 -> x18, local copies, waits for them, and re-layouts: none -> 28.2 us  [the longest x15 24.8 us: scatter_all(): parts = [g.reshape(groups, -1).astype(jnp.bfloat16) for g in grads]]
    unnamed x99 -> x97, local copies, waits for them, and re-layouts: 100 us -> 93.3 us
  transfers between devices with their start and end apart: 8 -> 8, of which waited for: 6 -> 6; matrix products, arithmetic and copies ran while one was open for 24% -> 27% of each run, Pallas kernels for 0% -> 0%
where the time goes in v2:
time: 985 us; the launch traced here: 972 us
  waiting for transfers between devices  581 us (59%)
  local copies, waits for them, and re-layouts  220 us (22%)
  matrix products  128 us (13%)
  other arithmetic  27.5 us (3%)
  between operations  15.3 us (2%)
    unnamed x11, waiting for transfers between devices  405 us
    all_gather x1, waiting for transfers between devices, gather_all(): lax.all_gather(pack(shards, sub), ALL, axis=0, tiled=True)  104 us
    unnamed x97, local copies, waits for them, and re-layouts  93.3 us
    all_gather x1, waiting for transfers between devices, per_device(): lax.all_gather(v.reshape(seqs, rows, width), 'ctx', axis=1, tiled=True)  45.3 us
    all_gather x1, waiting for transfers between devices, per_device(): lax.all_gather(k.reshape(seqs, rows, width), 'ctx', axis=1, tiled=True)  26.5 us
    convert_element_type x15, local copies, waits for them, and re-layouts, scatter_all(): parts = [g.reshape(groups, -1).astype(jnp.bfloat16) for g in grads]  24.8 us
    dot_general x6, matrix products, mm(): return jnp.dot(left, right, preferred_element_type=jnp.float32)  23.7 us
    dot_general x6, matrix products, outer(): lax.dot_general(left_rows, right_rows, (((0,), (0,)), ((), ())), preferre...  22.1 us
  transfers between devices with their start and end apart: 8, of which 6 were waited for; matrix products, arithmetic and copies ran while one was open for 27% of the time, Pallas kernels for 0%

profile of v2, /device:TPU:0, one launch (start us, length us, event | category | flops | bytes accessed | tf_op | source)
XLA Modules:
  0.0 972.5 jit_solution(13371582125452544968)
XLA Ops:
  12.6 10.5 %concatenate.12 = bf16[221472]{0:T(1024)(128)(2,1)S(1)} concatenate(bf16[24]{0:T(256)(128)(2,1)} %param.20, bf16[24]{0:T(256)(128)(2,1)} %param.21, bf16[18432]{0:T(1024)(128)(2,1)S(1)} %reshape.473, bf16[24]{0:T(256)(128)(2,1)} %param.23, bf16[18432]{0:T(1024)(128)(2,1)S(1)} %reshape.474, bf16[18432]{0:T(1024)(128)(2,1)S(1)} %reshape.475, bf16[24]{0:T(256)(128)(2,1)} %param.26, ...), dimensions={0} | concatenate | bytes 885888 | tf_op jit(solution)/shard_map/concatenate | solution.py:50
  26.3 104.0 %all-gather.4.cloned.1.call-done = bf16[512,13952]{1,0:T(8,128)(2,1)} async-done(((bf16[16,13952]{1,0:T(8,128)(2,1)}), bf16[512,13952]{1,0:T(8,128)(2,1)}) %all-gather.4.cloned.1.call-update) | async-done | bytes 14286864 | tf_op jit(solution)/shard_map/all_gather | solution.py:59
  130.3 13.4 %reshape.480 = bf16[32,223232]{1,0:T(8,128)(2,1)} reshape(bf16[512,13952]{1,0:T(8,128)(2,1)} %all-gather.4.cloned.1.call-done) | data formatting | bytes 28573696 | tf_op jit(solution)/shard_map/reshape | solution.py:59
  145.2 5.2 fusion.66
  163.1 10.3 %fusion.65 = (bf16[32,73728]{1,0:T(8,128)(2,1)}, bf16[32,73728]{1,0:T(8,128)(2,1)}) fusion(bf16[32,223232]{1,0:T(8,128)(2,1)} %reshape.480), kind=kLoop, calls=%fused_computation.108 | loop fusion | bytes 18874368 | tf_op jit(solution)/shard_map/slice | solution.py:63
  174.6 6.3 reshape.491
  186.3 6.4 reshape.490
  192.7 26.5 %all-gather.8.cloned.1.call-done = bf16[2,1024,768]{2,1,0:T(8,128)(2,1)} async-done(((bf16[2,256,768]{2,1,0:T(8,128)(2,1)}), bf16[2,1024,768]{2,1,0:T(8,128)(2,1)}) %all-gather.8.cloned.1.call-update) | async-done | bytes 3145744 | tf_op jit(solution)/shard_map/all_gather | solution.py:102
  219.2 4.7 copy.61
  223.9 14.2 %fusion.70 = (f32[2,12,256]{2,1,0:T(8,128)S(1)}, f32[2,12,256,1024]{3,2,1,0:T(8,128)}) fusion(pred[2,1024]{1,0:T(4,128)(4,1)S(1)} %iota_compare_fusion.1, bf16[2,1024,12,64]{1,3,2,0:T(8,128)(2,1)} %bitcast.127, bf16[2,256,12,64]{1,0,3,2:T(2,128)(2,1)S(1)} %reshape.485), kind=kOutput, calls=%fused_computation.113 | convolution fusion | flops 830473216 | bytes 29124608 | tf_op jit(solution)/shard_map/sub | solution.py:113
  238.1 45.3 %all-gather.6.cloned.1.call-done = bf16[2,1024,768]{2,1,0:T(8,128)(2,1)} async-done(((bf16[2,256,768]{2,1,0:T(8,128)(2,1)}), bf16[2,1024,768]{2,1,0:T(8,128)(2,1)}) %all-gather.6.cloned.1.call-update) | async-done | bytes 3145744 | tf_op jit(solution)/shard_map/all_gather | solution.py:103
  283.4 4.7 copy.59
  288.1 11.5 %fusion.43 = bf16[2,256,12,64]{1,3,2,0:T(8,128)(2,1)S(1)} fusion(bf16[2,1024,12,64]{1,3,2,0:T(8,128)(2,1)} %bitcast.135, f32[2,12,256,1024]{3,2,1,0:T(8,128)} %get-tuple-element.57, f32[2,12,256]{2,1,0:T(8,128)S(1)} %get-tuple-element.56), kind=kOutput, calls=%fused_computation.73 | convolution fusion | flops 818282496 | bytes 29122560 | tf_op jit(solution)/shard_map/shqk,skhd->sqhd/dot_general | solution.py:116
  302.2 7.4 multiply_convert_fusion.2
  309.7 4.7 fusion.77
  321.5 9.8 %fusion.20 = bf16[2,12,64,1024]{3,2,1,0:T(8,128)(2,1)S(1)} fusion(bf16[2,256,12,64]{1,0,3,2:T(2,128)(2,1)} %reshape.495, f32[2,12,256,1024]{3,2,1,0:T(8,128)} %get-tuple-element.57, f32[2,12,256]{2,1,0:T(8,128)S(1)} %get-tuple-element.56), kind=kOutput, calls=%fused_computation.33 | convolution fusion | flops 819462144 | bytes 29122560 | tf_op jit(solution)/shard_map/shqk,sqhd->skhd/dot_general | solution.py:149
  336.0 17.1 %multiply_reduce_fusion = (f32[2,12,256]{2,1,0:T(8,128)S(1)}, f32[2,12,256,1024]{3,2,1,0:T(8,128)}) fusion(f32[2,12,256,1024]{3,2,1,0:T(8,128)} %get-tuple-element.57, f32[2,12,256]{2,1,0:T(8,128)S(1)} %get-tuple-element.56, bf16[2,1024,12,64]{1,3,2,0:T(8,128)(2,1)S(1)} %bitcast.136, bf16[2,256,12,64]{1,0,3,2:T(2,128)(2,1)} %reshape.495), kind=kOutput, calls=%fused_computation.2 | convolution fusion | flops 824174592 | bytes 54312960 | tf_op jit(solution)/shard_map/sqhd,skhd->shqk/dot_general | solution.py:143
  353.1 16.5 %multiply_convert_fusion = bf16[2,12,256,1024]{3,2,1,0:T(8,128)(2,1)S(1)} fusion(f32[2,12,256,1024]{3,2,1,0:T(8,128)} %get-tuple-element.64, f32[2,12,256]{2,1,0:T(8,128)S(1)} %get-tuple-element.63, f32[2,12,256,1024]{3,2,1,0:T(8,128)} %get-tuple-element.57, f32[2,12,256]{2,1,0:T(8,128)S(1)} %get-tuple-element.56), kind=kLoop, calls=%fused_computation.1 | loop fusion | flops 25165824 | bytes 62963712 | tf_op jit(solution)/shard_map/convert_element_type | solution.py:145
  378.4 6.5 convolution_convert_fusion.1
  384.9 6.0 convert_element_type.367
  393.9 27.3 %dynamic-update-slice.2 = bf16[32,73872]{1,0:T(8,128)(2,1)} dynamic-update-slice(bf16[32,73872]{1,0:T(8,128)(2,1)} %dynamic-update-slice.1, bf16[32,73728]{1,0:T(8,128)(2,1)} %convert_element_type.367, s32[]{} %constant.74, s32[]{} %constant.76) | dynamic-update-slice | bytes 9437188
  429.4 6.7 convolution_convert_fusion
  436.1 6.1 convert_element_type.372
  451.5 9.6 fusion.76
  495.4 9.1 dynamic-update-slice.6
  506.0 9.0 dynamic-update-slice.8
  514.9 8.9 dynamic-update-slice.9
  525.4 8.4 dynamic-update-slice.11
  541.5 7.4 add_convert_fusion
  550.4 73.0 %reduce-scatter.21.cloned.1.call-done = bf16[1,8,9344]{2,1,0:T(8,128)(2,1)} async-done(((bf16[32,8,9344]{2,1,0:T(8,128)(2,1)}), bf16[1,8,9344]{2,1,0:T(8,128)(2,1)}) %reduce-scatter.21.cloned.1.call-update) | async-done | bytes 149520
  625.2 166.1 %reduce-scatter.23.cloned.1.call-done = bf16[1,8,9344]{2,1,0:T(8,128)(2,1)} async-done(((bf16[32,8,9344]{2,1,0:T(8,128)(2,1)}), bf16[1,8,9344]{2,1,0:T(8,128)(2,1)}) %reduce-scatter.23.cloned.1.call-update) | async-done | bytes 149520
  795.2 165.5 %reduce-scatter.19.cloned.1.call-done = bf16[1,8,9344]{2,1,0:T(8,128)(2,1)} async-done(((bf16[32,8,9344]{2,1,0:T(8,128)(2,1)}), bf16[1,8,9344]{2,1,0:T(8,128)(2,1)}) %reduce-scatter.19.cloned.1.call-update) | async-done | bytes 149520
  (208 shorter events, 129.1 us)
Async XLA Ops:
  7.2 17.3 %copy-start.1 = (bf16[2,256,768]{2,1,0:T(8,128)(2,1)S(1)}, bf16[2,256,768]{2,1,0:T(8,128)(2,1)}, u32[]{:S(2)}) copy-start(bf16[2,256,768]{2,1,0:T(8,128)(2,1)} %param.18) | copy-start | bytes 2359300
  7.2 123.1 %all-gather.4.cloned.1.call-start = ((), (), s32[]{:S(2)}) async-start(), calls=%async_computation.5 | async-start | bytes 14733312 | tf_op jit(solution)/shard_map/all_gather | solution.py:59
  24.5 194.7 %all-gather.8.cloned.1.call-start = ((), (), s32[]{:S(2)}) async-start(), calls=%async_computation.7 | async-start | bytes 3932160 | tf_op jit(solution)/shard_map/all_gather | solution.py:102
  150.4 6.7 copy-start.25
  153.0 4.2 copy-start.33
  157.2 126.3 %all-gather.6.cloned.1.call-start = ((), (), s32[]{:S(2)}) async-start(), calls=%async_computation.6 | async-start | bytes 3932160 | tf_op jit(solution)/shard_map/all_gather | solution.py:103
  163.0 309.3 %reduce-scatter.17.cloned.1.call-start = ((), (), s32[]{:S(2)}) async-start(), calls=%async_computation.9 | async-start | bytes 3932160 | tf_op jit(solution)/shard_map/reduce_scatter | solution.py:153
  186.3 37.6 %copy-start.8 = (bf16[2,256,12,64]{1,0,3,2:T(2,128)(2,1)}, bf16[2,256,12,64]{1,0,3,2:T(2,128)(2,1)S(1)}, u32[]{:S(2)}) copy-start(bf16[2,256,12,64]{1,0,3,2:T(2,128)(2,1)S(1)} %reshape.485) | copy-start | bytes 2359300
  300.9 8.7 slice-start
  301.9 15.6 %copy-start.6 = (f32[512,768]{1,0:T(8,128)}, f32[512,768]{1,0:T(8,128)S(1)}, u32[]{:S(2)}) copy-start(f32[512,768]{1,0:T(8,128)S(1)} %get-tuple-element.59) | copy-start | bytes 4718596
  302.2 7.4 slice-start.1
  302.2 7.4 copy-start.16
  302.2 12.1 %slice-start.2 = ((s8[4718592]{0:T(1024)(128)(4,1)}), s8[4194304]{0:T(1024)(128)(4,1)S(1)}, s32[]{:S(2)}) async-start(s8[4718592]{0:T(1024)(128)(4,1)} %bitcast.131), calls=%async_computation.15 | async-start | bytes 8388608
  309.6 4.7 slice-start.3
  314.3 3.1 copy-start.34
  334.1 145.7 %reduce-scatter.15.cloned.1.call-start = ((), (), s32[]{:S(2)}) async-start(), calls=%async_computation.8 | async-start | bytes 3932160 | tf_op jit(solution)/shard_map/reduce_scatter | solution.py:150
  353.1 16.5 %copy-start.9 = (bf16[2,256,12,64]{1,0,3,2:T(2,128)(2,1)S(1)}, bf16[2,256,12,64]{1,0,3,2:T(2,128)(2,1)}, u32[]{:S(2)}) copy-start(bf16[2,256,12,64]{1,0,3,2:T(2,128)(2,1)} %copy-done.8) | copy-start | bytes 2359300
  369.6 4.5 copy-start
  377.0 246.3 %reduce-scatter.21.cloned.1.call-start = ((), (), s32[]{:S(2)}) async-start(), calls=%async_computation.11 | async-start | bytes 4933632
  428.0 363.3 %reduce-scatter.23.cloned.1.call-start = ((), (), s32[]{:S(2)}) async-start(), calls=%async_computation.12 | async-start | bytes 4933632
  447.5 513.2 %reduce-scatter.19.cloned.1.call-start = ((), (), s32[]{:S(2)}) async-start(), calls=%async_computation.10 | async-start | bytes 4933632
  462.8 6.4 copy-start.20
  466.7 7.6 copy-start.23
  477.3 5.1 copy-start.2
  477.3 5.1 copy-start.10
  477.3 5.1 copy-start.26
  479.9 2.5 copy-start.18
  495.4 30.0 %copy-start.11 = (bf16[32,18432]{1,0:T(8,128)(2,1)S(1)}, bf16[32,18432]{1,0:T(8,128)(2,1)}, u32[]{:S(2)}) copy-start(bf16[32,18432]{1,0:T(8,128)(2,1)} %convert_element_type.358) | copy-start | bytes 3538948
  541.5 7.4 copy-start.30
  541.5 7.4 copy-start.29
  541.5 7.4 copy-start.5
  541.5 7.4 copy-start.28
  (15 other events, 18.9 us)
Sparse Core Ops, SparseCore 0:
  24.6 105.6 all-gather.3
  157.3 61.8 all-gather.7
  221.3 62.0 all-gather.5
  334.2 59.0 reduce-scatter.16
  395.5 60.3 reduce-scatter.14
  458.0 165.3 reduce-scatter.20
  625.7 165.6 reduce-scatter.22
  793.7 166.9 reduce-scatter.18

commit v3 on v2

--- a/solution.py
+++ b/solution.py
@@ -66,14 +66,17 @@
     return out
 
 
-def scatter_all(grads, groups):
+def scatter_all(grads, mesh_shape):
+    groups = mesh_shape[0] * mesh_shape[1]
     sub = 8
     parts = [g.reshape(groups, -1).astype(jnp.bfloat16) for g in grads]
     flat = jnp.concatenate(parts, axis=1)
     size = flat.shape[1]
     padded = -(-size // (sub * 128)) * sub * 128
-    flat = jnp.pad(flat, ((0, 0), (0, padded - size))).reshape(groups, sub, padded // sub)
-    mine = lax.psum_scatter(flat, ALL, scatter_dimension=0, tiled=True).reshape(-1).astype(jnp.float32)
+    flat = jnp.pad(flat, ((0, 0), (0, padded - size)))
+    flat = flat.reshape(mesh_shape[0], mesh_shape[1], sub, padded // sub)
+    flat = lax.psum_scatter(flat, "dp", scatter_dimension=0, tiled=True)
+    mine = lax.psum_scatter(flat, "ctx", scatter_dimension=1, tiled=True).reshape(-1).astype(jnp.float32)
     out, off = [], 0
     for g in grads:
         size = g.size // groups
@@ -162,12 +165,25 @@
     d_x, grad_ln1_gain, grad_ln1_bias = norm_back(d_normed, xhat1, rstd1, f32(ln1_gain))
     input_grad = (d_middle + d_x).astype(jnp.bfloat16).reshape(seqs, rows, width)
 
-    ffn_part = scatter_all((grad_ln2_gain, grad_ln2_bias, grad_wi, grad_bi), groups)
-    ffn_out_part = scatter_all((grad_wf, grad_bf), groups)
-    attn_part = scatter_all(
-        (grad_ln1_gain, grad_ln1_bias, grad_wq, grad_bq, grad_wk, grad_wv, grad_bv, grad_wo, grad_bo), groups
-    )
-    return (output, input_grad) + tuple(attn_part) + tuple(ffn_part) + tuple(ffn_out_part)
+    grads = (
+        grad_ln1_gain,
+        grad_ln1_bias,
+        grad_wq,
+        grad_bq,
+        grad_wk,
+        grad_wv,
+        grad_bv,
+        grad_wo,
+        grad_bo,
+        grad_ln2_gain,
+        grad_ln2_bias,
+        grad_wi,
+        grad_bi,
+        grad_wf,
+        grad_bf,
+    )
+    mesh_shape = (lax.axis_size("dp"), lax.axis_size("ctx"))
+    return (output, input_grad) + tuple(scatter_all(grads, mesh_shape))
 
 
 def solution(mesh):

time: 985 us -> 799 us (0.81)
  waiting for transfers between devices: 581 us -> 360 us
  local copies, waits for them, and re-layouts: 220 us -> 253 us
    unnamed x11 -> x8, waiting for transfers between devices: 405 us -> 31.5 us
    reduce_scatter x0 -> x1, waiting for transfers between devices: none -> 102 us  [scatter_all(): flat = lax.psum_scatter(flat, 'dp', scatter_dimension=0, tiled=True)]
    reduce_scatter x1, waiting for transfers between devices: 0.01 us -> 54 us  [per_device(): lax.psum_scatter(v_terms.reshape(seqs, total, width).astype(jnp.bfloat16)...]
    unnamed x97 -> x128, local copies, waits for them, and re-layouts: 93.3 us -> 116 us
  transfers between devices with their start and end apart: 8 -> 7, of which waited for: 6 -> 6; matrix products, arithmetic and copies ran while one was open for 27% -> 17% of each run, Pallas kernels for 0% -> 0%
where the time goes in v3:
time: 799 us; the launch traced here: 787 us
  waiting for transfers between devices  360 us (45%)
  local copies, waits for them, and re-layouts  253 us (32%)
  matrix products  130 us (16%)
  other arithmetic  27.9 us (3%)
  between operations  15.2 us (2%)
    unnamed x128, local copies, waits for them, and re-layouts  116 us
    all_gather x1, waiting for transfers between devices, gather_all(): lax.all_gather(pack(shards, sub), ALL, axis=0, tiled=True)  104 us
    reduce_scatter x1, waiting for transfers between devices, scatter_all(): flat = lax.psum_scatter(flat, 'dp', scatter_dimension=0, tiled=True)  102 us
    reduce_scatter x1, waiting for transfers between devices, per_device(): lax.psum_scatter(v_terms.reshape(seqs, total, width).astype(jnp.bfloat16)...  54 us
    all_gather x1, waiting for transfers between devices, per_device(): lax.all_gather(v.reshape(seqs, rows, width), 'ctx', axis=1, tiled=True)  45.4 us
    unnamed x8, waiting for transfers between devices  31.5 us
    convert_element_type x15, local copies, waits for them, and re-layouts, scatter_all(): parts = [g.reshape(groups, -1).astype(jnp.bfloat16) for g in grads]  28.9 us
    dot_general x6, matrix products, mm(): return jnp.dot(left, right, preferred_element_type=jnp.float32)  23.2 us
  transfers between devices with their start and end apart: 7, of which 6 were waited for; matrix products, arithmetic and copies ran while one was open for 17% of the time, Pallas kernels for 0%

profile of v3, /device:TPU:0, one launch (start us, length us, event | category | flops | bytes accessed | tf_op | source)
XLA Modules:
  0.0 786.5 jit_solution(1905648825334790903)
XLA Ops:
  12.5 10.6 %concatenate.6 = bf16[221472]{0:T(1024)(128)(2,1)S(1)} concatenate(bf16[24]{0:T(256)(128)(2,1)} %param.20, bf16[24]{0:T(256)(128)(2,1)} %param.21, bf16[18432]{0:T(1024)(128)(2,1)S(1)} %reshape.461, bf16[24]{0:T(256)(128)(2,1)} %param.23, bf16[18432]{0:T(1024)(128)(2,1)S(1)} %reshape.462, bf16[18432]{0:T(1024)(128)(2,1)S(1)} %reshape.463, bf16[24]{0:T(256)(128)(2,1)} %param.26, ...), dimensions={0} | concatenate | bytes 885888 | tf_op jit(solution)/shard_map/concatenate | solution.py:50
  26.3 104.1 %all-gather.4.cloned.1.call-done = bf16[512,13952]{1,0:T(8,128)(2,1)} async-done(((bf16[16,13952]{1,0:T(8,128)(2,1)}), bf16[512,13952]{1,0:T(8,128)(2,1)}) %all-gather.4.cloned.1.call-update) | async-done | bytes 14286864 | tf_op jit(solution)/shard_map/all_gather | solution.py:59
  130.3 13.3 %reshape.468 = bf16[32,223232]{1,0:T(8,128)(2,1)} reshape(bf16[512,13952]{1,0:T(8,128)(2,1)} %all-gather.4.cloned.1.call-done) | data formatting | bytes 28573696 | tf_op jit(solution)/shard_map/reshape | solution.py:59
  145.1 5.7 fusion.63
  162.6 10.1 %fusion.62 = (bf16[32,73728]{1,0:T(8,128)(2,1)}, bf16[32,73728]{1,0:T(8,128)(2,1)}) fusion(bf16[32,223232]{1,0:T(8,128)(2,1)} %reshape.468), kind=kLoop, calls=%fused_computation.104 | loop fusion | bytes 18874368 | tf_op jit(solution)/shard_map/slice | solution.py:63
  183.0 6.1 reshape.478
  189.3 6.0 reshape.479
  195.4 23.0 %all-gather.8.cloned.1.call-done = bf16[2,1024,768]{2,1,0:T(8,128)(2,1)} async-done(((bf16[2,256,768]{2,1,0:T(8,128)(2,1)}), bf16[2,1024,768]{2,1,0:T(8,128)(2,1)}) %all-gather.8.cloned.1.call-update) | async-done | bytes 3145744 | tf_op jit(solution)/shard_map/all_gather | solution.py:105
  223.1 14.3 %fusion.67 = (f32[2,12,256]{2,1,0:T(8,128)S(1)}, f32[2,12,256,1024]{3,2,1,0:T(8,128)}) fusion(pred[2,1024]{1,0:T(4,128)(4,1)S(1)} %copy-done.45, bf16[2,1024,12,64]{1,3,2,0:T(8,128)(2,1)} %bitcast.125, bf16[2,256,12,64]{1,0,3,2:T(2,128)(2,1)S(1)} %reshape.473), kind=kOutput, calls=%fused_computation.109 | convolution fusion | flops 830473216 | bytes 29124608 | tf_op jit(solution)/shard_map/sub | solution.py:116
  237.3 45.4 %all-gather.6.cloned.1.call-done = bf16[2,1024,768]{2,1,0:T(8,128)(2,1)} async-done(((bf16[2,256,768]{2,1,0:T(8,128)(2,1)}), bf16[2,1024,768]{2,1,0:T(8,128)(2,1)}) %all-gather.6.cloned.1.call-update) | async-done | bytes 3145744 | tf_op jit(solution)/shard_map/all_gather | solution.py:106
  287.3 11.5 %fusion.40 = bf16[2,256,12,64]{1,3,2,0:T(8,128)(2,1)S(1)} fusion(bf16[2,1024,12,64]{1,3,2,0:T(8,128)(2,1)} %bitcast.133, f32[2,12,256,1024]{3,2,1,0:T(8,128)} %get-tuple-element.60, f32[2,12,256]{2,1,0:T(8,128)S(1)} %get-tuple-element.59), kind=kOutput, calls=%fused_computation.69 | convolution fusion | flops 818282496 | bytes 29122560 | tf_op jit(solution)/shard_map/shqk,skhd->sqhd/dot_general | solution.py:119
  301.5 7.4 multiply_convert_fusion.2
  327.0 16.3 %multiply_reduce_fusion = (f32[2,12,256]{2,1,0:T(8,128)S(1)}, f32[2,12,256,1024]{3,2,1,0:T(8,128)}) fusion(f32[2,12,256,1024]{3,2,1,0:T(8,128)} %get-tuple-element.60, f32[2,12,256]{2,1,0:T(8,128)S(1)} %get-tuple-element.59, bf16[2,1024,12,64]{1,3,2,0:T(8,128)(2,1)S(1)} %bitcast.134, bf16[2,256,12,64]{1,0,3,2:T(2,128)(2,1)} %reshape.483), kind=kOutput, calls=%fused_computation.2 | convolution fusion | flops 824174592 | bytes 54312960 | tf_op jit(solution)/shard_map/sqhd,skhd->shqk/dot_general | solution.py:146
  343.3 16.5 %multiply_convert_fusion = bf16[2,12,256,1024]{3,2,1,0:T(8,128)(2,1)S(1)} fusion(f32[2,12,256,1024]{3,2,1,0:T(8,128)} %get-tuple-element.67, f32[2,12,256]{2,1,0:T(8,128)S(1)} %get-tuple-element.66, f32[2,12,256,1024]{3,2,1,0:T(8,128)} %get-tuple-element.60, f32[2,12,256]{2,1,0:T(8,128)S(1)} %get-tuple-element.59), kind=kLoop, calls=%fused_computation.1 | loop fusion | flops 25165824 | bytes 62963712 | tf_op jit(solution)/shard_map/convert_element_type | solution.py:148
  367.4 10.4 %fusion.17 = bf16[2,12,64,1024]{3,2,1,0:T(8,128)(2,1)S(1)} fusion(bf16[2,256,12,64]{1,0,3,2:T(2,128)(2,1)} %reshape.483, f32[2,12,256,1024]{3,2,1,0:T(8,128)} %get-tuple-element.60, f32[2,12,256]{2,1,0:T(8,128)S(1)} %get-tuple-element.59), kind=kOutput, calls=%fused_computation.29 | convolution fusion | flops 819462144 | bytes 29122560 | tf_op jit(solution)/shard_map/shqk,sqhd->skhd/dot_general | solution.py:152
  382.9 9.3 %fusion.73 = (bf16[12,64]{1,0:T(8,128)(2,1)}, bf16[2,256,12,64]{1,3,2,0:T(8,128)(2,1)S(1)}) fusion(bf16[2,1024,12,64]{1,3,2,0:T(8,128)(2,1)S(1)} %bitcast.126, bf16[2,12,256,1024]{3,2,1,0:T(8,128)(2,1)} %copy-done), kind=kOutput, calls=%fused_computation.111 | convolution fusion | flops 806485248 | bytes 16516608 | tf_op jit(solution)/shard_map/shqk,skhd->sqhd/dot_general | solution.py:149
  402.2 7.4 convolution_convert_fusion.1
  409.6 6.1 convert_element_type.349
  416.4 6.8 convolution_convert_fusion
  423.2 6.2 convert_element_type.352
  435.0 54.0 %reduce-scatter.10.cloned.1.call-done = bf16[2,256,768]{2,1,0:T(8,128)(2,1)} async-done(((bf16[2,1024,768]{2,1,0:T(8,128)(2,1)}), bf16[2,256,768]{2,1,0:T(8,128)(2,1)}) %reduce-scatter.10.cloned.1.call-update) | async-done | bytes 786448 | tf_op jit(solution)/shard_map/reduce_scatter | solution.py:156
  514.4 8.6 %dynamic-update-slice.2 = bf16[32,221472]{1,0:T(8,128)(2,1)} dynamic-update-slice(bf16[32,221472]{1,0:T(8,128)(2,1)} %dynamic-update-slice.1, bf16[32,18432]{1,0:T(8,128)(2,1)S(1)} %copy-done.12, s32[]{} %constant.64, s32[]{} %constant.66) | dynamic-update-slice | bytes 2359300
  524.6 8.9 %dynamic-update-slice.4 = bf16[32,221472]{1,0:T(8,128)(2,1)} dynamic-update-slice(bf16[32,221472]{1,0:T(8,128)(2,1)} %dynamic-update-slice.3, bf16[32,18432]{1,0:T(8,128)(2,1)} %convert_element_type.337, s32[]{} %constant.64, s32[]{} %constant.68) | dynamic-update-slice | bytes 2359300
  533.5 9.1 %dynamic-update-slice.5 = bf16[32,221472]{1,0:T(8,128)(2,1)} dynamic-update-slice(bf16[32,221472]{1,0:T(8,128)(2,1)} %dynamic-update-slice.4, bf16[32,18432]{1,0:T(8,128)(2,1)} %convert_element_type.339, s32[]{} %constant.64, s32[]{} %constant.69) | dynamic-update-slice | bytes 2359300
  544.1 8.6 %dynamic-update-slice.7 = bf16[32,221472]{1,0:T(8,128)(2,1)} dynamic-update-slice(bf16[32,221472]{1,0:T(8,128)(2,1)} %dynamic-update-slice.6, bf16[32,18432]{1,0:T(8,128)(2,1)S(1)} %copy-done.11, s32[]{} %constant.64, s32[]{} %constant.71) | dynamic-update-slice | bytes 2359300
  557.2 27.5 %dynamic-update-slice.11 = bf16[32,221472]{1,0:T(8,128)(2,1)} dynamic-update-slice(bf16[32,221472]{1,0:T(8,128)(2,1)} %dynamic-update-slice.10, bf16[32,73728]{1,0:T(8,128)(2,1)} %convert_element_type.349, s32[]{} %constant.64, s32[]{} %constant.75) | dynamic-update-slice | bytes 9437188
  586.3 27.1 %dynamic-update-slice.13 = bf16[32,221472]{1,0:T(8,128)(2,1)} dynamic-update-slice(bf16[32,221472]{1,0:T(8,128)(2,1)} %dynamic-update-slice.12, bf16[32,73728]{1,0:T(8,128)(2,1)} %convert_element_type.352, s32[]{} %constant.64, s32[]{} %constant.77) | dynamic-update-slice | bytes 9437188
  614.8 8.2 %pad.9 = bf16[32,222208]{1,0:T(8,128)(2,1)S(1)} pad(bf16[32,221472]{1,0:T(8,128)(2,1)} %dynamic-update-slice.14, bf16[]{:T(256)} %constant.31.clone.1), padding=0_0x0_736 | pad | bytes 28395522 | tf_op jit(solution)/shard_map/jit(_pad)/pad | solution.py:76
  623.0 6.3 copy.82
  629.4 102.1 %reduce-scatter.12.cloned.1.call-done = bf16[1,4,8,27776]{3,2,1,0:T(8,128)(2,1)} async-done(((bf16[8,4,8,27776]{3,2,1,0:T(8,128)(2,1)}), bf16[1,4,8,27776]{3,2,1,0:T(8,128)(2,1)}) %reduce-scatter.12.cloned.1.call-update) | async-done | bytes 1777680 | tf_op jit(solution)/shard_map/reduce_scatter | solution.py:78
  731.7 7.3 add_convert_fusion
  740.5 31.4 %reduce-scatter.14.cloned.1.call-done = bf16[1,1,8,27776]{3,2,1,0:T(8,128)(2,1)} async-done(((bf16[1,4,8,27776]{3,2,1,0:T(8,128)(2,1)}), bf16[1,1,8,27776]{3,2,1,0:T(8,128)(2,1)}) %reduce-scatter.14.cloned.1.call-update) | async-done | bytes 444432
  (227 shorter events, 135.5 us)
Async XLA Ops:
  7.2 123.1 %all-gather.4.cloned.1.call-start = ((), (), s32[]{:S(2)}) async-start(), calls=%async_computation.4 | async-start | bytes 14733312 | tf_op jit(solution)/shard_map/all_gather | solution.py:59
  12.5 12.0 %copy-start.1 = (bf16[2,256,768]{2,1,0:T(8,128)(2,1)S(1)}, bf16[2,256,768]{2,1,0:T(8,128)(2,1)}, u32[]{:S(2)}) copy-start(bf16[2,256,768]{2,1,0:T(8,128)(2,1)} %param.18) | copy-start | bytes 2359300
  24.5 193.9 %all-gather.8.cloned.1.call-start = ((), (), s32[]{:S(2)}) async-start(), calls=%async_computation.6 | async-start | bytes 3932160 | tf_op jit(solution)/shard_map/all_gather | solution.py:105
  153.8 22.4 %copy-start.22 = (bf16[2,256,768]{2,1,0:T(8,128)(2,1)}, bf16[2,256,768]{2,1,0:T(8,128)(2,1)S(1)}, u32[]{:S(2)}) copy-start(bf16[2,256,768]{2,1,0:T(8,128)(2,1)S(1)} %fusion.25) | copy-start | bytes 2359300
  156.4 126.3 %all-gather.6.cloned.1.call-start = ((), (), s32[]{:S(2)}) async-start(), calls=%async_computation.5 | async-start | bytes 3932160 | tf_op jit(solution)/shard_map/all_gather | solution.py:106
  162.6 268.7 %reduce-scatter.8.cloned.1.call-start = ((), (), s32[]{:S(2)}) async-start(), calls=%async_computation.7 | async-start | bytes 3932160 | tf_op jit(solution)/shard_map/reduce_scatter | solution.py:153
  180.7 42.3 %copy-start.8 = (bf16[2,256,12,64]{1,0,3,2:T(2,128)(2,1)}, bf16[2,256,12,64]{1,0,3,2:T(2,128)(2,1)S(1)}, u32[]{:S(2)}) copy-start(bf16[2,256,12,64]{1,0,3,2:T(2,128)(2,1)S(1)} %reshape.473) | copy-start | bytes 2359300
  189.2 112.2 %copy-start.42 = (f32[768]{0:T(1024)}, f32[768]{0:T(1024)S(1)}, u32[]{:S(2)}) copy-start(f32[768]{0:T(1024)S(1)} %reshape.500) | copy-start | bytes 9220
  189.3 128.4 %copy-start.32 = (f32[768]{0:T(1024)}, f32[768]{0:T(1024)S(1)}, u32[]{:S(2)}) copy-start(f32[768]{0:T(1024)S(1)} %reshape.499) | copy-start | bytes 9220
  195.4 27.7 %copy-start.45 = (pred[2,1024]{1,0:T(4,128)(4,1)S(1)}, pred[2,1024]{1,0:T(4,128)(4,1)}, u32[]{:S(2)}) copy-start(pred[2,1024]{1,0:T(4,128)(4,1)} %iota_compare_fusion) | copy-start | bytes 6148
  300.1 8.7 %slice-start = ((s8[4718592]{0:T(1024)(128)(4,1)}), s8[4194304]{0:T(1024)(128)(4,1)S(1)}, s32[]{:S(2)}) async-start(s8[4718592]{0:T(1024)(128)(4,1)} %bitcast.127), calls=%async_computation.11 | async-start | bytes 8388608
  301.1 16.6 %copy-start.7 = (f32[512,768]{1,0:T(8,128)}, f32[512,768]{1,0:T(8,128)S(1)}, u32[]{:S(2)}) copy-start(f32[512,768]{1,0:T(8,128)S(1)} %get-tuple-element.62) | copy-start | bytes 4718596
  301.4 16.3 %copy-start.37 = (f32[512]{0:T(512)}, f32[512]{0:T(512)S(1)}, u32[]{:S(2)}) copy-start(f32[512]{0:T(512)S(1)} %add_rsqrt_fusion) | copy-start | bytes 6148
  301.4 7.4 slice-start.1
  301.5 7.4 copy-start.17
  301.5 12.7 %slice-start.2 = ((s8[4718592]{0:T(1024)(128)(4,1)}), s8[4194304]{0:T(1024)(128)(4,1)S(1)}, s32[]{:S(2)}) async-start(s8[4718592]{0:T(1024)(128)(4,1)} %bitcast.129), calls=%async_computation.13 | async-start | bytes 8388608
  320.1 6.9 copy-start.15
  343.3 16.5 %copy-start.9 = (bf16[2,256,12,64]{1,0,3,2:T(2,128)(2,1)S(1)}, bf16[2,256,12,64]{1,0,3,2:T(2,128)(2,1)}, u32[]{:S(2)}) copy-start(bf16[2,256,12,64]{1,0,3,2:T(2,128)(2,1)} %copy-done.8) | copy-start | bytes 2359300
  367.3 121.7 %reduce-scatter.10.cloned.1.call-start = ((), (), s32[]{:S(2)}) async-start(), calls=%async_computation.8 | async-start | bytes 3932160 | tf_op jit(solution)/shard_map/reduce_scatter | solution.py:156
  380.7 350.8 %reduce-scatter.12.cloned.1.call-start = ((), (), s32[]{:S(2)}) async-start(), calls=%async_computation.9 | async-start | bytes 15998976 | tf_op jit(solution)/shard_map/reduce_scatter | solution.py:78
  431.3 57.7 %copy-start.2 = (bf16[2,256,768]{2,1,0:T(8,128)(2,1)S(1)}, bf16[2,256,768]{2,1,0:T(8,128)(2,1)}, u32[]{:S(2)}) copy-start(bf16[2,256,768]{2,1,0:T(8,128)(2,1)} %param.18) | copy-start | bytes 2359300
  431.3 57.7 %copy-start.10 = (bf16[768,768]{1,0:T(8,128)(2,1)S(1)}, bf16[768,768]{1,0:T(8,128)(2,1)}, u32[]{:S(2)}) copy-start(bf16[768,768]{1,0:T(8,128)(2,1)} %reshape.469) | copy-start | bytes 3538948
  431.3 57.7 %copy-start.27 = (f32[768]{0:T(1024)S(1)}, f32[768]{0:T(1024)}, u32[]{:S(2)}) copy-start(f32[768]{0:T(1024)} %copy-done.26) | copy-start | bytes 9220
  505.7 8.7 %copy-start.12 = (bf16[32,18432]{1,0:T(8,128)(2,1)S(1)}, bf16[32,18432]{1,0:T(8,128)(2,1)}, u32[]{:S(2)}) copy-start(bf16[32,18432]{1,0:T(8,128)(2,1)} %convert_element_type.334) | copy-start | bytes 3538948
  533.5 10.6 %copy-start.11 = (bf16[32,18432]{1,0:T(8,128)(2,1)S(1)}, bf16[32,18432]{1,0:T(8,128)(2,1)}, u32[]{:S(2)}) copy-start(bf16[32,18432]{1,0:T(8,128)(2,1)} %convert_element_type.342) | copy-start | bytes 3538948
  557.2 27.6 %copy-start.30 = (bf16[32,96]{1,0:T(8,128)(2,1)S(1)}, bf16[32,96]{1,0:T(8,128)(2,1)}, u32[]{:S(2)}) copy-start(bf16[32,96]{1,0:T(8,128)(2,1)} %convert_element_type.350) | copy-start | bytes 18436
  629.3 102.2 %copy-start.28 = (f32[32,24]{1,0:T(8,128)S(1)}, f32[32,24]{1,0:T(8,128)}, u32[]{:S(2)}) copy-start(f32[32,24]{1,0:T(8,128)} %get-tuple-element.27) | copy-start | bytes 9220
  629.4 142.5 %reduce-scatter.14.cloned.1.call-start = ((), (), s32[]{:S(2)}) async-start(), calls=%async_computation.10 | async-start | bytes 2222080
  731.6 7.4 copy-start.36
  731.7 7.4 copy-start.35
  731.7 7.4 copy-start.6
  731.7 7.4 copy-start.31
  (29 other events, 89.4 us)
Sparse Core Ops, SparseCore 0:
  24.6 105.6 all-gather.3
  156.5 61.8 all-gather.7
  220.5 62.0 all-gather.5
  367.5 59.0 reduce-scatter.7
  428.7 60.3 reduce-scatter.9
  629.5 102.0 reduce-scatter.11
  733.8 37.9 reduce-scatter.13

commit v4 on v3

v4 whole, which is shorter than its diff:
```python
import math

import jax
import jax.numpy as jnp
from jax import lax
from jax.sharding import PartitionSpec as P

H = 12
HD = 64
EPS = 1e-06
ALL = ("dp", "ctx")


def row_stats(rows):
    mean = jnp.mean(rows, axis=-1, keepdims=True)
    center = rows - mean
    rstd = lax.rsqrt(jnp.mean(center * center, axis=-1, keepdims=True) + EPS)
    return center * rstd, rstd


def norm_back_rows(d_normed, xhat, rstd, gain):
    e = d_normed * gain
    mean_e = jnp.mean(e, axis=-1, keepdims=True)
    mean_ex = jnp.mean(e * xhat, axis=-1, keepdims=True)
    return (e - mean_e - xhat * mean_ex) * rstd


def mm(left, right):
    return jnp.dot(left, right, preferred_element_type=jnp.float32)


def outer(left_rows, right_rows):
    return lax.dot_general(
        left_rows, right_rows, (((0,), (0,)), ((), ())), preferred_element_type=jnp.float32
    )


def back(grad_rows, weight):
    return lax.dot_general(
        grad_rows, weight, (((1,), (1,)), ((), ())), preferred_element_type=jnp.float32
    )


def col_sum(rows):
    return jnp.sum(rows.astype(jnp.float32), axis=0)


def round_up(value, step):
    return -(-value // step) * step


MATS = (2, 4, 5, 7, 11, 13)
VECS = (0, 1, 3, 6, 8, 9, 10, 12, 14)


def layout(shards, width, sub):
    rows = [shards[i].size // width for i in MATS]
    vec_len = sum(shards[i].size for i in VECS)
    vec_rows = round_up(vec_len, width) // width
    total = round_up(sum(rows) + vec_rows, sub)
    return rows, vec_len, vec_rows, total


def gather_all(shards, width, groups):
    rows, vec_len, vec_rows, total = layout(shards, width, 16)
    vec = jnp.concatenate([shards[i].reshape(-1) for i in VECS])
    vec = jnp.pad(vec, (0, vec_rows * width - vec_len)).reshape(vec_rows, width)
    blocks = [shards[i].reshape(-1, width) for i in MATS] + [vec]
    packed = jnp.concatenate(blocks, axis=0)
    packed = jnp.pad(packed, ((0, total - packed.shape[0]), (0, 0)))
    full = lax.all_gather(packed[None], ALL, axis=0, tiled=True)
    out = [None] * 15
    off = 0
    for i, r in zip(MATS, rows):
        s = shards[i]
        out[i] = full[:, off:off + r, :].reshape((groups * s.shape[0],) + s.shape[1:])
        off += r
    vecs = full[:, off:off + vec_rows, :].reshape(groups, vec_rows * width)
    voff = 0
    for i in VECS:
        size = shards[i].size
        out[i] = vecs[:, voff:voff + size].reshape(groups * size)
        voff += size
    return out


def scatter_all(grads, width, mesh_shape):
    groups = mesh_shape[0] * mesh_shape[1]
    shard_like = [jnp.zeros((g.shape[0] // groups,) + g.shape[1:], jnp.float32) for g in grads]
    rows, vec_len, vec_rows, total = layout(shard_like, width, 16)
    vec = jnp.concatenate([grads[i].reshape(groups, -1) for i in VECS], axis=1)
    vec = jnp.pad(vec, ((0, 0), (0, vec_rows * width - vec_len))).reshape(groups, vec_rows, width)
    blocks = [grads[i].reshape(groups, -1, width) for i in MATS] + [vec]
    packed = jnp.concatenate([b.astype(jnp.bfloat16) for b in blocks], axis=1)
    packed = jnp.pad(packed, ((0, 0), (0, total - packed.shape[1]), (0, 0)))
    packed = packed.reshape(mesh_shape[0], mesh_shape[1], total, width)
    packed = lax.psum_scatter(packed, "dp", scatter_dimension=0, tiled=True)
    mine = lax.psum_scatter(packed, "ctx", scatter_dimension=1, tiled=True)
    mine = mine.reshape(total, width).astype(jnp.float32)
    out = [None] * 15
    off = 0
    for i, r in zip(MATS, rows):
        out[i] = mine[off:off + r, :].reshape(shard_like[i].shape)
        off += r
    vecs = mine[off:off + vec_rows, :].reshape(-1)
    voff = 0
    for i in VECS:
        size = shard_like[i].size
        out[i] = vecs[voff:voff + size]
        voff += size
    return out


def per_device(inputs, lengths, *rest):
    shards = rest[:15]
    out_grad = rest[15]
    n_ctx = lax.axis_size("ctx")
    mesh_shape = (lax.axis_size("dp"), n_ctx)
    groups = mesh_shape[0] * mesh_shape[1]
    seqs, rows, width = inputs.shape
    f32 = lambda a: a.astype(jnp.float32)

    blocks = [inputs]
    for b in range(1, n_ctx):
        blocks.append(lax.ppermute(inputs, "ctx", [(i, (i + b) % n_ctx) for i in range(n_ctx)]))
    (ln1_gain, ln1_bias, wq, bq, wk, wv, bv, wo, bo, ln2_gain, ln2_bias, wi, bi, wf, bf) = gather_all(
        shards, width, groups
    )
    me = lax.axis_index("ctx")
    total = n_ctx * rows
    source = (me - jnp.arange(n_ctx)) % n_ctx
    positions = (source[:, None] * rows + jnp.arange(rows)[None, :]).reshape(total)
    n = seqs * rows

    x_all = f32(jnp.concatenate(blocks, axis=1)).reshape(seqs * total, width)
    xhat_all, rstd_all = row_stats(x_all)
    normed_all = (xhat_all * f32(ln1_gain) + f32(ln1_bias)).astype(jnp.bfloat16)
    own = lambda a: a.reshape(seqs, total, width)[:, :rows].reshape(n, width)
    normed = own(normed_all)
    xhat1 = own(xhat_all)
    rstd1 = rstd_all.reshape(seqs, total, 1)[:, :rows].reshape(n, 1)
    x = f32(inputs).reshape(n, width)
    q = (mm(normed, wq) + f32(bq)).astype(jnp.bfloat16)
    k = mm(normed_all, wk).astype(jnp.bfloat16)
    v = (mm(normed_all, wv) + f32(bv)).astype(jnp.bfloat16)
    qh = q.reshape(seqs, rows, H, HD)
    kh = k.reshape(seqs, total, H, HD)
    vh = v.reshape(seqs, total, H, HD)
    scale = HD ** (-0.5)
    scores = jnp.einsum("sqhd,skhd->shqk", qh, kh, preferred_element_type=jnp.float32) * scale
    valid = positions[None, :] < lengths[:, None]
    scores = jnp.where(valid[:, None, None, :], scores, -1e30)
    top = jnp.max(scores, axis=-1, keepdims=True)
    expd = jnp.exp(scores - top)
    probs = expd / jnp.sum(expd, axis=-1, keepdims=True)
    low_probs = probs.astype(jnp.bfloat16)
    mixed = jnp.einsum("shqk,skhd->sqhd", low_probs, vh, preferred_element_type=jnp.float32)
    mixed = mixed.reshape(n, width).astype(jnp.bfloat16)
    middle = x + mm(mixed, wo) + f32(bo)
    xhat2, rstd2 = row_stats(middle)
    normed_two = (xhat2 * f32(ln2_gain) + f32(ln2_bias)).astype(jnp.bfloat16)
    ffn_pre = mm(normed_two, wi) + f32(bi)
    cdf = 0.5 * (1.0 + lax.erf(ffn_pre * (1.0 / math.sqrt(2.0))))
    ffn_act = (ffn_pre * cdf).astype(jnp.bfloat16)
    result = middle + mm(ffn_act, wf) + f32(bf)
    output = result.astype(jnp.bfloat16).reshape(seqs, rows, width)

    g = f32(out_grad).reshape(n, width)
    g_low = g.astype(jnp.bfloat16)
    grad_bf = col_sum(g_low)
    grad_wf = outer(ffn_act, g_low)
    d_act = back(g_low, wf)
    pdf = jnp.exp(-0.5 * ffn_pre * ffn_pre) * (1.0 / math.sqrt(2.0 * math.pi))
    d_pre = (d_act * (cdf + ffn_pre * pdf)).astype(jnp.bfloat16)
    grad_bi = col_sum(d_pre)
    grad_wi = outer(normed_two, d_pre)
    d_normed_two = back(d_pre, wi)
    d_mid = norm_back_rows(d_normed_two, xhat2, rstd2, f32(ln2_gain))
    grad_ln2_gain = jnp.sum(d_normed_two * xhat2, axis=0)
    grad_ln2_bias = jnp.sum(d_normed_two, axis=0)
    d_middle = g + d_mid
    d_branch = d_middle.astype(jnp.bfloat16)
    grad_bo = col_sum(d_branch)
    grad_wo = outer(mixed, d_branch)
    d_mixed = back(d_branch, wo).astype(jnp.bfloat16).reshape(seqs, rows, H, HD)
    d_probs = jnp.einsum("sqhd,skhd->shqk", d_mixed, vh, preferred_element_type=jnp.float32)
    inner = jnp.sum(probs * d_probs, axis=-1, keepdims=True)
    d_scores = (probs * (d_probs - inner)).astype(jnp.bfloat16)
    d_q = jnp.einsum("shqk,skhd->sqhd", d_scores, kh, preferred_element_type=jnp.float32) * scale
    d_q = d_q.reshape(n, width).astype(jnp.bfloat16)
    k_part = (
        jnp.einsum("shqk,sqhd->skhd", d_scores, qh, preferred_element_type=jnp.float32) * scale
    ).reshape(seqs * total, width).astype(jnp.bfloat16)
    v_part = jnp.einsum("shqk,sqhd->skhd", low_probs, d_mixed, preferred_element_type=jnp.float32)
    v_part = v_part.reshape(seqs * total, width).astype(jnp.bfloat16)
    grad_bq = col_sum(d_q)
    grad_bv = col_sum(v_part)
    grad_wq = outer(normed, d_q)
    grad_wk = outer(normed_all, k_part)
    grad_wv = outer(normed_all, v_part)
    kv_back = back(k_part, wk) + back(v_part, wv)
    q_back = back(d_q, wq)
    grad_ln1_gain = jnp.sum(kv_back * xhat_all, axis=0) + jnp.sum(q_back * xhat1, axis=0)
    grad_ln1_bias = jnp.sum(kv_back, axis=0) + jnp.sum(q_back, axis=0)

    kv_blocks = kv_back.reshape(seqs, total, width)
    d_normed = kv_blocks[:, :rows] + q_back.reshape(seqs, rows, width)
    for b in range(1, n_ctx):
        sent = kv_blocks[:, b * rows:(b + 1) * rows].astype(jnp.bfloat16)
        got = lax.ppermute(sent, "ctx", [(i, (i - b) % n_ctx) for i in range(n_ctx)])
        d_normed = d_normed + f32(got)
    d_x = norm_back_rows(d_normed.reshape(n, width), xhat1, rstd1, f32(ln1_gain))
    input_grad = (d_middle + d_x).astype(jnp.bfloat16).reshape(seqs, rows, width)

    grads = (
        grad_ln1_gain,
        grad_ln1_bias,
        grad_wq,
        grad_bq,
        grad_wk,
        grad_wv,
        grad_bv,
        grad_wo,
        grad_bo,
        grad_ln2_gain,
        grad_ln2_bias,
        grad_wi,
        grad_bi,
        grad_wf,
        grad_bf,
    )
    return (output, input_grad) + tuple(scatter_all(grads, width, mesh_shape))


def solution(mesh):
    row = P(("dp", "ctx"))
    mat = P(("dp", "ctx"), None)
    act = P("dp", "ctx", None)
    weight_specs = (row, row, mat, row, mat, mat, row, mat, row, row, row, mat, row, mat, row)
    return jax.shard_map(
        per_device,
        mesh=mesh,
        in_specs=(act, P("dp")) + weight_specs + (act,),
        out_specs=(act, act) + weight_specs,
        check_vma=False,
    )
```

time: 799 us -> 649 us (0.81)
  local copies, waits for them, and re-layouts: 253 us -> 126 us
  waiting for transfers between devices: 360 us -> 302 us
  matrix products: 130 us -> 148 us
  starting transfers between devices: 0.29 us -> 10.8 us
  other arithmetic: 27.9 us -> 37.6 us
    all_gather x3 -> x1, waiting for transfers between devices: 172 us -> 43.1 us  [gather_all(): full = lax.all_gather(packed[None], ALL, axis=0, tiled=True)]
    ppermute x0 -> x6, waiting for transfers between devices: none -> 104 us  [the longest x3 94.3 us: per_device(): lax.ppermute(inputs, 'ctx', [(i, (i + b) % n_ctx) for i in range(n_ctx)])]
    unnamed x128 -> x115, local copies, waits for them, and re-layouts: 116 us -> 19.9 us
    unnamed x8 -> x3, waiting for transfers between devices: 31.5 us -> 0.05 us
    reshape x19 -> x13, local copies, waits for them, and re-layouts: 44.2 us -> 22.6 us  [the longest x1 8.5 us: gather_all(): full[:, off:off + r, :].reshape((groups * s.shape[0],) + s.shape[1:])]
    ppermute x0 -> x6, starting transfers between devices: none -> 10.6 us  [the longest x3 6.14 us: per_device(): lax.ppermute(inputs, 'ctx', [(i, (i + b) % n_ctx) for i in range(n_ctx)])]
    convert_element_type x18 -> x7, local copies, waits for them, and re-layouts: 36.3 us -> 25.9 us  [the longest x2 8.48 us: scatter_all(): packed = jnp.concatenate([b.astype(jnp.bfloat16) for b in blocks], axis=1)]
    all_gather x2 -> x0, local copies, waits for them, and re-layouts: 9.32 us -> none  [the longest x1 4.67 us: per_device(): lax.all_gather(v.reshape(seqs, rows, width), 'ctx', axis=1, tiled=True)]
  transfers between devices with their start and end apart: 7 -> 9, of which waited for: 6 -> 6; matrix products, arithmetic and copies ran while one was open for 17% -> 8% of each run, Pallas kernels for 0% -> 0%
where the time goes in v4:
time: 649 us; the launch traced here: 639 us
  waiting for transfers between devices  302 us (47%)
  matrix products  148 us (23%)
  local copies, waits for them, and re-layouts  126 us (19%)
  other arithmetic  37.6 us (6%)
  between operations  14.7 us (2%)
  starting transfers between devices  10.8 us (2%)
    reduce_scatter x1, waiting for transfers between devices, scatter_all(): packed = lax.psum_scatter(packed, 'dp', scatter_dimension=0, tiled=True)  120 us
    ppermute x3, waiting for transfers between devices, per_device(): lax.ppermute(inputs, 'ctx', [(i, (i + b) % n_ctx) for i in range(n_ctx)])  94.3 us
    all_gather x1, waiting for transfers between devices, gather_all(): full = lax.all_gather(packed[None], ALL, axis=0, tiled=True)  43.1 us
    reduce_scatter x1, waiting for transfers between devices, scatter_all(): mine = lax.psum_scatter(packed, 'ctx', scatter_dimension=1, tiled=True)  34.9 us
    dot_general x6, matrix products, mm(): return jnp.dot(left, right, preferred_element_type=jnp.float32)  27.1 us
    dot_general x6, matrix products, back(): lax.dot_general(grad_rows, weight, (((1,), (1,)), ((), ())), preferred_el...  24.7 us
    dot_general x6, matrix products, outer(): lax.dot_general(left_rows, right_rows, (((0,), (0,)), ((), ())), preferre...  24.6 us
    convert_element_type x1, other arithmetic, per_device(): d_scores = (probs * (d_probs - inner)).astype(jnp.bfloat16)  21.4 us
  transfers between devices with their start and end apart: 9, of which 6 were waited for; matrix products, arithmetic and copies ran while one was open for 8% of the time, Pallas kernels for 0%

profile of v4, /device:TPU:0, one launch (start us, length us, event | category | flops | bytes accessed | tf_op | source)
XLA Modules:
  0.0 639.4 jit_solution(11003315465177381048)
XLA Ops:
  12.4 6.1 concatenate.17
  19.4 5.1 collective-permute-start.2
  27.7 25.1 %collective-permute-done.2 = bf16[2,256,768]{2,1,0:T(8,128)(2,1)S(1)} collective-permute-done((bf16[2,256,768]{2,1,0:T(8,128)(2,1)}, bf16[2,256,768]{2,1,0:T(8,128)(2,1)S(1)}, u32[]{:S(2)}, u32[]{:S(2)}) %collective-permute-start.2) | collective-permute-done | bytes 786464 | tf_op jit(solution)/shard_map/ppermute | solution.py:125
  52.8 69.2 %collective-permute-done.1 = bf16[2,256,768]{2,1,0:T(8,128)(2,1)S(1)} collective-permute-done((bf16[2,256,768]{2,1,0:T(8,128)(2,1)}, bf16[2,256,768]{2,1,0:T(8,128)(2,1)S(1)}, u32[]{:S(2)}, u32[]{:S(2)}) %collective-permute-start.1) | collective-permute-done | bytes 786464 | tf_op jit(solution)/shard_map/ppermute | solution.py:125
  125.0 43.1 %all-gather.3.cloned.1.call-done = bf16[9728,768]{1,0:T(8,128)(2,1)} async-done(((bf16[304,768]{1,0:T(8,128)(2,1)}), bf16[9728,768]{1,0:T(8,128)(2,1)}) %all-gather.3.cloned.1.call-update) | async-done | bytes 14942224 | tf_op jit(solution)/shard_map/all_gather | solution.py:71
  169.2 4.6 fusion.105
  173.8 8.0 %fusion.104 = (bf16[32,96,768]{2,1,0:T(8,128)(2,1)}, bf16[32,96,768]{2,1,0:T(8,128)(2,1)}) fusion(bf16[32,304,768]{2,1,0:T(8,128)(2,1)} %bitcast.224), kind=kLoop, calls=%fused_computation.173 | loop fusion | bytes 18874368 | tf_op jit(solution)/shard_map/slice | solution.py:76
  183.0 4.8 subtract_multiply_fusion
  200.8 4.8 convolution_convert_fusion.1
  208.7 4.8 reshape.643
  221.9 14.8 %fusion.108 = (f32[2,12,256]{2,1,0:T(8,128)S(1)}, f32[2,12,256,1024]{3,2,1,0:T(8,128)}) fusion(pred[2,1024]{1,0:T(4,128)(4,1)S(1)} %broadcast_compare_fusion, bf16[2,1024,12,64]{1,0,3,2:T(2,128)(2,1)S(1)} %reshape.643, bf16[2,256,12,64]{1,0,3,2:T(2,128)(2,1)} %reshape.641), kind=kOutput, calls=%fused_computation.177 | convolution fusion | flops 830473216 | bytes 29124608 | tf_op jit(solution)/shard_map/sub | solution.py:154
  236.7 11.8 %fusion.74 = bf16[2,256,12,64]{1,3,2,0:T(8,128)(2,1)S(1)} fusion(bf16[2,1024,12,64]{1,0,3,2:T(2,128)(2,1)} %reshape.638, f32[2,12,256,1024]{3,2,1,0:T(8,128)} %get-tuple-element.72, f32[2,12,256]{2,1,0:T(8,128)S(1)} %get-tuple-element.71), kind=kOutput, calls=%fused_computation.98 | convolution fusion | flops 818282496 | bytes 29122560 | tf_op jit(solution)/shard_map/shqk,skhd->sqhd/dot_general | solution.py:157
  250.5 8.5 %reshape.645 = bf16[768,3072]{1,0:T(8,128)(2,1)} reshape(bf16[32,96,768]{2,1,0:T(8,128)(2,1)} %get-tuple-element.30) | data formatting | bytes 9437184 | tf_op jit(solution)/shard_map/reshape | solution.py:76
  262.4 5.0 fusion.19
  267.4 5.1 fusion.120
  284.4 16.7 %multiply_reduce_fusion = (f32[2,12,256]{2,1,0:T(8,128)S(1)}, f32[2,12,256,1024]{3,2,1,0:T(8,128)}) fusion(f32[2,12,256,1024]{3,2,1,0:T(8,128)} %get-tuple-element.72, f32[2,12,256]{2,1,0:T(8,128)S(1)} %get-tuple-element.71, bf16[2,1024,12,64]{1,0,3,2:T(2,128)(2,1)} %reshape.638, bf16[2,256,12,64]{1,0,3,2:T(2,128)(2,1)} %reshape.649), kind=kOutput, calls=%fused_computation.2 | convolution fusion | flops 824174592 | bytes 54312960 | tf_op jit(solution)/shard_map/sqhd,skhd->shqk/dot_general | solution.py:186
  301.1 21.4 %multiply_convert_fusion = bf16[2,12,256,1024]{3,2,1,0:T(8,128)(2,1)} fusion(f32[2,12,256,1024]{3,2,1,0:T(8,128)} %get-tuple-element.77, f32[2,12,256]{2,1,0:T(8,128)S(1)} %get-tuple-element.76, f32[2,12,256,1024]{3,2,1,0:T(8,128)} %get-tuple-element.72, f32[2,12,256]{2,1,0:T(8,128)S(1)} %get-tuple-element.71), kind=kLoop, calls=%fused_computation.1 | loop fusion | flops 25165824 | bytes 62963712 | tf_op jit(solution)/shard_map/convert_element_type | solution.py:188
  322.5 9.5 %fusion.118 = (bf16[12,64]{1,0:T(8,128)(2,1)S(1)}, bf16[2,256,12,64]{1,3,2,0:T(8,128)(2,1)}) fusion(bf16[2,12,256,1024]{3,2,1,0:T(8,128)(2,1)} %multiply_convert_fusion, bf16[2,1024,12,64]{1,0,3,2:T(2,128)(2,1)S(1)} %reshape.643), kind=kOutput, calls=%fused_computation.179 | convolution fusion | flops 806485248 | bytes 16516608 | tf_op jit(solution)/shard_map/shqk,skhd->sqhd/dot_general | solution.py:189
  332.1 7.0 %fusion.23 = bf16[2,1024,12,64]{1,3,2,0:T(8,128)(2,1)S(1)} fusion(bf16[2,12,256,1024]{3,2,1,0:T(8,128)(2,1)} %multiply_convert_fusion, bf16[2,256,12,64]{1,0,3,2:T(2,128)(2,1)S(1)} %copy-done.13), kind=kOutput, calls=%fused_computation.45 | convolution fusion | flops 808452096 | bytes 16515072 | tf_op jit(solution)/shard_map/shqk,sqhd->skhd/dot_general | solution.py:192
  339.1 11.7 %fusion.119 = (bf16[12,64]{1,0:T(8,128)(2,1)S(1)}, bf16[2,1024,12,64]{1,3,2,0:T(8,128)(2,1)}) fusion(f32[2,12,256,1024]{3,2,1,0:T(8,128)} %get-tuple-element.72, f32[2,12,256]{2,1,0:T(8,128)S(1)} %get-tuple-element.71, bf16[2,256,12,64]{1,0,3,2:T(2,128)(2,1)S(1)} %copy-done.32), kind=kOutput, calls=%fused_computation.180 | convolution fusion | flops 821034240 | bytes 29124096 | tf_op jit(solution)/shard_map/shqk,sqhd->skhd/dot_general | solution.py:194
  353.0 7.5 %convolution_convert_fusion = bf16[768,3072]{1,0:T(8,128)(2,1)} fusion(bf16[512,3072]{1,0:T(8,128)(2,1)} %copy-done.46, f32[512,768]{1,0:T(8,128)} %copy-done.11, f32[768]{0:T(1024)S(1)} %reshape.672, f32[768]{0:T(1024)S(1)} %reshape.671, f32[512]{0:T(512)S(1)} %add_rsqrt_fusion.1, f32[512]{0:T(512)S(1)} %broadcast_multiply_fusion.3), kind=kOutput, calls=%fused_computation.39 | convolution fusion | flops 2420244480 | bytes 9447424 | tf_op jit(solution)/shard_map/dot_general | solution.py:33
  367.0 5.0 fusion.121
  377.8 9.0 %fusion.101 = (f32[768]{0:T(1024)S(1)}, f32[768]{0:T(1024)S(1)}, bf16[2048,768]{1,0:T(8,128)(2,1)}, f32[2048,768]{1,0:T(8,128)S(1)}) fusion(f32[2048]{0:T(1024)S(1)} %copy-done.41, f32[2048]{0:T(1024)S(1)} %copy-done.42, bf16[2,256,768]{2,1,0:T(8,128)(2,1)S(1)} %copy-done.6, bf16[2,256,768]{2,1,0:T(8,128)(2,1)S(1)} %copy-done.8, ...), kind=kOutput, calls=%fused_computation.171 | convolution fusion | flops 2442656256 | bytes 23228416 | tf_op jit(solution)/shard_map/dot_general | solution.py:39
  395.4 4.9 copy.88
  414.0 8.5 %convert_element_type.352 = bf16[32,96,768]{2,1,0:T(8,128)(2,1)} reshape(bf16[768,3072]{1,0:T(8,128)(2,1)} %convolution_convert_fusion) | data formatting | bytes 9437184 | tf_op jit(solution)/shard_map/convert_element_type | solution.py:94
  422.5 4.7 copy.91
  427.7 4.9 constant_dynamic-update-slice_fusion.7
  436.9 9.7 %collective-permute-done.4 = bf16[2,256,768]{2,1,0:T(8,128)(2,1)} collective-permute-done((bf16[2,256,768]{2,1,0:T(8,128)(2,1)}, bf16[2,256,768]{2,1,0:T(8,128)(2,1)}, u32[]{:S(2)}, u32[]{:S(2)}) %collective-permute-start.4) | collective-permute-done | bytes 786464 | tf_op jit(solution)/shard_map/ppermute | solution.py:210
  452.6 12.7 %pad.20 = bf16[32,304,768]{2,1,0:T(8,128)(2,1)} pad(bf16[32,289,768]{2,1,0:T(8,128)(2,1)} %copy_dynamic-update-slice_fusion, bf16[]{:T(256)} %constant.46.clone.1), padding=0_0x0_15x0_0 | pad | bytes 29147138 | tf_op jit(solution)/shard_map/jit(_pad)/pad | solution.py:95
  465.4 120.2 %reduce-scatter.3.cloned.1.call-done = bf16[1,4,304,768]{3,2,1,0:T(8,128)(2,1)} async-done(((bf16[8,4,304,768]{3,2,1,0:T(8,128)(2,1)}), bf16[1,4,304,768]{3,2,1,0:T(8,128)(2,1)}) %reduce-scatter.3.cloned.1.call-update) | async-done | bytes 1867792 | tf_op jit(solution)/shard_map/reduce_scatter | solution.py:97
  585.7 7.4 %add_convert_fusion.3 = bf16[512,768]{1,0:T(8,128)(2,1)} fusion(f32[512,768]{1,0:T(8,128)S(1)} %copy-done.12, bf16[3072,768]{1,0:T(8,128)(2,1)} %bitcast.232, f32[512,3072]{1,0:T(8,128)} %copy-done.45, f32[3072]{0:T(1024)S(1)} %copy-done.40, f32[768]{0:T(1024)S(1)} %reshape.674), kind=kOutput, calls=%fused_computation.81 | convolution fusion | flops 2426535936 | bytes 13384704 | tf_op jit(solution)/shard_map/dot_general | solution.py:29
  593.1 34.9 %reduce-scatter.5.cloned.1.call-done = bf16[1,1,304,768]{3,2,1,0:T(8,128)(2,1)} async-done(((bf16[1,4,304,768]{3,2,1,0:T(8,128)(2,1)}), bf16[1,1,304,768]{3,2,1,0:T(8,128)(2,1)}) %reduce-scatter.5.cloned.1.call-update) | async-done | bytes 466960 | tf_op jit(solution)/shard_map/reduce_scatter | solution.py:98
  (210 shorter events, 108.1 us)
Async XLA Ops:
  7.2 114.8 %copy-start.3 = (bf16[2,256,768]{2,1,0:T(8,128)(2,1)S(1)}, bf16[2,256,768]{2,1,0:T(8,128)(2,1)}, u32[]{:S(2)}) copy-start(bf16[2,256,768]{2,1,0:T(8,128)(2,1)} %param.18) | copy-start | bytes 2359300
  7.2 20.4 %copy-start.44 = (s32[2]{0:T(128)S(1)}, s32[2]{0:T(128)}, u32[]{:S(2)}) copy-start(s32[2]{0:T(128)} %param.19) | copy-start | bytes 28
  7.2 161.0 %all-gather.3.cloned.1.call-start = ((), (), s32[]{:S(2)}) async-start(), calls=%async_computation.4 | async-start | bytes 15409152 | tf_op jit(solution)/shard_map/all_gather | solution.py:71
  19.3 566.3 %reduce-scatter.3.cloned.1.call-start = ((), (), s32[]{:S(2)}) async-start(), calls=%async_computation.2 | async-start | bytes 16809984 | tf_op jit(solution)/shard_map/reduce_scatter | solution.py:97
  19.4 33.4 %collective-permute-start.2 = (bf16[2,256,768]{2,1,0:T(8,128)(2,1)}, bf16[2,256,768]{2,1,0:T(8,128)(2,1)S(1)}, u32[]{:S(2)}, u32[]{:S(2)}) collective-permute-start(bf16[2,256,768]{2,1,0:T(8,128)(2,1)} %param.18), channel_id=1, source_target_pairs={{0,3},{1,0},{2,1},{3,2},{4,7},{5,4},{6,5},{7,6},{8,11},{9,8},{10,9... | collective-permute-start | bytes 2359304 | tf_op jit(solution)/shard_map/ppermute | solution.py:125
  24.5 97.5 %collective-permute-start.1 = (bf16[2,256,768]{2,1,0:T(8,128)(2,1)}, bf16[2,256,768]{2,1,0:T(8,128)(2,1)S(1)}, u32[]{:S(2)}, u32[]{:S(2)}) collective-permute-start(bf16[2,256,768]{2,1,0:T(8,128)(2,1)} %param.18), channel_id=1, source_target_pairs={{0,2},{1,3},{2,0},{3,1},{4,6},{5,7},{6,4},{7,5},{8,10},{9,11},{10,... | collective-permute-start | bytes 2359304 | tf_op jit(solution)/shard_map/ppermute | solution.py:125
  24.5 97.5 %collective-permute-start = (bf16[2,256,768]{2,1,0:T(8,128)(2,1)}, bf16[2,256,768]{2,1,0:T(8,128)(2,1)S(1)}, u32[]{:S(2)}, u32[]{:S(2)}) collective-permute-start(bf16[2,256,768]{2,1,0:T(8,128)(2,1)} %param.18), channel_id=1, source_target_pairs={{0,1},{1,2},{2,3},{3,0},{4,5},{5,6},{6,7},{7,4},{8,9},{9,10},{10,1... | collective-permute-start | bytes 2359304 | tf_op jit(solution)/shard_map/ppermute | solution.py:125
  52.8 130.2 %copy-start.5 = (bf16[2,256,768]{2,1,0:T(8,128)(2,1)}, bf16[2,256,768]{2,1,0:T(8,128)(2,1)S(1)}, u32[]{:S(2)}) copy-start(bf16[2,256,768]{2,1,0:T(8,128)(2,1)S(1)} %collective-permute-done.2) | copy-start | bytes 2359300
  122.0 61.0 %copy-start.7 = (bf16[2,256,768]{2,1,0:T(8,128)(2,1)}, bf16[2,256,768]{2,1,0:T(8,128)(2,1)S(1)}, u32[]{:S(2)}) copy-start(bf16[2,256,768]{2,1,0:T(8,128)(2,1)S(1)} %collective-permute-done.1) | copy-start | bytes 2359300
  122.0 61.0 %copy-start.9 = (bf16[2,256,768]{2,1,0:T(8,128)(2,1)}, bf16[2,256,768]{2,1,0:T(8,128)(2,1)S(1)}, u32[]{:S(2)}) copy-start(bf16[2,256,768]{2,1,0:T(8,128)(2,1)S(1)} %collective-permute-done) | copy-start | bytes 2359300
  182.8 5.1 copy-start.37
  182.9 5.0 copy-start.33
  183.0 6.7 %copy-start.27 = (bf16[32,24,768]{2,1,0:T(8,128)(2,1)S(1)}, bf16[32,24,768]{2,1,0:T(8,128)(2,1)}, u32[]{:S(2)}) copy-start(bf16[32,24,768]{2,1,0:T(8,128)(2,1)} %get-tuple-element.35) | copy-start | bytes 3538948
  250.5 16.9 %copy-start.39 = (f32[3072]{0:T(1024)}, f32[3072]{0:T(1024)S(1)}, u32[]{:S(2)}) copy-start(f32[3072]{0:T(1024)S(1)} %reshape.673) | copy-start | bytes 36868
  259.2 8.2 %slice-start = ((s8[4718592]{0:T(1024)(128)(4,1)}), s8[4194304]{0:T(1024)(128)(4,1)S(1)}, s32[]{:S(2)}) async-start(s8[4718592]{0:T(1024)(128)(4,1)} %bitcast.233), calls=%async_computation.5 | async-start | bytes 8388608
  262.0 13.6 %copy-start.11 = (f32[512,768]{1,0:T(8,128)}, f32[512,768]{1,0:T(8,128)S(1)}, u32[]{:S(2)}) copy-start(f32[512,768]{1,0:T(8,128)S(1)} %get-tuple-element.74) | copy-start | bytes 4718596
  262.3 5.0 slice-start.1
  262.4 5.0 copy-start.23
  267.4 5.1 copy-start.45
  322.5 9.5 %copy-start.13 = (bf16[2,256,12,64]{1,0,3,2:T(2,128)(2,1)S(1)}, bf16[2,256,12,64]{1,0,3,2:T(2,128)(2,1)}, u32[]{:S(2)}) copy-start(bf16[2,256,12,64]{1,0,3,2:T(2,128)(2,1)} %reshape.641) | copy-start | bytes 2359300
  332.0 7.0 %copy-start.32 = (bf16[2,256,12,64]{1,0,3,2:T(2,128)(2,1)S(1)}, bf16[2,256,12,64]{1,0,3,2:T(2,128)(2,1)}, u32[]{:S(2)}) copy-start(bf16[2,256,12,64]{1,0,3,2:T(2,128)(2,1)} %reshape.649) | copy-start | bytes 2359300
  353.0 7.5 %copy-start.16 = (bf16[2,256,12,64]{1,3,2,0:T(8,128)(2,1)S(1)}, bf16[2,256,12,64]{1,3,2,0:T(8,128)(2,1)}, u32[]{:S(2)}) copy-start(bf16[2,256,12,64]{1,3,2,0:T(8,128)(2,1)} %get-tuple-element.82) | copy-start | bytes 2359300
  367.0 5.0 copy-start.20
  376.4 10.4 %copy-start.18 = (bf16[96,8,2,1024]{3,1,2,0:T(8,128)(2,1)}, bf16[96,8,2,1024]{3,1,2,0:T(8,128)(2,1)S(1)}, u32[]{:S(2)}) copy-start(bf16[96,8,2,1024]{3,1,2,0:T(8,128)(2,1)S(1)} %copy.103) | copy-start | bytes 9437188
  390.9 46.0 %collective-permute-start.5 = (bf16[2,256,768]{2,1,0:T(8,128)(2,1)}, bf16[2,256,768]{2,1,0:T(8,128)(2,1)}, u32[]{:S(2)}, u32[]{:S(2)}) collective-permute-start(bf16[2,256,768]{2,1,0:T(8,128)(2,1)} %get-tuple-element.41), channel_id=1, source_target_pairs={{0,1},{1,2},{2,3},{3,0},{4,5},{5,6},{6,7},{7,4},{8,9},{9,10},{10,1... | collective-permute-start | bytes 2359304 | tf_op jit(solution)/shard_map/ppermute | solution.py:210
  391.8 54.8 %collective-permute-start.4 = (bf16[2,256,768]{2,1,0:T(8,128)(2,1)}, bf16[2,256,768]{2,1,0:T(8,128)(2,1)}, u32[]{:S(2)}, u32[]{:S(2)}) collective-permute-start(bf16[2,256,768]{2,1,0:T(8,128)(2,1)} %get-tuple-element.42), channel_id=1, source_target_pairs={{0,2},{1,3},{2,0},{3,1},{4,6},{5,7},{6,4},{7,5},{8,10},{9,11},{10,... | collective-permute-start | bytes 2359304 | tf_op jit(solution)/shard_map/ppermute | solution.py:210
  393.2 53.4 %collective-permute-start.3 = (bf16[2,256,768]{2,1,0:T(8,128)(2,1)}, bf16[2,256,768]{2,1,0:T(8,128)(2,1)}, u32[]{:S(2)}, u32[]{:S(2)}) collective-permute-start(bf16[2,256,768]{2,1,0:T(8,128)(2,1)} %get-tuple-element.40), channel_id=1, source_target_pairs={{0,3},{1,0},{2,1},{3,2},{4,7},{5,4},{6,5},{7,6},{8,11},{9,8},{10,9... | collective-permute-start | bytes 2359304 | tf_op jit(solution)/shard_map/ppermute | solution.py:210
  427.7 4.9 copy-start.24
  465.3 120.3 %copy-start.35 = (f32[32,24]{1,0:T(8,128)S(1)}, f32[32,24]{1,0:T(8,128)}, u32[]{:S(2)}) copy-start(f32[32,24]{1,0:T(8,128)} %get-tuple-element.58) | copy-start | bytes 9220
  465.3 120.4 %copy-start.12 = (f32[512,768]{1,0:T(8,128)S(1)}, f32[512,768]{1,0:T(8,128)}, u32[]{:S(2)}) copy-start(f32[512,768]{1,0:T(8,128)} %copy-done.11) | copy-start | bytes 4718596
  465.3 120.4 %copy-start.40 = (f32[3072]{0:T(1024)S(1)}, f32[3072]{0:T(1024)}, u32[]{:S(2)}) copy-start(f32[3072]{0:T(1024)} %copy-done.39) | copy-start | bytes 36868
  465.3 162.6 %reduce-scatter.5.cloned.1.call-start = ((), (), s32[]{:S(2)}) async-start(), calls=%async_computation.3 | async-start | bytes 2334720 | tf_op jit(solution)/shard_map/reduce_scatter | solution.py:98
  (26 other events, 65.8 us)
Sparse Core Ops, SparseCore 0:
  19.4 148.6 all-gather.2
  465.5 120.0 reduce-scatter.2
  587.9 40.0 reduce-scatter.4

commit v5 on v4

--- a/solution.py
+++ b/solution.py
@@ -49,66 +49,73 @@
     return -(-value // step) * step
 
 
-MATS = (2, 4, 5, 7, 11, 13)
-VECS = (0, 1, 3, 6, 8, 9, 10, 12, 14)
-
-
-def layout(shards, width, sub):
-    rows = [shards[i].size // width for i in MATS]
-    vec_len = sum(shards[i].size for i in VECS)
+def layout(shapes, group, width, sub):
+    mats = [i for i in group if len(shapes[i]) == 2]
+    vecs = [i for i in group if len(shapes[i]) == 1]
+    size = lambda i: math.prod(shapes[i])
+    rows = [size(i) // width for i in mats]
+    vec_len = sum(size(i) for i in vecs)
     vec_rows = round_up(vec_len, width) // width
     total = round_up(sum(rows) + vec_rows, sub)
-    return rows, vec_len, vec_rows, total
-
-
-def gather_all(shards, width, groups):
-    rows, vec_len, vec_rows, total = layout(shards, width, 16)
-    vec = jnp.concatenate([shards[i].reshape(-1) for i in VECS])
+    return mats, vecs, rows, vec_len, vec_rows, total
+
+
+def gather_group(shards, group, width, groups):
+    shapes = [s.shape for s in shards]
+    mats, vecs, rows, vec_len, vec_rows, total = layout(shapes, group, width, 16)
+    vec = jnp.concatenate([shards[i].reshape(-1) for i in vecs])
     vec = jnp.pad(vec, (0, vec_rows * width - vec_len)).reshape(vec_rows, width)
-    blocks = [shards[i].reshape(-1, width) for i in MATS] + [vec]
+    blocks = [shards[i].reshape(-1, width) for i in mats] + [vec]
+    spare = total - sum(rows) - vec_rows
+    if spare:
+        blocks.append(jnp.zeros((spare, width), vec.dtype))
     packed = jnp.concatenate(blocks, axis=0)
-    packed = jnp.pad(packed, ((0, total - packed.shape[0]), (0, 0)))
     full = lax.all_gather(packed[None], ALL, axis=0, tiled=True)
-    out = [None] * 15
+    out = {}
     off = 0
-    for i, r in zip(MATS, rows):
-        s = shards[i]
-        out[i] = full[:, off:off + r, :].reshape((groups * s.shape[0],) + s.shape[1:])
+    for i, r in zip(mats, rows):
+        out[i] = full[:, off:off + r, :].reshape((groups * shapes[i][0],) + shapes[i][1:])
         off += r
-    vecs = full[:, off:off + vec_rows, :].reshape(groups, vec_rows * width)
+    flat = full[:, off:off + vec_rows, :].reshape(groups, vec_rows * width)
     voff = 0
-    for i in VECS:
-        size = shards[i].size
-        out[i] = vecs[:, voff:voff + size].reshape(groups * size)
+    for i in vecs:
+        size = shapes[i][0]
+        out[i] = flat[:, voff:voff + size].reshape(groups * size)
         voff += size
     return out
 
 
-def scatter_all(grads, width, mesh_shape):
+def scatter_group(grads, group, width, mesh_shape):
     groups = mesh_shape[0] * mesh_shape[1]
-    shard_like = [jnp.zeros((g.shape[0] // groups,) + g.shape[1:], jnp.float32) for g in grads]
-    rows, vec_len, vec_rows, total = layout(shard_like, width, 16)
-    vec = jnp.concatenate([grads[i].reshape(groups, -1) for i in VECS], axis=1)
+    shapes = {i: (grads[i].shape[0] // groups,) + grads[i].shape[1:] for i in group}
+    mats, vecs, rows, vec_len, vec_rows, total = layout(shapes, group, width, 16)
+    vec = jnp.concatenate([grads[i].reshape(groups, -1) for i in vecs], axis=1)
     vec = jnp.pad(vec, ((0, 0), (0, vec_rows * width - vec_len))).reshape(groups, vec_rows, width)
-    blocks = [grads[i].reshape(groups, -1, width) for i in MATS] + [vec]
+    blocks = [grads[i].reshape(groups, -1, width) for i in mats] + [vec]
+    spare = total - sum(rows) - vec_rows
+    if spare:
+        blocks.append(jnp.zeros((groups, spare, width), jnp.float32))
     packed = jnp.concatenate([b.astype(jnp.bfloat16) for b in blocks], axis=1)
-    packed = jnp.pad(packed, ((0, 0), (0, total - packed.shape[1]), (0, 0)))
     packed = packed.reshape(mesh_shape[0], mesh_shape[1], total, width)
     packed = lax.psum_scatter(packed, "dp", scatter_dimension=0, tiled=True)
     mine = lax.psum_scatter(packed, "ctx", scatter_dimension=1, tiled=True)
     mine = mine.reshape(total, width).astype(jnp.float32)
-    out = [None] * 15
+    out = {}
     off = 0
-    for i, r in zip(MATS, rows):
-        out[i] = mine[off:off + r, :].reshape(shard_like[i].shape)
+    for i, r in zip(mats, rows):
+        out[i] = mine[off:off + r, :].reshape(shapes[i])
         off += r
-    vecs = mine[off:off + vec_rows, :].reshape(-1)
+    flat = mine[off:off + vec_rows, :].reshape(-1)
     voff = 0
-    for i in VECS:
-        size = shard_like[i].size
-        out[i] = vecs[voff:voff + size]
+    for i in vecs:
+        size = shapes[i][0]
+        out[i] = flat[voff:voff + size]
         voff += size
     return out
+
+
+FIRST = (0, 1, 2, 3, 4, 5, 6)
+SECOND = (7, 8, 9, 10, 11, 12, 13, 14)
 
 
 def per_device(inputs, lengths, *rest):
@@ -123,9 +130,10 @@
     blocks = [inputs]
     for b in range(1, n_ctx):
         blocks.append(lax.ppermute(inputs, "ctx", [(i, (i + b) % n_ctx) for i in range(n_ctx)]))
-    (ln1_gain, ln1_bias, wq, bq, wk, wv, bv, wo, bo, ln2_gain, ln2_bias, wi, bi, wf, bf) = gather_all(
-        shards, width, groups
-    )
+    early = gather_group(shards, FIRST, width, groups)
+    late = gather_group(shards, SECOND, width, groups)
+    (ln1_gain, ln1_bias, wq, bq, wk, wv, bv) = (early[i] for i in FIRST)
+    (wo, bo, ln2_gain, ln2_bias, wi, bi, wf, bf) = (late[i] for i in SECOND)
     me = lax.axis_index("ctx")
     total = n_ctx * rows
     source = (me - jnp.arange(n_ctx)) % n_ctx
@@ -182,6 +190,10 @@
     d_branch = d_middle.astype(jnp.bfloat16)
     grad_bo = col_sum(d_branch)
     grad_wo = outer(mixed, d_branch)
+    late_grads = dict(
+        zip(SECOND, (grad_wo, grad_bo, grad_ln2_gain, grad_ln2_bias, grad_wi, grad_bi, grad_wf, grad_bf))
+    )
+    late_out = scatter_group(late_grads, SECOND, width, mesh_shape)
     d_mixed = back(d_branch, wo).astype(jnp.bfloat16).reshape(seqs, rows, H, HD)
     d_probs = jnp.einsum("sqhd,skhd->shqk", d_mixed, vh, preferred_element_type=jnp.float32)
     inner = jnp.sum(probs * d_probs, axis=-1, keepdims=True)
@@ -212,24 +224,11 @@
     d_x = norm_back_rows(d_normed.reshape(n, width), xhat1, rstd1, f32(ln1_gain))
     input_grad = (d_middle + d_x).astype(jnp.bfloat16).reshape(seqs, rows, width)
 
-    grads = (
-        grad_ln1_gain,
-        grad_ln1_bias,
-        grad_wq,
-        grad_bq,
-        grad_wk,
-        grad_wv,
-        grad_bv,
-        grad_wo,
-        grad_bo,
-        grad_ln2_gain,
-        grad_ln2_bias,
-        grad_wi,
-        grad_bi,
-        grad_wf,
-        grad_bf,
-    )
-    return (output, input_grad) + tuple(scatter_all(grads, width, mesh_shape))
+    early_grads = dict(
+        zip(FIRST, (grad_ln1_gain, grad_ln1_bias, grad_wq, grad_bq, grad_wk, grad_wv, grad_bv))
+    )
+    early_out = scatter_group(early_grads, FIRST, width, mesh_shape)
+    return (output, input_grad) + tuple(early_out[i] for i in FIRST) + tuple(late_out[i] for i in SECOND)
 
 
 def solution(mesh):

time: 649 us -> 694 us (1.069)
  local copies, waits for them, and re-layouts: 126 us -> 184 us
  waiting for transfers between devices: 302 us -> 275 us
  matrix products: 148 us -> 156 us
    concatenate x4 -> x9, local copies, waits for them, and re-layouts: 6.97 us -> 77.3 us  [the longest x5 64 us: scatter_group(): packed = jnp.concatenate([b.astype(jnp.bfloat16) for b in blocks], axis=1)]
    ppermute x3, waiting for transfers between devices: 9.69 us -> 56.6 us  [per_device(): lax.ppermute(sent, 'ctx', [(i, (i - b) % n_ctx) for i in range(n_ctx)])]
    ppermute x3, waiting for transfers between devices: 94.3 us -> 50.5 us  [per_device(): lax.ppermute(inputs, 'ctx', [(i, (i + b) % n_ctx) for i in range(n_ctx)])]
    reduce_scatter x2 -> x4, waiting for transfers between devices: 155 us -> 130 us  [the longest x2 83.3 us: scatter_group(): packed = lax.psum_scatter(packed, 'dp', scatter_dimension=0, tiled=True)]
    pad x3 -> x2, local copies, waits for them, and re-layouts: 13.5 us -> 0.64 us  [the longest x1 0.63 us: scatter_group(): jnp.pad(vec, ((0, 0), (0, vec_rows * width - vec_len)))]
    unnamed x115 -> x141, local copies, waits for them, and re-layouts: 19.9 us -> 9.76 us
    all_gather x1 -> x2, waiting for transfers between devices: 43.1 us -> 37.6 us  [gather_group(): full = lax.all_gather(packed[None], ALL, axis=0, tiled=True)]
    reshape x10 -> x12, local copies, waits for them, and re-layouts: 11.6 us -> 16.7 us  [the longest x1 8.55 us: gather_group(): full[:, off:off + r, :].reshape((groups * shapes[i][0],) + shapes[i][1:])]
  transfers between devices with their start and end apart: 9 -> 12, of which waited for: 6 -> 10; matrix products, arithmetic and copies ran while one was open for 8% -> 29% of each run, Pallas kernels for 0% -> 0%
where the time goes in v5:
time: 694 us; the launch traced here: 683 us
  waiting for transfers between devices  275 us (40%)
  local copies, waits for them, and re-layouts  184 us (27%)
  matrix products  156 us (22%)
  other arithmetic  40.9 us (6%)
  between operations  15.4 us (2%)
  starting transfers between devices  12.3 us (2%)
    reduce_scatter x2, waiting for transfers between devices, scatter_group(): packed = lax.psum_scatter(packed, 'dp', scatter_dimension=0, tiled=True)  83.3 us
    concatenate x5, local copies, waits for them, and re-layouts, scatter_group(): packed = jnp.concatenate([b.astype(jnp.bfloat16) for b in blocks], axis=1)  64 us
    ppermute x3, waiting for transfers between devices, per_device(): lax.ppermute(sent, 'ctx', [(i, (i - b) % n_ctx) for i in range(n_ctx)])  56.6 us
    ppermute x3, waiting for transfers between devices, per_device(): lax.ppermute(inputs, 'ctx', [(i, (i + b) % n_ctx) for i in range(n_ctx)])  50.5 us
    reduce_scatter x2, waiting for transfers between devices, scatter_group(): mine = lax.psum_scatter(packed, 'ctx', scatter_dimension=1, tiled=True)  46.8 us
    all_gather x2, waiting for transfers between devices, gather_group(): full = lax.all_gather(packed[None], ALL, axis=0, tiled=True)  37.6 us
    dot_general x6, matrix products, mm(): return jnp.dot(left, right, preferred_element_type=jnp.float32)  29.6 us
    dot_general x6, matrix products, outer(): lax.dot_general(left_rows, right_rows, (((0,), (0,)), ((), ())), preferre...  29.4 us
  transfers between devices with their start and end apart: 12, of which 10 were waited for; matrix products, arithmetic and copies ran while one was open for 29% of the time, Pallas kernels for 0%

profile of v5, /device:TPU:0, one launch (start us, length us, event | category | flops | bytes accessed | tf_op | source)
XLA Modules:
  0.0 683.5 jit_solution(4729036828831438101)
XLA Ops:
  30.5 50.3 %collective-permute-done.1 = bf16[2,256,768]{2,1,0:T(8,128)(2,1)S(1)} collective-permute-done((bf16[2,256,768]{2,1,0:T(8,128)(2,1)}, bf16[2,256,768]{2,1,0:T(8,128)(2,1)S(1)}, u32[]{:S(2)}, u32[]{:S(2)}) %collective-permute-start.1) | collective-permute-done | bytes 786464 | tf_op jit(solution)/shard_map/ppermute | solution.py:132
  85.6 31.5 %all-gather.5.cloned.1.call-done = bf16[2560,768]{1,0:T(8,128)(2,1)} async-done(((bf16[80,768]{1,0:T(8,128)(2,1)}), bf16[2560,768]{1,0:T(8,128)(2,1)}) %all-gather.5.cloned.1.call-update) | async-done | bytes 3932176 | tf_op jit(solution)/shard_map/all_gather | solution.py:73
  139.3 5.2 convolution_convert_fusion.1
  154.0 7.8 %add_convert_fusion.1 = bf16[2048,768]{1,0:T(8,128)(2,1)} fusion(bf16[2048,768]{1,0:T(8,128)(2,1)} %bitcast.233, bf16[768,768]{1,0:T(8,128)(2,1)} %bitcast.259, f32[768]{0:T(1024)S(1)} %reshape.692), kind=kOutput, calls=%fused_computation.33 | convolution fusion | flops 2419064832 | bytes 7474176 | tf_op jit(solution)/shard_map/dot_general | solution.py:29
  166.5 6.3 reshape.660
  172.9 14.8 %fusion.112 = (f32[2,12,256]{2,1,0:T(8,128)S(1)}, f32[2,12,256,1024]{3,2,1,0:T(8,128)}) fusion(pred[2,1024]{1,0:T(4,128)(4,1)S(1)} %broadcast_compare_fusion, bf16[2,1024,12,64]{1,0,3,2:T(2,128)(2,1)S(1)} %reshape.665, bf16[2,256,12,64]{1,0,3,2:T(2,128)(2,1)} %reshape.663), kind=kOutput, calls=%fused_computation.179 | convolution fusion | flops 830473216 | bytes 29124608 | tf_op jit(solution)/shard_map/sub | solution.py:162
  187.7 12.2 %fusion.66 = bf16[2,256,12,64]{1,3,2,0:T(8,128)(2,1)S(1)} fusion(bf16[2,1024,12,64]{1,0,3,2:T(2,128)(2,1)} %reshape.660, f32[2,12,256,1024]{3,2,1,0:T(8,128)} %get-tuple-element.72, f32[2,12,256]{2,1,0:T(8,128)S(1)} %get-tuple-element.71), kind=kOutput, calls=%fused_computation.94 | convolution fusion | flops 818282496 | bytes 29122560 | tf_op jit(solution)/shard_map/shqk,skhd->sqhd/dot_general | solution.py:165
  200.9 6.1 all-gather.7.cloned.1.call-done
  210.2 8.1 %fusion.108 = (bf16[32,96,768]{2,1,0:T(8,128)(2,1)}, bf16[32,96,768]{2,1,0:T(8,128)(2,1)}) fusion(bf16[32,224,768]{2,1,0:T(8,128)(2,1)} %bitcast.229), kind=kLoop, calls=%fused_computation.175 | loop fusion | bytes 18874368 | tf_op jit(solution)/shard_map/slice | solution.py:77
  218.6 8.6 %reshape.670 = bf16[768,3072]{1,0:T(8,128)(2,1)} reshape(bf16[32,96,768]{2,1,0:T(8,128)(2,1)} %get-tuple-element.30) | data formatting | bytes 9437184 | tf_op jit(solution)/shard_map/reshape | solution.py:77
  230.1 5.4 fusion.19
  235.5 5.2 fusion.124
  249.8 12.3 %fusion.122 = (bf16[12,64]{1,0:T(8,128)(2,1)}, bf16[2,1024,12,64]{1,3,2,0:T(8,128)(2,1)}) fusion(f32[2,12,256,1024]{3,2,1,0:T(8,128)} %get-tuple-element.72, f32[2,12,256]{2,1,0:T(8,128)S(1)} %copy-done.41, bf16[2,256,12,64]{1,0,3,2:T(2,128)(2,1)} %reshape.674), kind=kOutput, calls=%fused_computation.181 | convolution fusion | flops 821034240 | bytes 29124096 | tf_op jit(solution)/shard_map/shqk,sqhd->skhd/dot_general | solution.py:206
  262.1 16.6 %multiply_reduce_fusion = (f32[2,12,256]{2,1,0:T(8,128)S(1)}, f32[2,12,256,1024]{3,2,1,0:T(8,128)}) fusion(f32[2,12,256,1024]{3,2,1,0:T(8,128)} %get-tuple-element.72, f32[2,12,256]{2,1,0:T(8,128)S(1)} %copy-done.41, bf16[2,1024,12,64]{1,0,3,2:T(2,128)(2,1)} %reshape.660, bf16[2,256,12,64]{1,0,3,2:T(2,128)(2,1)S(1)} %copy-done.35), kind=kOutput, calls=%fused_computation.2 | convolution fusion | flops 824174592 | bytes 54312960 | tf_op jit(solution)/shard_map/sqhd,skhd->shqk/dot_general | solution.py:198
  278.7 21.6 %multiply_convert_fusion = bf16[2,12,256,1024]{3,2,1,0:T(8,128)(2,1)} fusion(f32[2,12,256,1024]{3,2,1,0:T(8,128)} %get-tuple-element.77, f32[2,12,256]{2,1,0:T(8,128)S(1)} %get-tuple-element.76, f32[2,12,256,1024]{3,2,1,0:T(8,128)} %get-tuple-element.72, f32[2,12,256]{2,1,0:T(8,128)S(1)} %copy-done.41), kind=kLoop, calls=%fused_computation.1 | loop fusion | flops 25165824 | bytes 62963712 | tf_op jit(solution)/shard_map/convert_element_type | solution.py:200
  300.3 10.1 %fusion.123 = (bf16[12,64]{1,0:T(8,128)(2,1)}, bf16[2,256,12,64]{1,3,2,0:T(8,128)(2,1)}) fusion(bf16[2,12,256,1024]{3,2,1,0:T(8,128)(2,1)} %multiply_convert_fusion, bf16[2,1024,12,64]{1,0,3,2:T(2,128)(2,1)S(1)} %copy-done.1), kind=kOutput, calls=%fused_computation.182 | convolution fusion | flops 806485248 | bytes 16516608 | tf_op jit(solution)/shard_map/shqk,skhd->sqhd/dot_general | solution.py:201
  310.4 7.0 %fusion.23 = bf16[2,1024,12,64]{1,3,2,0:T(8,128)(2,1)S(1)} fusion(bf16[2,12,256,1024]{3,2,1,0:T(8,128)(2,1)} %multiply_convert_fusion, bf16[2,256,12,64]{1,0,3,2:T(2,128)(2,1)S(1)} %copy-done.14), kind=kOutput, calls=%fused_computation.44 | convolution fusion | flops 808452096 | bytes 16515072 | tf_op jit(solution)/shard_map/shqk,sqhd->skhd/dot_general | solution.py:204
  333.3 8.6 %multiply_reduce_fusion.1 = (f32[768]{0:T(1024)}, f32[768]{0:T(1024)}, bf16[2048,768]{1,0:T(8,128)(2,1)}, f32[2048,768]{1,0:T(8,128)}) fusion(f32[2048]{0:T(1024)S(1)} %copy-done.52, f32[2048]{0:T(1024)S(1)} %copy-done.53, bf16[2,256,768]{2,1,0:T(8,128)(2,1)S(1)} %copy-done.10, bf16[2,256,768]{2,1,0:T(8,128)(2,1)S(1)} %copy-done.6, ...), kind=kOutput, calls=%fused_computation.24 | convolution fusion | flops 2442656256 | bytes 23228416 | tf_op jit(solution)/shard_map/dot_general | solution.py:39
  346.6 5.6 fusion.56
  362.2 6.6 fusion.53
  368.8 5.5 collective-permute-done.3
  374.3 18.8 %collective-permute-done.5 = bf16[2,256,768]{2,1,0:T(8,128)(2,1)} collective-permute-done((bf16[2,256,768]{2,1,0:T(8,128)(2,1)}, bf16[2,256,768]{2,1,0:T(8,128)(2,1)}, u32[]{:S(2)}, u32[]{:S(2)}) %collective-permute-start.5) | collective-permute-done | bytes 786464 | tf_op jit(solution)/shard_map/ppermute | solution.py:222
  393.1 32.3 %collective-permute-done.4 = bf16[2,256,768]{2,1,0:T(8,128)(2,1)} collective-permute-done((bf16[2,256,768]{2,1,0:T(8,128)(2,1)}, bf16[2,256,768]{2,1,0:T(8,128)(2,1)}, u32[]{:S(2)}, u32[]{:S(2)}) %collective-permute-start.4) | collective-permute-done | bytes 786464 | tf_op jit(solution)/shard_map/ppermute | solution.py:222
  430.5 16.9 %concatenate.58 = bf16[8,4,80,768]{3,2,1,0:T(8,128)(2,1)} concatenate(bf16[8,4,24,768]{3,2,1,0:T(8,128)(2,1)} %bitcast.268, bf16[8,4,24,768]{3,2,1,0:T(8,128)(2,1)} %bitcast.269, bf16[8,4,24,768]{3,2,1,0:T(8,128)(2,1)S(1)} %bitcast.267, bf16[8,4,1,768]{3,2,1,0:T(2,128)(2,1)S(1)} %concatenate.64, bf16[8,4,7,768]{3,2,1,0:T(8,128)(2,1)S(1)} %concatenate.57), dimensions={2} | concatenate | bytes 7864320 | tf_op jit(solution)/shard_map/concatenate | solution.py:98
  455.8 6.8 convolution_convert_fusion
  462.5 8.5 %convert_element_type.366 = bf16[8,4,96,768]{3,2,1,0:T(8,128)(2,1)} reshape(bf16[768,3072]{1,0:T(8,128)(2,1)} %convolution_convert_fusion) | data formatting | bytes 9437184 | tf_op jit(solution)/shard_map/convert_element_type | solution.py:98
  479.3 5.4 convolution_convert_fusion.2
  484.7 45.6 %concatenate.63 = bf16[8,4,224,768]{3,2,1,0:T(8,128)(2,1)} concatenate(bf16[8,4,24,768]{3,2,1,0:T(8,128)(2,1)S(1)} %bitcast.240, bf16[8,4,96,768]{3,2,1,0:T(8,128)(2,1)} %convert_element_type.366, bf16[8,4,96,768]{3,2,1,0:T(8,128)(2,1)} %bitcast.239, bf16[8,4,1,768]{3,2,1,0:T(2,128)(2,1)S(1)} %copy-done.36, bf16[8,4,7,768]{3,2,1,0:T(8,128)(2,1)S(1)} %concatenate.57), dimensions={2} | concatenate | bytes 22020096 | tf_op jit(solution)/shard_map/concatenate | solution.py:98
  531.0 83.3 %reduce-scatter.9.cloned.1.call-done = bf16[1,4,224,768]{3,2,1,0:T(8,128)(2,1)} async-done(((bf16[8,4,224,768]{3,2,1,0:T(8,128)(2,1)}), bf16[1,4,224,768]{3,2,1,0:T(8,128)(2,1)}) %reduce-scatter.9.cloned.1.call-update) | async-done | bytes 1376272 | tf_op jit(solution)/shard_map/reduce_scatter | solution.py:100
  614.4 7.4 %add_convert_fusion.3 = bf16[512,768]{1,0:T(8,128)(2,1)} fusion(f32[512,768]{1,0:T(8,128)S(1)} %copy-done.12, bf16[3072,768]{1,0:T(8,128)(2,1)} %bitcast.235, f32[512,3072]{1,0:T(8,128)} %copy-done.61, f32[3072]{0:T(1024)S(1)} %copy-done.48, f32[768]{0:T(1024)S(1)} %reshape.698), kind=kOutput, calls=%fused_computation.81 | convolution fusion | flops 2426535936 | bytes 13384704 | tf_op jit(solution)/shard_map/dot_general | solution.py:29
  621.8 16.3 %reduce-scatter.7.cloned.1.call-done = bf16[1,1,80,768]{3,2,1,0:T(8,128)(2,1)} async-done(((bf16[1,4,80,768]{3,2,1,0:T(8,128)(2,1)}), bf16[1,1,80,768]{3,2,1,0:T(8,128)(2,1)}) %reduce-scatter.7.cloned.1.call-update) | async-done | bytes 122896 | tf_op jit(solution)/shard_map/reduce_scatter | solution.py:101
  640.3 30.6 %reduce-scatter.11.cloned.1.call-done = bf16[1,1,224,768]{3,2,1,0:T(8,128)(2,1)} async-done(((bf16[1,4,224,768]{3,2,1,0:T(8,128)(2,1)}), bf16[1,1,224,768]{3,2,1,0:T(8,128)(2,1)}) %reduce-scatter.11.cloned.1.call-update) | async-done | bytes 344080 | tf_op jit(solution)/shard_map/reduce_scatter | solution.py:101
  (259 shorter events, 140.9 us)
Async XLA Ops:
  7.2 75.9 %copy-start.3 = (bf16[2,256,768]{2,1,0:T(8,128)(2,1)S(1)}, bf16[2,256,768]{2,1,0:T(8,128)(2,1)}, u32[]{:S(2)}) copy-start(bf16[2,256,768]{2,1,0:T(8,128)(2,1)} %param.18) | copy-start | bytes 2359300
  7.2 109.9 %all-gather.5.cloned.1.call-start = ((), (), s32[]{:S(2)}) async-start(), calls=%async_computation.8 | async-start | bytes 4055040 | tf_op jit(solution)/shard_map/all_gather | solution.py:73
  12.9 194.0 %all-gather.7.cloned.1.call-start = ((), (), s32[]{:S(2)}) async-start(), calls=%async_computation.9 | async-start | bytes 11354112 | tf_op jit(solution)/shard_map/all_gather | solution.py:73
  21.7 508.7 %reduce-scatter.5.cloned.1.call-start = ((), (), s32[]{:S(2)}) async-start(), calls=%async_computation.4 | async-start | bytes 4423680 | tf_op jit(solution)/shard_map/reduce_scatter | solution.py:100
  21.7 59.1 %collective-permute-start.1 = (bf16[2,256,768]{2,1,0:T(8,128)(2,1)}, bf16[2,256,768]{2,1,0:T(8,128)(2,1)S(1)}, u32[]{:S(2)}, u32[]{:S(2)}) collective-permute-start(bf16[2,256,768]{2,1,0:T(8,128)(2,1)} %param.18), channel_id=1, source_target_pairs={{0,2},{1,3},{2,0},{3,1},{4,6},{5,7},{6,4},{7,5},{8,10},{9,11},{10,... | collective-permute-start | bytes 2359304 | tf_op jit(solution)/shard_map/ppermute | solution.py:132
  25.9 54.9 %collective-permute-start = (bf16[2,256,768]{2,1,0:T(8,128)(2,1)}, bf16[2,256,768]{2,1,0:T(8,128)(2,1)S(1)}, u32[]{:S(2)}, u32[]{:S(2)}) collective-permute-start(bf16[2,256,768]{2,1,0:T(8,128)(2,1)} %param.18), channel_id=1, source_target_pairs={{0,1},{1,2},{2,3},{3,0},{4,5},{5,6},{6,7},{7,4},{8,9},{9,10},{10,1... | collective-permute-start | bytes 2359304 | tf_op jit(solution)/shard_map/ppermute | solution.py:132
  27.4 53.6 %collective-permute-start.2 = (bf16[2,256,768]{2,1,0:T(8,128)(2,1)}, bf16[2,256,768]{2,1,0:T(8,128)(2,1)S(1)}, u32[]{:S(2)}, u32[]{:S(2)}) collective-permute-start(bf16[2,256,768]{2,1,0:T(8,128)(2,1)} %param.18), channel_id=1, source_target_pairs={{0,3},{1,0},{2,1},{3,2},{4,7},{5,4},{6,5},{7,6},{8,11},{9,8},{10,9... | collective-permute-start | bytes 2359304 | tf_op jit(solution)/shard_map/ppermute | solution.py:132
  80.8 37.8 %copy-start.5 = (bf16[2,256,768]{2,1,0:T(8,128)(2,1)}, bf16[2,256,768]{2,1,0:T(8,128)(2,1)S(1)}, u32[]{:S(2)}) copy-start(bf16[2,256,768]{2,1,0:T(8,128)(2,1)S(1)} %collective-permute-done.1) | copy-start | bytes 2359300
  80.8 37.8 %copy-start.7 = (bf16[2,256,768]{2,1,0:T(8,128)(2,1)}, bf16[2,256,768]{2,1,0:T(8,128)(2,1)S(1)}, u32[]{:S(2)}) copy-start(bf16[2,256,768]{2,1,0:T(8,128)(2,1)S(1)} %collective-permute-done) | copy-start | bytes 2359300
  81.1 37.5 %copy-start.9 = (bf16[2,256,768]{2,1,0:T(8,128)(2,1)}, bf16[2,256,768]{2,1,0:T(8,128)(2,1)S(1)}, u32[]{:S(2)}) copy-start(bf16[2,256,768]{2,1,0:T(8,128)(2,1)S(1)} %collective-permute-done.2) | copy-start | bytes 2359300
  154.0 18.9 %copy-start = (bf16[2,1024,12,64]{1,0,3,2:T(2,128)(2,1)}, bf16[2,1024,12,64]{1,0,3,2:T(2,128)(2,1)S(1)}, u32[]{:S(2)}) copy-start(bf16[2,1024,12,64]{1,0,3,2:T(2,128)(2,1)S(1)} %reshape.665) | copy-start | bytes 9437188
  187.7 12.2 %copy-start.40 = (f32[2,12,256]{2,1,0:T(8,128)}, f32[2,12,256]{2,1,0:T(8,128)S(1)}, u32[]{:S(2)}) copy-start(f32[2,12,256]{2,1,0:T(8,128)S(1)} %get-tuple-element.71) | copy-start | bytes 73732
  200.9 26.3 %copy-start.20 = (bf16[96,8,2,256]{3,1,2,0:T(8,128)(2,1)}, bf16[96,8,2,256]{3,1,2,0:T(8,128)(2,1)S(1)}, u32[]{:S(2)}) copy-start(bf16[96,8,2,256]{3,1,2,0:T(8,128)(2,1)S(1)} %copy.104) | copy-start | bytes 2359300
  218.3 17.2 %copy-start.47 = (f32[3072]{0:T(1024)}, f32[3072]{0:T(1024)S(1)}, u32[]{:S(2)}) copy-start(f32[3072]{0:T(1024)S(1)} %reshape.697) | copy-start | bytes 36868
  218.4 25.9 %copy-start.45 = (f32[768]{0:T(1024)}, f32[768]{0:T(1024)S(1)}, u32[]{:S(2)}) copy-start(f32[768]{0:T(1024)S(1)} %reshape.695) | copy-start | bytes 9220
  218.5 10.0 %copy-start.55 = (f32[768]{0:T(1024)}, f32[768]{0:T(1024)S(1)}, u32[]{:S(2)}) copy-start(f32[768]{0:T(1024)S(1)} %reshape.696) | copy-start | bytes 9220
  228.1 16.2 %copy-start.11 = (f32[512,768]{1,0:T(8,128)}, f32[512,768]{1,0:T(8,128)S(1)}, u32[]{:S(2)}) copy-start(f32[512,768]{1,0:T(8,128)S(1)} %get-tuple-element.74) | copy-start | bytes 4718596
  230.1 14.2 %copy-start.50 = (f32[512]{0:T(512)}, f32[512]{0:T(512)S(1)}, u32[]{:S(2)}) copy-start(f32[512]{0:T(512)S(1)} %add_rsqrt_fusion.1) | copy-start | bytes 6148
  249.8 12.3 %copy-start.35 = (bf16[2,256,12,64]{1,0,3,2:T(2,128)(2,1)S(1)}, bf16[2,256,12,64]{1,0,3,2:T(2,128)(2,1)}, u32[]{:S(2)}) copy-start(bf16[2,256,12,64]{1,0,3,2:T(2,128)(2,1)} %reshape.674) | copy-start | bytes 2359300
  278.7 21.6 %copy-start.1 = (bf16[2,1024,12,64]{1,0,3,2:T(2,128)(2,1)S(1)}, bf16[2,1024,12,64]{1,0,3,2:T(2,128)(2,1)}, u32[]{:S(2)}) copy-start(bf16[2,1024,12,64]{1,0,3,2:T(2,128)(2,1)} %copy-done) | copy-start | bytes 9437188
  300.3 10.1 %copy-start.14 = (bf16[2,256,12,64]{1,0,3,2:T(2,128)(2,1)S(1)}, bf16[2,256,12,64]{1,0,3,2:T(2,128)(2,1)}, u32[]{:S(2)}) copy-start(bf16[2,256,12,64]{1,0,3,2:T(2,128)(2,1)} %reshape.663) | copy-start | bytes 2359300
  321.7 11.5 %copy-start.23 = (bf16[96,8,2,1024]{3,1,2,0:T(8,128)(2,1)}, bf16[96,8,2,1024]{3,1,2,0:T(8,128)(2,1)S(1)}, u32[]{:S(2)}) copy-start(bf16[96,8,2,1024]{3,1,2,0:T(8,128)(2,1)S(1)} %copy.106) | copy-start | bytes 9437188
  354.1 20.2 %collective-permute-start.3 = (bf16[2,256,768]{2,1,0:T(8,128)(2,1)}, bf16[2,256,768]{2,1,0:T(8,128)(2,1)S(1)}, u32[]{:S(2)}, u32[]{:S(2)}) collective-permute-start(bf16[2,256,768]{2,1,0:T(8,128)(2,1)} %get-tuple-element.39), channel_id=1, source_target_pairs={{0,3},{1,0},{2,1},{3,2},{4,7},{5,4},{6,5},{7,6},{8,11},{9,8},{10,9... | collective-permute-start | bytes 2359304 | tf_op jit(solution)/shard_map/ppermute | solution.py:222
  356.0 37.1 %collective-permute-start.5 = (bf16[2,256,768]{2,1,0:T(8,128)(2,1)}, bf16[2,256,768]{2,1,0:T(8,128)(2,1)}, u32[]{:S(2)}, u32[]{:S(2)}) collective-permute-start(bf16[2,256,768]{2,1,0:T(8,128)(2,1)} %get-tuple-element.40), channel_id=1, source_target_pairs={{0,1},{1,2},{2,3},{3,0},{4,5},{5,6},{6,7},{7,4},{8,9},{9,10},{10,1... | collective-permute-start | bytes 2359304 | tf_op jit(solution)/shard_map/ppermute | solution.py:222
  356.3 69.1 %collective-permute-start.4 = (bf16[2,256,768]{2,1,0:T(8,128)(2,1)}, bf16[2,256,768]{2,1,0:T(8,128)(2,1)}, u32[]{:S(2)}, u32[]{:S(2)}) collective-permute-start(bf16[2,256,768]{2,1,0:T(8,128)(2,1)} %get-tuple-element.41), channel_id=1, source_target_pairs={{0,2},{1,3},{2,0},{3,1},{4,6},{5,7},{6,4},{7,5},{8,10},{9,11},{10,... | collective-permute-start | bytes 2359304 | tf_op jit(solution)/shard_map/ppermute | solution.py:222
  362.2 63.2 %copy-start.13 = (f32[512,768]{1,0:T(8,128)S(1)}, f32[512,768]{1,0:T(8,128)}, u32[]{:S(2)}) copy-start(f32[512,768]{1,0:T(8,128)} %fusion.126) | copy-start | bytes 4718596
  447.4 166.9 %reduce-scatter.9.cloned.1.call-start = ((), (), s32[]{:S(2)}) async-start(), calls=%async_computation.6 | async-start | bytes 12386304 | tf_op jit(solution)/shard_map/reduce_scatter | solution.py:100
  462.5 9.9 %copy-start.59 = (bf16[768]{0:T(1024)(128)(2,1)S(1)}, bf16[768]{0:T(1024)(128)(2,1)}, u32[]{:S(2)}) copy-start(bf16[768]{0:T(1024)(128)(2,1)} %get-tuple-element.24) | copy-start | bytes 4612
  530.3 84.0 %copy-start.39 = (f32[32,24]{1,0:T(8,128)S(1)}, f32[32,24]{1,0:T(8,128)}, u32[]{:S(2)}) copy-start(f32[32,24]{1,0:T(8,128)} %get-tuple-element.58) | copy-start | bytes 9220
  530.3 84.1 %copy-start.48 = (f32[3072]{0:T(1024)S(1)}, f32[3072]{0:T(1024)}, u32[]{:S(2)}) copy-start(f32[3072]{0:T(1024)} %copy-done.47) | copy-start | bytes 36868
  530.3 107.7 %reduce-scatter.7.cloned.1.call-start = ((), (), s32[]{:S(2)}) async-start(), calls=%async_computation.5 | async-start | bytes 614400 | tf_op jit(solution)/shard_map/reduce_scatter | solution.py:101
  530.9 139.9 %reduce-scatter.11.cloned.1.call-start = ((), (), s32[]{:S(2)}) async-start(), calls=%async_computation.7 | async-start | bytes 1720320 | tf_op jit(solution)/shard_map/reduce_scatter | solution.py:101
  (45 other events, 197.4 us)
Sparse Core Ops, SparseCore 0:
  13.0 103.9 all-gather.4
  119.9 87.0 all-gather.6
  447.5 49.3 reduce-scatter.4
  530.5 83.7 reduce-scatter.8
  616.4 21.5 reduce-scatter.6
  640.2 30.5 reduce-scatter.10

commit v6 on v4

--- a/solution.py
+++ b/solution.py
@@ -89,10 +89,11 @@
     shard_like = [jnp.zeros((g.shape[0] // groups,) + g.shape[1:], jnp.float32) for g in grads]
     rows, vec_len, vec_rows, total = layout(shard_like, width, 16)
     vec = jnp.concatenate([grads[i].reshape(groups, -1) for i in VECS], axis=1)
-    vec = jnp.pad(vec, ((0, 0), (0, vec_rows * width - vec_len))).reshape(groups, vec_rows, width)
+    spare = total - sum(rows) - vec_rows
+    vec = jnp.pad(vec, ((0, 0), (0, (vec_rows + spare) * width - vec_len)))
+    vec = vec.reshape(groups, vec_rows + spare, width)
     blocks = [grads[i].reshape(groups, -1, width) for i in MATS] + [vec]
     packed = jnp.concatenate([b.astype(jnp.bfloat16) for b in blocks], axis=1)
-    packed = jnp.pad(packed, ((0, 0), (0, total - packed.shape[1]), (0, 0)))
     packed = packed.reshape(mesh_shape[0], mesh_shape[1], total, width)
     packed = lax.psum_scatter(packed, "dp", scatter_dimension=0, tiled=True)
     mine = lax.psum_scatter(packed, "ctx", scatter_dimension=1, tiled=True)

time: 649 us -> 637 us (0.982)
  local copies, waits for them, and re-layouts: 126 us -> 114 us
    pad x1, local copies, waits for them, and re-layouts: 12.7 us -> 0.06 us  [scatter_all(): vec = jnp.pad(vec, ((0, 0), (0, (vec_rows + spare) * width - vec_len)))]
    unnamed x115 -> x116, local copies, waits for them, and re-layouts: 19.9 us -> 20 us
  transfers between devices with their start and end apart: 9 -> 9, of which waited for: 6 -> 6; matrix products, arithmetic and copies ran while one was open for 8% -> 9% of each run, Pallas kernels for 0% -> 0%
where the time goes in v6:
time: 637 us; the launch traced here: 627 us
  waiting for transfers between devices  303 us (48%)
  matrix products  148 us (23%)
  local copies, waits for them, and re-layouts  114 us (18%)
  other arithmetic  37.6 us (6%)
  between operations  14.7 us (2%)
  starting transfers between devices  10.8 us (2%)
    reduce_scatter x1, waiting for transfers between devices, scatter_all(): packed = lax.psum_scatter(packed, 'dp', scatter_dimension=0, tiled=True)  120 us
    ppermute x3, waiting for transfers between devices, per_device(): lax.ppermute(inputs, 'ctx', [(i, (i + b) % n_ctx) for i in range(n_ctx)])  94.3 us
    all_gather x1, waiting for transfers between devices, gather_all(): full = lax.all_gather(packed[None], ALL, axis=0, tiled=True)  43.1 us
    reduce_scatter x1, waiting for transfers between devices, scatter_all(): mine = lax.psum_scatter(packed, 'ctx', scatter_dimension=1, tiled=True)  34.9 us
    dot_general x6, matrix products, mm(): return jnp.dot(left, right, preferred_element_type=jnp.float32)  27.1 us
    dot_general x6, matrix products, back(): lax.dot_general(grad_rows, weight, (((1,), (1,)), ((), ())), preferred_el...  24.7 us
    dot_general x6, matrix products, outer(): lax.dot_general(left_rows, right_rows, (((0,), (0,)), ((), ())), preferre...  24.2 us
    convert_element_type x1, other arithmetic, per_device(): d_scores = (probs * (d_probs - inner)).astype(jnp.bfloat16)  21.4 us
  transfers between devices with their start and end apart: 9, of which 6 were waited for; matrix products, arithmetic and copies ran while one was open for 9% of the time, Pallas kernels for 0%

profile of v6, /device:TPU:0, one launch (start us, length us, event | category | flops | bytes accessed | tf_op | source)
XLA Modules:
  0.0 627.0 jit_solution(10809437049134382307)
XLA Ops:
  12.4 6.1 concatenate.17
  19.4 5.1 collective-permute-start.2
  27.7 25.1 %collective-permute-done.2 = bf16[2,256,768]{2,1,0:T(8,128)(2,1)S(1)} collective-permute-done((bf16[2,256,768]{2,1,0:T(8,128)(2,1)}, bf16[2,256,768]{2,1,0:T(8,128)(2,1)S(1)}, u32[]{:S(2)}, u32[]{:S(2)}) %collective-permute-start.2) | collective-permute-done | bytes 786464 | tf_op jit(solution)/shard_map/ppermute | solution.py:126
  52.8 69.2 %collective-permute-done.1 = bf16[2,256,768]{2,1,0:T(8,128)(2,1)S(1)} collective-permute-done((bf16[2,256,768]{2,1,0:T(8,128)(2,1)}, bf16[2,256,768]{2,1,0:T(8,128)(2,1)S(1)}, u32[]{:S(2)}, u32[]{:S(2)}) %collective-permute-start.1) | collective-permute-done | bytes 786464 | tf_op jit(solution)/shard_map/ppermute | solution.py:126
  125.0 43.1 %all-gather.3.cloned.1.call-done = bf16[9728,768]{1,0:T(8,128)(2,1)} async-done(((bf16[304,768]{1,0:T(8,128)(2,1)}), bf16[9728,768]{1,0:T(8,128)(2,1)}) %all-gather.3.cloned.1.call-update) | async-done | bytes 14942224 | tf_op jit(solution)/shard_map/all_gather | solution.py:71
  169.2 4.6 fusion.105
  173.8 8.0 %fusion.104 = (bf16[32,96,768]{2,1,0:T(8,128)(2,1)}, bf16[32,96,768]{2,1,0:T(8,128)(2,1)}) fusion(bf16[32,304,768]{2,1,0:T(8,128)(2,1)} %bitcast.223), kind=kLoop, calls=%fused_computation.172 | loop fusion | bytes 18874368 | tf_op jit(solution)/shard_map/slice | solution.py:76
  183.0 4.8 subtract_multiply_fusion
  200.8 4.8 convolution_convert_fusion.1
  208.7 4.8 reshape.643
  221.9 14.8 %fusion.108 = (f32[2,12,256]{2,1,0:T(8,128)S(1)}, f32[2,12,256,1024]{3,2,1,0:T(8,128)}) fusion(pred[2,1024]{1,0:T(4,128)(4,1)S(1)} %broadcast_compare_fusion, bf16[2,1024,12,64]{1,0,3,2:T(2,128)(2,1)S(1)} %reshape.643, bf16[2,256,12,64]{1,0,3,2:T(2,128)(2,1)} %reshape.641), kind=kOutput, calls=%fused_computation.176 | convolution fusion | flops 830473216 | bytes 29124608 | tf_op jit(solution)/shard_map/sub | solution.py:155
  236.7 11.8 %fusion.74 = bf16[2,256,12,64]{1,3,2,0:T(8,128)(2,1)S(1)} fusion(bf16[2,1024,12,64]{1,0,3,2:T(2,128)(2,1)} %reshape.638, f32[2,12,256,1024]{3,2,1,0:T(8,128)} %get-tuple-element.72, f32[2,12,256]{2,1,0:T(8,128)S(1)} %get-tuple-element.71), kind=kOutput, calls=%fused_computation.98 | convolution fusion | flops 818282496 | bytes 29122560 | tf_op jit(solution)/shard_map/shqk,skhd->sqhd/dot_general | solution.py:158
  250.5 8.5 %reshape.645 = bf16[768,3072]{1,0:T(8,128)(2,1)} reshape(bf16[32,96,768]{2,1,0:T(8,128)(2,1)} %get-tuple-element.30) | data formatting | bytes 9437184 | tf_op jit(solution)/shard_map/reshape | solution.py:76
  262.4 5.0 fusion.19
  267.4 5.1 fusion.120
  284.4 16.7 %multiply_reduce_fusion = (f32[2,12,256]{2,1,0:T(8,128)S(1)}, f32[2,12,256,1024]{3,2,1,0:T(8,128)}) fusion(f32[2,12,256,1024]{3,2,1,0:T(8,128)} %get-tuple-element.72, f32[2,12,256]{2,1,0:T(8,128)S(1)} %get-tuple-element.71, bf16[2,1024,12,64]{1,0,3,2:T(2,128)(2,1)} %reshape.638, bf16[2,256,12,64]{1,0,3,2:T(2,128)(2,1)} %reshape.649), kind=kOutput, calls=%fused_computation.2 | convolution fusion | flops 824174592 | bytes 54312960 | tf_op jit(solution)/shard_map/sqhd,skhd->shqk/dot_general | solution.py:187
  301.1 21.4 %multiply_convert_fusion = bf16[2,12,256,1024]{3,2,1,0:T(8,128)(2,1)} fusion(f32[2,12,256,1024]{3,2,1,0:T(8,128)} %get-tuple-element.77, f32[2,12,256]{2,1,0:T(8,128)S(1)} %get-tuple-element.76, f32[2,12,256,1024]{3,2,1,0:T(8,128)} %get-tuple-element.72, f32[2,12,256]{2,1,0:T(8,128)S(1)} %get-tuple-element.71), kind=kLoop, calls=%fused_computation.1 | loop fusion | flops 25165824 | bytes 62963712 | tf_op jit(solution)/shard_map/convert_element_type | solution.py:189
  322.5 9.6 %fusion.118 = (bf16[12,64]{1,0:T(8,128)(2,1)S(1)}, bf16[2,256,12,64]{1,3,2,0:T(8,128)(2,1)}) fusion(bf16[2,12,256,1024]{3,2,1,0:T(8,128)(2,1)} %multiply_convert_fusion, bf16[2,1024,12,64]{1,0,3,2:T(2,128)(2,1)S(1)} %reshape.643), kind=kOutput, calls=%fused_computation.178 | convolution fusion | flops 806485248 | bytes 16516608 | tf_op jit(solution)/shard_map/shqk,skhd->sqhd/dot_general | solution.py:190
  332.1 7.0 %fusion.23 = bf16[2,1024,12,64]{1,3,2,0:T(8,128)(2,1)S(1)} fusion(bf16[2,12,256,1024]{3,2,1,0:T(8,128)(2,1)} %multiply_convert_fusion, bf16[2,256,12,64]{1,0,3,2:T(2,128)(2,1)S(1)} %copy-done.13), kind=kOutput, calls=%fused_computation.45 | convolution fusion | flops 808452096 | bytes 16515072 | tf_op jit(solution)/shard_map/shqk,sqhd->skhd/dot_general | solution.py:193
  339.1 11.7 %fusion.119 = (bf16[12,64]{1,0:T(8,128)(2,1)S(1)}, bf16[2,1024,12,64]{1,3,2,0:T(8,128)(2,1)}) fusion(f32[2,12,256,1024]{3,2,1,0:T(8,128)} %get-tuple-element.72, f32[2,12,256]{2,1,0:T(8,128)S(1)} %get-tuple-element.71, bf16[2,256,12,64]{1,0,3,2:T(2,128)(2,1)S(1)} %copy-done.32), kind=kOutput, calls=%fused_computation.179 | convolution fusion | flops 821034240 | bytes 29124096 | tf_op jit(solution)/shard_map/shqk,sqhd->skhd/dot_general | solution.py:195
  353.1 7.5 %convolution_convert_fusion = bf16[768,3072]{1,0:T(8,128)(2,1)} fusion(bf16[512,3072]{1,0:T(8,128)(2,1)} %copy-done.46, f32[512,768]{1,0:T(8,128)} %copy-done.11, f32[768]{0:T(1024)S(1)} %reshape.672, f32[768]{0:T(1024)S(1)} %reshape.671, f32[512]{0:T(512)S(1)} %add_rsqrt_fusion.1, f32[512]{0:T(512)S(1)} %broadcast_multiply_fusion.3), kind=kOutput, calls=%fused_computation.39 | convolution fusion | flops 2420244480 | bytes 9447424 | tf_op jit(solution)/shard_map/dot_general | solution.py:33
  367.0 5.0 fusion.121
  377.8 9.0 %fusion.101 = (f32[768]{0:T(1024)S(1)}, f32[768]{0:T(1024)S(1)}, bf16[2048,768]{1,0:T(8,128)(2,1)}, f32[2048,768]{1,0:T(8,128)S(1)}) fusion(f32[2048]{0:T(1024)S(1)} %copy-done.41, f32[2048]{0:T(1024)S(1)} %copy-done.42, bf16[2,256,768]{2,1,0:T(8,128)(2,1)S(1)} %copy-done.6, bf16[2,256,768]{2,1,0:T(8,128)(2,1)S(1)} %copy-done.8, ...), kind=kOutput, calls=%fused_computation.170 | convolution fusion | flops 2442656256 | bytes 23228416 | tf_op jit(solution)/shard_map/dot_general | solution.py:39
  395.4 4.9 copy.87
  413.7 8.5 %convert_element_type.350 = bf16[32,96,768]{2,1,0:T(8,128)(2,1)} reshape(bf16[768,3072]{1,0:T(8,128)(2,1)} %convolution_convert_fusion) | data formatting | bytes 9437184 | tf_op jit(solution)/shard_map/convert_element_type | solution.py:96
  422.1 4.6 copy.90
  427.4 4.9 constant_dynamic-update-slice_fusion.8
  432.3 4.2 convert_dynamic-update-slice_fusion
  436.5 10.1 %collective-permute-done.4 = bf16[2,256,768]{2,1,0:T(8,128)(2,1)} collective-permute-done((bf16[2,256,768]{2,1,0:T(8,128)(2,1)}, bf16[2,256,768]{2,1,0:T(8,128)(2,1)}, u32[]{:S(2)}, u32[]{:S(2)}) %collective-permute-start.4) | collective-permute-done | bytes 786464 | tf_op jit(solution)/shard_map/ppermute | solution.py:211
  453.0 120.2 %reduce-scatter.3.cloned.1.call-done = bf16[1,4,304,768]{3,2,1,0:T(8,128)(2,1)} async-done(((bf16[8,4,304,768]{3,2,1,0:T(8,128)(2,1)}), bf16[1,4,304,768]{3,2,1,0:T(8,128)(2,1)}) %reduce-scatter.3.cloned.1.call-update) | async-done | bytes 1867792 | tf_op jit(solution)/shard_map/reduce_scatter | solution.py:98
  573.4 7.4 %add_convert_fusion.3 = bf16[512,768]{1,0:T(8,128)(2,1)} fusion(f32[512,768]{1,0:T(8,128)S(1)} %copy-done.12, bf16[3072,768]{1,0:T(8,128)(2,1)} %bitcast.231, f32[512,3072]{1,0:T(8,128)} %copy-done.45, f32[3072]{0:T(1024)S(1)} %copy-done.40, f32[768]{0:T(1024)S(1)} %reshape.674), kind=kOutput, calls=%fused_computation.81 | convolution fusion | flops 2426535936 | bytes 13384704 | tf_op jit(solution)/shard_map/dot_general | solution.py:29
  580.7 34.9 %reduce-scatter.5.cloned.1.call-done = bf16[1,1,304,768]{3,2,1,0:T(8,128)(2,1)} async-done(((bf16[1,4,304,768]{3,2,1,0:T(8,128)(2,1)}), bf16[1,1,304,768]{3,2,1,0:T(8,128)(2,1)}) %reduce-scatter.5.cloned.1.call-update) | async-done | bytes 466960 | tf_op jit(solution)/shard_map/reduce_scatter | solution.py:99
  (210 shorter events, 103.9 us)
Async XLA Ops:
  7.2 114.8 %copy-start.3 = (bf16[2,256,768]{2,1,0:T(8,128)(2,1)S(1)}, bf16[2,256,768]{2,1,0:T(8,128)(2,1)}, u32[]{:S(2)}) copy-start(bf16[2,256,768]{2,1,0:T(8,128)(2,1)} %param.18) | copy-start | bytes 2359300
  7.2 20.4 %copy-start.44 = (s32[2]{0:T(128)S(1)}, s32[2]{0:T(128)}, u32[]{:S(2)}) copy-start(s32[2]{0:T(128)} %param.19) | copy-start | bytes 28
  7.2 161.0 %all-gather.3.cloned.1.call-start = ((), (), s32[]{:S(2)}) async-start(), calls=%async_computation.4 | async-start | bytes 15409152 | tf_op jit(solution)/shard_map/all_gather | solution.py:71
  19.3 553.9 %reduce-scatter.3.cloned.1.call-start = ((), (), s32[]{:S(2)}) async-start(), calls=%async_computation.2 | async-start | bytes 16809984 | tf_op jit(solution)/shard_map/reduce_scatter | solution.py:98
  19.4 33.4 %collective-permute-start.2 = (bf16[2,256,768]{2,1,0:T(8,128)(2,1)}, bf16[2,256,768]{2,1,0:T(8,128)(2,1)S(1)}, u32[]{:S(2)}, u32[]{:S(2)}) collective-permute-start(bf16[2,256,768]{2,1,0:T(8,128)(2,1)} %param.18), channel_id=1, source_target_pairs={{0,3},{1,0},{2,1},{3,2},{4,7},{5,4},{6,5},{7,6},{8,11},{9,8},{10,9... | collective-permute-start | bytes 2359304 | tf_op jit(solution)/shard_map/ppermute | solution.py:126
  24.5 97.5 %collective-permute-start.1 = (bf16[2,256,768]{2,1,0:T(8,128)(2,1)}, bf16[2,256,768]{2,1,0:T(8,128)(2,1)S(1)}, u32[]{:S(2)}, u32[]{:S(2)}) collective-permute-start(bf16[2,256,768]{2,1,0:T(8,128)(2,1)} %param.18), channel_id=1, source_target_pairs={{0,2},{1,3},{2,0},{3,1},{4,6},{5,7},{6,4},{7,5},{8,10},{9,11},{10,... | collective-permute-start | bytes 2359304 | tf_op jit(solution)/shard_map/ppermute | solution.py:126
  24.5 97.5 %collective-permute-start = (bf16[2,256,768]{2,1,0:T(8,128)(2,1)}, bf16[2,256,768]{2,1,0:T(8,128)(2,1)S(1)}, u32[]{:S(2)}, u32[]{:S(2)}) collective-permute-start(bf16[2,256,768]{2,1,0:T(8,128)(2,1)} %param.18), channel_id=1, source_target_pairs={{0,1},{1,2},{2,3},{3,0},{4,5},{5,6},{6,7},{7,4},{8,9},{9,10},{10,1... | collective-permute-start | bytes 2359304 | tf_op jit(solution)/shard_map/ppermute | solution.py:126
  52.8 130.2 %copy-start.5 = (bf16[2,256,768]{2,1,0:T(8,128)(2,1)}, bf16[2,256,768]{2,1,0:T(8,128)(2,1)S(1)}, u32[]{:S(2)}) copy-start(bf16[2,256,768]{2,1,0:T(8,128)(2,1)S(1)} %collective-permute-done.2) | copy-start | bytes 2359300
  122.0 61.0 %copy-start.7 = (bf16[2,256,768]{2,1,0:T(8,128)(2,1)}, bf16[2,256,768]{2,1,0:T(8,128)(2,1)S(1)}, u32[]{:S(2)}) copy-start(bf16[2,256,768]{2,1,0:T(8,128)(2,1)S(1)} %collective-permute-done.1) | copy-start | bytes 2359300
  122.0 61.0 %copy-start.9 = (bf16[2,256,768]{2,1,0:T(8,128)(2,1)}, bf16[2,256,768]{2,1,0:T(8,128)(2,1)S(1)}, u32[]{:S(2)}) copy-start(bf16[2,256,768]{2,1,0:T(8,128)(2,1)S(1)} %collective-permute-done) | copy-start | bytes 2359300
  182.8 5.1 copy-start.37
  182.9 5.0 copy-start.33
  183.0 6.7 %copy-start.27 = (bf16[32,24,768]{2,1,0:T(8,128)(2,1)S(1)}, bf16[32,24,768]{2,1,0:T(8,128)(2,1)}, u32[]{:S(2)}) copy-start(bf16[32,24,768]{2,1,0:T(8,128)(2,1)} %get-tuple-element.35) | copy-start | bytes 3538948
  250.5 16.9 %copy-start.39 = (f32[3072]{0:T(1024)}, f32[3072]{0:T(1024)S(1)}, u32[]{:S(2)}) copy-start(f32[3072]{0:T(1024)S(1)} %reshape.673) | copy-start | bytes 36868
  259.2 8.2 %slice-start = ((s8[4718592]{0:T(1024)(128)(4,1)}), s8[4194304]{0:T(1024)(128)(4,1)S(1)}, s32[]{:S(2)}) async-start(s8[4718592]{0:T(1024)(128)(4,1)} %bitcast.232), calls=%async_computation.5 | async-start | bytes 8388608
  262.0 13.6 %copy-start.11 = (f32[512,768]{1,0:T(8,128)}, f32[512,768]{1,0:T(8,128)S(1)}, u32[]{:S(2)}) copy-start(f32[512,768]{1,0:T(8,128)S(1)} %get-tuple-element.74) | copy-start | bytes 4718596
  262.3 5.0 slice-start.1
  262.4 5.0 copy-start.23
  267.4 5.1 copy-start.45
  322.5 9.6 %copy-start.13 = (bf16[2,256,12,64]{1,0,3,2:T(2,128)(2,1)S(1)}, bf16[2,256,12,64]{1,0,3,2:T(2,128)(2,1)}, u32[]{:S(2)}) copy-start(bf16[2,256,12,64]{1,0,3,2:T(2,128)(2,1)} %reshape.641) | copy-start | bytes 2359300
  332.1 7.0 %copy-start.32 = (bf16[2,256,12,64]{1,0,3,2:T(2,128)(2,1)S(1)}, bf16[2,256,12,64]{1,0,3,2:T(2,128)(2,1)}, u32[]{:S(2)}) copy-start(bf16[2,256,12,64]{1,0,3,2:T(2,128)(2,1)} %reshape.649) | copy-start | bytes 2359300
  353.1 7.5 %copy-start.16 = (bf16[2,256,12,64]{1,3,2,0:T(8,128)(2,1)S(1)}, bf16[2,256,12,64]{1,3,2,0:T(8,128)(2,1)}, u32[]{:S(2)}) copy-start(bf16[2,256,12,64]{1,3,2,0:T(8,128)(2,1)} %get-tuple-element.82) | copy-start | bytes 2359300
  367.0 5.0 copy-start.20
  376.4 10.4 %copy-start.18 = (bf16[96,8,2,1024]{3,1,2,0:T(8,128)(2,1)}, bf16[96,8,2,1024]{3,1,2,0:T(8,128)(2,1)S(1)}, u32[]{:S(2)}) copy-start(bf16[96,8,2,1024]{3,1,2,0:T(8,128)(2,1)S(1)} %copy.101) | copy-start | bytes 9437188
  390.9 45.6 %collective-permute-start.5 = (bf16[2,256,768]{2,1,0:T(8,128)(2,1)}, bf16[2,256,768]{2,1,0:T(8,128)(2,1)}, u32[]{:S(2)}, u32[]{:S(2)}) collective-permute-start(bf16[2,256,768]{2,1,0:T(8,128)(2,1)} %get-tuple-element.41), channel_id=1, source_target_pairs={{0,1},{1,2},{2,3},{3,0},{4,5},{5,6},{6,7},{7,4},{8,9},{9,10},{10,1... | collective-permute-start | bytes 2359304 | tf_op jit(solution)/shard_map/ppermute | solution.py:211
  391.7 54.8 %collective-permute-start.4 = (bf16[2,256,768]{2,1,0:T(8,128)(2,1)}, bf16[2,256,768]{2,1,0:T(8,128)(2,1)}, u32[]{:S(2)}, u32[]{:S(2)}) collective-permute-start(bf16[2,256,768]{2,1,0:T(8,128)(2,1)} %get-tuple-element.42), channel_id=1, source_target_pairs={{0,2},{1,3},{2,0},{3,1},{4,6},{5,7},{6,4},{7,5},{8,10},{9,11},{10,... | collective-permute-start | bytes 2359304 | tf_op jit(solution)/shard_map/ppermute | solution.py:211
  393.1 53.4 %collective-permute-start.3 = (bf16[2,256,768]{2,1,0:T(8,128)(2,1)}, bf16[2,256,768]{2,1,0:T(8,128)(2,1)}, u32[]{:S(2)}, u32[]{:S(2)}) collective-permute-start(bf16[2,256,768]{2,1,0:T(8,128)(2,1)} %get-tuple-element.40), channel_id=1, source_target_pairs={{0,3},{1,0},{2,1},{3,2},{4,7},{5,4},{6,5},{7,6},{8,11},{9,8},{10,9... | collective-permute-start | bytes 2359304 | tf_op jit(solution)/shard_map/ppermute | solution.py:211
  427.3 4.9 copy-start.24
  452.9 120.3 %copy-start.35 = (f32[32,24]{1,0:T(8,128)S(1)}, f32[32,24]{1,0:T(8,128)}, u32[]{:S(2)}) copy-start(f32[32,24]{1,0:T(8,128)} %get-tuple-element.58) | copy-start | bytes 9220
  452.9 120.4 %copy-start.12 = (f32[512,768]{1,0:T(8,128)S(1)}, f32[512,768]{1,0:T(8,128)}, u32[]{:S(2)}) copy-start(f32[512,768]{1,0:T(8,128)} %copy-done.11) | copy-start | bytes 4718596
  452.9 120.4 %copy-start.40 = (f32[3072]{0:T(1024)S(1)}, f32[3072]{0:T(1024)}, u32[]{:S(2)}) copy-start(f32[3072]{0:T(1024)} %copy-done.39) | copy-start | bytes 36868
  453.0 162.6 %reduce-scatter.5.cloned.1.call-start = ((), (), s32[]{:S(2)}) async-start(), calls=%async_computation.3 | async-start | bytes 2334720 | tf_op jit(solution)/shard_map/reduce_scatter | solution.py:99
  (26 other events, 65.3 us)
Sparse Core Ops, SparseCore 0:
  19.4 148.6 all-gather.2
  453.1 120.0 reduce-scatter.2
  575.5 40.0 reduce-scatter.4

commit v7 on v6

--- a/solution.py
+++ b/solution.py
@@ -4,6 +4,7 @@
 import jax.numpy as jnp
 from jax import lax
 from jax.sharding import PartitionSpec as P
+
 
 H = 12
 HD = 64
@@ -84,35 +85,51 @@
     return out
 
 
-def scatter_all(grads, width, mesh_shape):
+def pack_group(grads, group, width, mesh_shape):
     groups = mesh_shape[0] * mesh_shape[1]
-    shard_like = [jnp.zeros((g.shape[0] // groups,) + g.shape[1:], jnp.float32) for g in grads]
-    rows, vec_len, vec_rows, total = layout(shard_like, width, 16)
-    vec = jnp.concatenate([grads[i].reshape(groups, -1) for i in VECS], axis=1)
+    mats = [i for i in group if grads[i].ndim == 2]
+    vecs = [i for i in group if grads[i].ndim == 1]
+    rows = [grads[i].size // groups // width for i in mats]
+    vec_len = sum(grads[i].size // groups for i in vecs)
+    vec_rows = round_up(vec_len, width) // width
+    total = round_up(sum(rows) + vec_rows, 16)
     spare = total - sum(rows) - vec_rows
+    vec = jnp.concatenate([grads[i].reshape(groups, -1) for i in vecs], axis=1)
     vec = jnp.pad(vec, ((0, 0), (0, (vec_rows + spare) * width - vec_len)))
     vec = vec.reshape(groups, vec_rows + spare, width)
-    blocks = [grads[i].reshape(groups, -1, width) for i in MATS] + [vec]
+    blocks = [grads[i].reshape(groups, -1, width) for i in mats] + [vec]
     packed = jnp.concatenate([b.astype(jnp.bfloat16) for b in blocks], axis=1)
-    packed = packed.reshape(mesh_shape[0], mesh_shape[1], total, width)
+    return packed.reshape(mesh_shape[0], mesh_shape[1], total, width)
+
+
+def reduce_group(packed):
     packed = lax.psum_scatter(packed, "dp", scatter_dimension=0, tiled=True)
     mine = lax.psum_scatter(packed, "ctx", scatter_dimension=1, tiled=True)
-    mine = mine.reshape(total, width).astype(jnp.float32)
-    out = [None] * 15
+    return mine.reshape(packed.shape[2], packed.shape[3]).astype(jnp.float32)
+
+
+def unpack_group(mine, grads, group, width, groups):
+    out = {}
     off = 0
-    for i, r in zip(MATS, rows):
-        out[i] = mine[off:off + r, :].reshape(shard_like[i].shape)
+    for i in [i for i in group if grads[i].ndim == 2]:
+        shape = (grads[i].shape[0] // groups,) + grads[i].shape[1:]
+        r = math.prod(shape) // width
+        out[i] = mine[off:off + r, :].reshape(shape)
         off += r
-    vecs = mine[off:off + vec_rows, :].reshape(-1)
+    flat = mine[off:, :].reshape(-1)
     voff = 0
-    for i in VECS:
-        size = shard_like[i].size
-        out[i] = vecs[voff:voff + size]
+    for i in [i for i in group if grads[i].ndim == 1]:
+        size = grads[i].shape[0] // groups
+        out[i] = flat[voff:voff + size]
         voff += size
     return out
 
 
-def per_device(inputs, lengths, *rest):
+EARLY = (7, 8, 9, 10, 11, 12, 13, 14)
+LATE = (0, 1, 2, 3, 4, 5, 6)
+
+
+def layer(inputs, lengths, *rest):
     shards = rest[:15]
     out_grad = rest[15]
     n_ctx = lax.axis_size("ctx")
@@ -183,6 +200,11 @@
     d_branch = d_middle.astype(jnp.bfloat16)
     grad_bo = col_sum(d_branch)
     grad_wo = outer(mixed, d_branch)
+    grads = {
+        7: grad_wo, 8: grad_bo, 9: grad_ln2_gain, 10: grad_ln2_bias,
+        11: grad_wi, 12: grad_bi, 13: grad_wf, 14: grad_bf,
+    }
+    early_sum = reduce_group(pack_group(grads, EARLY, width, mesh_shape))
     d_mixed = back(d_branch, wo).astype(jnp.bfloat16).reshape(seqs, rows, H, HD)
     d_probs = jnp.einsum("sqhd,skhd->shqk", d_mixed, vh, preferred_element_type=jnp.float32)
     inner = jnp.sum(probs * d_probs, axis=-1, keepdims=True)
@@ -210,27 +232,15 @@
         sent = kv_blocks[:, b * rows:(b + 1) * rows].astype(jnp.bfloat16)
         got = lax.ppermute(sent, "ctx", [(i, (i - b) % n_ctx) for i in range(n_ctx)])
         d_normed = d_normed + f32(got)
-    d_x = norm_back_rows(d_normed.reshape(n, width), xhat1, rstd1, f32(ln1_gain))
+
+    grads.update({0: grad_ln1_gain, 1: grad_ln1_bias, 2: grad_wq, 3: grad_bq, 4: grad_wk, 5: grad_wv, 6: grad_bv})
+    late_sum = reduce_group(pack_group(grads, LATE, width, mesh_shape))
+    xhat1_b, rstd1_b = lax.optimization_barrier((xhat1, rstd1))
+    d_x = norm_back_rows(d_normed.reshape(n, width), xhat1_b, rstd1_b, f32(ln1_gain))
     input_grad = (d_middle + d_x).astype(jnp.bfloat16).reshape(seqs, rows, width)
-
-    grads = (
-        grad_ln1_gain,
-        grad_ln1_bias,
-        grad_wq,
-        grad_bq,
-        grad_wk,
-        grad_wv,
-        grad_bv,
-        grad_wo,
-        grad_bo,
-        grad_ln2_gain,
-        grad_ln2_bias,
-        grad_wi,
-        grad_bi,
-        grad_wf,
-        grad_bf,
-    )
-    return (output, input_grad) + tuple(scatter_all(grads, width, mesh_shape))
+    out = unpack_group(early_sum, grads, EARLY, width, groups)
+    out.update(unpack_group(late_sum, grads, LATE, width, groups))
+    return (output, input_grad) + tuple(out[i] for i in range(15))
 
 
 def solution(mesh):
@@ -239,7 +249,7 @@
     act = P("dp", "ctx", None)
     weight_specs = (row, row, mat, row, mat, mat, row, mat, row, row, row, mat, row, mat, row)
     return jax.shard_map(
-        per_device,
+        layer,
         mesh=mesh,
         in_specs=(act, P("dp")) + weight_specs + (act,),
         out_specs=(act, act) + weight_specs,

time: 637 us -> 623 us (0.978)
  waiting for transfers between devices: 303 us -> 274 us
  other arithmetic: 37.6 us -> 50.7 us
    ppermute x6, waiting for transfers between devices: 104 us -> 65 us  [the longest x3 65 us: layer(): lax.ppermute(inputs, 'ctx', [(i, (i + b) % n_ctx) for i in range(n_ctx)])]
    all_gather x1, waiting for transfers between devices: 43.1 us -> 73.8 us  [gather_all(): full = lax.all_gather(packed[None], ALL, axis=0, tiled=True)]
    reduce_scatter x2 -> x4, waiting for transfers between devices: 155 us -> 135 us  [the longest x2 93 us: reduce_group(): packed = lax.psum_scatter(packed, 'dp', scatter_dimension=0, tiled=True)]
    unnamed x116 -> x117, local copies, waits for them, and re-layouts: 20 us -> 9.87 us
    concatenate x0 -> x3, other arithmetic: none -> 8.75 us  [the longest x2 8.66 us: pack_group(): packed = jnp.concatenate([b.astype(jnp.bfloat16) for b in blocks], axis=1)]
    convert_element_type x4 -> x6, other arithmetic: 23.3 us -> 25.6 us  [the longest x1 21.6 us: layer(): d_scores = (probs * (d_probs - inner)).astype(jnp.bfloat16)]
    reshape x13 -> x15, local copies, waits for them, and re-layouts: 18.9 us -> 17.5 us  [the longest x1 6.15 us: layer(): vh = v.reshape(seqs, total, H, HD)]
  transfers between devices with their start and end apart: 9 -> 11, of which waited for: 6 -> 7; matrix products, arithmetic and copies ran while one was open for 9% -> 9% of each run, Pallas kernels for 0% -> 0%
where the time goes in v7:
time: 623 us; the launch traced here: 612 us
  waiting for transfers between devices  274 us (44%)
  matrix products  151 us (24%)
  local copies, waits for them, and re-layouts  110 us (18%)
  other arithmetic  50.7 us (8%)
  between operations  14.9 us (2%)
  starting transfers between devices  12.6 us (2%)
    reduce_scatter x2, waiting for transfers between devices, reduce_group(): packed = lax.psum_scatter(packed, 'dp', scatter_dimension=0, tiled=True)  93 us
    all_gather x1, waiting for transfers between devices, gather_all(): full = lax.all_gather(packed[None], ALL, axis=0, tiled=True)  73.8 us
    ppermute x3, waiting for transfers between devices, layer(): lax.ppermute(inputs, 'ctx', [(i, (i + b) % n_ctx) for i in range(n_ctx)])  65 us
    reduce_scatter x2, waiting for transfers between devices, reduce_group(): mine = lax.psum_scatter(packed, 'ctx', scatter_dimension=1, tiled=True)  41.6 us
    dot_general x6, matrix products, mm(): return jnp.dot(left, right, preferred_element_type=jnp.float32)  31.6 us
    dot_general x6, matrix products, outer(): lax.dot_general(left_rows, right_rows, (((0,), (0,)), ((), ())), preferre...  24.9 us
    dot_general x6, matrix products, back(): lax.dot_general(grad_rows, weight, (((1,), (1,)), ((), ())), preferred_el...  22.4 us
    convert_element_type x1, other arithmetic, layer(): d_scores = (probs * (d_probs - inner)).astype(jnp.bfloat16)  21.6 us
  transfers between devices with their start and end apart: 11, of which 7 were waited for; matrix products, arithmetic and copies ran while one was open for 9% of the time, Pallas kernels for 0%

profile of v7, /device:TPU:0, one launch (start us, length us, event | category | flops | bytes accessed | tf_op | source)
XLA Modules:
  0.0 612.1 jit_solution(1739987854770117007)
XLA Ops:
  9.1 6.1 concatenate.24
  28.1 64.2 %collective-permute-done.1 = bf16[2,256,768]{2,1,0:T(8,128)(2,1)S(1)} collective-permute-done((bf16[2,256,768]{2,1,0:T(8,128)(2,1)}, bf16[2,256,768]{2,1,0:T(8,128)(2,1)S(1)}, u32[]{:S(2)}, u32[]{:S(2)}) %collective-permute-start.1) | collective-permute-done | bytes 786464 | tf_op jit(solution)/shard_map/ppermute | solution.py:143
  96.2 73.8 %all-gather.3.cloned.1.call-done = bf16[9728,768]{1,0:T(8,128)(2,1)} async-done(((bf16[304,768]{1,0:T(8,128)(2,1)}), bf16[9728,768]{1,0:T(8,128)(2,1)}) %all-gather.3.cloned.1.call-update) | async-done | bytes 14942224 | tf_op jit(solution)/shard_map/all_gather | solution.py:72
  176.5 8.1 %fusion.95 = (bf16[32,96,768]{2,1,0:T(8,128)(2,1)}, bf16[32,96,768]{2,1,0:T(8,128)(2,1)}) fusion(bf16[32,304,768]{2,1,0:T(8,128)(2,1)} %bitcast.200), kind=kLoop, calls=%fused_computation.158 | loop fusion | bytes 18874368 | tf_op jit(solution)/shard_map/slice | solution.py:77
  185.3 8.5 %reshape.642 = bf16[768,3072]{1,0:T(8,128)(2,1)} reshape(bf16[32,96,768]{2,1,0:T(8,128)(2,1)} %get-tuple-element.33) | data formatting | bytes 9437184 | tf_op jit(solution)/shard_map/reshape | solution.py:77
  193.8 4.8 subtract_multiply_fusion
  210.0 5.2 convolution_convert_fusion.1
  219.9 4.8 reshape.640
  224.7 7.7 %add_convert_fusion.1 = bf16[2048,768]{1,0:T(8,128)(2,1)} fusion(bf16[2048,768]{1,0:T(8,128)(2,1)} %bitcast.206, bf16[768,768]{1,0:T(8,128)(2,1)} %bitcast.238, f32[768]{0:T(1024)S(1)} %reshape.669), kind=kOutput, calls=%fused_computation.34 | convolution fusion | flops 2419064832 | bytes 7474176 | tf_op jit(solution)/shard_map/dot_general | solution.py:30
  232.4 4.7 copy.69
  237.1 6.1 %reshape.635 = bf16[2,1024,12,64]{1,0,3,2:T(2,128)(2,1)} reshape(bf16[2048,768]{0,1:T(8,128)(2,1)} %copy.69) | data formatting | bytes 6291456 | tf_op jit(solution)/shard_map/reshape | solution.py:166
  243.2 15.1 %fusion.100 = (f32[2,12,256]{2,1,0:T(8,128)S(1)}, f32[2,12,256,1024]{3,2,1,0:T(8,128)}) fusion(pred[2,1024]{1,0:T(4,128)(4,1)S(1)} %broadcast_compare_fusion, bf16[2,1024,12,64]{1,0,3,2:T(2,128)(2,1)S(1)} %reshape.640, bf16[2,256,12,64]{1,0,3,2:T(2,128)(2,1)} %reshape.638), kind=kOutput, calls=%fused_computation.163 | convolution fusion | flops 830473216 | bytes 29124608 | tf_op jit(solution)/shard_map/sub | solution.py:172
  258.3 11.8 %fusion.60 = bf16[2,256,12,64]{1,3,2,0:T(8,128)(2,1)S(1)} fusion(bf16[2,1024,12,64]{1,0,3,2:T(2,128)(2,1)} %reshape.635, f32[2,12,256,1024]{3,2,1,0:T(8,128)} %get-tuple-element.70, f32[2,12,256]{2,1,0:T(8,128)S(1)} %get-tuple-element.69), kind=kOutput, calls=%fused_computation.90 | convolution fusion | flops 818282496 | bytes 29122560 | tf_op jit(solution)/shard_map/shqk,skhd->sqhd/dot_general | solution.py:175
  273.0 6.8 %fusion.19 = (bf16[3072,512]{0,1:T(8,128)(2,1)}, f32[512,3072]{1,0:T(8,128)S(1)}) fusion(f32[3072]{0:T(1024)S(1)} %reshape.674, bf16[768,3072]{1,0:T(8,128)(2,1)} %reshape.642, f32[512,768]{1,0:T(8,128)S(1)} %get-tuple-element.72, f32[768]{0:T(1024)S(1)} %reshape.673, f32[768]{0:T(1024)S(1)} %reshape.672, f32[512]{0:T(512)S(1)} %add_rsqrt_fusion.1, ...), kind=kOutput, calls=%fused_computation.37 | convolution fusion | flops 2427322368 | bytes 15751168 | tf_op jit(solution)/shard_map/dot_general | solution.py:30
  279.8 4.8 fusion.112
  292.7 11.7 %fusion.110 = (bf16[12,64]{1,0:T(8,128)(2,1)S(1)}, bf16[2,1024,12,64]{1,3,2,0:T(8,128)(2,1)}) fusion(f32[2,12,256,1024]{3,2,1,0:T(8,128)} %get-tuple-element.70, f32[2,12,256]{2,1,0:T(8,128)S(1)} %get-tuple-element.69, bf16[2,256,12,64]{1,0,3,2:T(2,128)(2,1)} %reshape.646), kind=kOutput, calls=%fused_computation.165 | convolution fusion | flops 821034240 | bytes 29124096 | tf_op jit(solution)/shard_map/shqk,sqhd->skhd/dot_general | solution.py:217
  304.4 16.5 %multiply_reduce_fusion = (f32[2,12,256]{2,1,0:T(8,128)S(1)}, f32[2,12,256,1024]{3,2,1,0:T(8,128)}) fusion(f32[2,12,256,1024]{3,2,1,0:T(8,128)} %get-tuple-element.70, f32[2,12,256]{2,1,0:T(8,128)S(1)} %get-tuple-element.69, bf16[2,1024,12,64]{1,0,3,2:T(2,128)(2,1)} %reshape.635, bf16[2,256,12,64]{1,0,3,2:T(2,128)(2,1)S(1)} %copy-done.30), kind=kOutput, calls=%fused_computation.2 | convolution fusion | flops 824174592 | bytes 54312960 | tf_op jit(solution)/shard_map/sqhd,skhd->shqk/dot_general | solution.py:209
  320.9 21.6 %multiply_convert_fusion = bf16[2,12,256,1024]{3,2,1,0:T(8,128)(2,1)} fusion(f32[2,12,256,1024]{3,2,1,0:T(8,128)} %get-tuple-element.75, f32[2,12,256]{2,1,0:T(8,128)S(1)} %get-tuple-element.74, f32[2,12,256,1024]{3,2,1,0:T(8,128)} %get-tuple-element.70, f32[2,12,256]{2,1,0:T(8,128)S(1)} %get-tuple-element.69), kind=kLoop, calls=%fused_computation.1 | loop fusion | flops 25165824 | bytes 62963712 | tf_op jit(solution)/shard_map/convert_element_type | solution.py:211
  342.5 9.5 %fusion.111 = (bf16[12,64]{1,0:T(8,128)(2,1)S(1)}, bf16[2,256,12,64]{1,3,2,0:T(8,128)(2,1)}) fusion(bf16[2,12,256,1024]{3,2,1,0:T(8,128)(2,1)} %multiply_convert_fusion, bf16[2,1024,12,64]{1,0,3,2:T(2,128)(2,1)S(1)} %copy-done.1), kind=kOutput, calls=%fused_computation.166 | convolution fusion | flops 806485248 | bytes 16516608 | tf_op jit(solution)/shard_map/shqk,skhd->sqhd/dot_general | solution.py:212
  352.0 7.0 %fusion.23 = bf16[2,1024,12,64]{1,3,2,0:T(8,128)(2,1)S(1)} fusion(bf16[2,12,256,1024]{3,2,1,0:T(8,128)(2,1)} %multiply_convert_fusion, bf16[2,256,12,64]{1,0,3,2:T(2,128)(2,1)S(1)} %copy-done.12), kind=kOutput, calls=%fused_computation.46 | convolution fusion | flops 808452096 | bytes 16515072 | tf_op jit(solution)/shard_map/shqk,sqhd->skhd/dot_general | solution.py:215
  371.1 8.0 %multiply_reduce_fusion.1 = (f32[768]{0:T(1024)S(1)}, f32[768]{0:T(1024)S(1)}, bf16[2048,768]{1,0:T(8,128)(2,1)}, f32[2048,768]{1,0:T(8,128)}) fusion(f32[2048]{0:T(1024)S(1)} %copy-done.38, f32[2048]{0:T(1024)S(1)} %copy-done.39, bf16[2,256,768]{2,1,0:T(8,128)(2,1)S(1)} %copy-done.9, bf16[2,256,768]{2,1,0:T(8,128)(2,1)S(1)} %copy-done.5, ...), kind=kOutput, calls=%fused_computation.25 | convolution fusion | flops 2442656256 | bytes 23228416 | tf_op jit(solution)/shard_map/dot_general | solution.py:40
  379.1 5.2 copy.87
  384.3 6.7 %fusion.50 = bf16[32,24,768]{2,1,0:T(8,128)(2,1)} fusion(bf16[32,24,2048]{2,1,0:T(8,128)(2,1)} %bitcast.226, bf16[2048,768]{0,1:T(8,128)(2,1)} %bitcast.222), kind=kOutput, calls=%fused_computation.83 | convolution fusion | flops 2416508928 | bytes 7471104 | tf_op jit(solution)/shard_map/dot_general | solution.py:34
  407.8 4.8 copy.90
  412.7 7.8 %convolution_convert_fusion = bf16[768,3072]{1,0:T(8,128)(2,1)} fusion(bf16[512,3072]{1,0:T(8,128)(2,1)} %copy-done.43, f32[512,768]{1,0:T(8,128)} %copy-done.11, f32[768]{0:T(1024)S(1)} %copy-done.41, f32[768]{0:T(1024)S(1)} %reshape.672, f32[512]{0:T(512)S(1)} %add_rsqrt_fusion.1, f32[512]{0:T(512)S(1)} %broadcast_multiply_fusion.4), kind=kOutput, calls=%fused_computation.40 | convolution fusion | flops 2420244480 | bytes 9447424 | tf_op jit(solution)/shard_map/dot_general | solution.py:34
  420.5 8.5 %convert_element_type.362 = bf16[32,96,768]{2,1,0:T(8,128)(2,1)} reshape(bf16[768,3072]{1,0:T(8,128)(2,1)} %convolution_convert_fusion) | data formatting | bytes 9437184 | tf_op jit(solution)/shard_map/convert_element_type | solution.py:101
  434.5 5.2 pad_maximum_fusion
  439.8 14.8 %reduce-scatter.5.cloned.1.call-done = bf16[1,4,80,768]{3,2,1,0:T(8,128)(2,1)} async-done(((bf16[8,4,80,768]{3,2,1,0:T(8,128)(2,1)}), bf16[1,4,80,768]{3,2,1,0:T(8,128)(2,1)}) %reduce-scatter.5.cloned.1.call-update) | async-done | bytes 491536 | tf_op jit(solution)/shard_map/reduce_scatter | solution.py:106
  464.5 78.2 %reduce-scatter.9.cloned.1.call-done = bf16[1,4,224,768]{3,2,1,0:T(8,128)(2,1)} async-done(((bf16[8,4,224,768]{3,2,1,0:T(8,128)(2,1)}), bf16[1,4,224,768]{3,2,1,0:T(8,128)(2,1)}) %reduce-scatter.9.cloned.1.call-update) | async-done | bytes 1376272 | tf_op jit(solution)/shard_map/reduce_scatter | solution.py:106
  542.8 7.7 %add_convert_fusion.4 = bf16[512,768]{1,0:T(8,128)(2,1)} fusion(f32[512,768]{1,0:T(8,128)} %copy-done.11, bf16[3072,768]{1,0:T(8,128)(2,1)} %bitcast.212, f32[512,3072]{1,0:T(8,128)} %copy-done.42, f32[3072]{0:T(1024)S(1)} %copy-done.37, f32[768]{0:T(1024)S(1)} %reshape.675), kind=kOutput, calls=%fused_computation.78 | convolution fusion | flops 2426535936 | bytes 13384704 | tf_op jit(solution)/shard_map/dot_general | solution.py:30
  554.8 11.5 %reduce-scatter.7.cloned.1.call-done = bf16[1,1,80,768]{3,2,1,0:T(8,128)(2,1)} async-done(((bf16[1,4,80,768]{3,2,1,0:T(8,128)(2,1)}), bf16[1,1,80,768]{3,2,1,0:T(8,128)(2,1)}) %reduce-scatter.7.cloned.1.call-update) | async-done | bytes 122896 | tf_op jit(solution)/shard_map/reduce_scatter | solution.py:107
  569.3 30.0 %reduce-scatter.11.cloned.1.call-done = bf16[1,1,224,768]{3,2,1,0:T(8,128)(2,1)} async-done(((bf16[1,4,224,768]{3,2,1,0:T(8,128)(2,1)}), bf16[1,1,224,768]{3,2,1,0:T(8,128)(2,1)}) %reduce-scatter.11.cloned.1.call-update) | async-done | bytes 344080 | tf_op jit(solution)/shard_map/reduce_scatter | solution.py:107
  (230 shorter events, 109.9 us)
Async XLA Ops:
  7.2 86.0 %copy-start.2 = (bf16[2,256,768]{2,1,0:T(8,128)(2,1)S(1)}, bf16[2,256,768]{2,1,0:T(8,128)(2,1)}, u32[]{:S(2)}) copy-start(bf16[2,256,768]{2,1,0:T(8,128)(2,1)} %param.18) | copy-start | bytes 2359300
  7.2 162.8 %all-gather.3.cloned.1.call-start = ((), (), s32[]{:S(2)}) async-start(), calls=%async_computation.8 | async-start | bytes 15409152 | tf_op jit(solution)/shard_map/all_gather | solution.py:72
  19.3 435.3 %reduce-scatter.5.cloned.1.call-start = ((), (), s32[]{:S(2)}) async-start(), calls=%async_computation.4 | async-start | bytes 4423680 | tf_op jit(solution)/shard_map/reduce_scatter | solution.py:106
  19.3 73.0 %collective-permute-start.1 = (bf16[2,256,768]{2,1,0:T(8,128)(2,1)}, bf16[2,256,768]{2,1,0:T(8,128)(2,1)S(1)}, u32[]{:S(2)}, u32[]{:S(2)}) collective-permute-start(bf16[2,256,768]{2,1,0:T(8,128)(2,1)} %param.18), channel_id=1, source_target_pairs={{0,2},{1,3},{2,0},{3,1},{4,6},{5,7},{6,4},{7,5},{8,10},{9,11},{10,... | collective-permute-start | bytes 2359304 | tf_op jit(solution)/shard_map/ppermute | solution.py:143
  23.5 68.8 %collective-permute-start = (bf16[2,256,768]{2,1,0:T(8,128)(2,1)}, bf16[2,256,768]{2,1,0:T(8,128)(2,1)S(1)}, u32[]{:S(2)}, u32[]{:S(2)}) collective-permute-start(bf16[2,256,768]{2,1,0:T(8,128)(2,1)} %param.18), channel_id=1, source_target_pairs={{0,1},{1,2},{2,3},{3,0},{4,5},{5,6},{6,7},{7,4},{8,9},{9,10},{10,1... | collective-permute-start | bytes 2359304 | tf_op jit(solution)/shard_map/ppermute | solution.py:143
  25.1 68.1 %collective-permute-start.2 = (bf16[2,256,768]{2,1,0:T(8,128)(2,1)}, bf16[2,256,768]{2,1,0:T(8,128)(2,1)S(1)}, u32[]{:S(2)}, u32[]{:S(2)}) collective-permute-start(bf16[2,256,768]{2,1,0:T(8,128)(2,1)} %param.18), channel_id=1, source_target_pairs={{0,3},{1,0},{2,1},{3,2},{4,7},{5,4},{6,5},{7,6},{8,11},{9,8},{10,9... | collective-permute-start | bytes 2359304 | tf_op jit(solution)/shard_map/ppermute | solution.py:143
  92.3 101.5 %copy-start.4 = (bf16[2,256,768]{2,1,0:T(8,128)(2,1)}, bf16[2,256,768]{2,1,0:T(8,128)(2,1)S(1)}, u32[]{:S(2)}) copy-start(bf16[2,256,768]{2,1,0:T(8,128)(2,1)S(1)} %collective-permute-done.1) | copy-start | bytes 2359300
  92.3 101.5 %copy-start.6 = (bf16[2,256,768]{2,1,0:T(8,128)(2,1)}, bf16[2,256,768]{2,1,0:T(8,128)(2,1)S(1)}, u32[]{:S(2)}) copy-start(bf16[2,256,768]{2,1,0:T(8,128)(2,1)S(1)} %collective-permute-done) | copy-start | bytes 2359300
  93.1 100.7 %copy-start.8 = (bf16[2,256,768]{2,1,0:T(8,128)(2,1)}, bf16[2,256,768]{2,1,0:T(8,128)(2,1)S(1)}, u32[]{:S(2)}) copy-start(bf16[2,256,768]{2,1,0:T(8,128)(2,1)S(1)} %collective-permute-done.2) | copy-start | bytes 2359300
  184.7 95.1 %copy-start.36 = (f32[3072]{0:T(1024)}, f32[3072]{0:T(1024)S(1)}, u32[]{:S(2)}) copy-start(f32[3072]{0:T(1024)S(1)} %reshape.674) | copy-start | bytes 36868
  184.7 9.1 %copy-start.31 = (f32[768]{0:T(1024)}, f32[768]{0:T(1024)S(1)}, u32[]{:S(2)}) copy-start(f32[768]{0:T(1024)S(1)} %reshape.667) | copy-start | bytes 9220
  184.9 88.0 %copy-start.40 = (f32[768]{0:T(1024)}, f32[768]{0:T(1024)S(1)}, u32[]{:S(2)}) copy-start(f32[768]{0:T(1024)S(1)} %reshape.673) | copy-start | bytes 9220
  185.0 8.8 %copy-start.34 = (f32[768]{0:T(1024)}, f32[768]{0:T(1024)S(1)}, u32[]{:S(2)}) copy-start(f32[768]{0:T(1024)S(1)} %reshape.668) | copy-start | bytes 9220
  201.5 8.5 %copy-start.14 = (bf16[2,1024,768]{2,1,0:T(8,128)(2,1)S(1)}, bf16[2,1024,768]{2,1,0:T(8,128)(2,1)}, u32[]{:S(2)}) copy-start(bf16[2,1024,768]{2,1,0:T(8,128)(2,1)} %copy-done.13) | copy-start | bytes 9437188
  224.7 18.5 %copy-start = (bf16[2,1024,12,64]{1,0,3,2:T(2,128)(2,1)}, bf16[2,1024,12,64]{1,0,3,2:T(2,128)(2,1)S(1)}, u32[]{:S(2)}) copy-start(bf16[2,1024,12,64]{1,0,3,2:T(2,128)(2,1)S(1)} %reshape.640) | copy-start | bytes 9437188
  271.7 8.1 %slice-start.4 = ((s8[4718592]{0:T(1024)(128)(4,1)}), s8[4194304]{0:T(1024)(128)(4,1)S(1)}, s32[]{:S(2)}) async-start(s8[4718592]{0:T(1024)(128)(4,1)} %bitcast.213), calls=%async_computation.13 | async-start | bytes 8388608
  272.6 15.2 %copy-start.11 = (f32[512,768]{1,0:T(8,128)}, f32[512,768]{1,0:T(8,128)S(1)}, u32[]{:S(2)}) copy-start(f32[512,768]{1,0:T(8,128)S(1)} %get-tuple-element.72) | copy-start | bytes 4718596
  273.0 11.7 %slice-start.2 = ((s8[4718592]{0:T(1024)(128)(4,1)}), s8[4194304]{0:T(1024)(128)(4,1)S(1)}, s32[]{:S(2)}) async-start(s8[4718592]{0:T(1024)(128)(4,1)} %bitcast.210), calls=%async_computation.11 | async-start | bytes 8388608
  292.7 11.7 %copy-start.30 = (bf16[2,256,12,64]{1,0,3,2:T(2,128)(2,1)S(1)}, bf16[2,256,12,64]{1,0,3,2:T(2,128)(2,1)}, u32[]{:S(2)}) copy-start(bf16[2,256,12,64]{1,0,3,2:T(2,128)(2,1)} %reshape.646) | copy-start | bytes 2359300
  320.9 21.6 %copy-start.1 = (bf16[2,1024,12,64]{1,0,3,2:T(2,128)(2,1)S(1)}, bf16[2,1024,12,64]{1,0,3,2:T(2,128)(2,1)}, u32[]{:S(2)}) copy-start(bf16[2,1024,12,64]{1,0,3,2:T(2,128)(2,1)} %copy-done) | copy-start | bytes 9437188
  342.5 9.5 %copy-start.12 = (bf16[2,256,12,64]{1,0,3,2:T(2,128)(2,1)S(1)}, bf16[2,256,12,64]{1,0,3,2:T(2,128)(2,1)}, u32[]{:S(2)}) copy-start(bf16[2,256,12,64]{1,0,3,2:T(2,128)(2,1)} %reshape.638) | copy-start | bytes 2359300
  352.0 7.0 %copy-start.21 = (bf16[2,1024,12,64]{1,3,2,0:T(8,128)(2,1)S(1)}, bf16[2,1024,12,64]{1,3,2,0:T(8,128)(2,1)}, u32[]{:S(2)}) copy-start(bf16[2,1024,12,64]{1,3,2,0:T(8,128)(2,1)} %get-tuple-element.77) | copy-start | bytes 9437188
  363.3 7.6 %copy-start.18 = (bf16[96,8,2,1024]{3,1,2,0:T(8,128)(2,1)}, bf16[96,8,2,1024]{3,1,2,0:T(8,128)(2,1)S(1)}, u32[]{:S(2)}) copy-start(bf16[96,8,2,1024]{3,1,2,0:T(8,128)(2,1)S(1)} %copy.101) | copy-start | bytes 9437188
  406.3 136.4 %reduce-scatter.9.cloned.1.call-start = ((), (), s32[]{:S(2)}) async-start(), calls=%async_computation.6 | async-start | bytes 12386304 | tf_op jit(solution)/shard_map/reduce_scatter | solution.py:106
  439.7 15.7 %copy-start.33 = (f32[32,24]{1,0:T(8,128)S(1)}, f32[32,24]{1,0:T(8,128)}, u32[]{:S(2)}) copy-start(f32[32,24]{1,0:T(8,128)} %get-tuple-element.48) | copy-start | bytes 9220
  439.8 126.6 %reduce-scatter.7.cloned.1.call-start = ((), (), s32[]{:S(2)}) async-start(), calls=%async_computation.5 | async-start | bytes 614400 | tf_op jit(solution)/shard_map/reduce_scatter | solution.py:107
  454.7 144.7 %reduce-scatter.11.cloned.1.call-start = ((), (), s32[]{:S(2)}) async-start(), calls=%async_computation.7 | async-start | bytes 1720320 | tf_op jit(solution)/shard_map/reduce_scatter | solution.py:107
  458.6 84.2 %copy-start.37 = (f32[3072]{0:T(1024)S(1)}, f32[3072]{0:T(1024)}, u32[]{:S(2)}) copy-start(f32[3072]{0:T(1024)} %copy-done.36) | copy-start | bytes 36868
  460.0 90.4 %collective-permute-start.3 = (bf16[2,256,768]{2,1,0:T(8,128)(2,1)}, bf16[2,256,768]{2,1,0:T(8,128)(2,1)}, u32[]{:S(2)}, u32[]{:S(2)}) collective-permute-start(bf16[2,256,768]{2,1,0:T(8,128)(2,1)} %get-tuple-element.42), channel_id=1, source_target_pairs={{0,3},{1,0},{2,1},{3,2},{4,7},{5,4},{6,5},{7,6},{8,11},{9,8},{10,9... | collective-permute-start | bytes 2359304 | tf_op jit(solution)/shard_map/ppermute | solution.py:233
  463.4 87.1 %collective-permute-start.5 = (bf16[2,256,768]{2,1,0:T(8,128)(2,1)}, bf16[2,256,768]{2,1,0:T(8,128)(2,1)}, u32[]{:S(2)}, u32[]{:S(2)}) collective-permute-start(bf16[2,256,768]{2,1,0:T(8,128)(2,1)} %get-tuple-element.43), channel_id=1, source_target_pairs={{0,1},{1,2},{2,3},{3,0},{4,5},{5,6},{6,7},{7,4},{8,9},{9,10},{10,1... | collective-permute-start | bytes 2359304 | tf_op jit(solution)/shard_map/ppermute | solution.py:233
  463.4 87.1 %collective-permute-start.4 = (bf16[2,256,768]{2,1,0:T(8,128)(2,1)}, bf16[2,256,768]{2,1,0:T(8,128)(2,1)}, u32[]{:S(2)}, u32[]{:S(2)}) collective-permute-start(bf16[2,256,768]{2,1,0:T(8,128)(2,1)} %get-tuple-element.44), channel_id=1, source_target_pairs={{0,2},{1,3},{2,0},{3,1},{4,6},{5,7},{6,4},{7,5},{8,10},{9,11},{10,... | collective-permute-start | bytes 2359304 | tf_op jit(solution)/shard_map/ppermute | solution.py:233
  542.7 7.7 %copy-start.10 = (f32[512,768]{1,0:T(8,128)S(1)}, f32[512,768]{1,0:T(8,128)}, u32[]{:S(2)}) copy-start(f32[512,768]{1,0:T(8,128)} %get-tuple-element.81) | copy-start | bytes 4718596
  (29 other events, 98.2 us)
Sparse Core Ops, SparseCore 0:
  19.4 150.5 all-gather.2
  406.5 48.1 reduce-scatter.4
  458.2 84.4 reduce-scatter.8
  544.9 21.4 reduce-scatter.6
  568.5 30.7 reduce-scatter.10

commit v8 on v7

--- a/solution.py
+++ b/solution.py
@@ -158,21 +158,22 @@
     xhat1 = own(xhat_all)
     rstd1 = rstd_all.reshape(seqs, total, 1)[:, :rows].reshape(n, 1)
     x = f32(inputs).reshape(n, width)
-    q = (mm(normed, wq) + f32(bq)).astype(jnp.bfloat16)
-    k = mm(normed_all, wk).astype(jnp.bfloat16)
-    v = (mm(normed_all, wv) + f32(bv)).astype(jnp.bfloat16)
-    qh = q.reshape(seqs, rows, H, HD)
-    kh = k.reshape(seqs, total, H, HD)
-    vh = v.reshape(seqs, total, H, HD)
+    heads = lambda w: w.reshape(width, H, HD)
+    project = lambda a, w: jnp.einsum("snd,dhe->shne", a, heads(w), preferred_element_type=jnp.float32)
+    own_rows = normed.reshape(seqs, rows, width)
+    all_rows = normed_all.reshape(seqs, total, width)
+    qh = (project(own_rows, wq) + f32(bq).reshape(H, 1, HD)).astype(jnp.bfloat16)
+    kh = project(all_rows, wk).astype(jnp.bfloat16)
+    vh = (project(all_rows, wv) + f32(bv).reshape(H, 1, HD)).astype(jnp.bfloat16)
     scale = HD ** (-0.5)
-    scores = jnp.einsum("sqhd,skhd->shqk", qh, kh, preferred_element_type=jnp.float32) * scale
+    scores = jnp.einsum("shqd,shkd->shqk", qh, kh, preferred_element_type=jnp.float32) * scale
     valid = positions[None, :] < lengths[:, None]
     scores = jnp.where(valid[:, None, None, :], scores, -1e30)
     top = jnp.max(scores, axis=-1, keepdims=True)
     expd = jnp.exp(scores - top)
     probs = expd / jnp.sum(expd, axis=-1, keepdims=True)
     low_probs = probs.astype(jnp.bfloat16)
-    mixed = jnp.einsum("shqk,skhd->sqhd", low_probs, vh, preferred_element_type=jnp.float32)
+    mixed = jnp.einsum("shqk,shkd->sqhd", low_probs, vh, preferred_element_type=jnp.float32)
     mixed = mixed.reshape(n, width).astype(jnp.bfloat16)
     middle = x + mm(mixed, wo) + f32(bo)
     xhat2, rstd2 = row_stats(middle)
@@ -206,13 +207,13 @@
     }
     early_sum = reduce_group(pack_group(grads, EARLY, width, mesh_shape))
     d_mixed = back(d_branch, wo).astype(jnp.bfloat16).reshape(seqs, rows, H, HD)
-    d_probs = jnp.einsum("sqhd,skhd->shqk", d_mixed, vh, preferred_element_type=jnp.float32)
+    d_probs = jnp.einsum("sqhd,shkd->shqk", d_mixed, vh, preferred_element_type=jnp.float32)
     inner = jnp.sum(probs * d_probs, axis=-1, keepdims=True)
     d_scores = (probs * (d_probs - inner)).astype(jnp.bfloat16)
-    d_q = jnp.einsum("shqk,skhd->sqhd", d_scores, kh, preferred_element_type=jnp.float32) * scale
+    d_q = jnp.einsum("shqk,shkd->sqhd", d_scores, kh, preferred_element_type=jnp.float32) * scale
     d_q = d_q.reshape(n, width).astype(jnp.bfloat16)
     k_part = (
-        jnp.einsum("shqk,sqhd->skhd", d_scores, qh, preferred_element_type=jnp.float32) * scale
+        jnp.einsum("shqk,shqd->skhd", d_scores, qh, preferred_element_type=jnp.float32) * scale
     ).reshape(seqs * total, width).astype(jnp.bfloat16)
     v_part = jnp.einsum("shqk,sqhd->skhd", low_probs, d_mixed, preferred_element_type=jnp.float32)
     v_part = v_part.reshape(seqs * total, width).astype(jnp.bfloat16)

time: 623 us -> 606 us (0.973)
  local copies, waits for them, and re-layouts: 110 us -> 95.8 us
    dot_general x6 -> x3, matrix products: 31.6 us -> 15.5 us  [mm(): return jnp.dot(left, right, preferred_element_type=jnp.float32)]
    dot_general x4 -> x7, matrix products: 44.9 us -> 59.9 us  [the longest x1 16.6 us: layer(): jnp.einsum('sqhd,shkd->shqk', d_mixed, vh, preferred_element_type=jnp.flo...]
    reshape x4 -> x0, local copies, waits for them, and re-layouts: 15 us -> none  [the longest x1 6.15 us: layer(): vh = v.reshape(seqs, total, H, HD)]
    another operation x0 -> x3, local copies, waits for them, and re-layouts: none -> 12.7 us  [layer(): heads = lambda w: w.reshape(width, H, HD)]
    convert_element_type x4 -> x1, local copies, waits for them, and re-layouts: 15.2 us -> 3.49 us  [layer(): k_part = (jnp.einsum('shqk,shqd->skhd', d_scores, qh, preferred_element_t...]
  transfers between devices with their start and end apart: 11 -> 11, of which waited for: 7 -> 7; matrix products, arithmetic and copies ran while one was open for 9% -> 10% of each run, Pallas kernels for 0% -> 0%
where the time goes in v8:
time: 606 us; the launch traced here: 595 us
  waiting for transfers between devices  273 us (45%)
  matrix products  148 us (24%)
  local copies, waits for them, and re-layouts  95.8 us (16%)
  other arithmetic  50.7 us (8%)
  between operations  14.9 us (2%)
  starting transfers between devices  12.6 us (2%)
    reduce_scatter x2, waiting for transfers between devices, reduce_group(): packed = lax.psum_scatter(packed, 'dp', scatter_dimension=0, tiled=True)  93.1 us
    all_gather x1, waiting for transfers between devices, gather_all(): full = lax.all_gather(packed[None], ALL, axis=0, tiled=True)  73.8 us
    ppermute x3, waiting for transfers between devices, layer(): lax.ppermute(inputs, 'ctx', [(i, (i + b) % n_ctx) for i in range(n_ctx)])  65 us
    reduce_scatter x2, waiting for transfers between devices, reduce_group(): mine = lax.psum_scatter(packed, 'ctx', scatter_dimension=1, tiled=True)  41.5 us
    dot_general x6, matrix products, outer(): lax.dot_general(left_rows, right_rows, (((0,), (0,)), ((), ())), preferre...  24.9 us
    convert_element_type x1, other arithmetic, layer(): d_scores = (probs * (d_probs - inner)).astype(jnp.bfloat16)  21.6 us
    dot_general x6, matrix products, back(): lax.dot_general(grad_rows, weight, (((1,), (1,)), ((), ())), preferred_el...  21.5 us
    dot_general x1, matrix products, layer(): jnp.einsum('sqhd,shkd->shqk', d_mixed, vh, preferred_element_type=jnp.flo...  16.6 us
  transfers between devices with their start and end apart: 11, of which 7 were waited for; matrix products, arithmetic and copies ran while one was open for 10% of the time, Pallas kernels for 0%

profile of v8, /device:TPU:0, one launch (start us, length us, event | category | flops | bytes accessed | tf_op | source)
XLA Modules:
  0.0 595.5 jit_solution(6371080633291782412)
XLA Ops:
  9.1 6.1 %concatenate.28 = bf16[288]{0:T(512)(128)(2,1)S(1)} concatenate(bf16[24]{0:T(256)(128)(2,1)} %param.20, bf16[24]{0:T(256)(128)(2,1)} %param.21, bf16[24]{0:T(256)(128)(2,1)} %param.23, bf16[24]{0:T(256)(128)(2,1)} %param.26, bf16[24]{0:T(256)(128)(2,1)} %param.28, bf16[24]{0:T(256)(128)(2,1)} %param.29, bf16[24]{0:T(256)(128)(2,1)} %param.30, bf16[96]{0:T(256)(128)(2,1)} %param.32, ...), dimensions={0} | concatenate | bytes 1152 | tf_op jit(solution)/shard_map/concatenate | solution.py:67
  28.1 64.2 %collective-permute-done.1 = bf16[2,256,768]{2,1,0:T(8,128)(2,1)S(1)} collective-permute-done((bf16[2,256,768]{2,1,0:T(8,128)(2,1)}, bf16[2,256,768]{2,1,0:T(8,128)(2,1)S(1)}, u32[]{:S(2)}, u32[]{:S(2)}) %collective-permute-start.1) | collective-permute-done | bytes 786464 | tf_op jit(solution)/shard_map/ppermute | solution.py:143
  96.2 73.8 %all-gather.3.cloned.1.call-done = bf16[9728,768]{1,0:T(8,128)(2,1)} async-done(((bf16[304,768]{1,0:T(8,128)(2,1)}), bf16[9728,768]{1,0:T(8,128)(2,1)}) %all-gather.3.cloned.1.call-update) | async-done | bytes 14942224 | tf_op jit(solution)/shard_map/all_gather | solution.py:72
  171.9 4.3 fusion.120
  176.2 8.5 %fusion.119 = (bf16[32,96,768]{2,1,0:T(8,128)(2,1)}, bf16[32,96,768]{2,1,0:T(8,128)(2,1)}) fusion(bf16[32,304,768]{2,1,0:T(8,128)(2,1)} %bitcast.208), kind=kLoop, calls=%fused_computation.170 | loop fusion | bytes 18874368 | tf_op jit(solution)/shard_map/slice | solution.py:77
  185.3 8.5 %reshape.506 = bf16[768,3072]{1,0:T(8,128)(2,1)} reshape(bf16[32,96,768]{2,1,0:T(8,128)(2,1)} %get-tuple-element.33) | data formatting | bytes 9437184 | tf_op jit(solution)/shard_map/reshape | solution.py:77
  193.8 4.7 reshape_reshape.11
  201.7 4.8 reshape_reshape.9
  206.6 4.8 subtract_multiply_fusion
  212.3 6.6 %convert_bitcast_fusion.1 = bf16[2,12,1024,64]{2,3,0,1:T(8,128)(2,1)} fusion(bf16[2,1024,768]{2,1,0:T(8,128)(2,1)S(1)} %get-tuple-element.41, bf16[768,12,64,1]{2,1,0,3:T(8,128)(2,1)S(1)} %bitcast.240), kind=kOutput, calls=%fused_computation.58 | convolution fusion | flops 2417491968 | bytes 7471104 | tf_op jit(solution)/shard_map/snd,dhe->shne/dot_general | solution.py:162
  220.8 7.3 %fusion.22 = bf16[2,12,1024,64]{2,3,0,1:T(8,128)(2,1)} fusion(f32[12,64]{1,0:T(8,128)S(1)} %reshape.537, bf16[2,1024,768]{2,1,0:T(8,128)(2,1)S(1)} %get-tuple-element.41, bf16[768,12,64,1]{2,1,0,3:T(8,128)(2,1)S(1)} %bitcast.238), kind=kOutput, calls=%fused_computation.44 | convolution fusion | flops 2419064832 | bytes 7474176 | tf_op jit(solution)/shard_map/snd,dhe->shne/dot_general | solution.py:162
  228.1 14.7 %fusion.124 = (f32[2,12,256]{2,1,0:T(8,128)S(1)}, f32[2,12,256,1024]{3,2,1,0:T(8,128)}) fusion(pred[2,1024]{1,0:T(4,128)(4,1)S(1)} %broadcast_compare_fusion, bf16[2,12,1024,64]{2,3,0,1:T(8,128)(2,1)} %convert_bitcast_fusion.1, bf16[2,12,256,64]{2,3,0,1:T(8,128)(2,1)S(1)} %fusion.84), kind=kOutput, calls=%fused_computation.175 | convolution fusion | flops 830473216 | bytes 29124608 | tf_op jit(solution)/shard_map/sub | solution.py:173
  242.8 11.5 %fusion.79 = bf16[2,256,12,64]{1,3,2,0:T(8,128)(2,1)S(1)} fusion(bf16[2,12,1024,64]{2,3,0,1:T(8,128)(2,1)} %fusion.22, f32[2,12,256,1024]{3,2,1,0:T(8,128)} %get-tuple-element.70, f32[2,12,256]{2,1,0:T(8,128)S(1)} %get-tuple-element.69), kind=kOutput, calls=%fused_computation.99 | convolution fusion | flops 818282496 | bytes 29122560 | tf_op jit(solution)/shard_map/shqk,shkd->sqhd/dot_general | solution.py:176
  256.9 6.8 %fusion.19 = (bf16[3072,512]{0,1:T(8,128)(2,1)}, f32[512,3072]{1,0:T(8,128)S(1)}) fusion(f32[3072]{0:T(1024)S(1)} %reshape.542, bf16[768,3072]{1,0:T(8,128)(2,1)} %reshape.506, f32[512,768]{1,0:T(8,128)S(1)} %get-tuple-element.72, f32[768]{0:T(1024)S(1)} %reshape.541, f32[768]{0:T(1024)S(1)} %reshape.540, f32[512]{0:T(512)S(1)} %add_rsqrt_fusion.1, ...), kind=kOutput, calls=%fused_computation.37 | convolution fusion | flops 2427322368 | bytes 15751168 | tf_op jit(solution)/shard_map/dot_general | solution.py:30
  263.8 4.8 fusion.136
  273.8 11.5 %fusion.134 = (bf16[12,64]{1,0:T(8,128)(2,1)S(1)}, bf16[2,1024,12,64]{1,3,2,0:T(8,128)(2,1)}) fusion(f32[2,12,256,1024]{3,2,1,0:T(8,128)} %get-tuple-element.70, f32[2,12,256]{2,1,0:T(8,128)S(1)} %get-tuple-element.69, bf16[2,256,12,64]{1,0,3,2:T(2,128)(2,1)S(1)} %reshape.510), kind=kOutput, calls=%fused_computation.177 | convolution fusion | flops 821034240 | bytes 29124096 | tf_op jit(solution)/shard_map/shqk,sqhd->skhd/dot_general | solution.py:218
  285.3 16.6 %multiply_reduce_fusion = (f32[2,12,256]{2,1,0:T(8,128)S(1)}, f32[2,12,256,1024]{3,2,1,0:T(8,128)}) fusion(f32[2,12,256,1024]{3,2,1,0:T(8,128)} %get-tuple-element.70, f32[2,12,256]{2,1,0:T(8,128)S(1)} %get-tuple-element.69, bf16[2,12,1024,64]{2,3,0,1:T(8,128)(2,1)} %fusion.22, bf16[2,256,12,64]{1,0,3,2:T(2,128)(2,1)S(1)} %reshape.510), kind=kOutput, calls=%fused_computation.2 | convolution fusion | flops 824174592 | bytes 54312960 | tf_op jit(solution)/shard_map/sqhd,shkd->shqk/dot_general | solution.py:210
  301.8 21.6 %multiply_convert_fusion = bf16[2,12,256,1024]{3,2,1,0:T(8,128)(2,1)} fusion(f32[2,12,256,1024]{3,2,1,0:T(8,128)} %get-tuple-element.75, f32[2,12,256]{2,1,0:T(8,128)S(1)} %get-tuple-element.74, f32[2,12,256,1024]{3,2,1,0:T(8,128)} %get-tuple-element.70, f32[2,12,256]{2,1,0:T(8,128)S(1)} %get-tuple-element.69), kind=kLoop, calls=%fused_computation.1 | loop fusion | flops 25165824 | bytes 62963712 | tf_op jit(solution)/shard_map/convert_element_type | solution.py:212
  323.4 9.5 %fusion.135 = (bf16[12,64]{1,0:T(8,128)(2,1)S(1)}, bf16[2,256,12,64]{1,3,2,0:T(8,128)(2,1)}) fusion(bf16[2,12,256,1024]{3,2,1,0:T(8,128)(2,1)} %multiply_convert_fusion, bf16[2,12,1024,64]{2,3,0,1:T(8,128)(2,1)S(1)} %copy-done.16), kind=kOutput, calls=%fused_computation.178 | convolution fusion | flops 806485248 | bytes 16516608 | tf_op jit(solution)/shard_map/shqk,shkd->sqhd/dot_general | solution.py:213
  333.0 7.0 %fusion.24 = bf16[2,1024,12,64]{1,3,2,0:T(8,128)(2,1)S(1)} fusion(bf16[2,12,256,1024]{3,2,1,0:T(8,128)(2,1)} %multiply_convert_fusion, bf16[2,12,256,64]{2,3,0,1:T(8,128)(2,1)S(1)} %copy-done.30), kind=kOutput, calls=%fused_computation.46 | convolution fusion | flops 808452096 | bytes 16515072 | tf_op jit(solution)/shard_map/shqk,shqd->skhd/dot_general | solution.py:216
  352.2 8.0 %multiply_reduce_fusion.1 = (f32[768]{0:T(1024)S(1)}, f32[768]{0:T(1024)S(1)}, bf16[2048,768]{1,0:T(8,128)(2,1)}, f32[2048,768]{1,0:T(8,128)}) fusion(f32[2048]{0:T(1024)S(1)} %copy-done.40, f32[2048]{0:T(1024)S(1)} %copy-done.41, bf16[2,256,768]{2,1,0:T(8,128)(2,1)S(1)} %copy-done.11, bf16[2,256,768]{2,1,0:T(8,128)(2,1)S(1)} %copy-done.5, ...), kind=kOutput, calls=%fused_computation.25 | convolution fusion | flops 2442656256 | bytes 23228416 | tf_op jit(solution)/shard_map/dot_general | solution.py:40
  360.2 5.2 copy.96
  365.5 6.7 %fusion.67 = bf16[32,24,768]{2,1,0:T(8,128)(2,1)} fusion(bf16[32,24,2048]{2,1,0:T(8,128)(2,1)} %bitcast.233, bf16[2048,768]{0,1:T(8,128)(2,1)} %bitcast.229), kind=kOutput, calls=%fused_computation.92 | convolution fusion | flops 2416508928 | bytes 7471104 | tf_op jit(solution)/shard_map/dot_general | solution.py:34
  391.3 4.8 copy.99
  396.2 7.8 %convolution_convert_fusion = bf16[768,3072]{1,0:T(8,128)(2,1)} fusion(bf16[512,3072]{1,0:T(8,128)(2,1)} %copy-done.45, f32[512,768]{1,0:T(8,128)} %copy-done.13, f32[768]{0:T(1024)S(1)} %copy-done.43, f32[768]{0:T(1024)S(1)} %reshape.540, f32[512]{0:T(512)S(1)} %add_rsqrt_fusion.1, f32[512]{0:T(512)S(1)} %broadcast_multiply_fusion.4), kind=kOutput, calls=%fused_computation.40 | convolution fusion | flops 2420244480 | bytes 9447424 | tf_op jit(solution)/shard_map/dot_general | solution.py:34
  404.0 8.5 %convert_element_type.359 = bf16[32,96,768]{2,1,0:T(8,128)(2,1)} reshape(bf16[768,3072]{1,0:T(8,128)(2,1)} %convolution_convert_fusion) | data formatting | bytes 9437184 | tf_op jit(solution)/shard_map/convert_element_type | solution.py:101
  418.0 5.2 pad_maximum_fusion
  423.3 14.9 %reduce-scatter.5.cloned.1.call-done = bf16[1,4,80,768]{3,2,1,0:T(8,128)(2,1)} async-done(((bf16[8,4,80,768]{3,2,1,0:T(8,128)(2,1)}), bf16[1,4,80,768]{3,2,1,0:T(8,128)(2,1)}) %reduce-scatter.5.cloned.1.call-update) | async-done | bytes 491536 | tf_op jit(solution)/shard_map/reduce_scatter | solution.py:106
  448.0 78.2 %reduce-scatter.9.cloned.1.call-done = bf16[1,4,224,768]{3,2,1,0:T(8,128)(2,1)} async-done(((bf16[8,4,224,768]{3,2,1,0:T(8,128)(2,1)}), bf16[1,4,224,768]{3,2,1,0:T(8,128)(2,1)}) %reduce-scatter.9.cloned.1.call-update) | async-done | bytes 1376272 | tf_op jit(solution)/shard_map/reduce_scatter | solution.py:106
  526.3 7.7 %add_convert_fusion.4 = bf16[512,768]{1,0:T(8,128)(2,1)} fusion(f32[512,768]{1,0:T(8,128)} %copy-done.13, bf16[3072,768]{1,0:T(8,128)(2,1)} %bitcast.219, f32[512,3072]{1,0:T(8,128)} %copy-done.44, f32[3072]{0:T(1024)S(1)} %copy-done.39, f32[768]{0:T(1024)S(1)} %reshape.543), kind=kOutput, calls=%fused_computation.87 | convolution fusion | flops 2426535936 | bytes 13384704 | tf_op jit(solution)/shard_map/dot_general | solution.py:30
  538.3 11.7 %reduce-scatter.7.cloned.1.call-done = bf16[1,1,80,768]{3,2,1,0:T(8,128)(2,1)} async-done(((bf16[1,4,80,768]{3,2,1,0:T(8,128)(2,1)}), bf16[1,1,80,768]{3,2,1,0:T(8,128)(2,1)}) %reduce-scatter.7.cloned.1.call-update) | async-done | bytes 122896 | tf_op jit(solution)/shard_map/reduce_scatter | solution.py:107
  552.9 29.8 %reduce-scatter.11.cloned.1.call-done = bf16[1,1,224,768]{3,2,1,0:T(8,128)(2,1)} async-done(((bf16[1,4,224,768]{3,2,1,0:T(8,128)(2,1)}), bf16[1,1,224,768]{3,2,1,0:T(8,128)(2,1)}) %reduce-scatter.11.cloned.1.call-update) | async-done | bytes 344080 | tf_op jit(solution)/shard_map/reduce_scatter | solution.py:107
  (231 shorter events, 94.5 us)
Async XLA Ops:
  7.2 86.0 %copy-start.2 = (bf16[2,256,768]{2,1,0:T(8,128)(2,1)S(1)}, bf16[2,256,768]{2,1,0:T(8,128)(2,1)}, u32[]{:S(2)}) copy-start(bf16[2,256,768]{2,1,0:T(8,128)(2,1)} %param.18) | copy-start | bytes 2359300
  7.2 162.8 %all-gather.3.cloned.1.call-start = ((), (), s32[]{:S(2)}) async-start(), calls=%async_computation.8 | async-start | bytes 15409152 | tf_op jit(solution)/shard_map/all_gather | solution.py:72
  19.3 418.8 %reduce-scatter.5.cloned.1.call-start = ((), (), s32[]{:S(2)}) async-start(), calls=%async_computation.4 | async-start | bytes 4423680 | tf_op jit(solution)/shard_map/reduce_scatter | solution.py:106
  19.4 73.0 %collective-permute-start.1 = (bf16[2,256,768]{2,1,0:T(8,128)(2,1)}, bf16[2,256,768]{2,1,0:T(8,128)(2,1)S(1)}, u32[]{:S(2)}, u32[]{:S(2)}) collective-permute-start(bf16[2,256,768]{2,1,0:T(8,128)(2,1)} %param.18), channel_id=1, source_target_pairs={{0,2},{1,3},{2,0},{3,1},{4,6},{5,7},{6,4},{7,5},{8,10},{9,11},{10,... | collective-permute-start | bytes 2359304 | tf_op jit(solution)/shard_map/ppermute | solution.py:143
  23.5 68.8 %collective-permute-start = (bf16[2,256,768]{2,1,0:T(8,128)(2,1)}, bf16[2,256,768]{2,1,0:T(8,128)(2,1)S(1)}, u32[]{:S(2)}, u32[]{:S(2)}) collective-permute-start(bf16[2,256,768]{2,1,0:T(8,128)(2,1)} %param.18), channel_id=1, source_target_pairs={{0,1},{1,2},{2,3},{3,0},{4,5},{5,6},{6,7},{7,4},{8,9},{9,10},{10,1... | collective-permute-start | bytes 2359304 | tf_op jit(solution)/shard_map/ppermute | solution.py:143
  25.1 68.1 %collective-permute-start.2 = (bf16[2,256,768]{2,1,0:T(8,128)(2,1)}, bf16[2,256,768]{2,1,0:T(8,128)(2,1)S(1)}, u32[]{:S(2)}, u32[]{:S(2)}) collective-permute-start(bf16[2,256,768]{2,1,0:T(8,128)(2,1)} %param.18), channel_id=1, source_target_pairs={{0,3},{1,0},{2,1},{3,2},{4,7},{5,4},{6,5},{7,6},{8,11},{9,8},{10,9... | collective-permute-start | bytes 2359304 | tf_op jit(solution)/shard_map/ppermute | solution.py:143
  92.3 114.2 %copy-start.4 = (bf16[2,256,768]{2,1,0:T(8,128)(2,1)}, bf16[2,256,768]{2,1,0:T(8,128)(2,1)S(1)}, u32[]{:S(2)}) copy-start(bf16[2,256,768]{2,1,0:T(8,128)(2,1)S(1)} %collective-permute-done.1) | copy-start | bytes 2359300
  176.2 22.3 %copy-start = (bf16[32,24,768]{2,1,0:T(8,128)(2,1)}, bf16[32,24,768]{2,1,0:T(8,128)(2,1)S(1)}, u32[]{:S(2)}) copy-start(bf16[32,24,768]{2,1,0:T(8,128)(2,1)S(1)} %get-tuple-element.37) | copy-start | bytes 3538948
  184.7 79.1 %copy-start.38 = (f32[3072]{0:T(1024)}, f32[3072]{0:T(1024)S(1)}, u32[]{:S(2)}) copy-start(f32[3072]{0:T(1024)S(1)} %reshape.542) | copy-start | bytes 36868
  184.8 21.7 %copy-start.33 = (f32[768]{0:T(1024)}, f32[768]{0:T(1024)S(1)}, u32[]{:S(2)}) copy-start(f32[768]{0:T(1024)S(1)} %reshape.535) | copy-start | bytes 9220
  185.0 71.9 %copy-start.42 = (f32[768]{0:T(1024)}, f32[768]{0:T(1024)S(1)}, u32[]{:S(2)}) copy-start(f32[768]{0:T(1024)S(1)} %reshape.541) | copy-start | bytes 9220
  185.1 21.5 %copy-start.36 = (f32[768]{0:T(1024)}, f32[768]{0:T(1024)S(1)}, u32[]{:S(2)}) copy-start(f32[768]{0:T(1024)S(1)} %reshape.536) | copy-start | bytes 9220
  220.4 7.8 %copy-start.29 = (bf16[2,12,256,64]{2,3,0,1:T(8,128)(2,1)}, bf16[2,12,256,64]{2,3,0,1:T(8,128)(2,1)S(1)}, u32[]{:S(2)}) copy-start(bf16[2,12,256,64]{2,3,0,1:T(8,128)(2,1)S(1)} %fusion.84) | copy-start | bytes 2359300
  255.6 8.2 %slice-start.4 = ((s8[4718592]{0:T(1024)(128)(4,1)}), s8[4194304]{0:T(1024)(128)(4,1)S(1)}, s32[]{:S(2)}) async-start(s8[4718592]{0:T(1024)(128)(4,1)} %bitcast.220), calls=%async_computation.13 | async-start | bytes 8388608
  256.6 15.2 %copy-start.13 = (f32[512,768]{1,0:T(8,128)}, f32[512,768]{1,0:T(8,128)S(1)}, u32[]{:S(2)}) copy-start(f32[512,768]{1,0:T(8,128)S(1)} %get-tuple-element.72) | copy-start | bytes 4718596
  256.9 6.9 %slice-start.5 = ((s8[4718592]{0:T(1024)(128)(4,1)}), s8[524288]{0:T(1024)(128)(4,1)S(1)}, s32[]{:S(2)}) async-start(s8[4718592]{0:T(1024)(128)(4,1)} %bitcast.220), calls=%async_computation.14 | async-start | bytes 1048576
  256.9 6.9 %copy-start.27 = (bf16[2,256,768]{2,1,0:T(8,128)(2,1)S(1)}, bf16[2,256,768]{2,1,0:T(8,128)(2,1)}, u32[]{:S(2)}) copy-start(bf16[2,256,768]{2,1,0:T(8,128)(2,1)} %param.35) | copy-start | bytes 2359300
  256.9 11.8 %slice-start.2 = ((s8[4718592]{0:T(1024)(128)(4,1)}), s8[4194304]{0:T(1024)(128)(4,1)S(1)}, s32[]{:S(2)}) async-start(s8[4718592]{0:T(1024)(128)(4,1)} %bitcast.217), calls=%async_computation.11 | async-start | bytes 8388608
  301.8 21.6 %copy-start.16 = (bf16[2,12,1024,64]{2,3,0,1:T(8,128)(2,1)S(1)}, bf16[2,12,1024,64]{2,3,0,1:T(8,128)(2,1)}, u32[]{:S(2)}) copy-start(bf16[2,12,1024,64]{2,3,0,1:T(8,128)(2,1)} %convert_bitcast_fusion.1) | copy-start | bytes 9437188
  323.4 9.5 %copy-start.30 = (bf16[2,12,256,64]{2,3,0,1:T(8,128)(2,1)S(1)}, bf16[2,12,256,64]{2,3,0,1:T(8,128)(2,1)}, u32[]{:S(2)}) copy-start(bf16[2,12,256,64]{2,3,0,1:T(8,128)(2,1)} %copy-done.29) | copy-start | bytes 2359300
  333.0 7.0 %copy-start.22 = (bf16[2,1024,12,64]{1,3,2,0:T(8,128)(2,1)S(1)}, bf16[2,1024,12,64]{1,3,2,0:T(8,128)(2,1)}, u32[]{:S(2)}) copy-start(bf16[2,1024,12,64]{1,3,2,0:T(8,128)(2,1)} %get-tuple-element.77) | copy-start | bytes 9437188
  344.3 7.6 %copy-start.19 = (bf16[96,8,2,1024]{3,1,2,0:T(8,128)(2,1)}, bf16[96,8,2,1024]{3,1,2,0:T(8,128)(2,1)S(1)}, u32[]{:S(2)}) copy-start(bf16[96,8,2,1024]{3,1,2,0:T(8,128)(2,1)S(1)} %copy.119) | copy-start | bytes 9437188
  365.4 6.7 %copy-start.21 = (bf16[96,8,2,1024]{3,1,2,0:T(8,128)(2,1)S(1)}, bf16[96,8,2,1024]{3,1,2,0:T(8,128)(2,1)}, u32[]{:S(2)}) copy-start(bf16[96,8,2,1024]{3,1,2,0:T(8,128)(2,1)} %copy-done.20) | copy-start | bytes 9437188
  389.8 136.4 %reduce-scatter.9.cloned.1.call-start = ((), (), s32[]{:S(2)}) async-start(), calls=%async_computation.6 | async-start | bytes 12386304 | tf_op jit(solution)/shard_map/reduce_scatter | solution.py:106
  423.2 15.7 %copy-start.35 = (f32[32,24]{1,0:T(8,128)S(1)}, f32[32,24]{1,0:T(8,128)}, u32[]{:S(2)}) copy-start(f32[32,24]{1,0:T(8,128)} %get-tuple-element.48) | copy-start | bytes 9220
  423.2 126.8 %reduce-scatter.7.cloned.1.call-start = ((), (), s32[]{:S(2)}) async-start(), calls=%async_computation.5 | async-start | bytes 614400 | tf_op jit(solution)/shard_map/reduce_scatter | solution.py:107
  438.2 144.6 %reduce-scatter.11.cloned.1.call-start = ((), (), s32[]{:S(2)}) async-start(), calls=%async_computation.7 | async-start | bytes 1720320 | tf_op jit(solution)/shard_map/reduce_scatter | solution.py:107
  442.1 84.2 %copy-start.39 = (f32[3072]{0:T(1024)S(1)}, f32[3072]{0:T(1024)}, u32[]{:S(2)}) copy-start(f32[3072]{0:T(1024)} %copy-done.38) | copy-start | bytes 36868
  443.6 90.4 %collective-permute-start.3 = (bf16[2,256,768]{2,1,0:T(8,128)(2,1)}, bf16[2,256,768]{2,1,0:T(8,128)(2,1)}, u32[]{:S(2)}, u32[]{:S(2)}) collective-permute-start(bf16[2,256,768]{2,1,0:T(8,128)(2,1)} %get-tuple-element.42), channel_id=1, source_target_pairs={{0,3},{1,0},{2,1},{3,2},{4,7},{5,4},{6,5},{7,6},{8,11},{9,8},{10,9... | collective-permute-start | bytes 2359304 | tf_op jit(solution)/shard_map/ppermute | solution.py:234
  446.9 87.1 %collective-permute-start.5 = (bf16[2,256,768]{2,1,0:T(8,128)(2,1)}, bf16[2,256,768]{2,1,0:T(8,128)(2,1)}, u32[]{:S(2)}, u32[]{:S(2)}) collective-permute-start(bf16[2,256,768]{2,1,0:T(8,128)(2,1)} %get-tuple-element.43), channel_id=1, source_target_pairs={{0,1},{1,2},{2,3},{3,0},{4,5},{5,6},{6,7},{7,4},{8,9},{9,10},{10,1... | collective-permute-start | bytes 2359304 | tf_op jit(solution)/shard_map/ppermute | solution.py:234
  446.9 87.1 %collective-permute-start.4 = (bf16[2,256,768]{2,1,0:T(8,128)(2,1)}, bf16[2,256,768]{2,1,0:T(8,128)(2,1)}, u32[]{:S(2)}, u32[]{:S(2)}) collective-permute-start(bf16[2,256,768]{2,1,0:T(8,128)(2,1)} %get-tuple-element.44), channel_id=1, source_target_pairs={{0,2},{1,3},{2,0},{3,1},{4,6},{5,7},{6,4},{7,5},{8,10},{9,11},{10,... | collective-permute-start | bytes 2359304 | tf_op jit(solution)/shard_map/ppermute | solution.py:234
  526.3 7.7 %copy-start.12 = (f32[512,768]{1,0:T(8,128)S(1)}, f32[512,768]{1,0:T(8,128)}, u32[]{:S(2)}) copy-start(f32[512,768]{1,0:T(8,128)} %get-tuple-element.81) | copy-start | bytes 4718596
  (31 other events, 105.8 us)
Sparse Core Ops, SparseCore 0:
  19.4 150.5 all-gather.2
  390.0 48.1 reduce-scatter.4
  441.8 84.4 reduce-scatter.8
  528.4 21.5 reduce-scatter.6
  552.2 30.5 reduce-scatter.10

commit v9 on v8

--- a/solution.py
+++ b/solution.py
@@ -102,10 +102,19 @@
     return packed.reshape(mesh_shape[0], mesh_shape[1], total, width)
 
 
-def reduce_group(packed):
-    packed = lax.psum_scatter(packed, "dp", scatter_dimension=0, tiled=True)
-    mine = lax.psum_scatter(packed, "ctx", scatter_dimension=1, tiled=True)
-    return mine.reshape(packed.shape[2], packed.shape[3]).astype(jnp.float32)
+def dp_stage(packed):
+    return lax.psum_scatter(packed, "dp", scatter_dimension=0, tiled=True)
+
+
+def ctx_stage(parts):
+    joined = jnp.concatenate(parts, axis=2)
+    mine = lax.psum_scatter(joined, "ctx", scatter_dimension=1, tiled=True)
+    mine = mine.reshape(joined.shape[2], joined.shape[3]).astype(jnp.float32)
+    out, off = [], 0
+    for p in parts:
+        out.append(mine[off:off + p.shape[2]])
+        off += p.shape[2]
+    return out
 
 
 def unpack_group(mine, grads, group, width, groups):
@@ -205,7 +214,7 @@
         7: grad_wo, 8: grad_bo, 9: grad_ln2_gain, 10: grad_ln2_bias,
         11: grad_wi, 12: grad_bi, 13: grad_wf, 14: grad_bf,
     }
-    early_sum = reduce_group(pack_group(grads, EARLY, width, mesh_shape))
+    early_part = dp_stage(pack_group(grads, EARLY, width, mesh_shape))
     d_mixed = back(d_branch, wo).astype(jnp.bfloat16).reshape(seqs, rows, H, HD)
     d_probs = jnp.einsum("sqhd,shkd->shqk", d_mixed, vh, preferred_element_type=jnp.float32)
     inner = jnp.sum(probs * d_probs, axis=-1, keepdims=True)
@@ -235,10 +244,11 @@
         d_normed = d_normed + f32(got)
 
     grads.update({0: grad_ln1_gain, 1: grad_ln1_bias, 2: grad_wq, 3: grad_bq, 4: grad_wk, 5: grad_wv, 6: grad_bv})
-    late_sum = reduce_group(pack_group(grads, LATE, width, mesh_shape))
+    late_part = dp_stage(pack_group(grads, LATE, width, mesh_shape))
     xhat1_b, rstd1_b = lax.optimization_barrier((xhat1, rstd1))
     d_x = norm_back_rows(d_normed.reshape(n, width), xhat1_b, rstd1_b, f32(ln1_gain))
     input_grad = (d_middle + d_x).astype(jnp.bfloat16).reshape(seqs, rows, width)
+    early_sum, late_sum = ctx_stage([early_part, late_part])
     out = unpack_group(early_sum, grads, EARLY, width, groups)
     out.update(unpack_group(late_sum, grads, LATE, width, groups))
     return (output, input_grad) + tuple(out[i] for i in range(15))

time: 606 us -> 661 us (1.091)
  waiting for transfers between devices: 273 us -> 331 us
    ppermute x3, waiting for transfers between devices: 0.01 us -> 88.8 us  [layer(): lax.ppermute(sent, 'ctx', [(i, (i - b) % n_ctx) for i in range(n_ctx)])]
    reduce_scatter x4 -> x3, waiting for transfers between devices: 135 us -> 103 us  [the longest x2 103 us: dp_stage(): return lax.psum_scatter(packed, 'dp', scatter_dimension=0, tiled=True)]
  transfers between devices with their start and end apart: 11 -> 10, of which waited for: 7 -> 8; matrix products, arithmetic and copies ran while one was open for 10% -> 8% of each run, Pallas kernels for 0% -> 0%
where the time goes in v9:
time: 661 us; the launch traced here: 651 us
  waiting for transfers between devices  331 us (50%)
  matrix products  148 us (22%)
  local copies, waits for them, and re-layouts  93.2 us (14%)
  other arithmetic  52 us (8%)
  between operations  14.9 us (2%)
  starting transfers between devices  12.6 us (2%)
    reduce_scatter x2, waiting for transfers between devices, dp_stage(): return lax.psum_scatter(packed, 'dp', scatter_dimension=0, tiled=True)  103 us
    ppermute x3, waiting for transfers between devices, layer(): lax.ppermute(sent, 'ctx', [(i, (i - b) % n_ctx) for i in range(n_ctx)])  88.8 us
    all_gather x1, waiting for transfers between devices, gather_all(): full = lax.all_gather(packed[None], ALL, axis=0, tiled=True)  73.8 us
    ppermute x3, waiting for transfers between devices, layer(): lax.ppermute(inputs, 'ctx', [(i, (i + b) % n_ctx) for i in range(n_ctx)])  65 us
    dot_general x6, matrix products, outer(): lax.dot_general(left_rows, right_rows, (((0,), (0,)), ((), ())), preferre...  24.9 us
    convert_element_type x1, other arithmetic, layer(): d_scores = (probs * (d_probs - inner)).astype(jnp.bfloat16)  21.6 us
    dot_general x6, matrix products, back(): lax.dot_general(grad_rows, weight, (((1,), (1,)), ((), ())), preferred_el...  21.6 us
    dot_general x1, matrix products, layer(): jnp.einsum('sqhd,shkd->shqk', d_mixed, vh, preferred_element_type=jnp.flo...  16.6 us
  transfers between devices with their start and end apart: 10, of which 8 were waited for; matrix products, arithmetic and copies ran while one was open for 8% of the time, Pallas kernels for 0%

profile of v9, /device:TPU:0, one launch (start us, length us, event | category | flops | bytes accessed | tf_op | source)
XLA Modules:
  0.0 650.9 jit_solution(1993634992450466322)
XLA Ops:
  9.1 6.1 concatenate.31
  28.1 64.2 %collective-permute-done.1 = bf16[2,256,768]{2,1,0:T(8,128)(2,1)S(1)} collective-permute-done((bf16[2,256,768]{2,1,0:T(8,128)(2,1)}, bf16[2,256,768]{2,1,0:T(8,128)(2,1)S(1)}, u32[]{:S(2)}, u32[]{:S(2)}) %collective-permute-start.1) | collective-permute-done | bytes 786464 | tf_op jit(solution)/shard_map/ppermute | solution.py:152
  96.2 73.8 %all-gather.3.cloned.1.call-done = bf16[9728,768]{1,0:T(8,128)(2,1)} async-done(((bf16[304,768]{1,0:T(8,128)(2,1)}), bf16[9728,768]{1,0:T(8,128)(2,1)}) %all-gather.3.cloned.1.call-update) | async-done | bytes 14942224 | tf_op jit(solution)/shard_map/all_gather | solution.py:72
  176.2 8.5 %fusion.119 = (bf16[32,96,768]{2,1,0:T(8,128)(2,1)}, bf16[32,96,768]{2,1,0:T(8,128)(2,1)}) fusion(bf16[32,304,768]{2,1,0:T(8,128)(2,1)} %bitcast.208), kind=kLoop, calls=%fused_computation.171 | loop fusion | bytes 18874368 | tf_op jit(solution)/shard_map/slice | solution.py:77
  185.3 8.5 %reshape.504 = bf16[768,3072]{1,0:T(8,128)(2,1)} reshape(bf16[32,96,768]{2,1,0:T(8,128)(2,1)} %get-tuple-element.33) | data formatting | bytes 9437184 | tf_op jit(solution)/shard_map/reshape | solution.py:77
  193.8 4.7 reshape_reshape.11
  201.8 4.8 reshape_reshape.9
  206.6 4.8 subtract_multiply_fusion
  212.4 6.6 %convert_bitcast_fusion.1 = bf16[2,12,1024,64]{2,3,0,1:T(8,128)(2,1)} fusion(bf16[2,1024,768]{2,1,0:T(8,128)(2,1)S(1)} %get-tuple-element.41, bf16[768,12,64,1]{2,1,0,3:T(8,128)(2,1)S(1)} %bitcast.240), kind=kOutput, calls=%fused_computation.58 | convolution fusion | flops 2417491968 | bytes 7471104 | tf_op jit(solution)/shard_map/snd,dhe->shne/dot_general | solution.py:171
  220.9 7.3 %fusion.22 = bf16[2,12,1024,64]{2,3,0,1:T(8,128)(2,1)} fusion(f32[12,64]{1,0:T(8,128)S(1)} %reshape.535, bf16[2,1024,768]{2,1,0:T(8,128)(2,1)S(1)} %get-tuple-element.41, bf16[768,12,64,1]{2,1,0,3:T(8,128)(2,1)S(1)} %bitcast.238), kind=kOutput, calls=%fused_computation.44 | convolution fusion | flops 2419064832 | bytes 7474176 | tf_op jit(solution)/shard_map/snd,dhe->shne/dot_general | solution.py:171
  228.1 14.7 %fusion.125 = (f32[2,12,256]{2,1,0:T(8,128)S(1)}, f32[2,12,256,1024]{3,2,1,0:T(8,128)}) fusion(pred[2,1024]{1,0:T(4,128)(4,1)S(1)} %broadcast_compare_fusion, bf16[2,12,1024,64]{2,3,0,1:T(8,128)(2,1)} %convert_bitcast_fusion.1, bf16[2,12,256,64]{2,3,0,1:T(8,128)(2,1)S(1)} %fusion.84), kind=kOutput, calls=%fused_computation.177 | convolution fusion | flops 830473216 | bytes 29124608 | tf_op jit(solution)/shard_map/sub | solution.py:182
  242.9 11.5 %fusion.79 = bf16[2,256,12,64]{1,3,2,0:T(8,128)(2,1)S(1)} fusion(bf16[2,12,1024,64]{2,3,0,1:T(8,128)(2,1)} %fusion.22, f32[2,12,256,1024]{3,2,1,0:T(8,128)} %get-tuple-element.73, f32[2,12,256]{2,1,0:T(8,128)S(1)} %get-tuple-element.72), kind=kOutput, calls=%fused_computation.100 | convolution fusion | flops 818282496 | bytes 29122560 | tf_op jit(solution)/shard_map/shqk,shkd->sqhd/dot_general | solution.py:185
  257.0 6.7 %fusion.19 = (bf16[3072,512]{0,1:T(8,128)(2,1)}, f32[512,3072]{1,0:T(8,128)S(1)}) fusion(f32[3072]{0:T(1024)S(1)} %reshape.540, bf16[768,3072]{1,0:T(8,128)(2,1)} %reshape.504, f32[512,768]{1,0:T(8,128)S(1)} %get-tuple-element.75, f32[768]{0:T(1024)S(1)} %reshape.539, f32[768]{0:T(1024)S(1)} %reshape.538, f32[512]{0:T(512)S(1)} %add_rsqrt_fusion.1, ...), kind=kOutput, calls=%fused_computation.37 | convolution fusion | flops 2427322368 | bytes 15751168 | tf_op jit(solution)/shard_map/dot_general | solution.py:30
  263.8 4.8 fusion.137
  273.7 11.4 %fusion.135 = (bf16[12,64]{1,0:T(8,128)(2,1)S(1)}, bf16[2,1024,12,64]{1,3,2,0:T(8,128)(2,1)}) fusion(f32[2,12,256,1024]{3,2,1,0:T(8,128)} %get-tuple-element.73, f32[2,12,256]{2,1,0:T(8,128)S(1)} %get-tuple-element.72, bf16[2,256,12,64]{1,0,3,2:T(2,128)(2,1)S(1)} %reshape.508), kind=kOutput, calls=%fused_computation.179 | convolution fusion | flops 821034240 | bytes 29124096 | tf_op jit(solution)/shard_map/shqk,sqhd->skhd/dot_general | solution.py:227
  285.2 16.6 %multiply_reduce_fusion = (f32[2,12,256]{2,1,0:T(8,128)S(1)}, f32[2,12,256,1024]{3,2,1,0:T(8,128)}) fusion(f32[2,12,256,1024]{3,2,1,0:T(8,128)} %get-tuple-element.73, f32[2,12,256]{2,1,0:T(8,128)S(1)} %get-tuple-element.72, bf16[2,12,1024,64]{2,3,0,1:T(8,128)(2,1)} %fusion.22, bf16[2,256,12,64]{1,0,3,2:T(2,128)(2,1)S(1)} %reshape.508), kind=kOutput, calls=%fused_computation.2 | convolution fusion | flops 824174592 | bytes 54312960 | tf_op jit(solution)/shard_map/sqhd,shkd->shqk/dot_general | solution.py:219
  301.7 21.6 %multiply_convert_fusion = bf16[2,12,256,1024]{3,2,1,0:T(8,128)(2,1)} fusion(f32[2,12,256,1024]{3,2,1,0:T(8,128)} %get-tuple-element.78, f32[2,12,256]{2,1,0:T(8,128)S(1)} %get-tuple-element.77, f32[2,12,256,1024]{3,2,1,0:T(8,128)} %get-tuple-element.73, f32[2,12,256]{2,1,0:T(8,128)S(1)} %get-tuple-element.72), kind=kLoop, calls=%fused_computation.1 | loop fusion | flops 25165824 | bytes 62963712 | tf_op jit(solution)/shard_map/convert_element_type | solution.py:221
  323.3 9.5 %fusion.136 = (bf16[12,64]{1,0:T(8,128)(2,1)S(1)}, bf16[2,256,12,64]{1,3,2,0:T(8,128)(2,1)}) fusion(bf16[2,12,256,1024]{3,2,1,0:T(8,128)(2,1)} %multiply_convert_fusion, bf16[2,12,1024,64]{2,3,0,1:T(8,128)(2,1)S(1)} %copy-done.17), kind=kOutput, calls=%fused_computation.180 | convolution fusion | flops 806485248 | bytes 16516608 | tf_op jit(solution)/shard_map/shqk,shkd->sqhd/dot_general | solution.py:222
  332.9 7.0 %fusion.24 = bf16[2,1024,12,64]{1,3,2,0:T(8,128)(2,1)S(1)} fusion(bf16[2,12,256,1024]{3,2,1,0:T(8,128)(2,1)} %multiply_convert_fusion, bf16[2,12,256,64]{2,3,0,1:T(8,128)(2,1)S(1)} %copy-done.31), kind=kOutput, calls=%fused_computation.46 | convolution fusion | flops 808452096 | bytes 16515072 | tf_op jit(solution)/shard_map/shqk,shqd->skhd/dot_general | solution.py:225
  352.1 8.0 %multiply_reduce_fusion.1 = (f32[768]{0:T(1024)S(1)}, f32[768]{0:T(1024)S(1)}, bf16[2048,768]{1,0:T(8,128)(2,1)}, f32[2048,768]{1,0:T(8,128)}) fusion(f32[2048]{0:T(1024)S(1)} %copy-done.41, f32[2048]{0:T(1024)S(1)} %copy-done.42, bf16[2,256,768]{2,1,0:T(8,128)(2,1)S(1)} %copy-done.11, bf16[2,256,768]{2,1,0:T(8,128)(2,1)S(1)} %copy-done.5, ...), kind=kOutput, calls=%fused_computation.25 | convolution fusion | flops 2442656256 | bytes 23228416 | tf_op jit(solution)/shard_map/dot_general | solution.py:40
  360.2 5.2 copy.97
  365.4 6.7 %fusion.67 = bf16[32,24,768]{2,1,0:T(8,128)(2,1)} fusion(bf16[32,24,2048]{2,1,0:T(8,128)(2,1)} %bitcast.233, bf16[2048,768]{0,1:T(8,128)(2,1)} %bitcast.229), kind=kOutput, calls=%fused_computation.93 | convolution fusion | flops 2416508928 | bytes 7471104 | tf_op jit(solution)/shard_map/dot_general | solution.py:34
  391.2 4.9 copy.94
  396.2 7.8 %convolution_convert_fusion = bf16[768,3072]{1,0:T(8,128)(2,1)} fusion(bf16[512,3072]{1,0:T(8,128)(2,1)} %copy-done.46, f32[512,768]{1,0:T(8,128)} %copy-done.13, f32[768]{0:T(1024)S(1)} %copy-done.44, f32[768]{0:T(1024)S(1)} %reshape.538, f32[512]{0:T(512)S(1)} %add_rsqrt_fusion.1, f32[512]{0:T(512)S(1)} %broadcast_multiply_fusion.4), kind=kOutput, calls=%fused_computation.40 | convolution fusion | flops 2420244480 | bytes 9447424 | tf_op jit(solution)/shard_map/dot_general | solution.py:34
  404.0 8.5 %convert_element_type.345 = bf16[32,96,768]{2,1,0:T(8,128)(2,1)} reshape(bf16[768,3072]{1,0:T(8,128)(2,1)} %convolution_convert_fusion) | data formatting | bytes 9437184 | tf_op jit(solution)/shard_map/convert_element_type | solution.py:101
  418.0 5.2 pad_maximum_fusion
  423.3 14.8 %reduce-scatter.6.cloned.1.call-done = bf16[1,4,80,768]{3,2,1,0:T(8,128)(2,1)} async-done(((bf16[8,4,80,768]{3,2,1,0:T(8,128)(2,1)}), bf16[1,4,80,768]{3,2,1,0:T(8,128)(2,1)}) %reduce-scatter.6.cloned.1.call-update) | async-done | bytes 491536 | tf_op jit(solution)/shard_map/reduce_scatter | solution.py:106
  438.1 88.0 %reduce-scatter.4.cloned.1.call-done = bf16[1,4,224,768]{3,2,1,0:T(8,128)(2,1)} async-done(((bf16[8,4,224,768]{3,2,1,0:T(8,128)(2,1)}), bf16[1,4,224,768]{3,2,1,0:T(8,128)(2,1)}) %reduce-scatter.4.cloned.1.call-update) | async-done | bytes 1376272 | tf_op jit(solution)/shard_map/reduce_scatter | solution.py:106
  537.6 7.3 %add_convert_fusion.4 = bf16[512,768]{1,0:T(8,128)(2,1)} fusion(f32[512,768]{1,0:T(8,128)S(1)} %copy-done.14, bf16[3072,768]{1,0:T(8,128)(2,1)} %bitcast.219, f32[512,3072]{1,0:T(8,128)} %copy-done.45, f32[3072]{0:T(1024)S(1)} %copy-done.40, f32[768]{0:T(1024)S(1)} %reshape.541), kind=kOutput, calls=%fused_computation.88 | convolution fusion | flops 2426535936 | bytes 13384704 | tf_op jit(solution)/shard_map/dot_general | solution.py:30
  545.0 43.0 %collective-permute-done.3 = bf16[2,256,768]{2,1,0:T(8,128)(2,1)S(1)} collective-permute-done((bf16[2,256,768]{2,1,0:T(8,128)(2,1)S(1)}, bf16[2,256,768]{2,1,0:T(8,128)(2,1)S(1)}, u32[]{:S(2)}, u32[]{:S(2)}) %collective-permute-start.3) | collective-permute-done | bytes 786464 | tf_op jit(solution)/shard_map/ppermute | solution.py:243
  588.0 14.3 %collective-permute-done.5 = bf16[2,256,768]{2,1,0:T(8,128)(2,1)S(1)} collective-permute-done((bf16[2,256,768]{2,1,0:T(8,128)(2,1)S(1)}, bf16[2,256,768]{2,1,0:T(8,128)(2,1)S(1)}, u32[]{:S(2)}, u32[]{:S(2)}) %collective-permute-start.5) | collective-permute-done | bytes 786464 | tf_op jit(solution)/shard_map/ppermute | solution.py:243
  602.3 31.5 %collective-permute-done.4 = bf16[2,256,768]{2,1,0:T(8,128)(2,1)S(1)} collective-permute-done((bf16[2,256,768]{2,1,0:T(8,128)(2,1)S(1)}, bf16[2,256,768]{2,1,0:T(8,128)(2,1)S(1)}, u32[]{:S(2)}, u32[]{:S(2)}) %collective-permute-start.4) | collective-permute-done | bytes 786464 | tf_op jit(solution)/shard_map/ppermute | solution.py:243
  (228 shorter events, 97.5 us)
Async XLA Ops:
  7.2 86.0 %copy-start.2 = (bf16[2,256,768]{2,1,0:T(8,128)(2,1)S(1)}, bf16[2,256,768]{2,1,0:T(8,128)(2,1)}, u32[]{:S(2)}) copy-start(bf16[2,256,768]{2,1,0:T(8,128)(2,1)} %param.18) | copy-start | bytes 2359300
  7.2 162.8 %all-gather.3.cloned.1.call-start = ((), (), s32[]{:S(2)}) async-start(), calls=%async_computation.6 | async-start | bytes 15409152 | tf_op jit(solution)/shard_map/all_gather | solution.py:72
  19.3 418.8 %reduce-scatter.6.cloned.1.call-start = ((), (), s32[]{:S(2)}) async-start(), calls=%async_computation.4 | async-start | bytes 4423680 | tf_op jit(solution)/shard_map/reduce_scatter | solution.py:106
  19.4 73.0 %collective-permute-start.1 = (bf16[2,256,768]{2,1,0:T(8,128)(2,1)}, bf16[2,256,768]{2,1,0:T(8,128)(2,1)S(1)}, u32[]{:S(2)}, u32[]{:S(2)}) collective-permute-start(bf16[2,256,768]{2,1,0:T(8,128)(2,1)} %param.18), channel_id=1, source_target_pairs={{0,2},{1,3},{2,0},{3,1},{4,6},{5,7},{6,4},{7,5},{8,10},{9,11},{10,... | collective-permute-start | bytes 2359304 | tf_op jit(solution)/shard_map/ppermute | solution.py:152
  23.5 68.8 %collective-permute-start = (bf16[2,256,768]{2,1,0:T(8,128)(2,1)}, bf16[2,256,768]{2,1,0:T(8,128)(2,1)S(1)}, u32[]{:S(2)}, u32[]{:S(2)}) collective-permute-start(bf16[2,256,768]{2,1,0:T(8,128)(2,1)} %param.18), channel_id=1, source_target_pairs={{0,1},{1,2},{2,3},{3,0},{4,5},{5,6},{6,7},{7,4},{8,9},{9,10},{10,1... | collective-permute-start | bytes 2359304 | tf_op jit(solution)/shard_map/ppermute | solution.py:152
  25.1 68.1 %collective-permute-start.2 = (bf16[2,256,768]{2,1,0:T(8,128)(2,1)}, bf16[2,256,768]{2,1,0:T(8,128)(2,1)S(1)}, u32[]{:S(2)}, u32[]{:S(2)}) collective-permute-start(bf16[2,256,768]{2,1,0:T(8,128)(2,1)} %param.18), channel_id=1, source_target_pairs={{0,3},{1,0},{2,1},{3,2},{4,7},{5,4},{6,5},{7,6},{8,11},{9,8},{10,9... | collective-permute-start | bytes 2359304 | tf_op jit(solution)/shard_map/ppermute | solution.py:152
  92.3 114.2 %copy-start.4 = (bf16[2,256,768]{2,1,0:T(8,128)(2,1)}, bf16[2,256,768]{2,1,0:T(8,128)(2,1)S(1)}, u32[]{:S(2)}) copy-start(bf16[2,256,768]{2,1,0:T(8,128)(2,1)S(1)} %collective-permute-done.1) | copy-start | bytes 2359300
  176.2 22.4 %copy-start = (bf16[32,24,768]{2,1,0:T(8,128)(2,1)}, bf16[32,24,768]{2,1,0:T(8,128)(2,1)S(1)}, u32[]{:S(2)}) copy-start(bf16[32,24,768]{2,1,0:T(8,128)(2,1)S(1)} %get-tuple-element.37) | copy-start | bytes 3538948
  184.7 79.0 %copy-start.39 = (f32[3072]{0:T(1024)}, f32[3072]{0:T(1024)S(1)}, u32[]{:S(2)}) copy-start(f32[3072]{0:T(1024)S(1)} %reshape.540) | copy-start | bytes 36868
  184.8 21.7 %copy-start.34 = (f32[768]{0:T(1024)}, f32[768]{0:T(1024)S(1)}, u32[]{:S(2)}) copy-start(f32[768]{0:T(1024)S(1)} %reshape.533) | copy-start | bytes 9220
  185.0 72.0 %copy-start.43 = (f32[768]{0:T(1024)}, f32[768]{0:T(1024)S(1)}, u32[]{:S(2)}) copy-start(f32[768]{0:T(1024)S(1)} %reshape.539) | copy-start | bytes 9220
  185.1 21.5 %copy-start.37 = (f32[768]{0:T(1024)}, f32[768]{0:T(1024)S(1)}, u32[]{:S(2)}) copy-start(f32[768]{0:T(1024)S(1)} %reshape.534) | copy-start | bytes 9220
  212.4 6.6 %copy-start.26 = (bf16[768,12,64]{2,1,0:T(8,128)(2,1)S(1)}, bf16[768,12,64]{2,1,0:T(8,128)(2,1)}, u32[]{:S(2)}) copy-start(bf16[768,12,64]{2,1,0:T(8,128)(2,1)} %reshape_reshape.10) | copy-start | bytes 3538948
  220.4 7.8 %copy-start.30 = (bf16[2,12,256,64]{2,3,0,1:T(8,128)(2,1)}, bf16[2,12,256,64]{2,3,0,1:T(8,128)(2,1)S(1)}, u32[]{:S(2)}) copy-start(bf16[2,12,256,64]{2,3,0,1:T(8,128)(2,1)S(1)} %fusion.84) | copy-start | bytes 2359300
  255.7 8.1 %slice-start.4 = ((s8[4718592]{0:T(1024)(128)(4,1)}), s8[4194304]{0:T(1024)(128)(4,1)S(1)}, s32[]{:S(2)}) async-start(s8[4718592]{0:T(1024)(128)(4,1)} %bitcast.220), calls=%async_computation.11 | async-start | bytes 8388608
  256.6 15.1 %copy-start.13 = (f32[512,768]{1,0:T(8,128)}, f32[512,768]{1,0:T(8,128)S(1)}, u32[]{:S(2)}) copy-start(f32[512,768]{1,0:T(8,128)S(1)} %get-tuple-element.75) | copy-start | bytes 4718596
  257.0 6.8 %slice-start.5 = ((s8[4718592]{0:T(1024)(128)(4,1)}), s8[524288]{0:T(1024)(128)(4,1)S(1)}, s32[]{:S(2)}) async-start(s8[4718592]{0:T(1024)(128)(4,1)} %bitcast.220), calls=%async_computation.12 | async-start | bytes 1048576
  257.0 6.8 %copy-start.28 = (bf16[2,256,768]{2,1,0:T(8,128)(2,1)S(1)}, bf16[2,256,768]{2,1,0:T(8,128)(2,1)}, u32[]{:S(2)}) copy-start(bf16[2,256,768]{2,1,0:T(8,128)(2,1)} %param.35) | copy-start | bytes 2359300
  257.0 11.7 %slice-start.2 = ((s8[4718592]{0:T(1024)(128)(4,1)}), s8[4194304]{0:T(1024)(128)(4,1)S(1)}, s32[]{:S(2)}) async-start(s8[4718592]{0:T(1024)(128)(4,1)} %bitcast.217), calls=%async_computation.9 | async-start | bytes 8388608
  301.7 21.6 %copy-start.17 = (bf16[2,12,1024,64]{2,3,0,1:T(8,128)(2,1)S(1)}, bf16[2,12,1024,64]{2,3,0,1:T(8,128)(2,1)}, u32[]{:S(2)}) copy-start(bf16[2,12,1024,64]{2,3,0,1:T(8,128)(2,1)} %convert_bitcast_fusion.1) | copy-start | bytes 9437188
  323.3 9.5 %copy-start.31 = (bf16[2,12,256,64]{2,3,0,1:T(8,128)(2,1)S(1)}, bf16[2,12,256,64]{2,3,0,1:T(8,128)(2,1)}, u32[]{:S(2)}) copy-start(bf16[2,12,256,64]{2,3,0,1:T(8,128)(2,1)} %copy-done.30) | copy-start | bytes 2359300
  332.9 7.0 %copy-start.23 = (bf16[2,1024,12,64]{1,3,2,0:T(8,128)(2,1)S(1)}, bf16[2,1024,12,64]{1,3,2,0:T(8,128)(2,1)}, u32[]{:S(2)}) copy-start(bf16[2,1024,12,64]{1,3,2,0:T(8,128)(2,1)} %get-tuple-element.80) | copy-start | bytes 9437188
  344.2 7.6 %copy-start.20 = (bf16[96,8,2,1024]{3,1,2,0:T(8,128)(2,1)}, bf16[96,8,2,1024]{3,1,2,0:T(8,128)(2,1)S(1)}, u32[]{:S(2)}) copy-start(bf16[96,8,2,1024]{3,1,2,0:T(8,128)(2,1)S(1)} %copy.119) | copy-start | bytes 9437188
  365.4 6.7 %copy-start.22 = (bf16[96,8,2,1024]{3,1,2,0:T(8,128)(2,1)S(1)}, bf16[96,8,2,1024]{3,1,2,0:T(8,128)(2,1)}, u32[]{:S(2)}) copy-start(bf16[96,8,2,1024]{3,1,2,0:T(8,128)(2,1)} %copy-done.21) | copy-start | bytes 9437188
  365.4 6.7 %copy-start.24 = (bf16[768,2048]{1,0:T(8,128)(2,1)S(1)}, bf16[768,2048]{1,0:T(8,128)(2,1)}, u32[]{:S(2)}) copy-start(bf16[768,2048]{1,0:T(8,128)(2,1)} %copy.97) | copy-start | bytes 9437188
  389.8 136.4 %reduce-scatter.4.cloned.1.call-start = ((), (), s32[]{:S(2)}) async-start(), calls=%async_computation.3 | async-start | bytes 12386304 | tf_op jit(solution)/shard_map/reduce_scatter | solution.py:106
  423.2 106.5 %copy-start.36 = (f32[32,24]{1,0:T(8,128)S(1)}, f32[32,24]{1,0:T(8,128)}, u32[]{:S(2)}) copy-start(f32[32,24]{1,0:T(8,128)} %get-tuple-element.51) | copy-start | bytes 9220
  423.2 214.1 %reduce-scatter.8.cloned.1.call-start = ((), (), s32[]{:S(2)}) async-start(), calls=%async_computation.5 | async-start | bytes 2334720 | tf_op jit(solution)/shard_map/reduce_scatter | solution.py:111
  533.1 54.9 %collective-permute-start.3 = (bf16[2,256,768]{2,1,0:T(8,128)(2,1)S(1)}, bf16[2,256,768]{2,1,0:T(8,128)(2,1)S(1)}, u32[]{:S(2)}, u32[]{:S(2)}) collective-permute-start(bf16[2,256,768]{2,1,0:T(8,128)(2,1)S(1)} %get-tuple-element.42), channel_id=1, source_target_pairs={{0,3},{1,0},{2,1},{3,2},{4,7},{5,4},{6,5},{7,6},{8,11},{9,8},{10,9... | collective-permute-start | bytes 2359304 | tf_op jit(solution)/shard_map/ppermute | solution.py:243
  536.5 65.8 %collective-permute-start.5 = (bf16[2,256,768]{2,1,0:T(8,128)(2,1)S(1)}, bf16[2,256,768]{2,1,0:T(8,128)(2,1)S(1)}, u32[]{:S(2)}, u32[]{:S(2)}) collective-permute-start(bf16[2,256,768]{2,1,0:T(8,128)(2,1)S(1)} %get-tuple-element.43), channel_id=1, source_target_pairs={{0,1},{1,2},{2,3},{3,0},{4,5},{5,6},{6,7},{7,4},{8,9},{9,10},{10,1... | collective-permute-start | bytes 2359304 | tf_op jit(solution)/shard_map/ppermute | solution.py:243
  536.5 97.3 %copy-start.12 = (f32[512,768]{1,0:T(8,128)S(1)}, f32[512,768]{1,0:T(8,128)}, u32[]{:S(2)}) copy-start(f32[512,768]{1,0:T(8,128)} %get-tuple-element.84) | copy-start | bytes 4718596
  536.5 97.3 %collective-permute-start.4 = (bf16[2,256,768]{2,1,0:T(8,128)(2,1)S(1)}, bf16[2,256,768]{2,1,0:T(8,128)(2,1)S(1)}, u32[]{:S(2)}, u32[]{:S(2)}) collective-permute-start(bf16[2,256,768]{2,1,0:T(8,128)(2,1)S(1)} %get-tuple-element.44), channel_id=1, source_target_pairs={{0,2},{1,3},{2,0},{3,1},{4,6},{5,7},{6,4},{7,5},{8,10},{9,11},{10,... | collective-permute-start | bytes 2359304 | tf_op jit(solution)/shard_map/ppermute | solution.py:243
  (31 other events, 101.9 us)
Sparse Core Ops, SparseCore 0:
  19.4 150.5 all-gather.2
  389.9 48.1 reduce-scatter.5
  441.7 84.4 reduce-scatter.3
  529.2 75.0 reduce-scatter.7

commit v10 on v9

--- a/solution.py
+++ b/solution.py
@@ -50,39 +50,40 @@
     return -(-value // step) * step
 
 
-MATS = (2, 4, 5, 7, 11, 13)
-VECS = (0, 1, 3, 6, 8, 9, 10, 12, 14)
-
-
-def layout(shards, width, sub):
-    rows = [shards[i].size // width for i in MATS]
-    vec_len = sum(shards[i].size for i in VECS)
+def layout(shards, group, width, sub):
+    mats = [i for i in group if shards[i].ndim == 2]
+    vecs = [i for i in group if shards[i].ndim == 1]
+    rows = [shards[i].size // width for i in mats]
+    vec_len = sum(shards[i].size for i in vecs)
     vec_rows = round_up(vec_len, width) // width
     total = round_up(sum(rows) + vec_rows, sub)
-    return rows, vec_len, vec_rows, total
-
-
-def gather_all(shards, width, groups):
-    rows, vec_len, vec_rows, total = layout(shards, width, 16)
-    vec = jnp.concatenate([shards[i].reshape(-1) for i in VECS])
-    vec = jnp.pad(vec, (0, vec_rows * width - vec_len)).reshape(vec_rows, width)
-    blocks = [shards[i].reshape(-1, width) for i in MATS] + [vec]
+    return mats, vecs, rows, vec_len, vec_rows, total
+
+
+def gather_all(shards, group, width, groups):
+    mats, vecs, rows, vec_len, vec_rows, total = layout(shards, group, width, 16)
+    spare = total - sum(rows) - vec_rows
+    vec = jnp.concatenate([shards[i].reshape(-1) for i in vecs])
+    vec = jnp.pad(vec, (0, (vec_rows + spare) * width - vec_len)).reshape(vec_rows + spare, width)
+    blocks = [shards[i].reshape(-1, width) for i in mats] + [vec]
     packed = jnp.concatenate(blocks, axis=0)
-    packed = jnp.pad(packed, ((0, total - packed.shape[0]), (0, 0)))
     full = lax.all_gather(packed[None], ALL, axis=0, tiled=True)
-    out = [None] * 15
+    out = {}
     off = 0
-    for i, r in zip(MATS, rows):
+    for i, r in zip(mats, rows):
         s = shards[i]
         out[i] = full[:, off:off + r, :].reshape((groups * s.shape[0],) + s.shape[1:])
         off += r
-    vecs = full[:, off:off + vec_rows, :].reshape(groups, vec_rows * width)
+    flat = full[:, off:off + vec_rows, :].reshape(groups, vec_rows * width)
     voff = 0
-    for i in VECS:
+    for i in vecs:
         size = shards[i].size
-        out[i] = vecs[:, voff:voff + size].reshape(groups * size)
+        out[i] = flat[:, voff:voff + size].reshape(groups * size)
         voff += size
-    return out
+    return [out[i] for i in group]
+
+
+LATE_W = (11, 12, 13, 14)
 
 
 def pack_group(grads, group, width, mesh_shape):
@@ -150,9 +151,11 @@
     blocks = [inputs]
     for b in range(1, n_ctx):
         blocks.append(lax.ppermute(inputs, "ctx", [(i, (i + b) % n_ctx) for i in range(n_ctx)]))
-    (ln1_gain, ln1_bias, wq, bq, wk, wv, bv, wo, bo, ln2_gain, ln2_bias, wi, bi, wf, bf) = gather_all(
-        shards, width, groups
-    )
+    first = (0, 1, 2, 3, 4, 5, 6, 7, 8, 9, 10)
+    ln1_gain, ln1_bias, wq, bq, wk, wv, bv, wo, bo, ln2_gain, ln2_bias = gather_all(
+        shards, first, width, groups
+    )
+    wi, bi, wf, bf = gather_all(shards, LATE_W, width, groups)
     me = lax.axis_index("ctx")
     total = n_ctx * rows
     source = (me - jnp.arange(n_ctx)) % n_ctx

time: 661 us -> 636 us (0.962)
  waiting for transfers between devices: 331 us -> 294 us
  matrix products: 148 us -> 156 us
    all_gather x1 -> x2, waiting for transfers between devices: 73.8 us -> 50.9 us  [gather_all(): full = lax.all_gather(packed[None], ALL, axis=0, tiled=True)]
    ppermute x3, waiting for transfers between devices: 65 us -> 51.5 us  [layer(): lax.ppermute(inputs, 'ctx', [(i, (i + b) % n_ctx) for i in range(n_ctx)])]
  transfers between devices with their start and end apart: 10 -> 11, of which waited for: 8 -> 9; matrix products, arithmetic and copies ran while one was open for 8% -> 21% of each run, Pallas kernels for 0% -> 0%
where the time goes in v10:
time: 636 us; the launch traced here: 626 us
  waiting for transfers between devices  294 us (46%)
  matrix products  156 us (25%)
  local copies, waits for them, and re-layouts  92.8 us (15%)
  other arithmetic  54.4 us (9%)
  between operations  15.1 us (2%)
  starting transfers between devices  12.7 us (2%)
    reduce_scatter x2, waiting for transfers between devices, dp_stage(): return lax.psum_scatter(packed, 'dp', scatter_dimension=0, tiled=True)  103 us
    ppermute x3, waiting for transfers between devices, layer(): lax.ppermute(sent, 'ctx', [(i, (i - b) % n_ctx) for i in range(n_ctx)])  88.8 us
    ppermute x3, waiting for transfers between devices, layer(): lax.ppermute(inputs, 'ctx', [(i, (i + b) % n_ctx) for i in range(n_ctx)])  51.5 us
    all_gather x2, waiting for transfers between devices, gather_all(): full = lax.all_gather(packed[None], ALL, axis=0, tiled=True)  50.9 us
    dot_general x6, matrix products, back(): lax.dot_general(grad_rows, weight, (((1,), (1,)), ((), ())), preferred_el...  26.6 us
    dot_general x6, matrix products, outer(): lax.dot_general(left_rows, right_rows, (((0,), (0,)), ((), ())), preferre...  26 us
    convert_element_type x1, other arithmetic, layer(): d_scores = (probs * (d_probs - inner)).astype(jnp.bfloat16)  21.6 us
    dot_general x3, matrix products, layer(): jnp.einsum('snd,dhe->shne', a, heads(w), preferred_element_type=jnp.float32)  17.7 us
  transfers between devices with their start and end apart: 11, of which 9 were waited for; matrix products, arithmetic and copies ran while one was open for 21% of the time, Pallas kernels for 0%

profile of v10, /device:TPU:0, one launch (start us, length us, event | category | flops | bytes accessed | tf_op | source)
XLA Modules:
  0.0 625.5 jit_solution(10901140383783209505)
XLA Ops:
  7.2 4.8 concatenate.37
  28.9 50.8 %collective-permute-done.1 = bf16[2,256,768]{2,1,0:T(8,128)(2,1)S(1)} collective-permute-done((bf16[2,256,768]{2,1,0:T(8,128)(2,1)}, bf16[2,256,768]{2,1,0:T(8,128)(2,1)S(1)}, u32[]{:S(2)}, u32[]{:S(2)}) %collective-permute-start.1) | collective-permute-done | bytes 786464 | tf_op jit(solution)/shard_map/ppermute | solution.py:153
  84.7 38.8 %all-gather.5.cloned.1.call-done = bf16[3584,768]{1,0:T(8,128)(2,1)} async-done(((bf16[112,768]{1,0:T(8,128)(2,1)}), bf16[3584,768]{1,0:T(8,128)(2,1)}) %all-gather.5.cloned.1.call-update) | async-done | bytes 5505040 | tf_op jit(solution)/shard_map/all_gather | solution.py:70
  132.5 4.9 reshape_reshape.11
  140.6 4.8 reshape_reshape.9
  154.6 6.5 %convert_bitcast_fusion.1 = bf16[2,12,1024,64]{2,3,0,1:T(8,128)(2,1)} fusion(bf16[2,1024,768]{2,1,0:T(8,128)(2,1)S(1)} %copy-done.16, bf16[768,12,64,1]{2,1,0,3:T(8,128)(2,1)S(1)} %bitcast.244), kind=kOutput, calls=%fused_computation.58 | convolution fusion | flops 2417491968 | bytes 7471104 | tf_op jit(solution)/shard_map/snd,dhe->shne/dot_general | solution.py:174
  161.1 7.3 %fusion.22 = bf16[2,12,1024,64]{2,3,0,1:T(8,128)(2,1)} fusion(f32[12,64]{1,0:T(8,128)S(1)} %copy-done.47, bf16[2,1024,768]{2,1,0:T(8,128)(2,1)S(1)} %copy-done.16, bf16[768,12,64,1]{2,1,0,3:T(8,128)(2,1)S(1)} %bitcast.243), kind=kOutput, calls=%fused_computation.44 | convolution fusion | flops 2419064832 | bytes 7474176 | tf_op jit(solution)/shard_map/snd,dhe->shne/dot_general | solution.py:174
  168.4 15.2 %fusion.128 = (f32[2,12,256]{2,1,0:T(8,128)S(1)}, f32[2,12,256,1024]{3,2,1,0:T(8,128)}) fusion(pred[2,1024]{1,0:T(4,128)(4,1)S(1)} %copy-done.55, bf16[2,12,1024,64]{2,3,0,1:T(8,128)(2,1)} %convert_bitcast_fusion.1, bf16[2,12,256,64]{2,3,0,1:T(8,128)(2,1)S(1)} %fusion.84), kind=kOutput, calls=%fused_computation.181 | convolution fusion | flops 830473216 | bytes 29124608 | tf_op jit(solution)/shard_map/sub | solution.py:185
  183.7 11.6 %fusion.79 = bf16[2,256,12,64]{1,3,2,0:T(8,128)(2,1)S(1)} fusion(bf16[2,12,1024,64]{2,3,0,1:T(8,128)(2,1)} %fusion.22, f32[2,12,256,1024]{3,2,1,0:T(8,128)} %get-tuple-element.72, f32[2,12,256]{2,1,0:T(8,128)S(1)} %get-tuple-element.71), kind=kOutput, calls=%fused_computation.100 | convolution fusion | flops 818282496 | bytes 29122560 | tf_op jit(solution)/shard_map/shqk,shkd->sqhd/dot_general | solution.py:188
  197.9 12.1 %all-gather.7.cloned.1.call-done = bf16[6656,768]{1,0:T(8,128)(2,1)} async-done(((bf16[208,768]{1,0:T(8,128)(2,1)}), bf16[6656,768]{1,0:T(8,128)(2,1)}) %all-gather.7.cloned.1.call-update) | async-done | bytes 10223632 | tf_op jit(solution)/shard_map/all_gather | solution.py:70
  211.0 8.0 %fusion.122 = (bf16[32,96,768]{2,1,0:T(8,128)(2,1)}, bf16[32,96,768]{2,1,0:T(8,128)(2,1)}) fusion(bf16[32,208,768]{2,1,0:T(8,128)(2,1)} %bitcast.215), kind=kLoop, calls=%fused_computation.175 | loop fusion | bytes 18874368 | tf_op jit(solution)/shard_map/slice | solution.py:75
  219.0 8.5 %reshape.511 = bf16[768,3072]{1,0:T(8,128)(2,1)} reshape(bf16[32,96,768]{2,1,0:T(8,128)(2,1)} %get-tuple-element.33) | data formatting | bytes 9437184 | tf_op jit(solution)/shard_map/reshape | solution.py:75
  227.7 6.4 %fusion.19 = (bf16[3072,512]{0,1:T(8,128)(2,1)}, f32[512,3072]{1,0:T(8,128)S(1)}) fusion(f32[3072]{0:T(1024)S(1)} %reshape.548, bf16[768,3072]{1,0:T(8,128)(2,1)} %reshape.511, f32[512,768]{1,0:T(8,128)S(1)} %get-tuple-element.74, f32[768]{0:T(1024)S(1)} %copy-done.52, f32[768]{0:T(1024)S(1)} %copy-done.44, f32[512]{0:T(512)S(1)} %add_rsqrt_fusion.1, ...), kind=kOutput, calls=%fused_computation.37 | convolution fusion | flops 2427322368 | bytes 15751168 | tf_op jit(solution)/shard_map/dot_general | solution.py:30
  234.2 5.6 fusion.140
  246.8 11.4 %fusion.138 = (bf16[12,64]{1,0:T(8,128)(2,1)S(1)}, bf16[2,1024,12,64]{1,3,2,0:T(8,128)(2,1)}) fusion(f32[2,12,256,1024]{3,2,1,0:T(8,128)} %get-tuple-element.72, f32[2,12,256]{2,1,0:T(8,128)S(1)} %copy-done.40, bf16[2,256,12,64]{1,0,3,2:T(2,128)(2,1)S(1)} %reshape.516), kind=kOutput, calls=%fused_computation.183 | convolution fusion | flops 821034240 | bytes 29124096 | tf_op jit(solution)/shard_map/shqk,sqhd->skhd/dot_general | solution.py:230
  258.3 16.6 %multiply_reduce_fusion = (f32[2,12,256]{2,1,0:T(8,128)S(1)}, f32[2,12,256,1024]{3,2,1,0:T(8,128)}) fusion(f32[2,12,256,1024]{3,2,1,0:T(8,128)} %get-tuple-element.72, f32[2,12,256]{2,1,0:T(8,128)S(1)} %copy-done.40, bf16[2,12,1024,64]{2,3,0,1:T(8,128)(2,1)} %fusion.22, bf16[2,256,12,64]{1,0,3,2:T(2,128)(2,1)S(1)} %reshape.516), kind=kOutput, calls=%fused_computation.2 | convolution fusion | flops 824174592 | bytes 54312960 | tf_op jit(solution)/shard_map/sqhd,shkd->shqk/dot_general | solution.py:222
  274.9 21.6 %multiply_convert_fusion = bf16[2,12,256,1024]{3,2,1,0:T(8,128)(2,1)} fusion(f32[2,12,256,1024]{3,2,1,0:T(8,128)} %get-tuple-element.77, f32[2,12,256]{2,1,0:T(8,128)S(1)} %get-tuple-element.76, f32[2,12,256,1024]{3,2,1,0:T(8,128)} %get-tuple-element.72, f32[2,12,256]{2,1,0:T(8,128)S(1)} %copy-done.40), kind=kLoop, calls=%fused_computation.1 | loop fusion | flops 25165824 | bytes 62963712 | tf_op jit(solution)/shard_map/convert_element_type | solution.py:224
  296.5 9.5 %fusion.139 = (bf16[12,64]{1,0:T(8,128)(2,1)S(1)}, bf16[2,256,12,64]{1,3,2,0:T(8,128)(2,1)}) fusion(bf16[2,12,256,1024]{3,2,1,0:T(8,128)(2,1)} %multiply_convert_fusion, bf16[2,12,1024,64]{2,3,0,1:T(8,128)(2,1)S(1)} %copy-done.19), kind=kOutput, calls=%fused_computation.184 | convolution fusion | flops 806485248 | bytes 16516608 | tf_op jit(solution)/shard_map/shqk,shkd->sqhd/dot_general | solution.py:225
  306.0 7.0 %fusion.24 = bf16[2,1024,12,64]{1,3,2,0:T(8,128)(2,1)S(1)} fusion(bf16[2,12,256,1024]{3,2,1,0:T(8,128)(2,1)} %multiply_convert_fusion, bf16[2,12,256,64]{2,3,0,1:T(8,128)(2,1)S(1)} %copy-done.32), kind=kOutput, calls=%fused_computation.46 | convolution fusion | flops 808452096 | bytes 16515072 | tf_op jit(solution)/shard_map/shqk,shqd->skhd/dot_general | solution.py:228
  326.9 10.1 %multiply_reduce_fusion.1 = (f32[768]{0:T(1024)S(1)}, f32[768]{0:T(1024)S(1)}, bf16[2048,768]{1,0:T(8,128)(2,1)}, f32[2048,768]{1,0:T(8,128)}) fusion(f32[2048]{0:T(1024)S(1)} %copy-done.49, f32[2048]{0:T(1024)S(1)} %copy-done.50, bf16[2,256,768]{2,1,0:T(8,128)(2,1)S(1)} %copy-done.11, bf16[2,256,768]{2,1,0:T(8,128)(2,1)S(1)} %copy-done.6, ...), kind=kOutput, calls=%fused_computation.25 | convolution fusion | flops 2442656256 | bytes 23228416 | tf_op jit(solution)/shard_map/dot_general | solution.py:40
  337.0 4.7 copy.97
  341.7 6.6 %fusion.67 = bf16[32,24,768]{2,1,0:T(8,128)(2,1)} fusion(bf16[32,24,2048]{2,1,0:T(8,128)(2,1)} %bitcast.238, bf16[2048,768]{0,1:T(8,128)(2,1)} %bitcast.234), kind=kOutput, calls=%fused_computation.93 | convolution fusion | flops 2416508928 | bytes 7471104 | tf_op jit(solution)/shard_map/dot_general | solution.py:34
  364.8 4.9 copy.94
  369.8 7.8 %convolution_convert_fusion = bf16[768,3072]{1,0:T(8,128)(2,1)} fusion(bf16[512,3072]{1,0:T(8,128)(2,1)} %copy-done.58, f32[512,768]{1,0:T(8,128)} %copy-done.13, f32[768]{0:T(1024)S(1)} %copy-done.53, f32[768]{0:T(1024)S(1)} %copy-done.44, f32[512]{0:T(512)S(1)} %add_rsqrt_fusion.1, f32[512]{0:T(512)S(1)} %broadcast_multiply_fusion.4), kind=kOutput, calls=%fused_computation.40 | convolution fusion | flops 2420244480 | bytes 9447424 | tf_op jit(solution)/shard_map/dot_general | solution.py:34
  377.6 8.5 %convert_element_type.345 = bf16[32,96,768]{2,1,0:T(8,128)(2,1)} reshape(bf16[768,3072]{1,0:T(8,128)(2,1)} %convolution_convert_fusion) | data formatting | bytes 9437184 | tf_op jit(solution)/shard_map/convert_element_type | solution.py:102
  391.7 5.2 pad_maximum_fusion
  396.9 14.9 %reduce-scatter.6.cloned.1.call-done = bf16[1,4,80,768]{3,2,1,0:T(8,128)(2,1)} async-done(((bf16[8,4,80,768]{3,2,1,0:T(8,128)(2,1)}), bf16[1,4,80,768]{3,2,1,0:T(8,128)(2,1)}) %reduce-scatter.6.cloned.1.call-update) | async-done | bytes 491536 | tf_op jit(solution)/shard_map/reduce_scatter | solution.py:107
  411.8 87.9 %reduce-scatter.4.cloned.1.call-done = bf16[1,4,224,768]{3,2,1,0:T(8,128)(2,1)} async-done(((bf16[8,4,224,768]{3,2,1,0:T(8,128)(2,1)}), bf16[1,4,224,768]{3,2,1,0:T(8,128)(2,1)}) %reduce-scatter.4.cloned.1.call-update) | async-done | bytes 1376272 | tf_op jit(solution)/shard_map/reduce_scatter | solution.py:107
  512.0 7.3 %add_convert_fusion.4 = bf16[512,768]{1,0:T(8,128)(2,1)} fusion(f32[512,768]{1,0:T(8,128)S(1)} %copy-done.14, bf16[3072,768]{1,0:T(8,128)(2,1)} %bitcast.222, f32[512,3072]{1,0:T(8,128)} %copy-done.57, f32[3072]{0:T(1024)S(1)} %copy-done.46, f32[768]{0:T(1024)S(1)} %reshape.549), kind=kOutput, calls=%fused_computation.88 | convolution fusion | flops 2426535936 | bytes 13384704 | tf_op jit(solution)/shard_map/dot_general | solution.py:30
  519.4 36.1 %collective-permute-done.3 = bf16[2,256,768]{2,1,0:T(8,128)(2,1)S(1)} collective-permute-done((bf16[2,256,768]{2,1,0:T(8,128)(2,1)S(1)}, bf16[2,256,768]{2,1,0:T(8,128)(2,1)S(1)}, u32[]{:S(2)}, u32[]{:S(2)}) %collective-permute-start.3) | collective-permute-done | bytes 786464 | tf_op jit(solution)/shard_map/ppermute | solution.py:246
  555.5 20.9 %collective-permute-done.5 = bf16[2,256,768]{2,1,0:T(8,128)(2,1)S(1)} collective-permute-done((bf16[2,256,768]{2,1,0:T(8,128)(2,1)S(1)}, bf16[2,256,768]{2,1,0:T(8,128)(2,1)S(1)}, u32[]{:S(2)}, u32[]{:S(2)}) %collective-permute-start.5) | collective-permute-done | bytes 786464 | tf_op jit(solution)/shard_map/ppermute | solution.py:246
  576.4 31.7 %collective-permute-done.4 = bf16[2,256,768]{2,1,0:T(8,128)(2,1)S(1)} collective-permute-done((bf16[2,256,768]{2,1,0:T(8,128)(2,1)S(1)}, bf16[2,256,768]{2,1,0:T(8,128)(2,1)S(1)}, u32[]{:S(2)}, u32[]{:S(2)}) %collective-permute-start.4) | collective-permute-done | bytes 786464 | tf_op jit(solution)/shard_map/ppermute | solution.py:246
  (259 shorter events, 112.0 us)
Async XLA Ops:
  7.2 75.0 %copy-start.3 = (bf16[2,256,768]{2,1,0:T(8,128)(2,1)S(1)}, bf16[2,256,768]{2,1,0:T(8,128)(2,1)}, u32[]{:S(2)}) copy-start(bf16[2,256,768]{2,1,0:T(8,128)(2,1)} %param.18) | copy-start | bytes 2359300
  7.2 116.3 %all-gather.5.cloned.1.call-start = ((), (), s32[]{:S(2)}) async-start(), calls=%async_computation.6 | async-start | bytes 5677056 | tf_op jit(solution)/shard_map/all_gather | solution.py:70
  15.9 194.0 %all-gather.7.cloned.1.call-start = ((), (), s32[]{:S(2)}) async-start(), calls=%async_computation.7 | async-start | bytes 10543104 | tf_op jit(solution)/shard_map/all_gather | solution.py:70
  19.5 392.4 %reduce-scatter.6.cloned.1.call-start = ((), (), s32[]{:S(2)}) async-start(), calls=%async_computation.4 | async-start | bytes 4423680 | tf_op jit(solution)/shard_map/reduce_scatter | solution.py:107
  19.5 60.2 %collective-permute-start.1 = (bf16[2,256,768]{2,1,0:T(8,128)(2,1)}, bf16[2,256,768]{2,1,0:T(8,128)(2,1)S(1)}, u32[]{:S(2)}, u32[]{:S(2)}) collective-permute-start(bf16[2,256,768]{2,1,0:T(8,128)(2,1)} %param.18), channel_id=1, source_target_pairs={{0,2},{1,3},{2,0},{3,1},{4,6},{5,7},{6,4},{7,5},{8,10},{9,11},{10,... | collective-permute-start | bytes 2359304 | tf_op jit(solution)/shard_map/ppermute | solution.py:153
  23.7 56.0 %collective-permute-start = (bf16[2,256,768]{2,1,0:T(8,128)(2,1)}, bf16[2,256,768]{2,1,0:T(8,128)(2,1)S(1)}, u32[]{:S(2)}, u32[]{:S(2)}) collective-permute-start(bf16[2,256,768]{2,1,0:T(8,128)(2,1)} %param.18), channel_id=1, source_target_pairs={{0,1},{1,2},{2,3},{3,0},{4,5},{5,6},{6,7},{7,4},{8,9},{9,10},{10,1... | collective-permute-start | bytes 2359304 | tf_op jit(solution)/shard_map/ppermute | solution.py:153
  25.2 55.2 %collective-permute-start.2 = (bf16[2,256,768]{2,1,0:T(8,128)(2,1)}, bf16[2,256,768]{2,1,0:T(8,128)(2,1)S(1)}, u32[]{:S(2)}, u32[]{:S(2)}) collective-permute-start(bf16[2,256,768]{2,1,0:T(8,128)(2,1)} %param.18), channel_id=1, source_target_pairs={{0,3},{1,0},{2,1},{3,2},{4,7},{5,4},{6,5},{7,6},{8,11},{9,8},{10,9... | collective-permute-start | bytes 2359304 | tf_op jit(solution)/shard_map/ppermute | solution.py:153
  79.7 65.7 %copy-start.5 = (bf16[2,256,768]{2,1,0:T(8,128)(2,1)}, bf16[2,256,768]{2,1,0:T(8,128)(2,1)S(1)}, u32[]{:S(2)}) copy-start(bf16[2,256,768]{2,1,0:T(8,128)(2,1)S(1)} %collective-permute-done.1) | copy-start | bytes 2359300
  79.7 65.7 %copy-start.7 = (bf16[2,256,768]{2,1,0:T(8,128)(2,1)}, bf16[2,256,768]{2,1,0:T(8,128)(2,1)S(1)}, u32[]{:S(2)}) copy-start(bf16[2,256,768]{2,1,0:T(8,128)(2,1)S(1)} %collective-permute-done) | copy-start | bytes 2359300
  125.4 20.0 %copy-start.36 = (f32[768]{0:T(1024)}, f32[768]{0:T(1024)S(1)}, u32[]{:S(2)}) copy-start(f32[768]{0:T(1024)S(1)} %reshape.541) | copy-start | bytes 9220
  126.2 19.2 %copy-start.42 = (f32[768]{0:T(1024)}, f32[768]{0:T(1024)S(1)}, u32[]{:S(2)}) copy-start(f32[768]{0:T(1024)S(1)} %reshape.542) | copy-start | bytes 9220
  132.5 8.1 %copy-start.1 = (bf16[32,24,768]{2,1,0:T(8,128)(2,1)}, bf16[32,24,768]{2,1,0:T(8,128)(2,1)S(1)}, u32[]{:S(2)}) copy-start(bf16[32,24,768]{2,1,0:T(8,128)(2,1)S(1)} %get-tuple-element.37) | copy-start | bytes 3538948
  154.2 14.3 %copy-start.31 = (bf16[2,12,256,64]{2,3,0,1:T(8,128)(2,1)}, bf16[2,12,256,64]{2,3,0,1:T(8,128)(2,1)S(1)}, u32[]{:S(2)}) copy-start(bf16[2,12,256,64]{2,3,0,1:T(8,128)(2,1)S(1)} %fusion.84) | copy-start | bytes 2359300
  161.1 7.3 %copy-start.55 = (pred[2,1024]{1,0:T(4,128)(4,1)S(1)}, pred[2,1024]{1,0:T(4,128)(4,1)}, u32[]{:S(2)}) copy-start(pred[2,1024]{1,0:T(4,128)(4,1)} %broadcast_compare_fusion) | copy-start | bytes 6148
  183.7 11.7 %copy-start.39 = (f32[2,12,256]{2,1,0:T(8,128)}, f32[2,12,256]{2,1,0:T(8,128)S(1)}, u32[]{:S(2)}) copy-start(f32[2,12,256]{2,1,0:T(8,128)S(1)} %get-tuple-element.71) | copy-start | bytes 73732
  197.5 42.2 %copy-start.13 = (f32[512,768]{1,0:T(8,128)}, f32[512,768]{1,0:T(8,128)S(1)}, u32[]{:S(2)}) copy-start(f32[512,768]{1,0:T(8,128)S(1)} %get-tuple-element.74) | copy-start | bytes 4718596
  219.0 8.6 %copy-start.38 = (bf16[32,1,768]{2,0,1:T(8,128)(2,1)}, bf16[32,1,768]{2,0,1:T(8,128)(2,1)S(1)}, u32[]{:S(2)}) copy-start(bf16[32,1,768]{2,0,1:T(8,128)(2,1)S(1)} %copy.196) | copy-start | bytes 147460
  219.0 8.7 %copy-start.44 = (f32[768]{0:T(1024)S(1)}, f32[768]{0:T(1024)}, u32[]{:S(2)}) copy-start(f32[768]{0:T(1024)} %reshape.546) | copy-start | bytes 9220
  219.0 8.7 %copy-start.52 = (f32[768]{0:T(1024)S(1)}, f32[768]{0:T(1024)}, u32[]{:S(2)}) copy-start(f32[768]{0:T(1024)} %reshape.547) | copy-start | bytes 9220
  219.0 15.1 %slice-start.4 = ((s8[4718592]{0:T(1024)(128)(4,1)}), s8[524288]{0:T(1024)(128)(4,1)S(1)}, s32[]{:S(2)}) async-start(s8[4718592]{0:T(1024)(128)(4,1)} %bitcast.223), calls=%async_computation.12 | async-start | bytes 1048576
  227.7 12.1 %slice-start.2 = ((s8[4718592]{0:T(1024)(128)(4,1)}), s8[4194304]{0:T(1024)(128)(4,1)S(1)}, s32[]{:S(2)}) async-start(s8[4718592]{0:T(1024)(128)(4,1)} %bitcast.220), calls=%async_computation.10 | async-start | bytes 8388608
  274.9 21.6 %copy-start.19 = (bf16[2,12,1024,64]{2,3,0,1:T(8,128)(2,1)S(1)}, bf16[2,12,1024,64]{2,3,0,1:T(8,128)(2,1)}, u32[]{:S(2)}) copy-start(bf16[2,12,1024,64]{2,3,0,1:T(8,128)(2,1)} %convert_bitcast_fusion.1) | copy-start | bytes 9437188
  296.5 9.5 %copy-start.32 = (bf16[2,12,256,64]{2,3,0,1:T(8,128)(2,1)S(1)}, bf16[2,12,256,64]{2,3,0,1:T(8,128)(2,1)}, u32[]{:S(2)}) copy-start(bf16[2,12,256,64]{2,3,0,1:T(8,128)(2,1)} %copy-done.31) | copy-start | bytes 2359300
  306.0 7.0 %copy-start.25 = (bf16[2,1024,12,64]{1,3,2,0:T(8,128)(2,1)S(1)}, bf16[2,1024,12,64]{1,3,2,0:T(8,128)(2,1)}, u32[]{:S(2)}) copy-start(bf16[2,1024,12,64]{1,3,2,0:T(8,128)(2,1)} %get-tuple-element.79) | copy-start | bytes 9437188
  317.3 9.4 %copy-start.22 = (bf16[96,8,2,1024]{3,1,2,0:T(8,128)(2,1)}, bf16[96,8,2,1024]{3,1,2,0:T(8,128)(2,1)S(1)}, u32[]{:S(2)}) copy-start(bf16[96,8,2,1024]{3,1,2,0:T(8,128)(2,1)S(1)} %copy.120) | copy-start | bytes 9437188
  363.3 136.4 %reduce-scatter.4.cloned.1.call-start = ((), (), s32[]{:S(2)}) async-start(), calls=%async_computation.3 | async-start | bytes 12386304 | tf_op jit(solution)/shard_map/reduce_scatter | solution.py:107
  377.6 8.6 %copy-start.56 = (bf16[768]{0:T(1024)(128)(2,1)S(1)}, bf16[768]{0:T(1024)(128)(2,1)}, u32[]{:S(2)}) copy-start(bf16[768]{0:T(1024)(128)(2,1)} %get-tuple-element.23) | copy-start | bytes 4612
  396.9 214.9 %reduce-scatter.8.cloned.1.call-start = ((), (), s32[]{:S(2)}) async-start(), calls=%async_computation.5 | async-start | bytes 2334720 | tf_op jit(solution)/shard_map/reduce_scatter | solution.py:112
  507.5 48.0 %collective-permute-start.3 = (bf16[2,256,768]{2,1,0:T(8,128)(2,1)S(1)}, bf16[2,256,768]{2,1,0:T(8,128)(2,1)S(1)}, u32[]{:S(2)}, u32[]{:S(2)}) collective-permute-start(bf16[2,256,768]{2,1,0:T(8,128)(2,1)S(1)} %get-tuple-element.42), channel_id=1, source_target_pairs={{0,3},{1,0},{2,1},{3,2},{4,7},{5,4},{6,5},{7,6},{8,11},{9,8},{10,9... | collective-permute-start | bytes 2359304 | tf_op jit(solution)/shard_map/ppermute | solution.py:246
  510.9 65.5 %collective-permute-start.5 = (bf16[2,256,768]{2,1,0:T(8,128)(2,1)S(1)}, bf16[2,256,768]{2,1,0:T(8,128)(2,1)S(1)}, u32[]{:S(2)}, u32[]{:S(2)}) collective-permute-start(bf16[2,256,768]{2,1,0:T(8,128)(2,1)S(1)} %get-tuple-element.43), channel_id=1, source_target_pairs={{0,1},{1,2},{2,3},{3,0},{4,5},{5,6},{6,7},{7,4},{8,9},{9,10},{10,1... | collective-permute-start | bytes 2359304 | tf_op jit(solution)/shard_map/ppermute | solution.py:246
  510.9 97.3 %copy-start.12 = (f32[512,768]{1,0:T(8,128)S(1)}, f32[512,768]{1,0:T(8,128)}, u32[]{:S(2)}) copy-start(f32[512,768]{1,0:T(8,128)} %get-tuple-element.83) | copy-start | bytes 4718596
  510.9 97.3 %collective-permute-start.4 = (bf16[2,256,768]{2,1,0:T(8,128)(2,1)S(1)}, bf16[2,256,768]{2,1,0:T(8,128)(2,1)S(1)}, u32[]{:S(2)}, u32[]{:S(2)}) collective-permute-start(bf16[2,256,768]{2,1,0:T(8,128)(2,1)S(1)} %get-tuple-element.44), channel_id=1, source_target_pairs={{0,2},{1,3},{2,0},{3,1},{4,6},{5,7},{6,4},{7,5},{8,10},{9,11},{10,... | collective-permute-start | bytes 2359304 | tf_op jit(solution)/shard_map/ppermute | solution.py:246
  (44 other events, 186.4 us)
Sparse Core Ops, SparseCore 0:
  16.0 107.4 all-gather.4
  126.3 83.6 all-gather.6
  363.4 48.3 reduce-scatter.5
  415.3 84.4 reduce-scatter.3
  502.8 75.7 reduce-scatter.7

commit v11 on v10

--- a/solution.py
+++ b/solution.py
@@ -83,7 +83,7 @@
     return [out[i] for i in group]
 
 
-LATE_W = (11, 12, 13, 14)
+LATE_W = (7, 8, 9, 10, 11, 12, 13, 14)
 
 
 def pack_group(grads, group, width, mesh_shape):
@@ -151,11 +151,9 @@
     blocks = [inputs]
     for b in range(1, n_ctx):
         blocks.append(lax.ppermute(inputs, "ctx", [(i, (i + b) % n_ctx) for i in range(n_ctx)]))
-    first = (0, 1, 2, 3, 4, 5, 6, 7, 8, 9, 10)
-    ln1_gain, ln1_bias, wq, bq, wk, wv, bv, wo, bo, ln2_gain, ln2_bias = gather_all(
-        shards, first, width, groups
-    )
-    wi, bi, wf, bf = gather_all(shards, LATE_W, width, groups)
+    first = (0, 1, 2, 3, 4, 5, 6)
+    ln1_gain, ln1_bias, wq, bq, wk, wv, bv = gather_all(shards, first, width, groups)
+    wo, bo, ln2_gain, ln2_bias, wi, bi, wf, bf = gather_all(shards, LATE_W, width, groups)
     me = lax.axis_index("ctx")
     total = n_ctx * rows
     source = (me - jnp.arange(n_ctx)) % n_ctx
@@ -218,6 +216,7 @@
         11: grad_wi, 12: grad_bi, 13: grad_wf, 14: grad_bf,
     }
     early_part = dp_stage(pack_group(grads, EARLY, width, mesh_shape))
+    (early_sum,) = ctx_stage([early_part])
     d_mixed = back(d_branch, wo).astype(jnp.bfloat16).reshape(seqs, rows, H, HD)
     d_probs = jnp.einsum("sqhd,shkd->shqk", d_mixed, vh, preferred_element_type=jnp.float32)
     inner = jnp.sum(probs * d_probs, axis=-1, keepdims=True)
@@ -251,7 +250,7 @@
     xhat1_b, rstd1_b = lax.optimization_barrier((xhat1, rstd1))
     d_x = norm_back_rows(d_normed.reshape(n, width), xhat1_b, rstd1_b, f32(ln1_gain))
     input_grad = (d_middle + d_x).astype(jnp.bfloat16).reshape(seqs, rows, width)
-    early_sum, late_sum = ctx_stage([early_part, late_part])
+    (late_sum,) = ctx_stage([late_part])
     out = unpack_group(early_sum, grads, EARLY, width, groups)
     out.update(unpack_group(late_sum, grads, LATE, width, groups))
     return (output, input_grad) + tuple(out[i] for i in range(15))

time: 636 us -> 575 us (0.904)
  waiting for transfers between devices: 294 us -> 239 us
    ppermute x3, waiting for transfers between devices: 88.8 us -> 0.01 us  [layer(): lax.ppermute(sent, 'ctx', [(i, (i - b) % n_ctx) for i in range(n_ctx)])]
    reduce_scatter x1 -> x2, waiting for transfers between devices: 0.01 us -> 41.5 us  [ctx_stage(): mine = lax.psum_scatter(joined, 'ctx', scatter_dimension=1, tiled=True)]
    reduce_scatter x2, waiting for transfers between devices: 103 us -> 93 us  [dp_stage(): return lax.psum_scatter(packed, 'dp', scatter_dimension=0, tiled=True)]
    slice x2 -> x3, local copies, waits for them, and re-layouts: 12.3 us -> 13.4 us  [gather_all(): full[:, off:off + r, :].reshape((groups * s.shape[0],) + s.shape[1:])]
  transfers between devices with their start and end apart: 11 -> 12, of which waited for: 9 -> 8; matrix products, arithmetic and copies ran while one was open for 21% -> 24% of each run, Pallas kernels for 0% -> 0%
where the time goes in v11:
time: 575 us; the launch traced here: 565 us
  waiting for transfers between devices  239 us (42%)
  matrix products  154 us (27%)
  local copies, waits for them, and re-layouts  91.1 us (16%)
  other arithmetic  53.1 us (9%)
  between operations  15.4 us (3%)
  starting transfers between devices  12.6 us (2%)
    reduce_scatter x2, waiting for transfers between devices, dp_stage(): return lax.psum_scatter(packed, 'dp', scatter_dimension=0, tiled=True)  93 us
    all_gather x2, waiting for transfers between devices, gather_all(): full = lax.all_gather(packed[None], ALL, axis=0, tiled=True)  53.7 us
    ppermute x3, waiting for transfers between devices, layer(): lax.ppermute(inputs, 'ctx', [(i, (i + b) % n_ctx) for i in range(n_ctx)])  50.4 us
    reduce_scatter x2, waiting for transfers between devices, ctx_stage(): mine = lax.psum_scatter(joined, 'ctx', scatter_dimension=1, tiled=True)  41.5 us
    dot_general x6, matrix products, outer(): lax.dot_general(left_rows, right_rows, (((0,), (0,)), ((), ())), preferre...  26.1 us
    dot_general x6, matrix products, back(): lax.dot_general(grad_rows, weight, (((1,), (1,)), ((), ())), preferred_el...  25.7 us
    convert_element_type x1, other arithmetic, layer(): d_scores = (probs * (d_probs - inner)).astype(jnp.bfloat16)  21.5 us
    dot_general x3, matrix products, layer(): jnp.einsum('snd,dhe->shne', a, heads(w), preferred_element_type=jnp.float32)  17.5 us
  transfers between devices with their start and end apart: 12, of which 8 were waited for; matrix products, arithmetic and copies ran while one was open for 24% of the time, Pallas kernels for 0%

profile of v11, /device:TPU:0, one launch (start us, length us, event | category | flops | bytes accessed | tf_op | source)
XLA Modules:
  0.0 565.4 jit_solution(3217550552997572681)
XLA Ops:
  15.9 4.1 collective-permute-start.1
  25.3 49.8 %collective-permute-done.1 = bf16[2,256,768]{2,1,0:T(8,128)(2,1)S(1)} collective-permute-done((bf16[2,256,768]{2,1,0:T(8,128)(2,1)}, bf16[2,256,768]{2,1,0:T(8,128)(2,1)S(1)}, u32[]{:S(2)}, u32[]{:S(2)}) %collective-permute-start.1) | collective-permute-done | bytes 786464 | tf_op jit(solution)/shard_map/ppermute | solution.py:153
  80.0 33.5 %all-gather.5.cloned.1.call-done = bf16[2560,768]{1,0:T(8,128)(2,1)} async-done(((bf16[80,768]{1,0:T(8,128)(2,1)}), bf16[2560,768]{1,0:T(8,128)(2,1)}) %all-gather.5.cloned.1.call-update) | async-done | bytes 3932176 | tf_op jit(solution)/shard_map/all_gather | solution.py:70
  123.1 4.7 reshape_reshape.11
  127.8 4.7 reshape_reshape.9
  141.4 6.6 %convert_bitcast_fusion.1 = bf16[2,12,1024,64]{2,3,0,1:T(8,128)(2,1)} fusion(bf16[2,1024,768]{2,1,0:T(8,128)(2,1)S(1)} %copy-done.15, bf16[768,12,64,1]{2,1,0,3:T(8,128)(2,1)S(1)} %bitcast.243), kind=kOutput, calls=%fused_computation.58 | convolution fusion | flops 2417491968 | bytes 7471104 | tf_op jit(solution)/shard_map/snd,dhe->shne/dot_general | solution.py:172
  147.9 7.3 %fusion.22 = bf16[2,12,1024,64]{2,3,0,1:T(8,128)(2,1)} fusion(f32[12,64]{1,0:T(8,128)S(1)} %copy-done.44, bf16[2,1024,768]{2,1,0:T(8,128)(2,1)S(1)} %copy-done.15, bf16[768,12,64,1]{2,1,0,3:T(8,128)(2,1)S(1)} %bitcast.242), kind=kOutput, calls=%fused_computation.44 | convolution fusion | flops 2419064832 | bytes 7474176 | tf_op jit(solution)/shard_map/snd,dhe->shne/dot_general | solution.py:172
  155.2 15.3 %fusion.131 = (f32[2,12,256]{2,1,0:T(8,128)S(1)}, f32[2,12,256,1024]{3,2,1,0:T(8,128)}) fusion(pred[2,1024]{1,0:T(4,128)(4,1)S(1)} %copy-done.49, bf16[2,12,1024,64]{2,3,0,1:T(8,128)(2,1)} %convert_bitcast_fusion.1, bf16[2,12,256,64]{2,3,0,1:T(8,128)(2,1)S(1)} %fusion.84), kind=kOutput, calls=%fused_computation.179 | convolution fusion | flops 830473216 | bytes 29124608 | tf_op jit(solution)/shard_map/sub | solution.py:183
  170.5 11.7 %fusion.79 = bf16[2,256,12,64]{1,3,2,0:T(8,128)(2,1)S(1)} fusion(bf16[2,12,1024,64]{2,3,0,1:T(8,128)(2,1)} %fusion.22, f32[2,12,256,1024]{3,2,1,0:T(8,128)} %get-tuple-element.69, f32[2,12,256]{2,1,0:T(8,128)S(1)} %get-tuple-element.68), kind=kOutput, calls=%fused_computation.99 | convolution fusion | flops 818282496 | bytes 29122560 | tf_op jit(solution)/shard_map/shqk,shkd->sqhd/dot_general | solution.py:186
  183.2 20.2 %all-gather.7.cloned.1.call-done = bf16[7168,768]{1,0:T(8,128)(2,1)} async-done(((bf16[224,768]{1,0:T(8,128)(2,1)}), bf16[7168,768]{1,0:T(8,128)(2,1)}) %all-gather.7.cloned.1.call-update) | async-done | bytes 11010064 | tf_op jit(solution)/shard_map/all_gather | solution.py:70
  206.6 8.4 %fusion.126 = (bf16[32,96,768]{2,1,0:T(8,128)(2,1)}, bf16[32,96,768]{2,1,0:T(8,128)(2,1)}) fusion(bf16[32,224,768]{2,1,0:T(8,128)(2,1)} %bitcast.215), kind=kLoop, calls=%fused_computation.174 | loop fusion | bytes 18874368 | tf_op jit(solution)/shard_map/slice | solution.py:75
  215.4 8.5 %reshape.514 = bf16[768,3072]{1,0:T(8,128)(2,1)} reshape(bf16[32,96,768]{2,1,0:T(8,128)(2,1)} %get-tuple-element.33) | data formatting | bytes 9437184 | tf_op jit(solution)/shard_map/reshape | solution.py:75
  226.8 5.0 fusion.19
  231.8 5.1 fusion.143
  242.6 11.4 %fusion.141 = (bf16[12,64]{1,0:T(8,128)(2,1)S(1)}, bf16[2,1024,12,64]{1,3,2,0:T(8,128)(2,1)}) fusion(f32[2,12,256,1024]{3,2,1,0:T(8,128)} %get-tuple-element.69, f32[2,12,256]{2,1,0:T(8,128)S(1)} %get-tuple-element.68, bf16[2,256,12,64]{1,0,3,2:T(2,128)(2,1)S(1)} %reshape.518), kind=kOutput, calls=%fused_computation.181 | convolution fusion | flops 821034240 | bytes 29124096 | tf_op jit(solution)/shard_map/shqk,sqhd->skhd/dot_general | solution.py:229
  254.0 16.6 %multiply_reduce_fusion = (f32[2,12,256]{2,1,0:T(8,128)S(1)}, f32[2,12,256,1024]{3,2,1,0:T(8,128)}) fusion(f32[2,12,256,1024]{3,2,1,0:T(8,128)} %get-tuple-element.69, f32[2,12,256]{2,1,0:T(8,128)S(1)} %get-tuple-element.68, bf16[2,12,1024,64]{2,3,0,1:T(8,128)(2,1)} %fusion.22, bf16[2,256,12,64]{1,0,3,2:T(2,128)(2,1)S(1)} %reshape.518), kind=kOutput, calls=%fused_computation.2 | convolution fusion | flops 824174592 | bytes 54312960 | tf_op jit(solution)/shard_map/sqhd,shkd->shqk/dot_general | solution.py:221
  270.6 21.5 %multiply_convert_fusion = bf16[2,12,256,1024]{3,2,1,0:T(8,128)(2,1)} fusion(f32[2,12,256,1024]{3,2,1,0:T(8,128)} %get-tuple-element.74, f32[2,12,256]{2,1,0:T(8,128)S(1)} %get-tuple-element.73, f32[2,12,256,1024]{3,2,1,0:T(8,128)} %get-tuple-element.69, f32[2,12,256]{2,1,0:T(8,128)S(1)} %get-tuple-element.68), kind=kLoop, calls=%fused_computation.1 | loop fusion | flops 25165824 | bytes 62963712 | tf_op jit(solution)/shard_map/convert_element_type | solution.py:223
  292.1 9.5 %fusion.142 = (bf16[12,64]{1,0:T(8,128)(2,1)S(1)}, bf16[2,256,12,64]{1,3,2,0:T(8,128)(2,1)}) fusion(bf16[2,12,256,1024]{3,2,1,0:T(8,128)(2,1)} %multiply_convert_fusion, bf16[2,12,1024,64]{2,3,0,1:T(8,128)(2,1)S(1)} %copy-done.19), kind=kOutput, calls=%fused_computation.182 | convolution fusion | flops 806485248 | bytes 16516608 | tf_op jit(solution)/shard_map/shqk,shkd->sqhd/dot_general | solution.py:224
  301.6 7.0 %fusion.24 = bf16[2,1024,12,64]{1,3,2,0:T(8,128)(2,1)S(1)} fusion(bf16[2,12,256,1024]{3,2,1,0:T(8,128)(2,1)} %multiply_convert_fusion, bf16[2,12,256,64]{2,3,0,1:T(8,128)(2,1)S(1)} %copy-done.32), kind=kOutput, calls=%fused_computation.46 | convolution fusion | flops 808452096 | bytes 16515072 | tf_op jit(solution)/shard_map/shqk,shqd->skhd/dot_general | solution.py:227
  317.8 4.6 fusion.144
  322.5 10.1 %multiply_reduce_fusion.1 = (f32[768]{0:T(1024)S(1)}, f32[768]{0:T(1024)S(1)}, bf16[2048,768]{1,0:T(8,128)(2,1)}, f32[2048,768]{1,0:T(8,128)}) fusion(f32[2048]{0:T(1024)S(1)} %copy-done.45, f32[2048]{0:T(1024)S(1)} %copy-done.46, bf16[2,256,768]{2,1,0:T(8,128)(2,1)S(1)} %copy-done.11, bf16[2,256,768]{2,1,0:T(8,128)(2,1)S(1)} %copy-done.6, ...), kind=kOutput, calls=%fused_computation.25 | convolution fusion | flops 2442656256 | bytes 23228416 | tf_op jit(solution)/shard_map/dot_general | solution.py:40
  332.6 4.7 copy.96
  337.4 6.7 %fusion.67 = bf16[32,24,768]{2,1,0:T(8,128)(2,1)} fusion(bf16[32,24,2048]{2,1,0:T(8,128)(2,1)} %bitcast.237, bf16[2048,768]{0,1:T(8,128)(2,1)} %bitcast.233), kind=kOutput, calls=%fused_computation.92 | convolution fusion | flops 2416508928 | bytes 7471104 | tf_op jit(solution)/shard_map/dot_general | solution.py:34
  360.5 4.9 copy.99
  365.5 7.8 %convolution_convert_fusion = bf16[768,3072]{1,0:T(8,128)(2,1)} fusion(bf16[512,3072]{1,0:T(8,128)(2,1)} %copy-done.51, f32[512,768]{1,0:T(8,128)} %copy-done.13, f32[768]{0:T(1024)S(1)} %copy-done.48, f32[768]{0:T(1024)S(1)} %reshape.548, f32[512]{0:T(512)S(1)} %add_rsqrt_fusion.1, f32[512]{0:T(512)S(1)} %broadcast_multiply_fusion.4), kind=kOutput, calls=%fused_computation.40 | convolution fusion | flops 2420244480 | bytes 9447424 | tf_op jit(solution)/shard_map/dot_general | solution.py:34
  373.4 8.5 %convert_element_type.359 = bf16[32,96,768]{2,1,0:T(8,128)(2,1)} reshape(bf16[768,3072]{1,0:T(8,128)(2,1)} %convolution_convert_fusion) | data formatting | bytes 9437184 | tf_op jit(solution)/shard_map/convert_element_type | solution.py:102
  387.4 5.2 pad_maximum_fusion
  392.7 14.9 %reduce-scatter.5.cloned.1.call-done = bf16[1,4,80,768]{3,2,1,0:T(8,128)(2,1)} async-done(((bf16[8,4,80,768]{3,2,1,0:T(8,128)(2,1)}), bf16[1,4,80,768]{3,2,1,0:T(8,128)(2,1)}) %reduce-scatter.5.cloned.1.call-update) | async-done | bytes 491536 | tf_op jit(solution)/shard_map/reduce_scatter | solution.py:107
  417.4 78.1 %reduce-scatter.9.cloned.1.call-done = bf16[1,4,224,768]{3,2,1,0:T(8,128)(2,1)} async-done(((bf16[8,4,224,768]{3,2,1,0:T(8,128)(2,1)}), bf16[1,4,224,768]{3,2,1,0:T(8,128)(2,1)}) %reduce-scatter.9.cloned.1.call-update) | async-done | bytes 1376272 | tf_op jit(solution)/shard_map/reduce_scatter | solution.py:107
  495.6 7.7 %add_convert_fusion.4 = bf16[512,768]{1,0:T(8,128)(2,1)} fusion(f32[512,768]{1,0:T(8,128)} %copy-done.13, bf16[3072,768]{1,0:T(8,128)(2,1)} %bitcast.221, f32[512,3072]{1,0:T(8,128)} %copy-done.50, f32[3072]{0:T(1024)S(1)} %copy-done.42, f32[768]{0:T(1024)S(1)} %reshape.551), kind=kOutput, calls=%fused_computation.87 | convolution fusion | flops 2426535936 | bytes 13384704 | tf_op jit(solution)/shard_map/dot_general | solution.py:30
  507.6 11.6 %reduce-scatter.7.cloned.1.call-done = bf16[1,1,80,768]{3,2,1,0:T(8,128)(2,1)} async-done(((bf16[1,4,80,768]{3,2,1,0:T(8,128)(2,1)}), bf16[1,1,80,768]{3,2,1,0:T(8,128)(2,1)}) %reduce-scatter.7.cloned.1.call-update) | async-done | bytes 122896 | tf_op jit(solution)/shard_map/reduce_scatter | solution.py:112
  522.2 29.9 %reduce-scatter.11.cloned.1.call-done = bf16[1,1,224,768]{3,2,1,0:T(8,128)(2,1)} async-done(((bf16[1,4,224,768]{3,2,1,0:T(8,128)(2,1)}), bf16[1,1,224,768]{3,2,1,0:T(8,128)(2,1)}) %reduce-scatter.11.cloned.1.call-update) | async-done | bytes 344080 | tf_op jit(solution)/shard_map/reduce_scatter | solution.py:112
  (242 shorter events, 104.3 us)
Async XLA Ops:
  7.2 70.4 %copy-start.3 = (bf16[2,256,768]{2,1,0:T(8,128)(2,1)S(1)}, bf16[2,256,768]{2,1,0:T(8,128)(2,1)}, u32[]{:S(2)}) copy-start(bf16[2,256,768]{2,1,0:T(8,128)(2,1)} %param.18) | copy-start | bytes 2359300
  7.2 106.3 %all-gather.5.cloned.1.call-start = ((), (), s32[]{:S(2)}) async-start(), calls=%async_computation.8 | async-start | bytes 4055040 | tf_op jit(solution)/shard_map/all_gather | solution.py:70
  9.6 193.8 %all-gather.7.cloned.1.call-start = ((), (), s32[]{:S(2)}) async-start(), calls=%async_computation.9 | async-start | bytes 11354112 | tf_op jit(solution)/shard_map/all_gather | solution.py:70
  15.9 391.7 %reduce-scatter.5.cloned.1.call-start = ((), (), s32[]{:S(2)}) async-start(), calls=%async_computation.4 | async-start | bytes 4423680 | tf_op jit(solution)/shard_map/reduce_scatter | solution.py:107
  15.9 59.1 %collective-permute-start.1 = (bf16[2,256,768]{2,1,0:T(8,128)(2,1)}, bf16[2,256,768]{2,1,0:T(8,128)(2,1)S(1)}, u32[]{:S(2)}, u32[]{:S(2)}) collective-permute-start(bf16[2,256,768]{2,1,0:T(8,128)(2,1)} %param.18), channel_id=1, source_target_pairs={{0,2},{1,3},{2,0},{3,1},{4,6},{5,7},{6,4},{7,5},{8,10},{9,11},{10,... | collective-permute-start | bytes 2359304 | tf_op jit(solution)/shard_map/ppermute | solution.py:153
  20.0 55.0 %collective-permute-start = (bf16[2,256,768]{2,1,0:T(8,128)(2,1)}, bf16[2,256,768]{2,1,0:T(8,128)(2,1)S(1)}, u32[]{:S(2)}, u32[]{:S(2)}) collective-permute-start(bf16[2,256,768]{2,1,0:T(8,128)(2,1)} %param.18), channel_id=1, source_target_pairs={{0,1},{1,2},{2,3},{3,0},{4,5},{5,6},{6,7},{7,4},{8,9},{9,10},{10,1... | collective-permute-start | bytes 2359304 | tf_op jit(solution)/shard_map/ppermute | solution.py:153
  21.6 54.1 %collective-permute-start.2 = (bf16[2,256,768]{2,1,0:T(8,128)(2,1)}, bf16[2,256,768]{2,1,0:T(8,128)(2,1)S(1)}, u32[]{:S(2)}, u32[]{:S(2)}) collective-permute-start(bf16[2,256,768]{2,1,0:T(8,128)(2,1)} %param.18), channel_id=1, source_target_pairs={{0,3},{1,0},{2,1},{3,2},{4,7},{5,4},{6,5},{7,6},{8,11},{9,8},{10,9... | collective-permute-start | bytes 2359304 | tf_op jit(solution)/shard_map/ppermute | solution.py:153
  75.0 57.5 %copy-start.5 = (bf16[2,256,768]{2,1,0:T(8,128)(2,1)}, bf16[2,256,768]{2,1,0:T(8,128)(2,1)S(1)}, u32[]{:S(2)}) copy-start(bf16[2,256,768]{2,1,0:T(8,128)(2,1)S(1)} %collective-permute-done.1) | copy-start | bytes 2359300
  75.0 57.5 %copy-start.7 = (bf16[2,256,768]{2,1,0:T(8,128)(2,1)}, bf16[2,256,768]{2,1,0:T(8,128)(2,1)S(1)}, u32[]{:S(2)}) copy-start(bf16[2,256,768]{2,1,0:T(8,128)(2,1)S(1)} %collective-permute-done) | copy-start | bytes 2359300
  115.4 17.1 %copy-start.35 = (f32[768]{0:T(1024)}, f32[768]{0:T(1024)S(1)}, u32[]{:S(2)}) copy-start(f32[768]{0:T(1024)S(1)} %reshape.543) | copy-start | bytes 9220
  115.5 17.0 %copy-start.39 = (f32[768]{0:T(1024)}, f32[768]{0:T(1024)S(1)}, u32[]{:S(2)}) copy-start(f32[768]{0:T(1024)S(1)} %reshape.544) | copy-start | bytes 9220
  119.9 7.9 %copy-start.1 = (bf16[32,24,768]{2,1,0:T(8,128)(2,1)}, bf16[32,24,768]{2,1,0:T(8,128)(2,1)S(1)}, u32[]{:S(2)}) copy-start(bf16[32,24,768]{2,1,0:T(8,128)(2,1)S(1)} %get-tuple-element.35) | copy-start | bytes 3538948
  141.0 14.2 %copy-start.31 = (bf16[2,12,256,64]{2,3,0,1:T(8,128)(2,1)}, bf16[2,12,256,64]{2,3,0,1:T(8,128)(2,1)S(1)}, u32[]{:S(2)}) copy-start(bf16[2,12,256,64]{2,3,0,1:T(8,128)(2,1)S(1)} %fusion.84) | copy-start | bytes 2359300
  147.9 7.3 %copy-start.49 = (pred[2,1024]{1,0:T(4,128)(4,1)S(1)}, pred[2,1024]{1,0:T(4,128)(4,1)}, u32[]{:S(2)}) copy-start(pred[2,1024]{1,0:T(4,128)(4,1)} %broadcast_compare_fusion) | copy-start | bytes 6148
  183.2 40.7 %copy-start.20 = (bf16[96,8,2,256]{3,1,2,0:T(8,128)(2,1)}, bf16[96,8,2,256]{3,1,2,0:T(8,128)(2,1)S(1)}, u32[]{:S(2)}) copy-start(bf16[96,8,2,256]{3,1,2,0:T(8,128)(2,1)S(1)} %copy.118) | copy-start | bytes 2359300
  206.6 17.3 %copy-start.33 = (bf16[32,24,768]{2,1,0:T(8,128)(2,1)}, bf16[32,24,768]{2,1,0:T(8,128)(2,1)S(1)}, u32[]{:S(2)}) copy-start(bf16[32,24,768]{2,1,0:T(8,128)(2,1)S(1)} %slice.199) | copy-start | bytes 3538948
  215.1 16.7 %copy-start.41 = (f32[3072]{0:T(1024)}, f32[3072]{0:T(1024)S(1)}, u32[]{:S(2)}) copy-start(f32[3072]{0:T(1024)S(1)} %reshape.550) | copy-start | bytes 36868
  215.3 9.9 %copy-start.47 = (f32[768]{0:T(1024)}, f32[768]{0:T(1024)S(1)}, u32[]{:S(2)}) copy-start(f32[768]{0:T(1024)S(1)} %reshape.549) | copy-start | bytes 9220
  224.8 15.2 %copy-start.13 = (f32[512,768]{1,0:T(8,128)}, f32[512,768]{1,0:T(8,128)S(1)}, u32[]{:S(2)}) copy-start(f32[512,768]{1,0:T(8,128)S(1)} %get-tuple-element.71) | copy-start | bytes 4718596
  270.6 21.5 %copy-start.19 = (bf16[2,12,1024,64]{2,3,0,1:T(8,128)(2,1)S(1)}, bf16[2,12,1024,64]{2,3,0,1:T(8,128)(2,1)}, u32[]{:S(2)}) copy-start(bf16[2,12,1024,64]{2,3,0,1:T(8,128)(2,1)} %convert_bitcast_fusion.1) | copy-start | bytes 9437188
  292.1 9.5 %copy-start.32 = (bf16[2,12,256,64]{2,3,0,1:T(8,128)(2,1)S(1)}, bf16[2,12,256,64]{2,3,0,1:T(8,128)(2,1)}, u32[]{:S(2)}) copy-start(bf16[2,12,256,64]{2,3,0,1:T(8,128)(2,1)} %copy-done.31) | copy-start | bytes 2359300
  301.6 7.0 %copy-start.25 = (bf16[2,1024,12,64]{1,3,2,0:T(8,128)(2,1)S(1)}, bf16[2,1024,12,64]{1,3,2,0:T(8,128)(2,1)}, u32[]{:S(2)}) copy-start(bf16[2,1024,12,64]{1,3,2,0:T(8,128)(2,1)} %get-tuple-element.76) | copy-start | bytes 9437188
  313.0 9.4 %copy-start.22 = (bf16[96,8,2,1024]{3,1,2,0:T(8,128)(2,1)}, bf16[96,8,2,1024]{3,1,2,0:T(8,128)(2,1)S(1)}, u32[]{:S(2)}) copy-start(bf16[96,8,2,1024]{3,1,2,0:T(8,128)(2,1)S(1)} %copy.120) | copy-start | bytes 9437188
  359.1 136.4 %reduce-scatter.9.cloned.1.call-start = ((), (), s32[]{:S(2)}) async-start(), calls=%async_computation.6 | async-start | bytes 12386304 | tf_op jit(solution)/shard_map/reduce_scatter | solution.py:107
  392.6 15.8 %copy-start.37 = (f32[32,24]{1,0:T(8,128)S(1)}, f32[32,24]{1,0:T(8,128)}, u32[]{:S(2)}) copy-start(f32[32,24]{1,0:T(8,128)} %get-tuple-element.47) | copy-start | bytes 9220
  392.6 126.6 %reduce-scatter.7.cloned.1.call-start = ((), (), s32[]{:S(2)}) async-start(), calls=%async_computation.5 | async-start | bytes 614400 | tf_op jit(solution)/shard_map/reduce_scatter | solution.py:112
  407.6 144.4 %reduce-scatter.11.cloned.1.call-start = ((), (), s32[]{:S(2)}) async-start(), calls=%async_computation.7 | async-start | bytes 1720320 | tf_op jit(solution)/shard_map/reduce_scatter | solution.py:112
  411.6 84.0 %copy-start.42 = (f32[3072]{0:T(1024)S(1)}, f32[3072]{0:T(1024)}, u32[]{:S(2)}) copy-start(f32[3072]{0:T(1024)} %copy-done.41) | copy-start | bytes 36868
  413.0 90.2 %collective-permute-start.3 = (bf16[2,256,768]{2,1,0:T(8,128)(2,1)}, bf16[2,256,768]{2,1,0:T(8,128)(2,1)}, u32[]{:S(2)}, u32[]{:S(2)}) collective-permute-start(bf16[2,256,768]{2,1,0:T(8,128)(2,1)} %get-tuple-element.41), channel_id=1, source_target_pairs={{0,3},{1,0},{2,1},{3,2},{4,7},{5,4},{6,5},{7,6},{8,11},{9,8},{10,9... | collective-permute-start | bytes 2359304 | tf_op jit(solution)/shard_map/ppermute | solution.py:245
  416.4 86.9 %collective-permute-start.5 = (bf16[2,256,768]{2,1,0:T(8,128)(2,1)}, bf16[2,256,768]{2,1,0:T(8,128)(2,1)}, u32[]{:S(2)}, u32[]{:S(2)}) collective-permute-start(bf16[2,256,768]{2,1,0:T(8,128)(2,1)} %get-tuple-element.42), channel_id=1, source_target_pairs={{0,1},{1,2},{2,3},{3,0},{4,5},{5,6},{6,7},{7,4},{8,9},{9,10},{10,1... | collective-permute-start | bytes 2359304 | tf_op jit(solution)/shard_map/ppermute | solution.py:245
  416.4 86.9 %collective-permute-start.4 = (bf16[2,256,768]{2,1,0:T(8,128)(2,1)}, bf16[2,256,768]{2,1,0:T(8,128)(2,1)}, u32[]{:S(2)}, u32[]{:S(2)}) collective-permute-start(bf16[2,256,768]{2,1,0:T(8,128)(2,1)} %get-tuple-element.43), channel_id=1, source_target_pairs={{0,2},{1,3},{2,0},{3,1},{4,6},{5,7},{6,4},{7,5},{8,10},{9,11},{10,... | collective-permute-start | bytes 2359304 | tf_op jit(solution)/shard_map/ppermute | solution.py:245
  495.5 7.7 %copy-start.12 = (f32[512,768]{1,0:T(8,128)S(1)}, f32[512,768]{1,0:T(8,128)}, u32[]{:S(2)}) copy-start(f32[512,768]{1,0:T(8,128)} %get-tuple-element.80) | copy-start | bytes 4718596
  (36 other events, 158.5 us)
Sparse Core Ops, SparseCore 0:
  11.4 102.0 all-gather.4
  116.3 87.0 all-gather.6
  359.2 48.3 reduce-scatter.4
  411.1 84.4 reduce-scatter.8
  497.6 21.5 reduce-scatter.6
  521.4 30.5 reduce-scatter.10

commit v12 on v11

--- a/solution.py
+++ b/solution.py
@@ -181,7 +181,7 @@
     scores = jnp.where(valid[:, None, None, :], scores, -1e30)
     top = jnp.max(scores, axis=-1, keepdims=True)
     expd = jnp.exp(scores - top)
-    probs = expd / jnp.sum(expd, axis=-1, keepdims=True)
+    probs = expd * (1.0 / jnp.sum(expd, axis=-1, keepdims=True))
     low_probs = probs.astype(jnp.bfloat16)
     mixed = jnp.einsum("shqk,shkd->sqhd", low_probs, vh, preferred_element_type=jnp.float32)
     mixed = mixed.reshape(n, width).astype(jnp.bfloat16)
@@ -216,7 +216,6 @@
         11: grad_wi, 12: grad_bi, 13: grad_wf, 14: grad_bf,
     }
     early_part = dp_stage(pack_group(grads, EARLY, width, mesh_shape))
-    (early_sum,) = ctx_stage([early_part])
     d_mixed = back(d_branch, wo).astype(jnp.bfloat16).reshape(seqs, rows, H, HD)
     d_probs = jnp.einsum("sqhd,shkd->shqk", d_mixed, vh, preferred_element_type=jnp.float32)
     inner = jnp.sum(probs * d_probs, axis=-1, keepdims=True)
@@ -250,7 +249,7 @@
     xhat1_b, rstd1_b = lax.optimization_barrier((xhat1, rstd1))
     d_x = norm_back_rows(d_normed.reshape(n, width), xhat1_b, rstd1_b, f32(ln1_gain))
     input_grad = (d_middle + d_x).astype(jnp.bfloat16).reshape(seqs, rows, width)
-    (late_sum,) = ctx_stage([late_part])
+    early_sum, late_sum = ctx_stage([early_part, late_part])
     out = unpack_group(early_sum, grads, EARLY, width, groups)
     out.update(unpack_group(late_sum, grads, LATE, width, groups))
     return (output, input_grad) + tuple(out[i] for i in range(15))

time: 575 us -> 627 us (1.090)
  waiting for transfers between devices: 239 us -> 297 us
    ppermute x3, waiting for transfers between devices: 0.01 us -> 88.8 us  [layer(): lax.ppermute(sent, 'ctx', [(i, (i - b) % n_ctx) for i in range(n_ctx)])]
    reduce_scatter x2 -> x1, waiting for transfers between devices: 41.5 us -> 0.01 us  [ctx_stage(): mine = lax.psum_scatter(joined, 'ctx', scatter_dimension=1, tiled=True)]
    reduce_scatter x2, waiting for transfers between devices: 93 us -> 103 us  [dp_stage(): return lax.psum_scatter(packed, 'dp', scatter_dimension=0, tiled=True)]
  transfers between devices with their start and end apart: 12 -> 11, of which waited for: 8 -> 9; matrix products, arithmetic and copies ran while one was open for 24% -> 21% of each run, Pallas kernels for 0% -> 0%
where the time goes in v12:
time: 627 us; the launch traced here: 617 us
  waiting for transfers between devices  297 us (47%)
  matrix products  151 us (24%)
  local copies, waits for them, and re-layouts  86.2 us (14%)
  other arithmetic  55 us (9%)
  between operations  14.8 us (2%)
  starting transfers between devices  12.6 us (2%)
    reduce_scatter x2, waiting for transfers between devices, dp_stage(): return lax.psum_scatter(packed, 'dp', scatter_dimension=0, tiled=True)  103 us
    ppermute x3, waiting for transfers between devices, layer(): lax.ppermute(sent, 'ctx', [(i, (i - b) % n_ctx) for i in range(n_ctx)])  88.8 us
    all_gather x2, waiting for transfers between devices, gather_all(): full = lax.all_gather(packed[None], ALL, axis=0, tiled=True)  54.1 us
    ppermute x3, waiting for transfers between devices, layer(): lax.ppermute(inputs, 'ctx', [(i, (i + b) % n_ctx) for i in range(n_ctx)])  51 us
    dot_general x6, matrix products, outer(): lax.dot_general(left_rows, right_rows, (((0,), (0,)), ((), ())), preferre...  26 us
    convert_element_type x1, other arithmetic, layer(): d_scores = (probs * (d_probs - inner)).astype(jnp.bfloat16)  21.6 us
    dot_general x6, matrix products, back(): lax.dot_general(grad_rows, weight, (((1,), (1,)), ((), ())), preferred_el...  21.4 us
    dot_general x3, matrix products, layer(): jnp.einsum('snd,dhe->shne', a, heads(w), preferred_element_type=jnp.float32)  18.5 us
  transfers between devices with their start and end apart: 11, of which 9 were waited for; matrix products, arithmetic and copies ran while one was open for 21% of the time, Pallas kernels for 0%

profile of v12, /device:TPU:0, one launch (start us, length us, event | category | flops | bytes accessed | tf_op | source)
XLA Modules:
  0.0 616.9 jit_solution(17336867245861966718)
XLA Ops:
  15.9 4.1 collective-permute-start.1
  24.7 50.3 %collective-permute-done.1 = bf16[2,256,768]{2,1,0:T(8,128)(2,1)S(1)} collective-permute-done((bf16[2,256,768]{2,1,0:T(8,128)(2,1)}, bf16[2,256,768]{2,1,0:T(8,128)(2,1)S(1)}, u32[]{:S(2)}, u32[]{:S(2)}) %collective-permute-start.1) | collective-permute-done | bytes 786464 | tf_op jit(solution)/shard_map/ppermute | solution.py:153
  79.5 34.1 %all-gather.5.cloned.1.call-done = bf16[2560,768]{1,0:T(8,128)(2,1)} async-done(((bf16[80,768]{1,0:T(8,128)(2,1)}), bf16[2560,768]{1,0:T(8,128)(2,1)}) %all-gather.5.cloned.1.call-update) | async-done | bytes 3932176 | tf_op jit(solution)/shard_map/all_gather | solution.py:70
  118.7 4.8 reshape_reshape.9
  123.6 4.7 reshape_reshape.11
  141.3 6.6 %convert_bitcast_fusion.1 = bf16[2,12,1024,64]{2,3,0,1:T(8,128)(2,1)} fusion(bf16[2,1024,768]{2,1,0:T(8,128)(2,1)S(1)} %copy-done.17, bf16[768,12,64,1]{2,1,0,3:T(8,128)(2,1)S(1)} %bitcast.243), kind=kOutput, calls=%fused_computation.56 | convolution fusion | flops 2417491968 | bytes 7471104 | tf_op jit(solution)/shard_map/snd,dhe->shne/dot_general | solution.py:172
  147.9 14.7 %fusion.124 = (f32[2,12,256]{2,1,0:T(8,128)S(1)}, f32[2,12,256,1024]{3,2,1,0:T(8,128)}) fusion(pred[2,1024]{1,0:T(4,128)(4,1)S(1)} %broadcast_compare_fusion, bf16[2,12,1024,64]{2,3,0,1:T(8,128)(2,1)} %convert_bitcast_fusion.1, bf16[2,12,256,64]{2,3,0,1:T(8,128)(2,1)S(1)} %fusion.76), kind=kOutput, calls=%fused_computation.180 | convolution fusion | flops 830473216 | bytes 29124608 | tf_op jit(solution)/shard_map/sub | solution.py:183
  162.6 8.3 %fusion.20 = bf16[2,12,1024,64]{2,3,0,1:T(8,128)(2,1)S(1)} fusion(f32[12,64]{1,0:T(8,128)S(1)} %reshape.546, bf16[2,1024,768]{2,1,0:T(8,128)(2,1)} %copy-done.16, bf16[768,12,64,1]{2,1,0,3:T(8,128)(2,1)} %bitcast.242), kind=kOutput, calls=%fused_computation.42 | convolution fusion | flops 2419064832 | bytes 7474176 | tf_op jit(solution)/shard_map/snd,dhe->shne/dot_general | solution.py:172
  170.9 11.6 %fusion.73 = bf16[2,256,12,64]{1,3,2,0:T(8,128)(2,1)S(1)} fusion(f32[2,12,256,1024]{3,2,1,0:T(8,128)} %get-tuple-element.72, f32[2,12,256]{2,1,0:T(8,128)S(1)} %broadcast_divide_fusion, bf16[2,12,1024,64]{2,3,0,1:T(8,128)(2,1)S(1)} %fusion.20), kind=kOutput, calls=%fused_computation.98 | convolution fusion | flops 818282496 | bytes 29122560 | tf_op jit(solution)/shard_map/shqk,shkd->sqhd/dot_general | solution.py:186
  183.5 20.0 %all-gather.7.cloned.1.call-done = bf16[7168,768]{1,0:T(8,128)(2,1)} async-done(((bf16[224,768]{1,0:T(8,128)(2,1)}), bf16[7168,768]{1,0:T(8,128)(2,1)}) %all-gather.7.cloned.1.call-update) | async-done | bytes 11010064 | tf_op jit(solution)/shard_map/all_gather | solution.py:70
  207.7 8.0 %fusion.118 = (bf16[32,96,768]{2,1,0:T(8,128)(2,1)}, bf16[32,96,768]{2,1,0:T(8,128)(2,1)}) fusion(bf16[32,224,768]{2,1,0:T(8,128)(2,1)} %bitcast.215), kind=kLoop, calls=%fused_computation.174 | loop fusion | bytes 18874368 | tf_op jit(solution)/shard_map/slice | solution.py:75
  216.0 8.5 %reshape.515 = bf16[768,3072]{1,0:T(8,128)(2,1)} reshape(bf16[32,96,768]{2,1,0:T(8,128)(2,1)} %get-tuple-element.33) | data formatting | bytes 9437184 | tf_op jit(solution)/shard_map/reshape | solution.py:75
  227.2 5.0 fusion.15
  232.3 4.8 fusion.136
  242.8 11.4 %fusion.134 = (bf16[12,64]{1,0:T(8,128)(2,1)S(1)}, bf16[2,1024,12,64]{1,3,2,0:T(8,128)(2,1)}) fusion(f32[2,12,256,1024]{3,2,1,0:T(8,128)} %get-tuple-element.72, f32[2,12,256]{2,1,0:T(8,128)S(1)} %broadcast_divide_fusion, bf16[2,256,12,64]{1,0,3,2:T(2,128)(2,1)S(1)} %reshape.519), kind=kOutput, calls=%fused_computation.182 | convolution fusion | flops 821034240 | bytes 29124096 | tf_op jit(solution)/shard_map/shqk,sqhd->skhd/dot_general | solution.py:228
  254.2 16.5 %multiply_reduce_fusion = (f32[2,12,256]{2,1,0:T(8,128)S(1)}, f32[2,12,256,1024]{3,2,1,0:T(8,128)}) fusion(f32[2,12,256,1024]{3,2,1,0:T(8,128)} %get-tuple-element.72, f32[2,12,256]{2,1,0:T(8,128)S(1)} %broadcast_divide_fusion, bf16[2,12,1024,64]{2,3,0,1:T(8,128)(2,1)} %copy-done.2, bf16[2,256,12,64]{1,0,3,2:T(2,128)(2,1)S(1)} %reshape.519), kind=kOutput, calls=%fused_computation.2 | convolution fusion | flops 824174592 | bytes 54312960 | tf_op jit(solution)/shard_map/sqhd,shkd->shqk/dot_general | solution.py:220
  270.7 21.6 %multiply_convert_fusion = bf16[2,12,256,1024]{3,2,1,0:T(8,128)(2,1)} fusion(f32[2,12,256,1024]{3,2,1,0:T(8,128)} %get-tuple-element.77, f32[2,12,256,1024]{3,2,1,0:T(8,128)} %get-tuple-element.72, f32[2,12,256]{2,1,0:T(8,128)S(1)} %get-tuple-element.76, f32[2,12,256]{2,1,0:T(8,128)S(1)} %broadcast_divide_fusion), kind=kLoop, calls=%fused_computation.1 | loop fusion | flops 25165824 | bytes 62963712 | tf_op jit(solution)/shard_map/convert_element_type | solution.py:222
  292.3 9.5 %fusion.135 = (bf16[12,64]{1,0:T(8,128)(2,1)S(1)}, bf16[2,256,12,64]{1,3,2,0:T(8,128)(2,1)}) fusion(bf16[2,12,256,1024]{3,2,1,0:T(8,128)(2,1)} %multiply_convert_fusion, bf16[2,12,1024,64]{2,3,0,1:T(8,128)(2,1)S(1)} %copy-done.21), kind=kOutput, calls=%fused_computation.183 | convolution fusion | flops 806485248 | bytes 16516608 | tf_op jit(solution)/shard_map/shqk,shkd->sqhd/dot_general | solution.py:223
  301.8 7.0 %fusion.22 = bf16[2,1024,12,64]{1,3,2,0:T(8,128)(2,1)S(1)} fusion(bf16[2,12,256,1024]{3,2,1,0:T(8,128)(2,1)} %multiply_convert_fusion, bf16[2,12,256,64]{2,3,0,1:T(8,128)(2,1)S(1)} %copy-done.32), kind=kOutput, calls=%fused_computation.44 | convolution fusion | flops 808452096 | bytes 16515072 | tf_op jit(solution)/shard_map/shqk,shqd->skhd/dot_general | solution.py:226
  321.3 7.9 %multiply_reduce_fusion.1 = (f32[768]{0:T(1024)S(1)}, f32[768]{0:T(1024)S(1)}, bf16[2048,768]{1,0:T(8,128)(2,1)}, f32[2048,768]{1,0:T(8,128)}) fusion(f32[2048]{0:T(1024)S(1)} %get-tuple-element.90, f32[2048]{0:T(1024)S(1)} %get-tuple-element.91, bf16[2,256,768]{2,1,0:T(8,128)(2,1)S(1)} %copy-done.12, bf16[2,256,768]{2,1,0:T(8,128)(2,1)S(1)} %copy-done.8, ...), kind=kOutput, calls=%fused_computation.25 | convolution fusion | flops 2442656256 | bytes 23228416 | tf_op jit(solution)/shard_map/dot_general | solution.py:40
  329.3 4.7 copy.97
  334.0 6.7 %fusion.63 = bf16[32,24,768]{2,1,0:T(8,128)(2,1)} fusion(bf16[32,24,2048]{2,1,0:T(8,128)(2,1)} %bitcast.237, bf16[2048,768]{0,1:T(8,128)(2,1)} %bitcast.233), kind=kOutput, calls=%fused_computation.91 | convolution fusion | flops 2416508928 | bytes 7471104 | tf_op jit(solution)/shard_map/dot_general | solution.py:34
  357.1 4.9 copy.94
  362.1 7.8 %convolution_convert_fusion = bf16[768,3072]{1,0:T(8,128)(2,1)} fusion(bf16[512,3072]{1,0:T(8,128)(2,1)} %copy-done.36, f32[512,768]{1,0:T(8,128)} %copy-done.14, f32[768]{0:T(1024)S(1)} %reshape.550, f32[768]{0:T(1024)S(1)} %reshape.549, f32[512]{0:T(512)S(1)} %add_rsqrt_fusion.1, f32[512]{0:T(512)S(1)} %broadcast_multiply_fusion.4), kind=kOutput, calls=%fused_computation.36 | convolution fusion | flops 2420244480 | bytes 9447424 | tf_op jit(solution)/shard_map/dot_general | solution.py:34
  369.9 8.5 %convert_element_type.345 = bf16[32,96,768]{2,1,0:T(8,128)(2,1)} reshape(bf16[768,3072]{1,0:T(8,128)(2,1)} %convolution_convert_fusion) | data formatting | bytes 9437184 | tf_op jit(solution)/shard_map/convert_element_type | solution.py:102
  383.9 5.2 pad_maximum_fusion
  389.2 15.0 %reduce-scatter.6.cloned.1.call-done = bf16[1,4,80,768]{3,2,1,0:T(8,128)(2,1)} async-done(((bf16[8,4,80,768]{3,2,1,0:T(8,128)(2,1)}), bf16[1,4,80,768]{3,2,1,0:T(8,128)(2,1)}) %reduce-scatter.6.cloned.1.call-update) | async-done | bytes 491536 | tf_op jit(solution)/shard_map/reduce_scatter | solution.py:107
  404.3 87.9 %reduce-scatter.4.cloned.1.call-done = bf16[1,4,224,768]{3,2,1,0:T(8,128)(2,1)} async-done(((bf16[8,4,224,768]{3,2,1,0:T(8,128)(2,1)}), bf16[1,4,224,768]{3,2,1,0:T(8,128)(2,1)}) %reduce-scatter.4.cloned.1.call-update) | async-done | bytes 1376272 | tf_op jit(solution)/shard_map/reduce_scatter | solution.py:107
  503.6 7.4 %add_convert_fusion.4 = bf16[512,768]{1,0:T(8,128)(2,1)} fusion(f32[512,768]{1,0:T(8,128)S(1)} %copy-done.15, bf16[3072,768]{1,0:T(8,128)(2,1)} %bitcast.221, f32[512,3072]{1,0:T(8,128)} %copy-done.35, f32[3072]{0:T(1024)S(1)} %reshape.551, f32[768]{0:T(1024)S(1)} %reshape.552), kind=kOutput, calls=%fused_computation.86 | convolution fusion | flops 2426535936 | bytes 13384704 | tf_op jit(solution)/shard_map/dot_general | solution.py:30
  511.0 43.5 %collective-permute-done.3 = bf16[2,256,768]{2,1,0:T(8,128)(2,1)S(1)} collective-permute-done((bf16[2,256,768]{2,1,0:T(8,128)(2,1)S(1)}, bf16[2,256,768]{2,1,0:T(8,128)(2,1)S(1)}, u32[]{:S(2)}, u32[]{:S(2)}) %collective-permute-start.3) | collective-permute-done | bytes 786464 | tf_op jit(solution)/shard_map/ppermute | solution.py:244
  554.5 13.8 %collective-permute-done.5 = bf16[2,256,768]{2,1,0:T(8,128)(2,1)S(1)} collective-permute-done((bf16[2,256,768]{2,1,0:T(8,128)(2,1)S(1)}, bf16[2,256,768]{2,1,0:T(8,128)(2,1)S(1)}, u32[]{:S(2)}, u32[]{:S(2)}) %collective-permute-start.5) | collective-permute-done | bytes 786464 | tf_op jit(solution)/shard_map/ppermute | solution.py:244
  568.3 31.5 %collective-permute-done.4 = bf16[2,256,768]{2,1,0:T(8,128)(2,1)S(1)} collective-permute-done((bf16[2,256,768]{2,1,0:T(8,128)(2,1)S(1)}, bf16[2,256,768]{2,1,0:T(8,128)(2,1)S(1)}, u32[]{:S(2)}, u32[]{:S(2)}) %collective-permute-start.4) | collective-permute-done | bytes 786464 | tf_op jit(solution)/shard_map/ppermute | solution.py:244
  (208 shorter events, 105.7 us)
Async XLA Ops:
  7.2 70.4 %copy-start.5 = (bf16[2,256,768]{2,1,0:T(8,128)(2,1)S(1)}, bf16[2,256,768]{2,1,0:T(8,128)(2,1)}, u32[]{:S(2)}) copy-start(bf16[2,256,768]{2,1,0:T(8,128)(2,1)} %param.18) | copy-start | bytes 2359300
  7.2 106.3 %all-gather.5.cloned.1.call-start = ((), (), s32[]{:S(2)}) async-start(), calls=%async_computation.6 | async-start | bytes 4055040 | tf_op jit(solution)/shard_map/all_gather | solution.py:70
  9.6 193.8 %all-gather.7.cloned.1.call-start = ((), (), s32[]{:S(2)}) async-start(), calls=%async_computation.7 | async-start | bytes 11354112 | tf_op jit(solution)/shard_map/all_gather | solution.py:70
  15.9 388.4 %reduce-scatter.6.cloned.1.call-start = ((), (), s32[]{:S(2)}) async-start(), calls=%async_computation.4 | async-start | bytes 4423680 | tf_op jit(solution)/shard_map/reduce_scatter | solution.py:107
  15.9 59.1 %collective-permute-start.1 = (bf16[2,256,768]{2,1,0:T(8,128)(2,1)}, bf16[2,256,768]{2,1,0:T(8,128)(2,1)S(1)}, u32[]{:S(2)}, u32[]{:S(2)}) collective-permute-start(bf16[2,256,768]{2,1,0:T(8,128)(2,1)} %param.18), channel_id=1, source_target_pairs={{0,2},{1,3},{2,0},{3,1},{4,6},{5,7},{6,4},{7,5},{8,10},{9,11},{10,... | collective-permute-start | bytes 2359304 | tf_op jit(solution)/shard_map/ppermute | solution.py:153
  20.1 55.0 %collective-permute-start = (bf16[2,256,768]{2,1,0:T(8,128)(2,1)}, bf16[2,256,768]{2,1,0:T(8,128)(2,1)S(1)}, u32[]{:S(2)}, u32[]{:S(2)}) collective-permute-start(bf16[2,256,768]{2,1,0:T(8,128)(2,1)} %param.18), channel_id=1, source_target_pairs={{0,1},{1,2},{2,3},{3,0},{4,5},{5,6},{6,7},{7,4},{8,9},{9,10},{10,1... | collective-permute-start | bytes 2359304 | tf_op jit(solution)/shard_map/ppermute | solution.py:153
  21.6 54.1 %collective-permute-start.2 = (bf16[2,256,768]{2,1,0:T(8,128)(2,1)}, bf16[2,256,768]{2,1,0:T(8,128)(2,1)S(1)}, u32[]{:S(2)}, u32[]{:S(2)}) collective-permute-start(bf16[2,256,768]{2,1,0:T(8,128)(2,1)} %param.18), channel_id=1, source_target_pairs={{0,3},{1,0},{2,1},{3,2},{4,7},{5,4},{6,5},{7,6},{8,11},{9,8},{10,9... | collective-permute-start | bytes 2359304 | tf_op jit(solution)/shard_map/ppermute | solution.py:153
  75.1 56.4 %copy-start.7 = (bf16[2,256,768]{2,1,0:T(8,128)(2,1)}, bf16[2,256,768]{2,1,0:T(8,128)(2,1)S(1)}, u32[]{:S(2)}) copy-start(bf16[2,256,768]{2,1,0:T(8,128)(2,1)S(1)} %collective-permute-done.1) | copy-start | bytes 2359300
  118.7 9.5 %copy-start.3 = (bf16[32,24,768]{2,1,0:T(8,128)(2,1)}, bf16[32,24,768]{2,1,0:T(8,128)(2,1)S(1)}, u32[]{:S(2)}) copy-start(bf16[32,24,768]{2,1,0:T(8,128)(2,1)S(1)} %get-tuple-element.37) | copy-start | bytes 3538948
  141.0 6.9 %copy-start.31 = (bf16[2,12,256,64]{2,3,0,1:T(8,128)(2,1)}, bf16[2,12,256,64]{2,3,0,1:T(8,128)(2,1)S(1)}, u32[]{:S(2)}) copy-start(bf16[2,12,256,64]{2,3,0,1:T(8,128)(2,1)S(1)} %fusion.76) | copy-start | bytes 2359300
  170.9 11.6 %copy-start.2 = (bf16[2,12,1024,64]{2,3,0,1:T(8,128)(2,1)}, bf16[2,12,1024,64]{2,3,0,1:T(8,128)(2,1)S(1)}, u32[]{:S(2)}) copy-start(bf16[2,12,1024,64]{2,3,0,1:T(8,128)(2,1)S(1)} %fusion.20) | copy-start | bytes 9437188
  183.5 41.1 %copy-start.22 = (bf16[96,8,2,256]{3,1,2,0:T(8,128)(2,1)}, bf16[96,8,2,256]{3,1,2,0:T(8,128)(2,1)S(1)}, u32[]{:S(2)}) copy-start(bf16[96,8,2,256]{3,1,2,0:T(8,128)(2,1)S(1)} %copy.118) | copy-start | bytes 2359300
  226.9 13.3 %copy-start.14 = (f32[512,768]{1,0:T(8,128)}, f32[512,768]{1,0:T(8,128)S(1)}, u32[]{:S(2)}) copy-start(f32[512,768]{1,0:T(8,128)S(1)} %get-tuple-element.74) | copy-start | bytes 4718596
  226.9 5.4 slice-start.2
  227.2 5.1 slice-start.3
  227.2 5.1 copy-start.29
  270.7 21.6 %copy-start.21 = (bf16[2,12,1024,64]{2,3,0,1:T(8,128)(2,1)S(1)}, bf16[2,12,1024,64]{2,3,0,1:T(8,128)(2,1)}, u32[]{:S(2)}) copy-start(bf16[2,12,1024,64]{2,3,0,1:T(8,128)(2,1)} %convert_bitcast_fusion.1) | copy-start | bytes 9437188
  292.3 9.5 %copy-start.32 = (bf16[2,12,256,64]{2,3,0,1:T(8,128)(2,1)S(1)}, bf16[2,12,256,64]{2,3,0,1:T(8,128)(2,1)}, u32[]{:S(2)}) copy-start(bf16[2,12,256,64]{2,3,0,1:T(8,128)(2,1)} %copy-done.31) | copy-start | bytes 2359300
  301.8 7.0 %copy-start.1 = (bf16[2,1024,12,64]{1,3,2,0:T(8,128)(2,1)S(1)}, bf16[2,1024,12,64]{1,3,2,0:T(8,128)(2,1)}, u32[]{:S(2)}) copy-start(bf16[2,1024,12,64]{1,3,2,0:T(8,128)(2,1)} %get-tuple-element.79) | copy-start | bytes 9437188
  313.2 7.8 %copy-start.24 = (bf16[96,8,2,1024]{3,1,2,0:T(8,128)(2,1)}, bf16[96,8,2,1024]{3,1,2,0:T(8,128)(2,1)S(1)}, u32[]{:S(2)}) copy-start(bf16[96,8,2,1024]{3,1,2,0:T(8,128)(2,1)S(1)} %copy.120) | copy-start | bytes 9437188
  334.0 6.7 %copy-start.26 = (bf16[96,8,2,1024]{3,1,2,0:T(8,128)(2,1)S(1)}, bf16[96,8,2,1024]{3,1,2,0:T(8,128)(2,1)}, u32[]{:S(2)}) copy-start(bf16[96,8,2,1024]{3,1,2,0:T(8,128)(2,1)} %copy-done.25) | copy-start | bytes 9437188
  334.0 6.7 %copy-start.27 = (bf16[768,2048]{1,0:T(8,128)(2,1)S(1)}, bf16[768,2048]{1,0:T(8,128)(2,1)}, u32[]{:S(2)}) copy-start(bf16[768,2048]{1,0:T(8,128)(2,1)} %copy.97) | copy-start | bytes 9437188
  344.5 5.3 copy-start
  344.5 5.3 copy-start.4
  355.7 136.5 %reduce-scatter.4.cloned.1.call-start = ((), (), s32[]{:S(2)}) async-start(), calls=%async_computation.3 | async-start | bytes 12386304 | tf_op jit(solution)/shard_map/reduce_scatter | solution.py:107
  378.9 5.0 slice-start
  389.2 106.6 %copy-start.34 = (f32[32,24]{1,0:T(8,128)S(1)}, f32[32,24]{1,0:T(8,128)}, u32[]{:S(2)}) copy-start(f32[32,24]{1,0:T(8,128)} %get-tuple-element.50) | copy-start | bytes 9220
  389.2 214.2 %reduce-scatter.8.cloned.1.call-start = ((), (), s32[]{:S(2)}) async-start(), calls=%async_computation.5 | async-start | bytes 2334720 | tf_op jit(solution)/shard_map/reduce_scatter | solution.py:112
  499.1 55.4 %collective-permute-start.3 = (bf16[2,256,768]{2,1,0:T(8,128)(2,1)S(1)}, bf16[2,256,768]{2,1,0:T(8,128)(2,1)S(1)}, u32[]{:S(2)}, u32[]{:S(2)}) collective-permute-start(bf16[2,256,768]{2,1,0:T(8,128)(2,1)S(1)} %get-tuple-element.41), channel_id=1, source_target_pairs={{0,3},{1,0},{2,1},{3,2},{4,7},{5,4},{6,5},{7,6},{8,11},{9,8},{10,9... | collective-permute-start | bytes 2359304 | tf_op jit(solution)/shard_map/ppermute | solution.py:244
  502.5 65.8 %collective-permute-start.5 = (bf16[2,256,768]{2,1,0:T(8,128)(2,1)S(1)}, bf16[2,256,768]{2,1,0:T(8,128)(2,1)S(1)}, u32[]{:S(2)}, u32[]{:S(2)}) collective-permute-start(bf16[2,256,768]{2,1,0:T(8,128)(2,1)S(1)} %get-tuple-element.42), channel_id=1, source_target_pairs={{0,1},{1,2},{2,3},{3,0},{4,5},{5,6},{6,7},{7,4},{8,9},{9,10},{10,1... | collective-permute-start | bytes 2359304 | tf_op jit(solution)/shard_map/ppermute | solution.py:244
  502.5 97.3 %copy-start.13 = (f32[512,768]{1,0:T(8,128)S(1)}, f32[512,768]{1,0:T(8,128)}, u32[]{:S(2)}) copy-start(f32[512,768]{1,0:T(8,128)} %get-tuple-element.83) | copy-start | bytes 4718596
  502.5 97.3 %collective-permute-start.4 = (bf16[2,256,768]{2,1,0:T(8,128)(2,1)S(1)}, bf16[2,256,768]{2,1,0:T(8,128)(2,1)S(1)}, u32[]{:S(2)}, u32[]{:S(2)}) collective-permute-start(bf16[2,256,768]{2,1,0:T(8,128)(2,1)S(1)} %get-tuple-element.43), channel_id=1, source_target_pairs={{0,2},{1,3},{2,0},{3,1},{4,6},{5,7},{6,4},{7,5},{8,10},{9,11},{10,... | collective-permute-start | bytes 2359304 | tf_op jit(solution)/shard_map/ppermute | solution.py:244
  (20 other events, 59.3 us)
Sparse Core Ops, SparseCore 0:
  11.4 102.1 all-gather.4
  116.3 87.0 all-gather.6
  355.8 48.4 reduce-scatter.5
  407.7 84.4 reduce-scatter.3
  495.2 75.0 reduce-scatter.7

commit v13 on v12

--- a/solution.py
+++ b/solution.py
@@ -176,12 +176,13 @@
     kh = project(all_rows, wk).astype(jnp.bfloat16)
     vh = (project(all_rows, wv) + f32(bv).reshape(H, 1, HD)).astype(jnp.bfloat16)
     scale = HD ** (-0.5)
-    scores = jnp.einsum("shqd,shkd->shqk", qh, kh, preferred_element_type=jnp.float32) * scale
+    qh_scaled = qh * jnp.asarray(scale, jnp.bfloat16)
+    scores = jnp.einsum("shqd,shkd->shqk", qh_scaled, kh, preferred_element_type=jnp.float32)
     valid = positions[None, :] < lengths[:, None]
     scores = jnp.where(valid[:, None, None, :], scores, -1e30)
     top = jnp.max(scores, axis=-1, keepdims=True)
     expd = jnp.exp(scores - top)
-    probs = expd * (1.0 / jnp.sum(expd, axis=-1, keepdims=True))
+    probs = expd / jnp.sum(expd, axis=-1, keepdims=True)
     low_probs = probs.astype(jnp.bfloat16)
     mixed = jnp.einsum("shqk,shkd->sqhd", low_probs, vh, preferred_element_type=jnp.float32)
     mixed = mixed.reshape(n, width).astype(jnp.bfloat16)
@@ -223,7 +224,7 @@
     d_q = jnp.einsum("shqk,shkd->sqhd", d_scores, kh, preferred_element_type=jnp.float32) * scale
     d_q = d_q.reshape(n, width).astype(jnp.bfloat16)
     k_part = (
-        jnp.einsum("shqk,shqd->skhd", d_scores, qh, preferred_element_type=jnp.float32) * scale
+        jnp.einsum("shqk,shqd->skhd", d_scores, qh_scaled, preferred_element_type=jnp.float32)
     ).reshape(seqs * total, width).astype(jnp.bfloat16)
     v_part = jnp.einsum("shqk,sqhd->skhd", low_probs, d_mixed, preferred_element_type=jnp.float32)
     v_part = v_part.reshape(seqs * total, width).astype(jnp.bfloat16)

time: 627 us -> 630 us (level)
  no operation moved by 1% of the time
where the time goes in v13:
time: 630 us; the launch traced here: 620 us
  waiting for transfers between devices  296 us (47%)
  matrix products  154 us (24%)
  local copies, waits for them, and re-layouts  88.4 us (14%)
  other arithmetic  54.4 us (9%)
  between operations  15.1 us (2%)
  starting transfers between devices  12.6 us (2%)
    reduce_scatter x2, waiting for transfers between devices, dp_stage(): return lax.psum_scatter(packed, 'dp', scatter_dimension=0, tiled=True)  103 us
    ppermute x3, waiting for transfers between devices, layer(): lax.ppermute(sent, 'ctx', [(i, (i - b) % n_ctx) for i in range(n_ctx)])  88.8 us
    all_gather x2, waiting for transfers between devices, gather_all(): full = lax.all_gather(packed[None], ALL, axis=0, tiled=True)  54.2 us
    ppermute x3, waiting for transfers between devices, layer(): lax.ppermute(inputs, 'ctx', [(i, (i + b) % n_ctx) for i in range(n_ctx)])  50.4 us
    dot_general x6, matrix products, outer(): lax.dot_general(left_rows, right_rows, (((0,), (0,)), ((), ())), preferre...  26.1 us
    dot_general x6, matrix products, back(): lax.dot_general(grad_rows, weight, (((1,), (1,)), ((), ())), preferred_el...  25.6 us
    convert_element_type x1, other arithmetic, layer(): d_scores = (probs * (d_probs - inner)).astype(jnp.bfloat16)  21.5 us
    dot_general x3, matrix products, layer(): jnp.einsum('snd,dhe->shne', a, heads(w), preferred_element_type=jnp.float32)  17.5 us
  transfers between devices with their start and end apart: 11, of which 9 were waited for; matrix products, arithmetic and copies ran while one was open for 21% of the time, Pallas kernels for 0%

profile of v13, /device:TPU:0, one launch (start us, length us, event | category | flops | bytes accessed | tf_op | source)
XLA Modules:
  0.0 620.5 jit_solution(9434580247503037976)
XLA Ops:
  25.3 49.8 %collective-permute-done.1 = bf16[2,256,768]{2,1,0:T(8,128)(2,1)S(1)} collective-permute-done((bf16[2,256,768]{2,1,0:T(8,128)(2,1)}, bf16[2,256,768]{2,1,0:T(8,128)(2,1)S(1)}, u32[]{:S(2)}, u32[]{:S(2)}) %collective-permute-start.1) | collective-permute-done | bytes 786464 | tf_op jit(solution)/shard_map/ppermute | solution.py:153
  80.1 33.5 %all-gather.5.cloned.1.call-done = bf16[2560,768]{1,0:T(8,128)(2,1)} async-done(((bf16[80,768]{1,0:T(8,128)(2,1)}), bf16[2560,768]{1,0:T(8,128)(2,1)}) %all-gather.5.cloned.1.call-update) | async-done | bytes 3932176 | tf_op jit(solution)/shard_map/all_gather | solution.py:70
  123.1 4.7 reshape_reshape.11
  127.8 4.8 reshape_reshape.9
  141.4 6.5 %convert_bitcast_fusion.2 = bf16[2,12,1024,64]{2,3,0,1:T(8,128)(2,1)} fusion(bf16[2,1024,768]{2,1,0:T(8,128)(2,1)S(1)} %copy-done.16, bf16[768,12,64,1]{2,1,0,3:T(8,128)(2,1)S(1)} %bitcast.243), kind=kOutput, calls=%fused_computation.56 | convolution fusion | flops 2417491968 | bytes 7471104 | tf_op jit(solution)/shard_map/snd,dhe->shne/dot_general | solution.py:172
  148.0 7.3 %fusion.23 = bf16[2,12,1024,64]{2,3,0,1:T(8,128)(2,1)} fusion(f32[12,64]{1,0:T(8,128)S(1)} %copy-done.45, bf16[2,1024,768]{2,1,0:T(8,128)(2,1)S(1)} %copy-done.16, bf16[768,12,64,1]{2,1,0,3:T(8,128)(2,1)S(1)} %bitcast.242), kind=kOutput, calls=%fused_computation.42 | convolution fusion | flops 2419064832 | bytes 7474176 | tf_op jit(solution)/shard_map/snd,dhe->shne/dot_general | solution.py:172
  155.3 14.8 %fusion.134 = (f32[2,12,256]{2,1,0:T(8,128)S(1)}, f32[2,12,256,1024]{3,2,1,0:T(8,128)}) fusion(pred[2,1024]{1,0:T(4,128)(4,1)S(1)} %copy-done.50, bf16[2,12,1024,64]{2,3,0,1:T(8,128)(2,1)} %convert_bitcast_fusion.2, bf16[2,12,256,64]{2,3,0,1:T(8,128)(2,1)S(1)} %fusion.90), kind=kOutput, calls=%fused_computation.179 | convolution fusion | flops 824181760 | bytes 29124608 | tf_op jit(solution)/shard_map/sub | solution.py:184
  170.1 11.7 %fusion.79 = bf16[2,256,12,64]{1,3,2,0:T(8,128)(2,1)S(1)} fusion(bf16[2,12,1024,64]{2,3,0,1:T(8,128)(2,1)} %fusion.23, f32[2,12,256,1024]{3,2,1,0:T(8,128)} %get-tuple-element.72, f32[2,12,256]{2,1,0:T(8,128)S(1)} %get-tuple-element.71), kind=kOutput, calls=%fused_computation.98 | convolution fusion | flops 818282496 | bytes 29122560 | tf_op jit(solution)/shard_map/shqk,shkd->sqhd/dot_general | solution.py:187
  182.8 20.7 %all-gather.7.cloned.1.call-done = bf16[7168,768]{1,0:T(8,128)(2,1)} async-done(((bf16[224,768]{1,0:T(8,128)(2,1)}), bf16[7168,768]{1,0:T(8,128)(2,1)}) %all-gather.7.cloned.1.call-update) | async-done | bytes 11010064 | tf_op jit(solution)/shard_map/all_gather | solution.py:70
  206.7 8.4 %fusion.128 = (bf16[32,96,768]{2,1,0:T(8,128)(2,1)}, bf16[32,96,768]{2,1,0:T(8,128)(2,1)}) fusion(bf16[32,224,768]{2,1,0:T(8,128)(2,1)} %bitcast.215), kind=kLoop, calls=%fused_computation.173 | loop fusion | bytes 18874368 | tf_op jit(solution)/shard_map/slice | solution.py:75
  215.4 8.5 %reshape.512 = bf16[768,3072]{1,0:T(8,128)(2,1)} reshape(bf16[32,96,768]{2,1,0:T(8,128)(2,1)} %get-tuple-element.33) | data formatting | bytes 9437184 | tf_op jit(solution)/shard_map/reshape | solution.py:75
  226.8 5.0 fusion.20
  231.8 5.1 fusion.146
  242.5 11.4 %fusion.144 = (bf16[12,64]{1,0:T(8,128)(2,1)S(1)}, bf16[2,1024,12,64]{1,3,2,0:T(8,128)(2,1)}) fusion(f32[2,12,256,1024]{3,2,1,0:T(8,128)} %get-tuple-element.72, f32[2,12,256]{2,1,0:T(8,128)S(1)} %get-tuple-element.71, bf16[2,256,12,64]{1,0,3,2:T(2,128)(2,1)S(1)} %reshape.516), kind=kOutput, calls=%fused_computation.181 | convolution fusion | flops 821034240 | bytes 29124096 | tf_op jit(solution)/shard_map/shqk,sqhd->skhd/dot_general | solution.py:229
  254.0 16.6 %multiply_reduce_fusion = (f32[2,12,256]{2,1,0:T(8,128)S(1)}, f32[2,12,256,1024]{3,2,1,0:T(8,128)}) fusion(f32[2,12,256,1024]{3,2,1,0:T(8,128)} %get-tuple-element.72, f32[2,12,256]{2,1,0:T(8,128)S(1)} %get-tuple-element.71, bf16[2,12,1024,64]{2,3,0,1:T(8,128)(2,1)} %fusion.23, bf16[2,256,12,64]{1,0,3,2:T(2,128)(2,1)S(1)} %reshape.516), kind=kOutput, calls=%fused_computation.2 | convolution fusion | flops 824174592 | bytes 54312960 | tf_op jit(solution)/shard_map/sqhd,shkd->shqk/dot_general | solution.py:221
  270.5 21.5 %multiply_convert_fusion = bf16[2,12,256,1024]{3,2,1,0:T(8,128)(2,1)} fusion(f32[2,12,256,1024]{3,2,1,0:T(8,128)} %get-tuple-element.77, f32[2,12,256]{2,1,0:T(8,128)S(1)} %get-tuple-element.76, f32[2,12,256,1024]{3,2,1,0:T(8,128)} %get-tuple-element.72, f32[2,12,256]{2,1,0:T(8,128)S(1)} %get-tuple-element.71), kind=kLoop, calls=%fused_computation.1 | loop fusion | flops 25165824 | bytes 62963712 | tf_op jit(solution)/shard_map/convert_element_type | solution.py:223
  292.1 9.5 %fusion.145 = (bf16[12,64]{1,0:T(8,128)(2,1)S(1)}, bf16[2,256,12,64]{1,3,2,0:T(8,128)(2,1)}) fusion(bf16[2,12,256,1024]{3,2,1,0:T(8,128)(2,1)} %multiply_convert_fusion, bf16[2,12,1024,64]{2,3,0,1:T(8,128)(2,1)S(1)} %copy-done.20), kind=kOutput, calls=%fused_computation.182 | convolution fusion | flops 806485248 | bytes 16516608 | tf_op jit(solution)/shard_map/shqk,shkd->sqhd/dot_general | solution.py:224
  301.6 7.0 %convert_bitcast_fusion.1 = bf16[2,1024,12,64]{1,3,2,0:T(8,128)(2,1)S(1)} fusion(bf16[2,12,256,1024]{3,2,1,0:T(8,128)(2,1)} %multiply_convert_fusion, bf16[2,12,256,64]{2,3,0,1:T(8,128)(2,1)S(1)} %copy-done.33), kind=kOutput, calls=%fused_computation.54 | convolution fusion | flops 806879232 | bytes 16515072 | tf_op jit(solution)/shard_map/shqk,shqd->skhd/dot_general | solution.py:227
  317.8 4.6 fusion.147
  322.5 10.1 %multiply_reduce_fusion.1 = (f32[768]{0:T(1024)S(1)}, f32[768]{0:T(1024)S(1)}, bf16[2048,768]{1,0:T(8,128)(2,1)}, f32[2048,768]{1,0:T(8,128)}) fusion(f32[2048]{0:T(1024)S(1)} %copy-done.46, f32[2048]{0:T(1024)S(1)} %copy-done.47, bf16[2,256,768]{2,1,0:T(8,128)(2,1)S(1)} %copy-done.11, bf16[2,256,768]{2,1,0:T(8,128)(2,1)S(1)} %copy-done.6, ...), kind=kOutput, calls=%fused_computation.24 | convolution fusion | flops 2442656256 | bytes 23228416 | tf_op jit(solution)/shard_map/dot_general | solution.py:40
  332.6 4.8 copy.97
  337.4 6.7 %fusion.67 = bf16[32,24,768]{2,1,0:T(8,128)(2,1)} fusion(bf16[32,24,2048]{2,1,0:T(8,128)(2,1)} %bitcast.237, bf16[2048,768]{0,1:T(8,128)(2,1)} %bitcast.233), kind=kOutput, calls=%fused_computation.91 | convolution fusion | flops 2416508928 | bytes 7471104 | tf_op jit(solution)/shard_map/dot_general | solution.py:34
  360.5 4.9 copy.94
  365.5 7.8 %convolution_convert_fusion = bf16[768,3072]{1,0:T(8,128)(2,1)} fusion(bf16[512,3072]{1,0:T(8,128)(2,1)} %copy-done.52, f32[512,768]{1,0:T(8,128)} %copy-done.13, f32[768]{0:T(1024)S(1)} %copy-done.49, f32[768]{0:T(1024)S(1)} %reshape.546, f32[512]{0:T(512)S(1)} %add_rsqrt_fusion.1, f32[512]{0:T(512)S(1)} %broadcast_multiply_fusion.4), kind=kOutput, calls=%fused_computation.38 | convolution fusion | flops 2420244480 | bytes 9447424 | tf_op jit(solution)/shard_map/dot_general | solution.py:34
  373.4 8.5 %convert_element_type.342 = bf16[32,96,768]{2,1,0:T(8,128)(2,1)} reshape(bf16[768,3072]{1,0:T(8,128)(2,1)} %convolution_convert_fusion) | data formatting | bytes 9437184 | tf_op jit(solution)/shard_map/convert_element_type | solution.py:102
  387.4 5.2 pad_maximum_fusion
  392.7 14.9 %reduce-scatter.6.cloned.1.call-done = bf16[1,4,80,768]{3,2,1,0:T(8,128)(2,1)} async-done(((bf16[8,4,80,768]{3,2,1,0:T(8,128)(2,1)}), bf16[1,4,80,768]{3,2,1,0:T(8,128)(2,1)}) %reduce-scatter.6.cloned.1.call-update) | async-done | bytes 491536 | tf_op jit(solution)/shard_map/reduce_scatter | solution.py:107
  407.6 87.9 %reduce-scatter.4.cloned.1.call-done = bf16[1,4,224,768]{3,2,1,0:T(8,128)(2,1)} async-done(((bf16[8,4,224,768]{3,2,1,0:T(8,128)(2,1)}), bf16[1,4,224,768]{3,2,1,0:T(8,128)(2,1)}) %reduce-scatter.4.cloned.1.call-update) | async-done | bytes 1376272 | tf_op jit(solution)/shard_map/reduce_scatter | solution.py:107
  507.0 7.3 %add_convert_fusion.4 = bf16[512,768]{1,0:T(8,128)(2,1)} fusion(f32[512,768]{1,0:T(8,128)S(1)} %copy-done.14, bf16[3072,768]{1,0:T(8,128)(2,1)} %bitcast.221, f32[512,3072]{1,0:T(8,128)} %copy-done.51, f32[3072]{0:T(1024)S(1)} %copy-done.43, f32[768]{0:T(1024)S(1)} %reshape.549), kind=kOutput, calls=%fused_computation.86 | convolution fusion | flops 2426535936 | bytes 13384704 | tf_op jit(solution)/shard_map/dot_general | solution.py:30
  514.3 43.4 %collective-permute-done.3 = bf16[2,256,768]{2,1,0:T(8,128)(2,1)S(1)} collective-permute-done((bf16[2,256,768]{2,1,0:T(8,128)(2,1)S(1)}, bf16[2,256,768]{2,1,0:T(8,128)(2,1)S(1)}, u32[]{:S(2)}, u32[]{:S(2)}) %collective-permute-start.3) | collective-permute-done | bytes 786464 | tf_op jit(solution)/shard_map/ppermute | solution.py:245
  557.7 14.0 %collective-permute-done.5 = bf16[2,256,768]{2,1,0:T(8,128)(2,1)S(1)} collective-permute-done((bf16[2,256,768]{2,1,0:T(8,128)(2,1)S(1)}, bf16[2,256,768]{2,1,0:T(8,128)(2,1)S(1)}, u32[]{:S(2)}, u32[]{:S(2)}) %collective-permute-start.5) | collective-permute-done | bytes 786464 | tf_op jit(solution)/shard_map/ppermute | solution.py:245
  571.7 31.5 %collective-permute-done.4 = bf16[2,256,768]{2,1,0:T(8,128)(2,1)S(1)} collective-permute-done((bf16[2,256,768]{2,1,0:T(8,128)(2,1)S(1)}, bf16[2,256,768]{2,1,0:T(8,128)(2,1)S(1)}, u32[]{:S(2)}, u32[]{:S(2)}) %collective-permute-start.4) | collective-permute-done | bytes 786464 | tf_op jit(solution)/shard_map/ppermute | solution.py:245
  (239 shorter events, 107.1 us)
Async XLA Ops:
  7.2 70.4 %copy-start.3 = (bf16[2,256,768]{2,1,0:T(8,128)(2,1)S(1)}, bf16[2,256,768]{2,1,0:T(8,128)(2,1)}, u32[]{:S(2)}) copy-start(bf16[2,256,768]{2,1,0:T(8,128)(2,1)} %param.18) | copy-start | bytes 2359300
  7.2 106.3 %all-gather.5.cloned.1.call-start = ((), (), s32[]{:S(2)}) async-start(), calls=%async_computation.6 | async-start | bytes 4055040 | tf_op jit(solution)/shard_map/all_gather | solution.py:70
  9.6 193.8 %all-gather.7.cloned.1.call-start = ((), (), s32[]{:S(2)}) async-start(), calls=%async_computation.7 | async-start | bytes 11354112 | tf_op jit(solution)/shard_map/all_gather | solution.py:70
  15.9 391.8 %reduce-scatter.6.cloned.1.call-start = ((), (), s32[]{:S(2)}) async-start(), calls=%async_computation.4 | async-start | bytes 4423680 | tf_op jit(solution)/shard_map/reduce_scatter | solution.py:107
  15.9 59.1 %collective-permute-start.1 = (bf16[2,256,768]{2,1,0:T(8,128)(2,1)}, bf16[2,256,768]{2,1,0:T(8,128)(2,1)S(1)}, u32[]{:S(2)}, u32[]{:S(2)}) collective-permute-start(bf16[2,256,768]{2,1,0:T(8,128)(2,1)} %param.18), channel_id=1, source_target_pairs={{0,2},{1,3},{2,0},{3,1},{4,6},{5,7},{6,4},{7,5},{8,10},{9,11},{10,... | collective-permute-start | bytes 2359304 | tf_op jit(solution)/shard_map/ppermute | solution.py:153
  20.1 55.0 %collective-permute-start = (bf16[2,256,768]{2,1,0:T(8,128)(2,1)}, bf16[2,256,768]{2,1,0:T(8,128)(2,1)S(1)}, u32[]{:S(2)}, u32[]{:S(2)}) collective-permute-start(bf16[2,256,768]{2,1,0:T(8,128)(2,1)} %param.18), channel_id=1, source_target_pairs={{0,1},{1,2},{2,3},{3,0},{4,5},{5,6},{6,7},{7,4},{8,9},{9,10},{10,1... | collective-permute-start | bytes 2359304 | tf_op jit(solution)/shard_map/ppermute | solution.py:153
  21.6 54.1 %collective-permute-start.2 = (bf16[2,256,768]{2,1,0:T(8,128)(2,1)}, bf16[2,256,768]{2,1,0:T(8,128)(2,1)S(1)}, u32[]{:S(2)}, u32[]{:S(2)}) collective-permute-start(bf16[2,256,768]{2,1,0:T(8,128)(2,1)} %param.18), channel_id=1, source_target_pairs={{0,3},{1,0},{2,1},{3,2},{4,7},{5,4},{6,5},{7,6},{8,11},{9,8},{10,9... | collective-permute-start | bytes 2359304 | tf_op jit(solution)/shard_map/ppermute | solution.py:153
  75.1 57.5 %copy-start.5 = (bf16[2,256,768]{2,1,0:T(8,128)(2,1)}, bf16[2,256,768]{2,1,0:T(8,128)(2,1)S(1)}, u32[]{:S(2)}) copy-start(bf16[2,256,768]{2,1,0:T(8,128)(2,1)S(1)} %collective-permute-done.1) | copy-start | bytes 2359300
  75.1 57.5 %copy-start.7 = (bf16[2,256,768]{2,1,0:T(8,128)(2,1)}, bf16[2,256,768]{2,1,0:T(8,128)(2,1)S(1)}, u32[]{:S(2)}) copy-start(bf16[2,256,768]{2,1,0:T(8,128)(2,1)S(1)} %collective-permute-done) | copy-start | bytes 2359300
  115.5 17.1 %copy-start.36 = (f32[768]{0:T(1024)}, f32[768]{0:T(1024)S(1)}, u32[]{:S(2)}) copy-start(f32[768]{0:T(1024)S(1)} %reshape.541) | copy-start | bytes 9220
  115.6 17.0 %copy-start.40 = (f32[768]{0:T(1024)}, f32[768]{0:T(1024)S(1)}, u32[]{:S(2)}) copy-start(f32[768]{0:T(1024)S(1)} %reshape.542) | copy-start | bytes 9220
  119.9 7.9 %copy-start.1 = (bf16[32,24,768]{2,1,0:T(8,128)(2,1)}, bf16[32,24,768]{2,1,0:T(8,128)(2,1)S(1)}, u32[]{:S(2)}) copy-start(bf16[32,24,768]{2,1,0:T(8,128)(2,1)S(1)} %get-tuple-element.35) | copy-start | bytes 3538948
  141.1 14.2 %copy-start.32 = (bf16[2,12,256,64]{2,3,0,1:T(8,128)(2,1)}, bf16[2,12,256,64]{2,3,0,1:T(8,128)(2,1)S(1)}, u32[]{:S(2)}) copy-start(bf16[2,12,256,64]{2,3,0,1:T(8,128)(2,1)S(1)} %fusion.90) | copy-start | bytes 2359300
  148.0 7.3 %copy-start.50 = (pred[2,1024]{1,0:T(4,128)(4,1)S(1)}, pred[2,1024]{1,0:T(4,128)(4,1)}, u32[]{:S(2)}) copy-start(pred[2,1024]{1,0:T(4,128)(4,1)} %broadcast_compare_fusion) | copy-start | bytes 6148
  182.8 41.1 %copy-start.21 = (bf16[96,8,2,256]{3,1,2,0:T(8,128)(2,1)}, bf16[96,8,2,256]{3,1,2,0:T(8,128)(2,1)S(1)}, u32[]{:S(2)}) copy-start(bf16[96,8,2,256]{3,1,2,0:T(8,128)(2,1)S(1)} %copy.118) | copy-start | bytes 2359300
  206.6 17.2 %copy-start.34 = (bf16[32,24,768]{2,1,0:T(8,128)(2,1)}, bf16[32,24,768]{2,1,0:T(8,128)(2,1)S(1)}, u32[]{:S(2)}) copy-start(bf16[32,24,768]{2,1,0:T(8,128)(2,1)S(1)} %slice.209) | copy-start | bytes 3538948
  215.1 16.6 %copy-start.42 = (f32[3072]{0:T(1024)}, f32[3072]{0:T(1024)S(1)}, u32[]{:S(2)}) copy-start(f32[3072]{0:T(1024)S(1)} %reshape.548) | copy-start | bytes 36868
  215.3 9.9 %copy-start.48 = (f32[768]{0:T(1024)}, f32[768]{0:T(1024)S(1)}, u32[]{:S(2)}) copy-start(f32[768]{0:T(1024)S(1)} %reshape.547) | copy-start | bytes 9220
  224.8 15.1 %copy-start.13 = (f32[512,768]{1,0:T(8,128)}, f32[512,768]{1,0:T(8,128)S(1)}, u32[]{:S(2)}) copy-start(f32[512,768]{1,0:T(8,128)S(1)} %get-tuple-element.74) | copy-start | bytes 4718596
  224.8 6.9 %slice-start.2 = ((s8[4718592]{0:T(1024)(128)(4,1)}), s8[4194304]{0:T(1024)(128)(4,1)S(1)}, s32[]{:S(2)}) async-start(s8[4718592]{0:T(1024)(128)(4,1)} %bitcast.222), calls=%async_computation.10 | async-start | bytes 8388608
  270.5 21.6 %copy-start.20 = (bf16[2,12,1024,64]{2,3,0,1:T(8,128)(2,1)S(1)}, bf16[2,12,1024,64]{2,3,0,1:T(8,128)(2,1)}, u32[]{:S(2)}) copy-start(bf16[2,12,1024,64]{2,3,0,1:T(8,128)(2,1)} %convert_bitcast_fusion.2) | copy-start | bytes 9437188
  292.1 9.5 %copy-start.33 = (bf16[2,12,256,64]{2,3,0,1:T(8,128)(2,1)S(1)}, bf16[2,12,256,64]{2,3,0,1:T(8,128)(2,1)}, u32[]{:S(2)}) copy-start(bf16[2,12,256,64]{2,3,0,1:T(8,128)(2,1)} %copy-done.32) | copy-start | bytes 2359300
  301.6 7.1 %copy-start.26 = (bf16[2,1024,12,64]{1,3,2,0:T(8,128)(2,1)S(1)}, bf16[2,1024,12,64]{1,3,2,0:T(8,128)(2,1)}, u32[]{:S(2)}) copy-start(bf16[2,1024,12,64]{1,3,2,0:T(8,128)(2,1)} %get-tuple-element.79) | copy-start | bytes 9437188
  313.0 9.4 %copy-start.23 = (bf16[96,8,2,1024]{3,1,2,0:T(8,128)(2,1)}, bf16[96,8,2,1024]{3,1,2,0:T(8,128)(2,1)S(1)}, u32[]{:S(2)}) copy-start(bf16[96,8,2,1024]{3,1,2,0:T(8,128)(2,1)S(1)} %copy.120) | copy-start | bytes 9437188
  337.4 6.7 %copy-start.27 = (bf16[768,2048]{1,0:T(8,128)(2,1)S(1)}, bf16[768,2048]{1,0:T(8,128)(2,1)}, u32[]{:S(2)}) copy-start(bf16[768,2048]{1,0:T(8,128)(2,1)} %copy.97) | copy-start | bytes 9437188
  359.1 136.5 %reduce-scatter.4.cloned.1.call-start = ((), (), s32[]{:S(2)}) async-start(), calls=%async_computation.3 | async-start | bytes 12386304 | tf_op jit(solution)/shard_map/reduce_scatter | solution.py:107
  392.6 106.5 %copy-start.38 = (f32[32,24]{1,0:T(8,128)S(1)}, f32[32,24]{1,0:T(8,128)}, u32[]{:S(2)}) copy-start(f32[32,24]{1,0:T(8,128)} %get-tuple-element.50) | copy-start | bytes 9220
  392.7 214.1 %reduce-scatter.8.cloned.1.call-start = ((), (), s32[]{:S(2)}) async-start(), calls=%async_computation.5 | async-start | bytes 2334720 | tf_op jit(solution)/shard_map/reduce_scatter | solution.py:112
  502.5 55.2 %collective-permute-start.3 = (bf16[2,256,768]{2,1,0:T(8,128)(2,1)S(1)}, bf16[2,256,768]{2,1,0:T(8,128)(2,1)S(1)}, u32[]{:S(2)}, u32[]{:S(2)}) collective-permute-start(bf16[2,256,768]{2,1,0:T(8,128)(2,1)S(1)} %get-tuple-element.41), channel_id=1, source_target_pairs={{0,3},{1,0},{2,1},{3,2},{4,7},{5,4},{6,5},{7,6},{8,11},{9,8},{10,9... | collective-permute-start | bytes 2359304 | tf_op jit(solution)/shard_map/ppermute | solution.py:245
  505.9 65.8 %collective-permute-start.5 = (bf16[2,256,768]{2,1,0:T(8,128)(2,1)S(1)}, bf16[2,256,768]{2,1,0:T(8,128)(2,1)S(1)}, u32[]{:S(2)}, u32[]{:S(2)}) collective-permute-start(bf16[2,256,768]{2,1,0:T(8,128)(2,1)S(1)} %get-tuple-element.42), channel_id=1, source_target_pairs={{0,1},{1,2},{2,3},{3,0},{4,5},{5,6},{6,7},{7,4},{8,9},{9,10},{10,1... | collective-permute-start | bytes 2359304 | tf_op jit(solution)/shard_map/ppermute | solution.py:245
  505.9 97.3 %copy-start.12 = (f32[512,768]{1,0:T(8,128)S(1)}, f32[512,768]{1,0:T(8,128)}, u32[]{:S(2)}) copy-start(f32[512,768]{1,0:T(8,128)} %get-tuple-element.83) | copy-start | bytes 4718596
  505.9 97.3 %collective-permute-start.4 = (bf16[2,256,768]{2,1,0:T(8,128)(2,1)S(1)}, bf16[2,256,768]{2,1,0:T(8,128)(2,1)S(1)}, u32[]{:S(2)}, u32[]{:S(2)}) collective-permute-start(bf16[2,256,768]{2,1,0:T(8,128)(2,1)S(1)} %get-tuple-element.43), channel_id=1, source_target_pairs={{0,2},{1,3},{2,0},{3,1},{4,6},{5,7},{6,4},{7,5},{8,10},{9,11},{10,... | collective-permute-start | bytes 2359304 | tf_op jit(solution)/shard_map/ppermute | solution.py:245
  (36 other events, 154.2 us)
Sparse Core Ops, SparseCore 0:
  11.4 102.1 all-gather.4
  116.3 87.0 all-gather.6
  359.2 48.4 reduce-scatter.5
  411.1 84.4 reduce-scatter.3
  498.6 75.0 reduce-scatter.7
